TPU v7x, 256 devices: a whole 4x4x8 slice. The times are simulated.
256 devices in a mesh: tm: 128 (over z, x_lo, y, core), head: 2 (over x_hi).
Axes of the slice: x: 4 (x_hi: 2, x_lo: 2; x = x_hi * 2 + x_lo), y: 4, z: 8, core: 2. Of those that a mesh axis runs over, the one named last changes fastest.
Arguments:
- queries: bfloat16 [32768, 2048], P('tm', 'head'), may hold values from -48 to 48
- keys: bfloat16 [32768, 2048], P('tm', 'head'), may hold values from -6 to 6
- values_in: bfloat16 [32768, 2048], P('tm', 'head'), may hold values from -32 to 32
- teacher: bfloat16 [32768, 2048], P('tm', 'head'), may hold values from -6 to 6
- gain: float32 [2048], P('head'), may hold values from 0.25 to 1.75
- conv_weight: float32 [4, 2048], P(None, 'head'), may hold values from -3 to 3
- block_bits: int32 [256, 6], P('tm'), may hold values from 0 to 1, as said below
- mask_pos: int32 [256, 64], P('tm'), may hold values from 0 to 127, as said below
Outputs:
- query_grad: bfloat16 [32768, 2048], P('tm', 'head')
- key_grad: bfloat16 [32768, 2048], P('tm', 'head')
- value_grad: bfloat16 [32768, 2048], P('tm', 'head')
- conv_grad: float32 [4, 2048], P(None, 'head')
Inputs may be any that keep to these rules, and one draw needn't show every extreme that they name: `block_bits`: column 0 of every row is 1. `mask_pos`: each row names 64 different positions.
All inputs are finite; a program needn't handle non-finite values.
Results may differ from a plain program's by a relative error of at most 0.0095.
Values may be sent and summed in bfloat16 or wider, within the bound.
No kernel may reach another device: no remote copies, remote signals or barrier semaphores. Data moves between devices by JAX's collectives and lax.ppermute only.
A program may use at most 64 MiB of HBM per device.

v0:
```python
from functools import reduce

import jax
import jax.numpy as jnp
from jax import lax
from jax.sharding import PartitionSpec as P

D = 2048
HD = 128
BLK = 128
REACH = 3


NEG_FILL = -1e30
NORM_EPS = 1e-06


def from_behind(block, axis, distance):
    devices = range(lax.axis_size(axis))
    route = [(i - distance, i) for i in devices if i - distance in devices]
    return lax.ppermute(block, axis, route)


def split_heads(array):
    return array.reshape(array.shape[0], array.shape[1] // HD, HD)


def pair_mask(block_bits, device, distance, row_count):
    per_device = row_count // BLK
    window = block_bits.shape[1]
    block_index = jnp.arange(per_device, dtype=jnp.int32)
    relative = distance * per_device + block_index[:, None] - block_index[None, :]
    one_hot = relative[:, :, None] == jnp.arange(window, dtype=jnp.int32)[None, None, :]
    picked_bits = jnp.sum(jnp.where(one_hot, block_bits[:, None, :], 0), axis=2)
    coarse_mask = (picked_bits > 0) & (relative < window)
    fine_mask = jnp.repeat(jnp.repeat(coarse_mask, BLK, axis=0), BLK, axis=1)
    offsets = jnp.arange(row_count, dtype=jnp.int32)
    causal = (distance > 0) | (offsets[None, :] <= offsets[:, None])
    return fine_mask & causal & (device >= distance)


def body(queries, keys, values_in, teacher, gain, conv_weight, block_bits, mask_pos):
    row_count, channels = queries.shape
    tap_count = conv_weight.shape[0]
    rim_rows = tap_count - 1
    device = lax.axis_index("tm")
    score_scale = HD ** (-0.5)
    prior = from_behind(values_in[row_count - rim_rows :], "tm", 1)
    extended = jnp.concatenate([prior, values_in], 0).astype(jnp.float32)
    conv_sum = jnp.zeros((row_count, channels), jnp.float32)
    for tap_index in range(tap_count):
        conv_sum = (
            conv_sum
            + conv_weight[tap_index]
            * extended[rim_rows - tap_index : rim_rows - tap_index + row_count]
        )
    values = conv_sum.astype(jnp.bfloat16)
    blocks = [(keys, values)]
    for distance in range(1, REACH + 1):
        moved_keys, moved_values = from_behind((keys, values), "tm", distance)
        blocks.append((moved_keys, moved_values))
    heads_query = split_heads(queries)
    pair_masks = [
        pair_mask(block_bits, device, distance, row_count) for distance in range(REACH + 1)
    ]
    scores = []
    for distance in range(REACH + 1):
        raw_scores = (
            jnp.einsum(
                "thd,uhd->htu",
                heads_query,
                split_heads(blocks[distance][0]),
                preferred_element_type=jnp.float32,
            )
            * score_scale
        )
        scores.append(jnp.where(pair_masks[distance][None], raw_scores, NEG_FILL))
    row_peak = reduce(jnp.maximum, [jnp.max(block_scores, axis=2) for block_scores in scores])
    expos = [
        jnp.where(pair_masks[distance][None], jnp.exp(scores[distance] - row_peak[..., None]), 0.0)
        for distance in range(REACH + 1)
    ]
    row_total = reduce(jnp.add, [jnp.sum(expo_block, axis=2) for expo_block in expos])
    probs = [expo_block / row_total[..., None] for expo_block in expos]
    attended = jnp.zeros((row_count, channels // HD, HD), jnp.float32)
    for distance in range(REACH + 1):
        weights = probs[distance].astype(jnp.bfloat16)
        attended = attended + jnp.einsum(
            "htu,uhd->thd",
            weights,
            split_heads(blocks[distance][1]),
            preferred_element_type=jnp.float32,
        )
    flattened = attended.reshape(row_count, channels)
    squares = lax.psum(jnp.sum(flattened * flattened, axis=1), "head")
    inverse = lax.rsqrt(squares / D + NORM_EPS)
    prediction = flattened * inverse[:, None] * gain
    position = jnp.arange(row_count, dtype=jnp.int32) % BLK
    chosen = jnp.any(jnp.repeat(mask_pos, BLK, axis=0) == position[:, None], axis=1)
    residual = jnp.where(chosen[:, None], prediction - teacher.astype(jnp.float32), 0.0)
    scaled = residual * gain
    cross_term = lax.psum(jnp.sum(scaled * flattened, axis=1), "head")
    out_grad = (
        inverse[:, None] * scaled - flattened * (inverse**3 * cross_term / D)[:, None]
    ).astype(jnp.bfloat16)
    heads_grad = split_heads(out_grad)
    delta = jnp.sum(heads_grad.astype(jnp.float32) * attended, axis=2).T
    query_acc = jnp.zeros((row_count, channels // HD, HD), jnp.float32)
    partials = []
    for distance in range(REACH + 1):
        block_keys, block_values = blocks[distance]
        prob = probs[distance]
        prob_grad = jnp.einsum(
            "thd,uhd->htu",
            heads_grad,
            split_heads(block_values),
            preferred_element_type=jnp.float32,
        )
        score_grad = (prob * (prob_grad - delta[:, :, None])).astype(jnp.bfloat16)
        query_acc = (
            query_acc
            + jnp.einsum(
                "htu,uhd->thd",
                score_grad,
                split_heads(block_keys),
                preferred_element_type=jnp.float32,
            )
            * score_scale
        )
        key_part = (
            jnp.einsum("htu,thd->uhd", score_grad, heads_query, preferred_element_type=jnp.float32)
            * score_scale
        )
        value_part = jnp.einsum(
            "htu,thd->uhd",
            prob.astype(jnp.bfloat16),
            heads_grad,
            preferred_element_type=jnp.float32,
        )
        partials.append(
            (key_part.reshape(row_count, channels), value_part.reshape(row_count, channels))
        )
    key_acc, value_acc = partials[0]
    for distance in range(1, REACH + 1):
        back_keys, back_values = (
            from_behind(partials[distance][0].astype(jnp.bfloat16), "tm", -distance).astype(
                jnp.float32
            ),
            from_behind(partials[distance][1].astype(jnp.bfloat16), "tm", -distance).astype(
                jnp.float32
            ),
        )
        key_acc = key_acc + back_keys
        value_acc = value_acc + back_values
    following = from_behind(value_acc[:rim_rows], "tm", -1)
    padded_acc = jnp.concatenate([value_acc, following], 0)
    value_sum = jnp.zeros((row_count, channels), jnp.float32)
    for tap_index in range(tap_count):
        value_sum = (
            value_sum + conv_weight[tap_index] * padded_acc[tap_index : tap_index + row_count]
        )
    local_taps = jnp.stack(
        [
            jnp.sum(
                value_acc * extended[rim_rows - tap_index : rim_rows - tap_index + row_count],
                axis=0,
            )
            for tap_index in range(tap_count)
        ]
    )
    conv_grad = lax.psum(local_taps, "tm")
    return (
        query_acc.reshape(row_count, channels).astype(jnp.bfloat16),
        key_acc.astype(jnp.bfloat16),
        value_sum.astype(jnp.bfloat16),
        conv_grad,
    )


def solution(mesh):
    placed = (
        P("tm", "head"),
        P("tm", "head"),
        P("tm", "head"),
        P("tm", "head"),
        P("head"),
        P(None, "head"),
        P("tm", None),
        P("tm", None),
    )
    return jax.shard_map(
        body,
        mesh=mesh,
        in_specs=placed,
        out_specs=(P("tm", "head"), P("tm", "head"), P("tm", "head"), P(None, "head")),
        check_vma=False,
    )
```

profile of v0, /device:TPU:4, one launch (start us, length us, event | category | flops | bytes accessed | tf_op | source)
XLA Modules:
  0.0 762.9 jit_solution(11530021563278397573)
XLA Ops:
  1.9 3.0 collective-permute-start.2
  4.8 4.3 collective-permute-start.1
  9.2 3.0 collective-permute-start
  21.6 19.1 %collective-permute-start.5 = (bf16[256,1024]{1,0:T(8,128)(2,1)}, bf16[256,1024]{1,0:T(8,128)(2,1)}, u32[]{:S(2)}, u32[]{:S(2)}) collective-permute-start(bf16[256,1024]{1,0:T(8,128)(2,1)} %add_convert_fusion.1), channel_id=1, source_target_pairs={{0,4},{2,6},{4,8},{6,10},{8,12},{10,14},{12,16},{14,18},{16,20},{1... | collective-permute-start | bytes 1572872 | tf_op jit(solution)/shard_map/ppermute | solution.py:21
  40.7 2.1 collective-permute-start.4
  43.3 3.1 collective-permute-start.6
  47.0 2.0 fusion.2
  49.6 2.1 fusion.7
  53.5 10.2 %collective-permute-done.6 = bf16[256,1024]{1,0:T(8,128)(2,1)} collective-permute-done((bf16[256,1024]{1,0:T(8,128)(2,1)}, bf16[256,1024]{1,0:T(8,128)(2,1)}, u32[]{:S(2)}, u32[]{:S(2)}) %collective-permute-start.6) | collective-permute-done | bytes 524320 | tf_op jit(solution)/shard_map/ppermute | solution.py:21
  65.0 3.6 fusion.34
  69.9 3.8 convolution_add_fusion.3
  75.0 4.2 fusion.28
  79.2 6.6 psum.21
  88.9 6.6 psum.22
  95.5 2.2 subtract_convert_fusion
  100.6 3.4 convolution_convert_fusion.2
  104.0 2.1 multiply_convert_fusion.2
  106.1 1.9 multiply_convert_fusion.1
  109.7 1.9 multiply_convert_fusion
  117.0 2.1 copy.197
  119.0 2.0 copy.200
  121.1 2.0 copy.202
  127.5 2.5 fusion.17
  130.0 2.6 fusion.16
  132.6 2.1 copy.191
  134.7 2.1 copy.194
  143.8 2.2 fusion.18
  146.0 39.0 %collective-permute-done.12 = bf16[256,1024]{1,0:T(8,128)(2,1)S(1)} collective-permute-done((bf16[256,1024]{1,0:T(8,128)(2,1)}, bf16[256,1024]{1,0:T(8,128)(2,1)S(1)}, u32[]{:S(2)}, u32[]{:S(2)}) %collective-permute-start.12) | collective-permute-done | bytes 524320 | tf_op jit(solution)/shard_map/ppermute | solution.py:21
  191.0 2.0 copy.203
  193.1 2.2 multiply_reduce_fusion.3
  196.6 2.5 add_convert_fusion
  199.1 562.6 %psum.23 = f32[4,1024]{1,0:T(4,128)} all-reduce(f32[4,1024]{1,0:T(4,128)S(1)} %pad_maximum_fusion.1), channel_id=1, replica_groups=mesh['tm'=128,'head'=2] {'tm'}, use_global_device_ids=true, to_apply=%region_22.23 | all-reduce | flops 4096 | bytes 32768 | tf_op jit(solution)/shard_map/psum | solution.py:171
  (149 shorter events, 50.5 us)
Async XLA Ops:
  1.9 47.1 %collective-permute-start.2 = (bf16[256,1024]{0,1:T(8,128)(2,1)S(1)}, bf16[256,1024]{0,1:T(8,128)(2,1)S(1)}, u32[]{:S(2)}, u32[]{:S(2)}) collective-permute-start(bf16[256,1024]{0,1:T(8,128)(2,1)S(1)} %copy.234), channel_id=1, source_target_pairs={{0,6},{2,8},{4,10},{6,12},{8,14},{10,16},{12,18},{14,20},{16,22},{... | collective-permute-start | bytes 1572872 | tf_op jit(solution)/shard_map/ppermute | solution.py:21
  4.8 42.1 %collective-permute-start.1 = (bf16[256,1024]{0,1:T(8,128)(2,1)S(1)}, bf16[256,1024]{0,1:T(8,128)(2,1)}, u32[]{:S(2)}, u32[]{:S(2)}) collective-permute-start(bf16[256,1024]{0,1:T(8,128)(2,1)S(1)} %copy.234), channel_id=1, source_target_pairs={{0,4},{2,6},{4,8},{6,10},{8,12},{10,14},{12,16},{14,18},{16,20},{1... | collective-permute-start | bytes 1572872 | tf_op jit(solution)/shard_map/ppermute | solution.py:21
  9.2 34.1 %collective-permute-start = (bf16[256,1024]{0,1:T(8,128)(2,1)S(1)}, bf16[256,1024]{0,1:T(8,128)(2,1)S(1)}, u32[]{:S(2)}, u32[]{:S(2)}) collective-permute-start(bf16[256,1024]{0,1:T(8,128)(2,1)S(1)} %copy.234), channel_id=1, source_target_pairs={{0,2},{2,4},{4,6},{6,8},{8,10},{10,12},{12,14},{14,16},{16,18},{18... | collective-permute-start | bytes 1572872 | tf_op jit(solution)/shard_map/ppermute | solution.py:21
  12.9 7.0 collective-permute-start.3
  19.7 32.0 %copy-start = (f32[8,256,256]{1,2,0:T(8,128)}, f32[8,256,256]{1,2,0:T(8,128)S(1)}, u32[]{:S(2)}) copy-start(f32[8,256,256]{1,2,0:T(8,128)S(1)} %get-tuple-element.38) | copy-start | bytes 6291460
  21.6 52.2 %collective-permute-start.5 = (bf16[256,1024]{1,0:T(8,128)(2,1)}, bf16[256,1024]{1,0:T(8,128)(2,1)}, u32[]{:S(2)}, u32[]{:S(2)}) collective-permute-start(bf16[256,1024]{1,0:T(8,128)(2,1)} %add_convert_fusion.1), channel_id=1, source_target_pairs={{0,4},{2,6},{4,8},{6,10},{8,12},{10,14},{12,16},{14,18},{16,20},{1... | collective-permute-start | bytes 1572872 | tf_op jit(solution)/shard_map/ppermute | solution.py:21
  40.7 28.0 %collective-permute-start.4 = (bf16[256,1024]{1,0:T(8,128)(2,1)}, bf16[256,1024]{1,0:T(8,128)(2,1)}, u32[]{:S(2)}, u32[]{:S(2)}) collective-permute-start(bf16[256,1024]{1,0:T(8,128)(2,1)} %add_convert_fusion.1), channel_id=1, source_target_pairs={{0,2},{2,4},{4,6},{6,8},{8,10},{10,12},{12,14},{14,16},{16,18},{18... | collective-permute-start | bytes 1572872 | tf_op jit(solution)/shard_map/ppermute | solution.py:21
  43.2 8.5 %copy-start.21 = (bf16[32,8,8,128]{3,2,1,0:T(8,128)(2,1)}, bf16[32,8,8,128]{3,2,1,0:T(8,128)(2,1)S(1)}, u32[]{:S(2)}) copy-start(bf16[32,8,8,128]{3,2,1,0:T(8,128)(2,1)S(1)} %fusion.102) | copy-start | bytes 1572868
  43.3 5.7 copy-start.16
  43.3 20.5 %collective-permute-start.6 = (bf16[256,1024]{1,0:T(8,128)(2,1)}, bf16[256,1024]{1,0:T(8,128)(2,1)}, u32[]{:S(2)}, u32[]{:S(2)}) collective-permute-start(bf16[256,1024]{1,0:T(8,128)(2,1)} %add_convert_fusion.1), channel_id=1, source_target_pairs={{0,6},{2,8},{4,10},{6,12},{8,14},{10,16},{12,18},{14,20},{16,22},{... | collective-permute-start | bytes 1572872 | tf_op jit(solution)/shard_map/ppermute | solution.py:21
  48.9 2.7 copy-start.4
  65.0 3.6 copy-start.23
  69.9 3.8 copy-start.25
  75.0 4.2 copy-start.27
  79.2 8.1 %copy-start.30 = (f32[1024]{0:T(1024)S(1)}, f32[1024]{0:T(1024)}, u32[]{:S(2)}) copy-start(f32[1024]{0:T(1024)} %param.12) | copy-start | bytes 12292
  99.0 4.9 copy-start.18
  100.5 3.4 copy-start.3
  100.5 3.4 copy-start.26
  130.0 13.4 %copy-start.10 = (bf16[8,256,256]{1,2,0:T(8,128)(2,1)S(1)}, bf16[8,256,256]{1,2,0:T(8,128)(2,1)}, u32[]{:S(2)}) copy-start(bf16[8,256,256]{1,2,0:T(8,128)(2,1)} %multiply_convert_fusion) | copy-start | bytes 3145732
  130.0 13.4 %copy-start.15 = (bf16[256,1024]{0,1:T(8,128)(2,1)S(1)}, bf16[256,1024]{0,1:T(8,128)(2,1)}, u32[]{:S(2)}) copy-start(bf16[256,1024]{0,1:T(8,128)(2,1)} %copy-done.14) | copy-start | bytes 1572868
  136.8 7.0 copy-start.11
  136.8 7.0 copy-start.13
  136.8 59.8 %collective-permute-start.9 = (bf16[256,1024]{1,0:T(8,128)(2,1)}, bf16[256,1024]{1,0:T(8,128)(2,1)}, u32[]{:S(2)}, u32[]{:S(2)}) collective-permute-start(bf16[256,1024]{1,0:T(8,128)(2,1)} %copy.194), channel_id=1, source_target_pairs={{6,0},{8,2},{10,4},{12,6},{14,8},{16,10},{18,12},{20,14},{22,16},{... | collective-permute-start | bytes 1572872 | tf_op jit(solution)/shard_map/ppermute | solution.py:21
  138.2 58.4 %collective-permute-start.8 = (bf16[256,1024]{1,0:T(8,128)(2,1)}, bf16[256,1024]{1,0:T(8,128)(2,1)}, u32[]{:S(2)}, u32[]{:S(2)}) collective-permute-start(bf16[256,1024]{1,0:T(8,128)(2,1)} %copy.191), channel_id=1, source_target_pairs={{4,0},{6,2},{8,4},{10,6},{12,8},{14,10},{16,12},{18,14},{20,16},{2... | collective-permute-start | bytes 1572872 | tf_op jit(solution)/shard_map/ppermute | solution.py:21
  139.5 45.5 %collective-permute-start.12 = (bf16[256,1024]{1,0:T(8,128)(2,1)}, bf16[256,1024]{1,0:T(8,128)(2,1)S(1)}, u32[]{:S(2)}, u32[]{:S(2)}) collective-permute-start(bf16[256,1024]{1,0:T(8,128)(2,1)} %copy.202), channel_id=1, source_target_pairs={{6,0},{8,2},{10,4},{12,6},{14,8},{16,10},{18,12},{20,14},{22,16},{... | collective-permute-start | bytes 1572872 | tf_op jit(solution)/shard_map/ppermute | solution.py:21
  140.8 52.3 %collective-permute-start.11 = (bf16[256,1024]{1,0:T(8,128)(2,1)}, bf16[256,1024]{1,0:T(8,128)(2,1)}, u32[]{:S(2)}, u32[]{:S(2)}) collective-permute-start(bf16[256,1024]{1,0:T(8,128)(2,1)} %copy.200), channel_id=1, source_target_pairs={{4,0},{6,2},{8,4},{10,6},{12,8},{14,10},{16,12},{18,14},{20,16},{2... | collective-permute-start | bytes 1572872 | tf_op jit(solution)/shard_map/ppermute | solution.py:21
  142.1 51.0 %collective-permute-start.10 = (bf16[256,1024]{1,0:T(8,128)(2,1)}, bf16[256,1024]{1,0:T(8,128)(2,1)}, u32[]{:S(2)}, u32[]{:S(2)}) collective-permute-start(bf16[256,1024]{1,0:T(8,128)(2,1)} %copy.197), channel_id=1, source_target_pairs={{2,0},{4,2},{6,4},{8,6},{10,8},{12,10},{14,12},{16,14},{18,16},{20... | collective-permute-start | bytes 1572872 | tf_op jit(solution)/shard_map/ppermute | solution.py:21
  143.7 42.8 %copy-start.9 = (bf16[8,256,256]{1,2,0:T(8,128)(2,1)S(1)}, bf16[8,256,256]{1,2,0:T(8,128)(2,1)}, u32[]{:S(2)}) copy-start(bf16[8,256,256]{1,2,0:T(8,128)(2,1)} %multiply_convert_fusion.3) | copy-start | bytes 3145732
  185.0 3.0 copy-start.29
  185.0 11.6 %collective-permute-start.7 = (bf16[256,1024]{1,0:T(8,128)(2,1)}, bf16[256,1024]{1,0:T(8,128)(2,1)}, u32[]{:S(2)}, u32[]{:S(2)}) collective-permute-start(bf16[256,1024]{1,0:T(8,128)(2,1)} %copy.187), channel_id=1, source_target_pairs={{2,0},{4,2},{6,4},{8,6},{10,8},{12,10},{14,12},{16,14},{18,16},{20... | collective-permute-start | bytes 1572872 | tf_op jit(solution)/shard_map/ppermute | solution.py:21
  193.1 3.5 copy-start.8
  195.2 566.4 %collective-permute-start.13 = (f32[3,1024]{1,0:T(4,128)S(1)}, f32[3,1024]{1,0:T(4,128)S(1)}, u32[]{:S(2)}, u32[]{:S(2)}) collective-permute-start(f32[3,1024]{1,0:T(4,128)S(1)} %slice.64), channel_id=1, source_target_pairs={{2,0},{4,2},{6,4},{8,6},{10,8},{12,10},{14,12},{16,14},{18,16},{20... | collective-permute-start | bytes 36872 | tf_op jit(solution)/shard_map/ppermute | solution.py:21
  (14 other events, 27.2 us)
where the time goes:
time: 776 us; the launch traced here: 763 us
  blocking collectives  576 us (74%)
  waiting for transfers between devices  49.2 us (6%)
  starting transfers between devices  45.8 us (6%)
  matrix products  45.7 us (6%)
  local copies, waits for them, and re-layouts  28.4 us (4%)
  other arithmetic  16.7 us (2%)
    psum x1, blocking collectives, body(): conv_grad = lax.psum(local_taps, 'tm')  563 us
    ppermute x14, waiting for transfers between devices, from_behind(): return lax.ppermute(block, axis, route)  49.2 us
    ppermute x14, starting transfers between devices, from_behind(): return lax.ppermute(block, axis, route)  45.8 us
  transfers between devices with their start and end apart: 14, of which 2 were waited for; matrix products, arithmetic and copies ran while one was open for 5% of the time, Pallas kernels for 0%

commit v1 on v0

--- a/solution.py
+++ b/solution.py
@@ -19,6 +19,17 @@
     devices = range(lax.axis_size(axis))
     route = [(i - distance, i) for i in devices if i - distance in devices]
     return lax.ppermute(block, axis, route)
+
+
+def all_sum(block, axis):
+    size = lax.axis_size(axis)
+    if size & (size - 1):
+        return lax.psum(block, axis)
+    stride = 1
+    while stride < size:
+        block = block + lax.ppermute(block, axis, [(i, i ^ stride) for i in range(size)])
+        stride *= 2
+    return block
 
 
 def split_heads(array):
@@ -168,7 +179,7 @@
             for tap_index in range(tap_count)
         ]
     )
-    conv_grad = lax.psum(local_taps, "tm")
+    conv_grad = all_sum(local_taps, "tm")
     return (
         query_acc.reshape(row_count, channels).astype(jnp.bfloat16),
         key_acc.astype(jnp.bfloat16),

time: 776 us -> 241 us (0.31); the launches traced: 763 us -> 239 us
  blocking collectives: 576 us -> 13.2 us
  starting transfers between devices: 45.8 us -> 90.7 us
    psum x1 -> x0, blocking collectives: 563 us -> none  [body(): conv_grad = lax.psum(local_taps, 'tm')]
    ppermute x0 -> x7, starting transfers between devices: none -> 45.1 us  [all_sum(): lax.ppermute(block, axis, [(i, i ^ stride) for i in range(size)])]
    ppermute x14, waiting for transfers between devices: 49.2 us -> 18.5 us  [from_behind(): return lax.ppermute(block, axis, route)]
    ppermute x0 -> x7, waiting for transfers between devices: none -> 27.7 us  [all_sum(): lax.ppermute(block, axis, [(i, i ^ stride) for i in range(size)])]
  transfers between devices with their start and end apart: 14 -> 21, of which waited for: 2 -> 7; matrix products, arithmetic and copies ran while one was open for 5% -> 20% of each run, Pallas kernels for 0% -> 0%
where the time goes in v1:
time: 241 us; the launch traced here: 239 us
  starting transfers between devices  90.7 us (38%)
  waiting for transfers between devices  46.2 us (19%)
  matrix products  44 us (18%)
  local copies, waits for them, and re-layouts  26.4 us (11%)
  other arithmetic  17.3 us (7%)
  blocking collectives  13.2 us (5%)
    ppermute x14, starting transfers between devices, from_behind(): return lax.ppermute(block, axis, route)  45.6 us
    ppermute x7, starting transfers between devices, all_sum(): lax.ppermute(block, axis, [(i, i ^ stride) for i in range(size)])  45.1 us
    ppermute x7, waiting for transfers between devices, all_sum(): lax.ppermute(block, axis, [(i, i ^ stride) for i in range(size)])  27.7 us
    ppermute x14, waiting for transfers between devices, from_behind(): return lax.ppermute(block, axis, route)  18.5 us
    dot_general x4, matrix products, body(): jnp.einsum('htu,uhd->thd', weights, split_heads(blocks[distance][1]), pre...  13.4 us
    dot_general x4, matrix products, body(): jnp.einsum('thd,uhd->htu', heads_grad, split_heads(block_values), preferr...  8.49 us
    dot_general x4, matrix products, body(): jnp.einsum('htu,thd->uhd', prob.astype(jnp.bfloat16), heads_grad, preferr...  8.28 us
    psum x1, blocking collectives, body(): cross_term = lax.psum(jnp.sum(scaled * flattened, axis=1), 'head')  6.63 us
  transfers between devices with their start and end apart: 21, of which 7 were waited for; matrix products, arithmetic and copies ran while one was open for 20% of the time, Pallas kernels for 0%

profile of v1, /device:TPU:4, one launch (start us, length us, event | category | flops | bytes accessed | tf_op | source)
XLA Modules:
  0.0 239.1 jit_solution(3024737920199653043)
XLA Ops:
  1.9 3.0 %collective-permute-start.2 = (bf16[256,1024]{0,1:T(8,128)(2,1)S(1)}, bf16[256,1024]{0,1:T(8,128)(2,1)S(1)}, u32[]{:S(2)}, u32[]{:S(2)}) collective-permute-start(bf16[256,1024]{0,1:T(8,128)(2,1)S(1)} %copy.234), channel_id=1, source_target_pairs={{0,6},{2,8},{4,10},{6,12},{8,14},{10,16},{12,18},{14,20},{16,22},{... | collective-permute-start | bytes 1572872 | tf_op jit(solution)/shard_map/ppermute | solution.py:21
  4.8 4.3 %collective-permute-start.1 = (bf16[256,1024]{0,1:T(8,128)(2,1)S(1)}, bf16[256,1024]{0,1:T(8,128)(2,1)}, u32[]{:S(2)}, u32[]{:S(2)}) collective-permute-start(bf16[256,1024]{0,1:T(8,128)(2,1)S(1)} %copy.234), channel_id=1, source_target_pairs={{0,4},{2,6},{4,8},{6,10},{8,12},{10,14},{12,16},{14,18},{16,20},{1... | collective-permute-start | bytes 1572872 | tf_op jit(solution)/shard_map/ppermute | solution.py:21
  9.2 3.0 %collective-permute-start = (bf16[256,1024]{0,1:T(8,128)(2,1)S(1)}, bf16[256,1024]{0,1:T(8,128)(2,1)S(1)}, u32[]{:S(2)}, u32[]{:S(2)}) collective-permute-start(bf16[256,1024]{0,1:T(8,128)(2,1)S(1)} %copy.234), channel_id=1, source_target_pairs={{0,2},{2,4},{4,6},{6,8},{8,10},{10,12},{12,14},{14,16},{16,18},{18... | collective-permute-start | bytes 1572872 | tf_op jit(solution)/shard_map/ppermute | solution.py:21
  21.6 19.1 %collective-permute-start.5 = (bf16[256,1024]{1,0:T(8,128)(2,1)}, bf16[256,1024]{1,0:T(8,128)(2,1)}, u32[]{:S(2)}, u32[]{:S(2)}) collective-permute-start(bf16[256,1024]{1,0:T(8,128)(2,1)} %add_convert_fusion.1), channel_id=1, source_target_pairs={{0,4},{2,6},{4,8},{6,10},{8,12},{10,14},{12,16},{14,18},{16,20},{1... | collective-permute-start | bytes 1572872 | tf_op jit(solution)/shard_map/ppermute | solution.py:21
  40.6 2.1 collective-permute-start.4
  43.3 3.1 %collective-permute-start.6 = (bf16[256,1024]{1,0:T(8,128)(2,1)}, bf16[256,1024]{1,0:T(8,128)(2,1)}, u32[]{:S(2)}, u32[]{:S(2)}) collective-permute-start(bf16[256,1024]{1,0:T(8,128)(2,1)} %add_convert_fusion.1), channel_id=1, source_target_pairs={{0,6},{2,8},{4,10},{6,12},{8,14},{10,16},{12,18},{14,20},{16,22},{... | collective-permute-start | bytes 1572872 | tf_op jit(solution)/shard_map/ppermute | solution.py:21
  49.6 2.1 fusion.7
  53.5 10.2 %collective-permute-done.6 = bf16[256,1024]{1,0:T(8,128)(2,1)} collective-permute-done((bf16[256,1024]{1,0:T(8,128)(2,1)}, bf16[256,1024]{1,0:T(8,128)(2,1)}, u32[]{:S(2)}, u32[]{:S(2)}) %collective-permute-start.6) | collective-permute-done | bytes 524320 | tf_op jit(solution)/shard_map/ppermute | solution.py:21
  65.0 3.6 %fusion.34 = f32[8,128,256]{2,1,0:T(8,128)} fusion(bf16[256,8,128]{0,2,1:T(8,128)(2,1)S(1)} %bitcast.180, f32[8,256,256]{1,2,0:T(8,128)} %copy-done.6, f32[8,256]{1,0:T(8,128)S(1)} %add_add_fusion, f32[8,256]{1,0:T(8,128)S(1)} %maximum_maximum_fusion, pred[256,256]{0,1:T(8,128)(4,1)S(1)} %bitcast.175), kind=kOutput, calls=%fused_computation.73 | convolution fusion | flops 137363456 | bytes 3751936 | tf_op jit(solution)/shard_map/htu,uhd->thd/dot_general | solution.py:99
  69.9 3.8 %convolution_add_fusion.3 = f32[8,128,256]{2,1,0:T(8,128)} fusion(f32[8,128,256]{2,1,0:T(8,128)} %fusion.30, bf16[256,8,128]{0,2,1:T(8,128)(2,1)S(1)} %bitcast.182, f32[8,256,256]{1,2,0:T(8,128)} %copy-done.4, f32[8,256]{1,0:T(8,128)S(1)} %add_add_fusion, f32[8,256]{1,0:T(8,128)S(1)} %maximum_maximum_fusion, pred[256,256]{0,1:T(8,128)(4,1)S(1)} %bitcast.170), kind=kOutput, calls=%fused_computation.36 | convolution fusion | flops 137625600 | bytes 4800512 | tf_op jit(solution)/shard_map/htu,uhd->thd/dot_general | solution.py:99
  75.0 4.2 %fusion.28 = (f32[256]{0:T(256)S(1)}, f32[8,128,256]{2,1,0:T(8,128)}) fusion(f32[8,128,256]{2,1,0:T(8,128)} %fusion.34, f32[8,128,256]{2,1,0:T(8,128)} %convolution_add_fusion.3, bf16[256,8,128]{0,2,1:T(8,128)(2,1)S(1)} %bitcast.178, f32[8,256]{1,0:T(8,128)S(1)} %add_add_fusion, f32[8,256]{1,0:T(8,128)S(1)} %maximum_maximum_fusion, ...), kind=kOutput, calls=%fused_computation.56 | convolution fusion | flops 138411776 | bytes 5850112 | tf_op jit(solution)/shard_map/htu,uhd->thd/dot_general | solution.py:99
  79.2 6.6 %psum.14 = f32[256]{0:T(256)S(1)} all-reduce(f32[256]{0:T(256)S(1)} %get-tuple-element.41), channel_id=1, replica_groups=mesh['tm'=128,'head'=2] {'head'}, use_global_device_ids=true, to_apply=%region_13.14 | all-reduce | flops 256 | bytes 2048 | tf_op jit(solution)/shard_map/psum | solution.py:106
  88.8 6.6 %psum.15 = f32[256]{0:T(256)S(1)} all-reduce(f32[256]{0:T(256)S(1)} %multiply_reduce_fusion.4), channel_id=1, replica_groups=mesh['tm'=128,'head'=2] {'head'}, use_global_device_ids=true, to_apply=%region_16.17 | all-reduce | flops 256 | bytes 2048 | tf_op jit(solution)/shard_map/psum | solution.py:113
  95.5 2.2 subtract_convert_fusion
  100.5 3.4 %convolution_convert_fusion.2 = bf16[8,128,256]{2,1,0:T(8,128)(2,1)} fusion(bf16[256,8,128]{0,2,1:T(8,128)(2,1)S(1)} %bitcast.150, f32[8,256,256]{1,2,0:T(8,128)} %copy-done.4, f32[8,256]{1,0:T(8,128)S(1)} %add_add_fusion, f32[8,256]{1,0:T(8,128)S(1)} %maximum_maximum_fusion, pred[256,256]{0,1:T(8,128)(4,1)S(1)} %bitcast.171), kind=kOutput, calls=%fused_computation.43 | convolution fusion | flops 137625600 | bytes 3227648 | tf_op jit(solution)/shard_map/htu,thd->uhd/dot_general | solution.py:145
  105.6 2.1 multiply_convert_fusion.2
  129.4 2.6 %copy.198 = f32[256,1024]{1,0:T(8,128)} copy(f32[256,1024]{0,1:T(8,128)} %bitcast.162) | data formatting | bytes 2097152 | tf_op jit(solution)/shard_map/reshape | solution.py:152
  132.1 2.6 %multiply_convert_fusion.1 = bf16[8,256,256]{1,2,0:T(8,128)(2,1)S(1)} fusion(bf16[256,8,128]{0,2,1:T(8,128)(2,1)S(1)} %bitcast.157, bf16[256,8,128]{0,2,1:T(8,128)(2,1)S(1)} %bitcast.179, f32[8,256]{1,0:T(8,128)S(1)} %bitcast.214, f32[8,256]{1,0:T(8,128)S(1)} %add_add_fusion, f32[8,256]{1,0:T(8,128)S(1)} %maximum_maximum_fusion, ...), kind=kOutput, calls=%fused_computation.1 | convolution fusion | flops 138412032 | bytes 4284416 | tf_op jit(solution)/shard_map/thd,uhd->htu/dot_general | solution.py:124
  134.7 2.7 %collective-permute-done.12 = bf16[256,1024]{1,0:T(8,128)(2,1)} collective-permute-done((bf16[256,1024]{1,0:T(8,128)(2,1)}, bf16[256,1024]{1,0:T(8,128)(2,1)}, u32[]{:S(2)}, u32[]{:S(2)}) %collective-permute-start.12) | collective-permute-done | bytes 524320 | tf_op jit(solution)/shard_map/ppermute | solution.py:21
  137.4 5.6 %collective-permute-done.11 = bf16[256,1024]{1,0:T(8,128)(2,1)} collective-permute-done((bf16[256,1024]{1,0:T(8,128)(2,1)}, bf16[256,1024]{1,0:T(8,128)(2,1)}, u32[]{:S(2)}, u32[]{:S(2)}) %collective-permute-start.11) | collective-permute-done | bytes 524320 | tf_op jit(solution)/shard_map/ppermute | solution.py:21
  142.9 2.1 multiply_reduce_fusion.3
  145.0 13.1 %collective-permute-start.14 = (f32[4,1024]{1,0:T(4,128)S(1)}, f32[4,1024]{1,0:T(4,128)S(1)}, u32[]{:S(2)}, u32[]{:S(2)}) collective-permute-start(f32[4,1024]{1,0:T(4,128)S(1)} %pad_maximum_fusion.1), channel_id=1, source_target_pairs={{0,2},{2,0},{4,6},{6,4},{8,10},{10,8},{12,14},{14,12},{16,18},{18,... | collective-permute-start | bytes 49160 | tf_op jit(solution)/shard_map/ppermute | solution.py:30
  160.5 2.4 %collective-permute-done.15 = f32[4,1024]{1,0:T(4,128)S(1)} collective-permute-done((f32[4,1024]{1,0:T(4,128)S(1)}, f32[4,1024]{1,0:T(4,128)S(1)}, u32[]{:S(2)}, u32[]{:S(2)}) %collective-permute-start.15) | collective-permute-done | bytes 16416 | tf_op jit(solution)/shard_map/ppermute | solution.py:30
  162.9 12.6 %collective-permute-start.16 = (f32[4,1024]{1,0:T(4,128)S(1)}, f32[4,1024]{1,0:T(4,128)S(1)}, u32[]{:S(2)}, u32[]{:S(2)}) collective-permute-start(f32[4,1024]{1,0:T(4,128)S(1)} %fusion.103), channel_id=1, source_target_pairs={{0,8},{2,10},{4,12},{6,14},{8,0},{10,2},{12,4},{14,6},{16,24},{18,... | collective-permute-start | bytes 49160 | tf_op jit(solution)/shard_map/ppermute | solution.py:30
  182.9 6.9 %collective-permute-start.17 = (f32[4,1024]{1,0:T(4,128)S(1)}, f32[4,1024]{1,0:T(4,128)S(1)}, u32[]{:S(2)}, u32[]{:S(2)}) collective-permute-start(f32[4,1024]{1,0:T(4,128)S(1)} %add.188), channel_id=1, source_target_pairs={{0,16},{2,18},{4,20},{6,22},{8,24},{10,26},{12,28},{14,30},{16,0},... | collective-permute-start | bytes 49160 | tf_op jit(solution)/shard_map/ppermute | solution.py:30
  189.8 2.3 fusion.18
  192.1 21.0 %collective-permute-done.17 = f32[4,1024]{1,0:T(4,128)S(1)} collective-permute-done((f32[4,1024]{1,0:T(4,128)S(1)}, f32[4,1024]{1,0:T(4,128)S(1)}, u32[]{:S(2)}, u32[]{:S(2)}) %collective-permute-start.17) | collective-permute-done | bytes 16416 | tf_op jit(solution)/shard_map/ppermute | solution.py:30
  213.2 3.4 %collective-permute-start.18 = (f32[4,1024]{1,0:T(4,128)S(1)}, f32[4,1024]{1,0:T(4,128)S(1)}, u32[]{:S(2)}, u32[]{:S(2)}) collective-permute-start(f32[4,1024]{1,0:T(4,128)S(1)} %add.189), channel_id=1, source_target_pairs={{0,32},{2,34},{4,36},{6,38},{8,40},{10,42},{12,44},{14,46},{16,48}... | collective-permute-start | bytes 49160 | tf_op jit(solution)/shard_map/ppermute | solution.py:30
  222.0 6.3 %collective-permute-start.19 = (f32[4,1024]{1,0:T(4,128)S(1)}, f32[4,1024]{1,0:T(4,128)S(1)}, u32[]{:S(2)}, u32[]{:S(2)}) collective-permute-start(f32[4,1024]{1,0:T(4,128)S(1)} %add.190), channel_id=1, source_target_pairs={{0,64},{2,66},{4,68},{6,70},{8,72},{10,74},{12,76},{14,78},{16,80}... | collective-permute-start | bytes 49160 | tf_op jit(solution)/shard_map/ppermute | solution.py:30
  228.3 2.5 %add_convert_fusion = bf16[256,1024]{1,0:T(8,128)(2,1)} fusion(bf16[256,1024]{1,0:T(8,128)(2,1)} %collective-permute-done.9, bf16[256,1024]{1,0:T(8,128)(2,1)} %collective-permute-done.8, f32[256,1024]{1,0:T(8,128)S(1)} %copy.188, bf16[256,1024]{1,0:T(8,128)(2,1)} %collective-permute-done.7), kind=kLoop, calls=%fused_computation.63 | loop fusion | flops 1835008 | bytes 3145728 | tf_op jit(solution)/shard_map/convert_element_type | solution.py:185
  230.8 2.6 %collective-permute-start.20 = (f32[4,1024]{1,0:T(4,128)S(1)}, f32[4,1024]{1,0:T(4,128)S(1)}, u32[]{:S(2)}, u32[]{:S(2)}) collective-permute-start(f32[4,1024]{1,0:T(4,128)S(1)} %add.191), channel_id=1, source_target_pairs={{0,128},{2,130},{4,132},{6,134},{8,136},{10,138},{12,140},{14,142}... | collective-permute-start | bytes 49160 | tf_op jit(solution)/shard_map/ppermute | solution.py:30
  234.6 3.9 %collective-permute-done.20 = f32[4,1024]{1,0:T(4,128)S(1)} collective-permute-done((f32[4,1024]{1,0:T(4,128)S(1)}, f32[4,1024]{1,0:T(4,128)S(1)}, u32[]{:S(2)}, u32[]{:S(2)}) %collective-permute-start.20) | collective-permute-done | bytes 16416 | tf_op jit(solution)/shard_map/ppermute | solution.py:30
  (173 shorter events, 65.7 us)
Async XLA Ops:
  1.9 47.1 %collective-permute-start.2 = (bf16[256,1024]{0,1:T(8,128)(2,1)S(1)}, bf16[256,1024]{0,1:T(8,128)(2,1)S(1)}, u32[]{:S(2)}, u32[]{:S(2)}) collective-permute-start(bf16[256,1024]{0,1:T(8,128)(2,1)S(1)} %copy.234), channel_id=1, source_target_pairs={{0,6},{2,8},{4,10},{6,12},{8,14},{10,16},{12,18},{14,20},{16,22},{... | collective-permute-start | bytes 1572872 | tf_op jit(solution)/shard_map/ppermute | solution.py:21
  4.8 42.1 %collective-permute-start.1 = (bf16[256,1024]{0,1:T(8,128)(2,1)S(1)}, bf16[256,1024]{0,1:T(8,128)(2,1)}, u32[]{:S(2)}, u32[]{:S(2)}) collective-permute-start(bf16[256,1024]{0,1:T(8,128)(2,1)S(1)} %copy.234), channel_id=1, source_target_pairs={{0,4},{2,6},{4,8},{6,10},{8,12},{10,14},{12,16},{14,18},{16,20},{1... | collective-permute-start | bytes 1572872 | tf_op jit(solution)/shard_map/ppermute | solution.py:21
  9.2 34.1 %collective-permute-start = (bf16[256,1024]{0,1:T(8,128)(2,1)S(1)}, bf16[256,1024]{0,1:T(8,128)(2,1)S(1)}, u32[]{:S(2)}, u32[]{:S(2)}) collective-permute-start(bf16[256,1024]{0,1:T(8,128)(2,1)S(1)} %copy.234), channel_id=1, source_target_pairs={{0,2},{2,4},{4,6},{6,8},{8,10},{10,12},{12,14},{14,16},{16,18},{18... | collective-permute-start | bytes 1572872 | tf_op jit(solution)/shard_map/ppermute | solution.py:21
  12.9 7.0 %collective-permute-start.3 = (bf16[3,1024]{1,0:T(4,128)(2,1)S(1)}, bf16[3,1024]{1,0:T(4,128)(2,1)S(1)}, u32[]{:S(2)}, u32[]{:S(2)}) collective-permute-start(bf16[3,1024]{1,0:T(4,128)(2,1)S(1)} %slice.48), channel_id=1, source_target_pairs={{0,2},{2,4},{4,6},{6,8},{8,10},{10,12},{12,14},{14,16},{16,18},{18... | collective-permute-start | bytes 18440 | tf_op jit(solution)/shard_map/ppermute | solution.py:21
  19.7 32.0 %copy-start = (f32[8,256,256]{1,2,0:T(8,128)}, f32[8,256,256]{1,2,0:T(8,128)S(1)}, u32[]{:S(2)}) copy-start(f32[8,256,256]{1,2,0:T(8,128)S(1)} %get-tuple-element.38) | copy-start | bytes 6291460
  21.6 52.2 %collective-permute-start.5 = (bf16[256,1024]{1,0:T(8,128)(2,1)}, bf16[256,1024]{1,0:T(8,128)(2,1)}, u32[]{:S(2)}, u32[]{:S(2)}) collective-permute-start(bf16[256,1024]{1,0:T(8,128)(2,1)} %add_convert_fusion.1), channel_id=1, source_target_pairs={{0,4},{2,6},{4,8},{6,10},{8,12},{10,14},{12,16},{14,18},{16,20},{1... | collective-permute-start | bytes 1572872 | tf_op jit(solution)/shard_map/ppermute | solution.py:21
  40.6 28.0 %collective-permute-start.4 = (bf16[256,1024]{1,0:T(8,128)(2,1)}, bf16[256,1024]{1,0:T(8,128)(2,1)}, u32[]{:S(2)}, u32[]{:S(2)}) collective-permute-start(bf16[256,1024]{1,0:T(8,128)(2,1)} %add_convert_fusion.1), channel_id=1, source_target_pairs={{0,2},{2,4},{4,6},{6,8},{8,10},{10,12},{12,14},{14,16},{16,18},{18... | collective-permute-start | bytes 1572872 | tf_op jit(solution)/shard_map/ppermute | solution.py:21
  43.2 8.5 %copy-start.24 = (bf16[32,8,8,128]{3,2,1,0:T(8,128)(2,1)}, bf16[32,8,8,128]{3,2,1,0:T(8,128)(2,1)S(1)}, u32[]{:S(2)}) copy-start(bf16[32,8,8,128]{3,2,1,0:T(8,128)(2,1)S(1)} %fusion.104) | copy-start | bytes 1572868
  43.3 5.7 %copy-start.17 = (bf16[256,1024]{0,1:T(8,128)(2,1)}, bf16[256,1024]{0,1:T(8,128)(2,1)S(1)}, u32[]{:S(2)}) copy-start(bf16[256,1024]{0,1:T(8,128)(2,1)S(1)} %collective-permute-done) | copy-start | bytes 1572868
  43.3 20.5 %collective-permute-start.6 = (bf16[256,1024]{1,0:T(8,128)(2,1)}, bf16[256,1024]{1,0:T(8,128)(2,1)}, u32[]{:S(2)}, u32[]{:S(2)}) collective-permute-start(bf16[256,1024]{1,0:T(8,128)(2,1)} %add_convert_fusion.1), channel_id=1, source_target_pairs={{0,6},{2,8},{4,10},{6,12},{8,14},{10,16},{12,18},{14,20},{16,22},{... | collective-permute-start | bytes 1572872 | tf_op jit(solution)/shard_map/ppermute | solution.py:21
  79.2 8.1 %copy-start.32 = (f32[1024]{0:T(1024)S(1)}, f32[1024]{0:T(1024)}, u32[]{:S(2)}) copy-start(f32[1024]{0:T(1024)} %param.12) | copy-start | bytes 12292
  107.7 19.0 %copy-start.8 = (bf16[8,256,256]{1,2,0:T(8,128)(2,1)}, bf16[8,256,256]{1,2,0:T(8,128)(2,1)S(1)}, u32[]{:S(2)}) copy-start(bf16[8,256,256]{1,2,0:T(8,128)(2,1)S(1)} %multiply_convert_fusion.2) | copy-start | bytes 3145732
  122.7 14.6 %collective-permute-start.12 = (bf16[256,1024]{1,0:T(8,128)(2,1)}, bf16[256,1024]{1,0:T(8,128)(2,1)}, u32[]{:S(2)}, u32[]{:S(2)}) collective-permute-start(bf16[256,1024]{1,0:T(8,128)(2,1)} %copy.202), channel_id=1, source_target_pairs={{6,0},{8,2},{10,4},{12,6},{14,8},{16,10},{18,12},{20,14},{22,16},{... | collective-permute-start | bytes 1572872 | tf_op jit(solution)/shard_map/ppermute | solution.py:21
  124.2 18.8 %collective-permute-start.11 = (bf16[256,1024]{1,0:T(8,128)(2,1)}, bf16[256,1024]{1,0:T(8,128)(2,1)}, u32[]{:S(2)}, u32[]{:S(2)}) collective-permute-start(bf16[256,1024]{1,0:T(8,128)(2,1)} %copy.200), channel_id=1, source_target_pairs={{4,0},{6,2},{8,4},{10,6},{12,8},{14,10},{16,12},{18,14},{20,16},{2... | collective-permute-start | bytes 1572872 | tf_op jit(solution)/shard_map/ppermute | solution.py:21
  125.5 17.5 %collective-permute-start.10 = (bf16[256,1024]{1,0:T(8,128)(2,1)}, bf16[256,1024]{1,0:T(8,128)(2,1)}, u32[]{:S(2)}, u32[]{:S(2)}) collective-permute-start(bf16[256,1024]{1,0:T(8,128)(2,1)} %copy.197), channel_id=1, source_target_pairs={{2,0},{4,2},{6,4},{8,6},{10,8},{12,10},{14,12},{16,14},{18,16},{20... | collective-permute-start | bytes 1572872 | tf_op jit(solution)/shard_map/ppermute | solution.py:21
  132.0 10.9 %copy-start.10 = (f32[256,1024]{1,0:T(8,128)S(1)}, f32[256,1024]{1,0:T(8,128)}, u32[]{:S(2)}) copy-start(f32[256,1024]{1,0:T(8,128)} %copy.198) | copy-start | bytes 3145732
  134.6 40.9 %copy-start.14 = (bf16[8,256,256]{1,2,0:T(8,128)(2,1)}, bf16[8,256,256]{1,2,0:T(8,128)(2,1)S(1)}, u32[]{:S(2)}) copy-start(bf16[8,256,256]{1,2,0:T(8,128)(2,1)S(1)} %multiply_convert_fusion.1) | copy-start | bytes 3145732
  134.7 23.5 %copy-start.9 = (bf16[8,256,256]{1,2,0:T(8,128)(2,1)S(1)}, bf16[8,256,256]{1,2,0:T(8,128)(2,1)}, u32[]{:S(2)}) copy-start(bf16[8,256,256]{1,2,0:T(8,128)(2,1)} %copy-done.8) | copy-start | bytes 3145732
  145.0 14.2 %copy-start.13 = (bf16[8,256,256]{1,2,0:T(8,128)(2,1)S(1)}, bf16[8,256,256]{1,2,0:T(8,128)(2,1)}, u32[]{:S(2)}) copy-start(bf16[8,256,256]{1,2,0:T(8,128)(2,1)} %multiply_convert_fusion) | copy-start | bytes 3145732
  145.0 14.0 %collective-permute-start.14 = (f32[4,1024]{1,0:T(4,128)S(1)}, f32[4,1024]{1,0:T(4,128)S(1)}, u32[]{:S(2)}, u32[]{:S(2)}) collective-permute-start(f32[4,1024]{1,0:T(4,128)S(1)} %pad_maximum_fusion.1), channel_id=1, source_target_pairs={{0,2},{2,0},{4,6},{6,4},{8,10},{10,8},{12,14},{14,12},{16,18},{18,... | collective-permute-start | bytes 49160 | tf_op jit(solution)/shard_map/ppermute | solution.py:30
  159.0 3.8 %collective-permute-start.15 = (f32[4,1024]{1,0:T(4,128)S(1)}, f32[4,1024]{1,0:T(4,128)S(1)}, u32[]{:S(2)}, u32[]{:S(2)}) collective-permute-start(f32[4,1024]{1,0:T(4,128)S(1)} %fusion.53), channel_id=1, source_target_pairs={{0,4},{2,6},{4,0},{6,2},{8,12},{10,14},{12,8},{14,10},{16,20},{18,... | collective-permute-start | bytes 49160 | tf_op jit(solution)/shard_map/ppermute | solution.py:30
  162.9 15.1 %copy-start.22 = (bf16[8,256,128]{1,2,0:T(8,128)(2,1)S(1)}, bf16[8,256,128]{1,2,0:T(8,128)(2,1)}, u32[]{:S(2)}) copy-start(bf16[8,256,128]{1,2,0:T(8,128)(2,1)} %fusion.17) | copy-start | bytes 1572868
  162.9 20.0 %collective-permute-start.16 = (f32[4,1024]{1,0:T(4,128)S(1)}, f32[4,1024]{1,0:T(4,128)S(1)}, u32[]{:S(2)}, u32[]{:S(2)}) collective-permute-start(f32[4,1024]{1,0:T(4,128)S(1)} %fusion.103), channel_id=1, source_target_pairs={{0,8},{2,10},{4,12},{6,14},{8,0},{10,2},{12,4},{14,6},{16,24},{18,... | collective-permute-start | bytes 49160 | tf_op jit(solution)/shard_map/ppermute | solution.py:30
  179.0 49.3 %collective-permute-start.9 = (bf16[256,1024]{1,0:T(8,128)(2,1)}, bf16[256,1024]{1,0:T(8,128)(2,1)}, u32[]{:S(2)}, u32[]{:S(2)}) collective-permute-start(bf16[256,1024]{1,0:T(8,128)(2,1)} %copy.194), channel_id=1, source_target_pairs={{6,0},{8,2},{10,4},{12,6},{14,8},{16,10},{18,12},{20,14},{22,16},{... | collective-permute-start | bytes 1572872 | tf_op jit(solution)/shard_map/ppermute | solution.py:21
  180.3 48.0 %collective-permute-start.8 = (bf16[256,1024]{1,0:T(8,128)(2,1)}, bf16[256,1024]{1,0:T(8,128)(2,1)}, u32[]{:S(2)}, u32[]{:S(2)}) collective-permute-start(bf16[256,1024]{1,0:T(8,128)(2,1)} %copy.191), channel_id=1, source_target_pairs={{4,0},{6,2},{8,4},{10,6},{12,8},{14,10},{16,12},{18,14},{20,16},{2... | collective-permute-start | bytes 1572872 | tf_op jit(solution)/shard_map/ppermute | solution.py:21
  181.6 46.7 %collective-permute-start.7 = (bf16[256,1024]{1,0:T(8,128)(2,1)}, bf16[256,1024]{1,0:T(8,128)(2,1)}, u32[]{:S(2)}, u32[]{:S(2)}) collective-permute-start(bf16[256,1024]{1,0:T(8,128)(2,1)} %copy.187), channel_id=1, source_target_pairs={{2,0},{4,2},{6,4},{8,6},{10,8},{12,10},{14,12},{16,14},{18,16},{20... | collective-permute-start | bytes 1572872 | tf_op jit(solution)/shard_map/ppermute | solution.py:21
  182.9 33.7 %copy-start.11 = (bf16[8,256,256]{1,2,0:T(8,128)(2,1)S(1)}, bf16[8,256,256]{1,2,0:T(8,128)(2,1)}, u32[]{:S(2)}) copy-start(bf16[8,256,256]{1,2,0:T(8,128)(2,1)} %multiply_convert_fusion.3) | copy-start | bytes 3145732
  182.9 30.2 %collective-permute-start.17 = (f32[4,1024]{1,0:T(4,128)S(1)}, f32[4,1024]{1,0:T(4,128)S(1)}, u32[]{:S(2)}, u32[]{:S(2)}) collective-permute-start(f32[4,1024]{1,0:T(4,128)S(1)} %add.188), channel_id=1, source_target_pairs={{0,16},{2,18},{4,20},{6,22},{8,24},{10,26},{12,28},{14,30},{16,0},... | collective-permute-start | bytes 49160 | tf_op jit(solution)/shard_map/ppermute | solution.py:30
  213.2 8.8 %collective-permute-start.18 = (f32[4,1024]{1,0:T(4,128)S(1)}, f32[4,1024]{1,0:T(4,128)S(1)}, u32[]{:S(2)}, u32[]{:S(2)}) collective-permute-start(f32[4,1024]{1,0:T(4,128)S(1)} %add.189), channel_id=1, source_target_pairs={{0,32},{2,34},{4,36},{6,38},{8,40},{10,42},{12,44},{14,46},{16,48}... | collective-permute-start | bytes 49160 | tf_op jit(solution)/shard_map/ppermute | solution.py:30
  220.6 12.7 %collective-permute-start.13 = (f32[3,1024]{1,0:T(4,128)S(1)}, f32[3,1024]{1,0:T(4,128)S(1)}, u32[]{:S(2)}, u32[]{:S(2)}) collective-permute-start(f32[3,1024]{1,0:T(4,128)S(1)} %slice.64), channel_id=1, source_target_pairs={{2,0},{4,2},{6,4},{8,6},{10,8},{12,10},{14,12},{16,14},{18,16},{20... | collective-permute-start | bytes 36872 | tf_op jit(solution)/shard_map/ppermute | solution.py:21
  222.0 8.8 %collective-permute-start.19 = (f32[4,1024]{1,0:T(4,128)S(1)}, f32[4,1024]{1,0:T(4,128)S(1)}, u32[]{:S(2)}, u32[]{:S(2)}) collective-permute-start(f32[4,1024]{1,0:T(4,128)S(1)} %add.190), channel_id=1, source_target_pairs={{0,64},{2,66},{4,68},{6,70},{8,72},{10,74},{12,76},{14,78},{16,80}... | collective-permute-start | bytes 49160 | tf_op jit(solution)/shard_map/ppermute | solution.py:30
  230.8 7.7 %collective-permute-start.20 = (f32[4,1024]{1,0:T(4,128)S(1)}, f32[4,1024]{1,0:T(4,128)S(1)}, u32[]{:S(2)}, u32[]{:S(2)}) collective-permute-start(f32[4,1024]{1,0:T(4,128)S(1)} %add.191), channel_id=1, source_target_pairs={{0,128},{2,130},{4,132},{6,134},{8,136},{10,138},{12,140},{14,142}... | collective-permute-start | bytes 49160 | tf_op jit(solution)/shard_map/ppermute | solution.py:30
  (23 other events, 70.4 us)

commit v2 on v1

v2 whole, which is shorter than its diff:
```python
import jax
import jax.numpy as jnp
from jax import lax
from jax.sharding import PartitionSpec as P

D = 2048
HD = 128
BLK = 128
REACH = 3
WIN = 6


NEG_FILL = -1e30
NORM_EPS = 1e-06


def from_behind(block, axis, distance):
    devices = range(lax.axis_size(axis))
    route = [(i - distance, i) for i in devices if i - distance in devices]
    return lax.ppermute(block, axis, route)


def chip_swap(block, axis):
    size = lax.axis_size(axis)
    return lax.ppermute(block, axis, [(i, i ^ 1) for i in range(size)])


def all_sum(block, axis):
    size = lax.axis_size(axis)
    if size & (size - 1):
        return lax.psum(block, axis)
    stride = 1
    while stride < size:
        block = block + lax.ppermute(block, axis, [(i, i ^ stride) for i in range(size)])
        stride *= 2
    return block


def pair_sum(block, axis):
    if lax.axis_size(axis) != 2:
        return lax.psum(block, axis)
    return block + lax.ppermute(block, axis, [(0, 1), (1, 0)])


def split_heads(array):
    return array.reshape(array.shape[0], array.shape[1] // HD, HD)


def window_mask(block_bits, device, row_count, key_count):
    per_device = row_count // BLK
    key_blocks = key_count // BLK
    first_block = device * per_device - (key_blocks - per_device)
    qb = jnp.arange(per_device, dtype=jnp.int32)
    kb = jnp.arange(key_blocks, dtype=jnp.int32)
    relative = qb[:, None] + (key_blocks - per_device) - kb[None, :]
    one_hot = relative[:, :, None] == jnp.arange(WIN, dtype=jnp.int32)[None, None, :]
    picked_bits = jnp.sum(jnp.where(one_hot, block_bits[:, None, :], 0), axis=2)
    coarse = (picked_bits > 0) & (relative >= 0) & (relative < WIN) & (first_block + kb[None, :] >= 0)
    fine = jnp.repeat(jnp.repeat(coarse, BLK, axis=0), BLK, axis=1)
    q = jnp.arange(row_count, dtype=jnp.int32)
    s = jnp.arange(key_count, dtype=jnp.int32)
    causal = s[None, :] <= q[:, None] + (key_count - row_count)
    return fine & causal


def body(queries, keys, values_in, teacher, gain, conv_weight, block_bits, mask_pos):
    row_count, channels = queries.shape
    tap_count = conv_weight.shape[0]
    rim_rows = tap_count - 1
    device = lax.axis_index("tm")
    even = device % 2 == 0
    score_scale = HD ** (-0.5)
    far_rows = row_count - BLK
    far_lead = 8
    key_count = REACH * row_count + (row_count - far_rows)

    own = jnp.concatenate([keys, values_in], 1)
    second = from_behind(own, "tm", 2)
    first = chip_swap(jnp.where(even, own, second), "tm")
    third = from_behind(second[far_rows - far_lead :], "tm", 1)
    window = jnp.concatenate([third, second, first, own], 0)
    key_win = window[far_lead:, :channels]
    vin_win = window[:, channels:].astype(jnp.float32)

    conv_sum = jnp.zeros((key_count, channels), jnp.float32)
    for tap_index in range(tap_count):
        conv_sum = conv_sum + conv_weight[tap_index] * vin_win[far_lead - tap_index : far_lead - tap_index + key_count]
    value_win = conv_sum.astype(jnp.bfloat16)

    heads_query = split_heads(queries)
    heads_key = split_heads(key_win)
    heads_value = split_heads(value_win)
    mask = window_mask(block_bits, device, row_count, key_count)

    raw_scores = (
        jnp.einsum("thd,uhd->htu", heads_query, heads_key, preferred_element_type=jnp.float32)
        * score_scale
    )
    scores = jnp.where(mask[None], raw_scores, NEG_FILL)
    row_peak = jnp.max(scores, axis=2)
    expo = jnp.where(mask[None], jnp.exp(scores - row_peak[..., None]), 0.0)
    row_total = jnp.sum(expo, axis=2)
    prob = expo / row_total[..., None]
    weights = prob.astype(jnp.bfloat16)
    attended = jnp.einsum("htu,uhd->thd", weights, heads_value, preferred_element_type=jnp.float32)

    flattened = attended.reshape(row_count, channels)
    squares = pair_sum(jnp.sum(flattened * flattened, axis=1), "head")
    inverse = lax.rsqrt(squares / D + NORM_EPS)
    prediction = flattened * inverse[:, None] * gain
    position = jnp.arange(row_count, dtype=jnp.int32) % BLK
    chosen = jnp.any(jnp.repeat(mask_pos, BLK, axis=0) == position[:, None], axis=1)
    residual = jnp.where(chosen[:, None], prediction - teacher.astype(jnp.float32), 0.0)
    scaled = residual * gain
    cross_term = pair_sum(jnp.sum(scaled * flattened, axis=1), "head")
    out_grad = (
        inverse[:, None] * scaled - flattened * (inverse**3 * cross_term / D)[:, None]
    ).astype(jnp.bfloat16)
    heads_grad = split_heads(out_grad)
    delta = jnp.sum(heads_grad.astype(jnp.float32) * attended, axis=2).T

    prob_grad = jnp.einsum("thd,uhd->htu", heads_grad, heads_value, preferred_element_type=jnp.float32)
    score_grad = (prob * (prob_grad - delta[:, :, None])).astype(jnp.bfloat16)
    query_grad = (
        jnp.einsum("htu,uhd->thd", score_grad, heads_key, preferred_element_type=jnp.float32)
        * score_scale
    )
    key_part = (
        jnp.einsum("htu,thd->uhd", score_grad, heads_query, preferred_element_type=jnp.float32)
        * score_scale
    ).reshape(key_count, channels)
    value_part = jnp.einsum(
        "htu,thd->uhd", weights, heads_grad, preferred_element_type=jnp.float32
    ).reshape(key_count, channels)

    local_taps = jnp.stack(
        [
            jnp.sum(value_part * vin_win[far_lead - tap_index : far_lead - tap_index + key_count], axis=0)
            for tap_index in range(tap_count)
        ]
    )
    conv_grad = all_sum(local_taps, "tm")

    lead = jnp.zeros((far_lead, channels), jnp.float32)
    padded_value = jnp.concatenate([lead, value_part, jnp.zeros((rim_rows, channels), jnp.float32)], 0)
    value_sum = jnp.zeros((key_count + far_lead, channels), jnp.float32)
    for tap_index in range(tap_count):
        value_sum = value_sum + conv_weight[tap_index] * padded_value[tap_index : tap_index + key_count + far_lead]
    grads = jnp.concatenate([jnp.concatenate([lead, key_part], 0), value_sum], 1)

    cut_third = row_count - far_rows + far_lead
    grad_third = grads[:cut_third]
    grad_second = grads[cut_third : cut_third + row_count]
    grad_first = grads[cut_third + row_count : cut_third + 2 * row_count]
    grad_own = grads[cut_third + 2 * row_count :]

    back_third = from_behind(grad_third.astype(jnp.bfloat16), "tm", -1).astype(jnp.float32)
    back_first = chip_swap(grad_first.astype(jnp.bfloat16), "tm").astype(jnp.float32)
    grad_second = grad_second + jnp.concatenate(
        [jnp.zeros((far_rows - far_lead, 2 * channels), jnp.float32), back_third], 0
    )
    grad_second = grad_second + jnp.where(even, 0.0, back_first)
    back_second = from_behind(grad_second.astype(jnp.bfloat16), "tm", -2).astype(jnp.float32)
    total = grad_own + jnp.where(even, back_first, 0.0) + back_second

    return (
        query_grad.reshape(row_count, channels).astype(jnp.bfloat16),
        total[:, :channels].astype(jnp.bfloat16),
        total[:, channels:].astype(jnp.bfloat16),
        conv_grad,
    )


def solution(mesh):
    placed = (
        P("tm", "head"),
        P("tm", "head"),
        P("tm", "head"),
        P("tm", "head"),
        P("head"),
        P(None, "head"),
        P("tm", None),
        P("tm", None),
    )
    return jax.shard_map(
        body,
        mesh=mesh,
        in_specs=placed,
        out_specs=(P("tm", "head"), P("tm", "head"), P("tm", "head"), P(None, "head")),
        check_vma=False,
    )
```

time: 241 us -> 196 us (0.81)
  starting transfers between devices: 90.7 us -> 48.9 us
  other arithmetic: 17.3 us -> 48.7 us
  matrix products: 44 us -> 19.6 us
  waiting for transfers between devices: 46.2 us -> 62.3 us
  blocking collectives: 13.2 us -> 0 us
  local copies, waits for them, and re-layouts: 26.4 us -> 15 us
    ppermute x14 -> x4, starting transfers between devices: 45.6 us -> 9.84 us  [from_behind(): return lax.ppermute(block, axis, route)]
    dot_general x20 -> x4, matrix products: 40.3 us -> 10.7 us  [the longest x1 5.85 us: body(): jnp.einsum('thd,uhd->htu', heads_grad, heads_value, preferred_element_typ...]
    psum x2 -> x0, blocking collectives: 13.2 us -> none  [the longest x1 6.63 us: body(): cross_term = lax.psum(jnp.sum(scaled * flattened, axis=1), 'head')]
    convert_element_type x4, other arithmetic: 5.14 us -> 18.2 us  [the longest x1 5.28 us: body(): value_win = conv_sum.astype(jnp.bfloat16)]
    ppermute x7, starting transfers between devices: 45.1 us -> 32.8 us  [all_sum(): lax.ppermute(block, axis, [(i, i ^ stride) for i in range(size)])]
    concatenate x0 -> x3, other arithmetic: none -> 9.58 us  [the longest x1 8.36 us: body(): jnp.concatenate([jnp.concatenate([lead, key_part], 0), value_sum], 1)]
    convert_element_type x6 -> x0, local copies, waits for them, and re-layouts: 9.14 us -> none  [the longest x3 6.14 us: body(): partials[distance][1].astype(jnp.bfloat16)]
    ppermute x0 -> x4, waiting for transfers between devices: none -> 8.61 us  [the longest x2 8.6 us: pair_sum(): return block + lax.ppermute(block, axis, [(0, 1), (1, 0)])]
  transfers between devices with their start and end apart: 21 -> 15, of which waited for: 7 -> 10; matrix products, arithmetic and copies ran while one was open for 20% -> 12% of each run, Pallas kernels for 0% -> 0%
where the time goes in v2:
time: 196 us
  waiting for transfers between devices  62.3 us (32%)
  starting transfers between devices  48.9 us (25%)
  other arithmetic  48.7 us (25%)
  matrix products  19.6 us (10%)
  local copies, waits for them, and re-layouts  15 us (8%)
    ppermute x7, starting transfers between devices, all_sum(): lax.ppermute(block, axis, [(i, i ^ stride) for i in range(size)])  32.8 us
    ppermute x7, waiting for transfers between devices, all_sum(): lax.ppermute(block, axis, [(i, i ^ stride) for i in range(size)])  30.7 us
    ppermute x4, waiting for transfers between devices, from_behind(): return lax.ppermute(block, axis, route)  23 us
    ppermute x4, starting transfers between devices, from_behind(): return lax.ppermute(block, axis, route)  9.84 us
    ppermute x2, waiting for transfers between devices, pair_sum(): return block + lax.ppermute(block, axis, [(0, 1), (1, 0)])  8.6 us
    concatenate x1, other arithmetic, body(): jnp.concatenate([jnp.concatenate([lead, key_part], 0), value_sum], 1)  8.36 us
    sub x1, matrix products, body(): expo = jnp.where(mask[None], jnp.exp(scores - row_peak[..., None]), 0.0)  7.68 us
    unnamed x42, local copies, waits for them, and re-layouts  6.71 us
  transfers between devices with their start and end apart: 15, of which 10 were waited for; matrix products, arithmetic and copies ran while one was open for 12% of the time, Pallas kernels for 0%

profile of v2, /device:TPU:4, one launch (start us, length us, event | category | flops | bytes accessed | tf_op | source)
XLA Modules:
  0.0 195.7 jit_solution(9215539822901045846)
XLA Ops:
  3.2 3.5 %collective-permute-start = (bf16[256,2048]{0,1:T(8,128)(2,1)S(1)}, bf16[256,2048]{0,1:T(8,128)(2,1)S(1)}, u32[]{:S(2)}, u32[]{:S(2)}) collective-permute-start(bf16[256,2048]{0,1:T(8,128)(2,1)S(1)} %pad_maximum_fusion.3), channel_id=1, source_target_pairs={{0,4},{2,6},{4,8},{6,10},{8,12},{10,14},{12,16},{14,18},{16,20},{1... | collective-permute-start | bytes 3145736 | tf_op jit(solution)/shard_map/ppermute | solution.py:20
  6.9 22.2 %collective-permute-done = bf16[256,2048]{0,1:T(8,128)(2,1)S(1)} collective-permute-done((bf16[256,2048]{0,1:T(8,128)(2,1)S(1)}, bf16[256,2048]{0,1:T(8,128)(2,1)S(1)}, u32[]{:S(2)}, u32[]{:S(2)}) %collective-permute-start) | collective-permute-done | bytes 1048608 | tf_op jit(solution)/shard_map/ppermute | solution.py:20
  30.4 2.0 %copy.110 = bf16[256,1024]{0,1:T(8,128)(2,1)} copy(bf16[256,1024]{1,0:T(8,128)(2,1)} %param.8) | data formatting | bytes 1048576 | tf_op jit(solution)/shard_map/reshape | solution.py:46
  34.2 3.2 %collective-permute-start.1 = (bf16[136,2048]{1,0:T(8,128)(2,1)}, bf16[136,2048]{1,0:T(8,128)(2,1)}, u32[]{:S(2)}, u32[]{:S(2)}) collective-permute-start(bf16[136,2048]{1,0:T(8,128)(2,1)} %copy.80), channel_id=1, source_target_pairs={{0,2},{2,4},{4,6},{6,8},{8,10},{10,12},{12,14},{14,16},{16,18},{18... | collective-permute-start | bytes 1671176 | tf_op jit(solution)/shard_map/ppermute | solution.py:20
  39.9 2.7 %maximum_maximum_fusion.1 = bf16[896,1024]{0,1:T(8,128)(2,1)} fusion(bf16[256,1024]{0,1:T(8,128)(2,1)S(1)} %copy.79, bf16[256,1024]{0,1:T(8,128)(2,1)S(1)} %copy.78, bf16[256,2048]{0,1:T(8,128)(2,1)} %collective-permute-done.2, bf16[256,2048]{0,1:T(8,128)(2,1)S(1)} %collective-permute-done, bf16[136,2048]{0,1:T(8,128)(2,1)S(1)} %copy.81), kind=kLoop, calls=%fused_computation.38 | loop fusion | flops 9175040 | bytes 5537792 | tf_op jit(solution)/shard_map/slice | solution.py:82
  42.6 7.7 %fusion.31 = (f32[8,256]{1,0:T(8,128)S(1)}, f32[8,256,896]{1,2,0:T(8,128)}) fusion(pred[256,896]{0,1:T(8,128)(4,1)S(1)} %fusion.19, bf16[896,8,128]{0,2,1:T(8,128)(2,1)} %bitcast.73, bf16[256,8,128]{0,2,1:T(8,128)(2,1)} %bitcast.78), kind=kOutput, calls=%fused_computation.74 | convolution fusion | flops 478937984 | bytes 9936896 | tf_op jit(solution)/shard_map/sub | solution.py:101
  50.3 3.7 %fusion.8 = bf16[8,256,896]{1,2,0:T(8,128)(2,1)S(1)} fusion(f32[8,256,896]{1,2,0:T(8,128)} %get-tuple-element.31, f32[8,256]{1,0:T(8,128)S(1)} %get-tuple-element.30), kind=kLoop, calls=%fused_computation.23 | loop fusion | flops 3670016 | bytes 11018240 | tf_op jit(solution)/shard_map/convert_element_type | solution.py:104
  54.0 4.8 %fusion.15 = f32[904,1024]{0,1:T(8,128)S(1)} fusion(bf16[256,1024]{0,1:T(8,128)(2,1)S(1)} %copy.79, bf16[256,1024]{0,1:T(8,128)(2,1)S(1)} %copy.78, bf16[256,2048]{0,1:T(8,128)(2,1)} %collective-permute-done.2, bf16[256,2048]{0,1:T(8,128)(2,1)S(1)} %collective-permute-done, bf16[136,2048]{0,1:T(8,128)(2,1)S(1)} %copy.81), kind=kLoop, calls=%fused_computation.34 | loop fusion | flops 9256960 | bytes 7405568 | tf_op jit(solution)/shard_map/convert_element_type | solution.py:83
  58.9 5.3 %add_convert_fusion = bf16[896,1024]{0,1:T(8,128)(2,1)S(1)} fusion(f32[904,1024]{0,1:T(8,128)S(1)} %fusion.15, f32[1024]{0:T(1024)S(1)} %bitcast.96, f32[1024]{0:T(1024)S(1)} %bitcast.98, f32[1024]{0:T(1024)S(1)} %bitcast.94, f32[1024]{0:T(1024)S(1)} %bitcast.92), kind=kLoop, calls=%fused_computation.18 | loop fusion | flops 7340032 | bytes 16531456 | tf_op jit(solution)/shard_map/convert_element_type | solution.py:88
  66.1 4.1 %collective-permute-done.3 = f32[256]{0:T(256)S(1)} collective-permute-done((f32[256]{0:T(256)S(1)}, f32[256]{0:T(256)S(1)}, u32[]{:S(2)}, u32[]{:S(2)}) %collective-permute-start.3) | collective-permute-done | bytes 1056 | tf_op jit(solution)/shard_map/ppermute | solution.py:42
  71.6 4.5 %collective-permute-done.4 = f32[256]{0:T(256)S(1)} collective-permute-done((f32[256]{0:T(256)S(1)}, f32[256]{0:T(256)S(1)}, u32[]{:S(2)}, u32[]{:S(2)}) %collective-permute-start.4) | collective-permute-done | bytes 1056 | tf_op jit(solution)/shard_map/ppermute | solution.py:42
  76.8 3.4 %fusion.32 = f32[8,128,896]{2,1,0:T(8,128)S(1)} fusion(bf16[256,8,128]{0,2,1:T(8,128)(2,1)S(1)} %bitcast.75, bf16[8,256,896]{1,2,0:T(8,128)(2,1)} %copy-done.5), kind=kOutput, calls=%fused_computation.75 | convolution fusion | flops 469762048 | bytes 7864320 | tf_op jit(solution)/shard_map/htu,thd->uhd/dot_general | solution.py:132
  80.2 5.8 %multiply_convert_fusion = bf16[8,256,896]{1,2,0:T(8,128)(2,1)S(1)} fusion(f32[8,256]{1,0:T(8,128)S(1)} %bitcast.100, f32[8,256,896]{1,2,0:T(8,128)} %get-tuple-element.31, f32[8,256]{1,0:T(8,128)S(1)} %get-tuple-element.30, bf16[256,8,128]{0,2,1:T(8,128)(2,1)S(1)} %bitcast.76, bf16[896,8,128]{0,2,1:T(8,128)(2,1)S(1)} %bitcast.72), kind=kOutput, calls=%fused_computation.4 | convolution fusion | flops 477102080 | bytes 13385728 | tf_op jit(solution)/shard_map/thd,uhd->htu/dot_general | solution.py:122
  89.0 5.2 %fusion.2 = f32[904,1024]{0,1:T(8,128)S(1)} fusion(f32[907,1024]{0,1:T(8,128)S(1)} %maximum_maximum_fusion, f32[896,1024]{0,1:T(8,128)S(1)} %bitcast.67, f32[1024]{0:T(1024)S(1)} %bitcast.97, f32[1024]{0:T(1024)S(1)} %bitcast.99, f32[1024]{0:T(1024)S(1)} %bitcast.95, f32[1024]{0:T(1024)S(1)} %bitcast.93), kind=kLoop, calls=%fused_computation.8 | loop fusion | flops 6479872 | bytes 18497536 | tf_op jit(solution)/shard_map/add | solution.py:148
  94.3 1.5 fusion.28
  97.6 4.8 %collective-permute-start.5 = (bf16[256,2048]{0,1:T(8,128)(2,1)}, bf16[256,2048]{0,1:T(8,128)(2,1)}, u32[]{:S(2)}, u32[]{:S(2)}) collective-permute-start(bf16[256,2048]{0,1:T(8,128)(2,1)} %slice.103), channel_id=1, source_target_pairs={{0,2},{2,0},{4,6},{6,4},{8,10},{10,8},{12,14},{14,12},{16,18},{18,... | collective-permute-start | bytes 3145736 | tf_op jit(solution)/shard_map/ppermute | solution.py:25
  103.0 1.8 collective-permute-start.6
  104.8 8.4 %select_maximum_fusion = f32[904,2048]{0,1:T(8,128)} fusion(f32[896,1024]{0,1:T(8,128)} %bitcast.69, f32[904,1024]{0,1:T(8,128)} %copy-done.4), kind=kLoop, calls=%fused_computation.1 | loop fusion | flops 5554176 | bytes 14778368 | tf_op jit(solution)/shard_map/concatenate | solution.py:149
  113.2 5.2 %multiply_reduce_fusion.3 = (f32[1024]{0:T(1024)S(1)}, f32[1024]{0:T(1024)S(1)}, f32[1024]{0:T(1024)S(1)}, f32[1024]{0:T(1024)S(1)}) fusion(f32[904,1024]{0,1:T(8,128)S(1)} %copy-done.1, f32[8,128,896]{2,1,0:T(8,128)S(1)} %copy-done.3), kind=kLoop, calls=%fused_computation.17 | loop fusion | flops 7335936 | bytes 18366464 | tf_op jit(solution)/shard_map/reduce_sum | solution.py:138
  119.0 4.4 %fusion.13 = bf16[256,2048]{0,1:T(8,128)(2,1)} fusion(bf16[256,2048]{0,1:T(8,128)(2,1)} %collective-permute-done.5, f32[904,2048]{0,1:T(8,128)} %select_maximum_fusion, bf16[136,2048]{0,1:T(8,128)(2,1)S(1)} %copy.98, pred[]{:T(512)S(6)} %eq.29), kind=kLoop, calls=%fused_computation.30 | loop fusion | flops 3145728 | bytes 4751361 | tf_op jit(solution)/shard_map/convert_element_type | solution.py:163
  126.7 5.2 %collective-permute-start.9 = (f32[4,1024]{1,0:T(4,128)S(1)}, f32[4,1024]{1,0:T(4,128)S(1)}, u32[]{:S(2)}, u32[]{:S(2)}) collective-permute-start(f32[4,1024]{1,0:T(4,128)S(1)} %fusion.27), channel_id=1, source_target_pairs={{0,4},{2,6},{4,0},{6,2},{8,12},{10,14},{12,8},{14,10},{16,20},{18,... | collective-permute-start | bytes 49160 | tf_op jit(solution)/shard_map/ppermute | solution.py:34
  132.0 22.8 %collective-permute-done.9 = f32[4,1024]{1,0:T(4,128)S(1)} collective-permute-done((f32[4,1024]{1,0:T(4,128)S(1)}, f32[4,1024]{1,0:T(4,128)S(1)}, u32[]{:S(2)}, u32[]{:S(2)}) %collective-permute-start.9) | collective-permute-done | bytes 16416 | tf_op jit(solution)/shard_map/ppermute | solution.py:34
  154.8 3.4 %collective-permute-start.10 = (f32[4,1024]{1,0:T(4,128)S(1)}, f32[4,1024]{1,0:T(4,128)S(1)}, u32[]{:S(2)}, u32[]{:S(2)}) collective-permute-start(f32[4,1024]{1,0:T(4,128)S(1)} %fusion.47), channel_id=1, source_target_pairs={{0,8},{2,10},{4,12},{6,14},{8,0},{10,2},{12,4},{14,6},{16,24},{18,... | collective-permute-start | bytes 49160 | tf_op jit(solution)/shard_map/ppermute | solution.py:34
  158.3 1.9 collective-permute-done.10
  160.2 5.6 %collective-permute-start.11 = (f32[4,1024]{1,0:T(4,128)S(1)}, f32[4,1024]{1,0:T(4,128)S(1)}, u32[]{:S(2)}, u32[]{:S(2)}) collective-permute-start(f32[4,1024]{1,0:T(4,128)S(1)} %add.142), channel_id=1, source_target_pairs={{0,16},{2,18},{4,20},{6,22},{8,24},{10,26},{12,28},{14,30},{16,0},... | collective-permute-start | bytes 49160 | tf_op jit(solution)/shard_map/ppermute | solution.py:34
  165.7 1.7 collective-permute-done.11
  167.5 4.5 %collective-permute-start.12 = (f32[4,1024]{1,0:T(4,128)S(1)}, f32[4,1024]{1,0:T(4,128)S(1)}, u32[]{:S(2)}, u32[]{:S(2)}) collective-permute-start(f32[4,1024]{1,0:T(4,128)S(1)} %add.143), channel_id=1, source_target_pairs={{0,32},{2,34},{4,36},{6,38},{8,40},{10,42},{12,44},{14,46},{16,48}... | collective-permute-start | bytes 49160 | tf_op jit(solution)/shard_map/ppermute | solution.py:34
  172.0 1.7 collective-permute-done.12
  173.7 3.4 %collective-permute-start.13 = (f32[4,1024]{1,0:T(4,128)S(1)}, f32[4,1024]{1,0:T(4,128)S(1)}, u32[]{:S(2)}, u32[]{:S(2)}) collective-permute-start(f32[4,1024]{1,0:T(4,128)S(1)} %add.144), channel_id=1, source_target_pairs={{0,64},{2,66},{4,68},{6,70},{8,72},{10,74},{12,76},{14,78},{16,80}... | collective-permute-start | bytes 49160 | tf_op jit(solution)/shard_map/ppermute | solution.py:34
  177.1 1.7 collective-permute-done.13
  178.8 9.4 %collective-permute-start.14 = (f32[4,1024]{1,0:T(4,128)S(1)}, f32[4,1024]{1,0:T(4,128)S(1)}, u32[]{:S(2)}, u32[]{:S(2)}) collective-permute-start(f32[4,1024]{1,0:T(4,128)S(1)} %add.145), channel_id=1, source_target_pairs={{0,128},{2,130},{4,132},{6,134},{8,136},{10,138},{12,140},{14,142}... | collective-permute-start | bytes 49160 | tf_op jit(solution)/shard_map/ppermute | solution.py:34
  190.6 2.9 %fusion.11 = bf16[256,2048]{0,1:T(8,128)(2,1)S(1)} fusion(bf16[256,2048]{0,1:T(8,128)(2,1)} %collective-permute-done.5, f32[904,2048]{0,1:T(8,128)} %select_maximum_fusion, bf16[256,2048]{0,1:T(8,128)(2,1)S(1)} %collective-permute-done.7, pred[]{:T(512)S(6)} %eq.29), kind=kLoop, calls=%fused_computation.28 | loop fusion | flops 3145728 | bytes 5242881 | tf_op jit(solution)/shard_map/convert.3
  (98 shorter events, 25.9 us)
Async XLA Ops:
  0.6 29.7 %copy-start.16 = (s32[2,6]{1,0:T(2,128)S(1)}, s32[2,6]{1,0:T(2,128)}, u32[]{:S(2)}) copy-start(s32[2,6]{1,0:T(2,128)} %param.14) | copy-start | bytes 148
  3.2 25.9 %collective-permute-start = (bf16[256,2048]{0,1:T(8,128)(2,1)S(1)}, bf16[256,2048]{0,1:T(8,128)(2,1)S(1)}, u32[]{:S(2)}, u32[]{:S(2)}) collective-permute-start(bf16[256,2048]{0,1:T(8,128)(2,1)S(1)} %pad_maximum_fusion.3), channel_id=1, source_target_pairs={{0,4},{2,6},{4,8},{6,10},{8,12},{10,14},{12,16},{14,18},{16,20},{1... | collective-permute-start | bytes 3145736 | tf_op jit(solution)/shard_map/ppermute | solution.py:20
  6.9 30.8 %copy-start.15 = (f32[4,1024]{1,0:T(4,128)S(1)}, f32[4,1024]{1,0:T(4,128)}, u32[]{:S(2)}) copy-start(f32[4,1024]{1,0:T(4,128)} %param.13) | copy-start | bytes 49156
  30.3 9.6 %collective-permute-start.2 = (bf16[256,2048]{0,1:T(8,128)(2,1)}, bf16[256,2048]{0,1:T(8,128)(2,1)}, u32[]{:S(2)}, u32[]{:S(2)}) collective-permute-start(bf16[256,2048]{0,1:T(8,128)(2,1)} %broadcast_select_fusion), channel_id=1, source_target_pairs={{0,2},{2,0},{4,6},{6,4},{8,10},{10,8},{12,14},{14,12},{16,18},{18,... | collective-permute-start | bytes 3145736 | tf_op jit(solution)/shard_map/ppermute | solution.py:25
  34.2 4.3 %collective-permute-start.1 = (bf16[136,2048]{1,0:T(8,128)(2,1)}, bf16[136,2048]{1,0:T(8,128)(2,1)}, u32[]{:S(2)}, u32[]{:S(2)}) collective-permute-start(bf16[136,2048]{1,0:T(8,128)(2,1)} %copy.80), channel_id=1, source_target_pairs={{0,2},{2,4},{4,6},{6,8},{8,10},{10,12},{12,14},{14,16},{16,18},{18... | collective-permute-start | bytes 1671176 | tf_op jit(solution)/shard_map/ppermute | solution.py:20
  54.0 10.2 %copy-start.5 = (bf16[8,256,896]{1,2,0:T(8,128)(2,1)}, bf16[8,256,896]{1,2,0:T(8,128)(2,1)S(1)}, u32[]{:S(2)}) copy-start(bf16[8,256,896]{1,2,0:T(8,128)(2,1)S(1)} %fusion.8) | copy-start | bytes 11010052
  58.9 5.3 %copy-start = (f32[904,1024]{0,1:T(8,128)}, f32[904,1024]{0,1:T(8,128)S(1)}, u32[]{:S(2)}) copy-start(f32[904,1024]{0,1:T(8,128)S(1)} %fusion.15) | copy-start | bytes 11108356
  64.2 1.5 copy-start.9
  64.2 6.0 %copy-start.12 = (bf16[256,1024]{1,0:T(8,128)(2,1)S(1)}, bf16[256,1024]{1,0:T(8,128)(2,1)}, u32[]{:S(2)}) copy-start(bf16[256,1024]{1,0:T(8,128)(2,1)} %param.11) | copy-start | bytes 1572868
  64.2 6.0 %copy-start.14 = (f32[1024]{0:T(1024)S(1)}, f32[1024]{0:T(1024)}, u32[]{:S(2)}) copy-start(f32[1024]{0:T(1024)} %param.12) | copy-start | bytes 12292
  65.0 5.2 %collective-permute-start.3 = (f32[256]{0:T(256)S(1)}, f32[256]{0:T(256)S(1)}, u32[]{:S(2)}, u32[]{:S(2)}) collective-permute-start(f32[256]{0:T(256)S(1)} %get-tuple-element.32), channel_id=1, source_target_pairs={{0,1},{1,0},{2,3},{3,2},{4,5},{5,4},{6,7},{7,6},{8,9},{9,8},{10,11... | collective-permute-start | bytes 3080 | tf_op jit(solution)/shard_map/ppermute | solution.py:42
  70.7 5.4 %collective-permute-start.4 = (f32[256]{0:T(256)S(1)}, f32[256]{0:T(256)S(1)}, u32[]{:S(2)}, u32[]{:S(2)}) collective-permute-start(f32[256]{0:T(256)S(1)} %multiply_reduce_fusion.4), channel_id=1, source_target_pairs={{0,1},{1,0},{2,3},{3,2},{4,5},{5,4},{6,7},{7,6},{8,9},{9,8},{10,11... | collective-permute-start | bytes 3080 | tf_op jit(solution)/shard_map/ppermute | solution.py:42
  76.8 3.4 %copy-start.10 = (bf16[896,1024]{0,1:T(8,128)(2,1)S(1)}, bf16[896,1024]{0,1:T(8,128)(2,1)}, u32[]{:S(2)}) copy-start(bf16[896,1024]{0,1:T(8,128)(2,1)} %copy-done.9) | copy-start | bytes 5505028
  80.2 8.9 %copy-start.2 = (f32[8,128,896]{2,1,0:T(8,128)}, f32[8,128,896]{2,1,0:T(8,128)S(1)}, u32[]{:S(2)}) copy-start(f32[8,128,896]{2,1,0:T(8,128)S(1)} %fusion.32) | copy-start | bytes 11010052
  80.2 5.9 %copy-start.13 = (bf16[256,1024]{0,1:T(8,128)(2,1)S(1)}, bf16[256,1024]{0,1:T(8,128)(2,1)}, u32[]{:S(2)}) copy-start(bf16[256,1024]{0,1:T(8,128)(2,1)} %copy.110) | copy-start | bytes 1572868
  86.1 1.8 copy-start.7
  87.9 6.4 %copy-start.6 = (f32[8,896,128]{1,2,0:T(8,128)}, f32[8,896,128]{1,2,0:T(8,128)S(1)}, u32[]{:S(2)}) copy-start(f32[8,896,128]{1,2,0:T(8,128)S(1)} %convolution_multiply_fusion) | copy-start | bytes 11010052
  94.2 1.9 copy-start.4
  97.6 21.4 %collective-permute-start.5 = (bf16[256,2048]{0,1:T(8,128)(2,1)}, bf16[256,2048]{0,1:T(8,128)(2,1)}, u32[]{:S(2)}, u32[]{:S(2)}) collective-permute-start(bf16[256,2048]{0,1:T(8,128)(2,1)} %slice.103), channel_id=1, source_target_pairs={{0,2},{2,0},{4,6},{6,4},{8,10},{10,8},{12,14},{14,12},{16,18},{18,... | collective-permute-start | bytes 3145736 | tf_op jit(solution)/shard_map/ppermute | solution.py:25
  103.0 10.2 %copy-start.3 = (f32[8,128,896]{2,1,0:T(8,128)S(1)}, f32[8,128,896]{2,1,0:T(8,128)}, u32[]{:S(2)}) copy-start(f32[8,128,896]{2,1,0:T(8,128)} %copy-done.2) | copy-start | bytes 11010052
  103.0 15.5 %collective-permute-start.6 = (bf16[136,2048]{1,0:T(8,128)(2,1)S(1)}, bf16[136,2048]{1,0:T(8,128)(2,1)S(1)}, u32[]{:S(2)}, u32[]{:S(2)}) collective-permute-start(bf16[136,2048]{1,0:T(8,128)(2,1)S(1)} %copy.97), channel_id=1, source_target_pairs={{2,0},{4,2},{6,4},{8,6},{10,8},{12,10},{14,12},{16,14},{18,16},{20... | collective-permute-start | bytes 1671176 | tf_op jit(solution)/shard_map/ppermute | solution.py:20
  104.8 8.4 %copy-start.1 = (f32[904,1024]{0,1:T(8,128)S(1)}, f32[904,1024]{0,1:T(8,128)}, u32[]{:S(2)}) copy-start(f32[904,1024]{0,1:T(8,128)} %copy-done) | copy-start | bytes 11108356
  118.4 69.8 %copy-start.11 = (bf16[896,1024]{0,1:T(8,128)(2,1)S(1)}, bf16[896,1024]{0,1:T(8,128)(2,1)}, u32[]{:S(2)}) copy-start(bf16[896,1024]{0,1:T(8,128)(2,1)} %maximum_maximum_fusion.1) | copy-start | bytes 5505028
  119.0 69.3 %copy-start.8 = (bf16[8,256,896]{1,2,0:T(8,128)(2,1)S(1)}, bf16[8,256,896]{1,2,0:T(8,128)(2,1)}, u32[]{:S(2)}) copy-start(bf16[8,256,896]{1,2,0:T(8,128)(2,1)} %copy-done.7) | copy-start | bytes 11010052
  123.4 67.3 %collective-permute-start.7 = (bf16[256,2048]{0,1:T(8,128)(2,1)}, bf16[256,2048]{0,1:T(8,128)(2,1)S(1)}, u32[]{:S(2)}, u32[]{:S(2)}) collective-permute-start(bf16[256,2048]{0,1:T(8,128)(2,1)} %fusion.13), channel_id=1, source_target_pairs={{4,0},{6,2},{8,4},{10,6},{12,8},{14,10},{16,12},{18,14},{20,16},{2... | collective-permute-start | bytes 3145736 | tf_op jit(solution)/shard_map/ppermute | solution.py:20
  124.7 2.1 %collective-permute-start.8 = (f32[4,1024]{1,0:T(4,128)S(1)}, f32[4,1024]{1,0:T(4,128)S(1)}, u32[]{:S(2)}, u32[]{:S(2)}) collective-permute-start(f32[4,1024]{1,0:T(4,128)S(1)} %pad_maximum_fusion.4), channel_id=1, source_target_pairs={{0,2},{2,0},{4,6},{6,4},{8,10},{10,8},{12,14},{14,12},{16,18},{18,... | collective-permute-start | bytes 49160 | tf_op jit(solution)/shard_map/ppermute | solution.py:34
  126.7 28.0 %collective-permute-start.9 = (f32[4,1024]{1,0:T(4,128)S(1)}, f32[4,1024]{1,0:T(4,128)S(1)}, u32[]{:S(2)}, u32[]{:S(2)}) collective-permute-start(f32[4,1024]{1,0:T(4,128)S(1)} %fusion.27), channel_id=1, source_target_pairs={{0,4},{2,6},{4,0},{6,2},{8,12},{10,14},{12,8},{14,10},{16,20},{18,... | collective-permute-start | bytes 49160 | tf_op jit(solution)/shard_map/ppermute | solution.py:34
  154.8 5.3 %collective-permute-start.10 = (f32[4,1024]{1,0:T(4,128)S(1)}, f32[4,1024]{1,0:T(4,128)S(1)}, u32[]{:S(2)}, u32[]{:S(2)}) collective-permute-start(f32[4,1024]{1,0:T(4,128)S(1)} %fusion.47), channel_id=1, source_target_pairs={{0,8},{2,10},{4,12},{6,14},{8,0},{10,2},{12,4},{14,6},{16,24},{18,... | collective-permute-start | bytes 49160 | tf_op jit(solution)/shard_map/ppermute | solution.py:34
  160.2 7.3 %collective-permute-start.11 = (f32[4,1024]{1,0:T(4,128)S(1)}, f32[4,1024]{1,0:T(4,128)S(1)}, u32[]{:S(2)}, u32[]{:S(2)}) collective-permute-start(f32[4,1024]{1,0:T(4,128)S(1)} %add.142), channel_id=1, source_target_pairs={{0,16},{2,18},{4,20},{6,22},{8,24},{10,26},{12,28},{14,30},{16,0},... | collective-permute-start | bytes 49160 | tf_op jit(solution)/shard_map/ppermute | solution.py:34
  167.5 6.3 %collective-permute-start.12 = (f32[4,1024]{1,0:T(4,128)S(1)}, f32[4,1024]{1,0:T(4,128)S(1)}, u32[]{:S(2)}, u32[]{:S(2)}) collective-permute-start(f32[4,1024]{1,0:T(4,128)S(1)} %add.143), channel_id=1, source_target_pairs={{0,32},{2,34},{4,36},{6,38},{8,40},{10,42},{12,44},{14,46},{16,48}... | collective-permute-start | bytes 49160 | tf_op jit(solution)/shard_map/ppermute | solution.py:34
  173.7 5.1 %collective-permute-start.13 = (f32[4,1024]{1,0:T(4,128)S(1)}, f32[4,1024]{1,0:T(4,128)S(1)}, u32[]{:S(2)}, u32[]{:S(2)}) collective-permute-start(f32[4,1024]{1,0:T(4,128)S(1)} %add.144), channel_id=1, source_target_pairs={{0,64},{2,66},{4,68},{6,70},{8,72},{10,74},{12,76},{14,78},{16,80}... | collective-permute-start | bytes 49160 | tf_op jit(solution)/shard_map/ppermute | solution.py:34
  178.8 11.2 %collective-permute-start.14 = (f32[4,1024]{1,0:T(4,128)S(1)}, f32[4,1024]{1,0:T(4,128)S(1)}, u32[]{:S(2)}, u32[]{:S(2)}) collective-permute-start(f32[4,1024]{1,0:T(4,128)S(1)} %add.145), channel_id=1, source_target_pairs={{0,128},{2,130},{4,132},{6,134},{8,136},{10,138},{12,140},{14,142}... | collective-permute-start | bytes 49160 | tf_op jit(solution)/shard_map/ppermute | solution.py:34
  (1 other events, 1.4 us)

commit v3 on v2

v3 whole, which is shorter than its diff:
```python
import jax
import jax.numpy as jnp
from jax import lax
from jax.experimental import pallas as pl
from jax.sharding import PartitionSpec as P

D = 2048
HD = 128
BLK = 128
REACH = 3
WIN = 6


NEG_FILL = -1e30
NORM_EPS = 1e-06


def from_behind(block, axis, distance):
    devices = range(lax.axis_size(axis))
    route = [(i - distance, i) for i in devices if i - distance in devices]
    return lax.ppermute(block, axis, route)


def chip_swap(block, axis):
    size = lax.axis_size(axis)
    return lax.ppermute(block, axis, [(i, i ^ 1) for i in range(size)])


def all_sum(block, axis):
    size = lax.axis_size(axis)
    if size & (size - 1):
        return lax.psum(block, axis)
    stride = 1
    while stride < size:
        block = block + lax.ppermute(block, axis, [(i, i ^ stride) for i in range(size)])
        stride *= 2
    return block


def pair_sum(block, axis):
    if lax.axis_size(axis) != 2:
        return lax.psum(block, axis)
    return block + lax.ppermute(block, axis, [(0, 1), (1, 0)])


def split_heads(array):
    return array.reshape(array.shape[0], array.shape[1] // HD, HD)


def _scores(q_ref, k_ref, allowed_ref):
    raw = lax.dot_general(
        q_ref[...], k_ref[...], (((1,), (1,)), ((), ())), preferred_element_type=jnp.float32
    ) * (HD ** (-0.5))
    allowed = allowed_ref[...] > 0
    return jnp.where(allowed, raw, NEG_FILL), allowed


def _forward_kernel(q_ref, k_ref, v_ref, allowed_ref, out_ref, peak_ref, total_ref):
    scores, allowed = _scores(q_ref, k_ref, allowed_ref)
    peak = jnp.max(scores, axis=1, keepdims=True)
    expo = jnp.where(allowed, jnp.exp(scores - peak), 0.0)
    total = jnp.sum(expo, axis=1, keepdims=True)
    weights = (expo / total).astype(jnp.bfloat16)
    out_ref[...] = jnp.dot(weights, v_ref[...], preferred_element_type=jnp.float32)
    peak_ref[...] = jnp.broadcast_to(peak, peak_ref.shape)
    total_ref[...] = jnp.broadcast_to(total, total_ref.shape)


def _backward_kernel(q_ref, k_ref, v_ref, allowed_ref, g_ref, peak_ref, total_ref, delta_ref,
                     dq_ref, dk_ref, dv_ref):
    scores, allowed = _scores(q_ref, k_ref, allowed_ref)
    expo = jnp.where(allowed, jnp.exp(scores - peak_ref[:, :1]), 0.0)
    prob = expo / total_ref[:, :1]
    grad = g_ref[...]
    prob_grad = lax.dot_general(
        grad, v_ref[...], (((1,), (1,)), ((), ())), preferred_element_type=jnp.float32
    )
    score_grad = (prob * (prob_grad - delta_ref[:, :1])).astype(jnp.bfloat16)
    scale = HD ** (-0.5)
    dq_ref[...] = jnp.dot(score_grad, k_ref[...], preferred_element_type=jnp.float32) * scale
    dk_ref[...] = lax.dot_general(
        score_grad, q_ref[...], (((0,), (0,)), ((), ())), preferred_element_type=jnp.float32
    ) * scale
    dv_ref[...] = lax.dot_general(
        prob.astype(jnp.bfloat16), grad, (((0,), (0,)), ((), ())), preferred_element_type=jnp.float32
    )


def _head_spec(rows):
    return pl.BlockSpec((rows, HD), lambda h: (0, h))


def attention_forward(queries, key_win, value_win, allowed, interpret=False):
    rows, channels = queries.shape
    keys_n = key_win.shape[0]
    heads = channels // HD
    return pl.pallas_call(
        _forward_kernel,
        grid=(heads,),
        in_specs=[_head_spec(rows), _head_spec(keys_n), _head_spec(keys_n),
                  pl.BlockSpec((rows, keys_n), lambda h: (0, 0))],
        out_specs=[_head_spec(rows), _head_spec(rows), _head_spec(rows)],
        out_shape=[jax.ShapeDtypeStruct((rows, channels), jnp.float32)] * 3,
        interpret=interpret,
    )(queries, key_win, value_win, allowed)


def attention_backward(queries, key_win, value_win, allowed, grad, peak, total, delta, interpret=False):
    rows, channels = queries.shape
    keys_n = key_win.shape[0]
    heads = channels // HD
    return pl.pallas_call(
        _backward_kernel,
        grid=(heads,),
        in_specs=[_head_spec(rows), _head_spec(keys_n), _head_spec(keys_n),
                  pl.BlockSpec((rows, keys_n), lambda h: (0, 0)),
                  _head_spec(rows), _head_spec(rows), _head_spec(rows), _head_spec(rows)],
        out_specs=[_head_spec(rows), _head_spec(keys_n), _head_spec(keys_n)],
        out_shape=[jax.ShapeDtypeStruct((rows, channels), jnp.float32),
                   jax.ShapeDtypeStruct((keys_n, channels), jnp.float32),
                   jax.ShapeDtypeStruct((keys_n, channels), jnp.float32)],
        interpret=interpret,
    )(queries, key_win, value_win, allowed, grad, peak, total, delta)


def window_mask(block_bits, device, row_count, key_count):
    per_device = row_count // BLK
    key_blocks = key_count // BLK
    first_block = device * per_device - (key_blocks - per_device)
    qb = jnp.arange(per_device, dtype=jnp.int32)
    kb = jnp.arange(key_blocks, dtype=jnp.int32)
    relative = qb[:, None] + (key_blocks - per_device) - kb[None, :]
    one_hot = relative[:, :, None] == jnp.arange(WIN, dtype=jnp.int32)[None, None, :]
    picked_bits = jnp.sum(jnp.where(one_hot, block_bits[:, None, :], 0), axis=2)
    coarse = (picked_bits > 0) & (relative >= 0) & (relative < WIN) & (first_block + kb[None, :] >= 0)
    fine = jnp.repeat(jnp.repeat(coarse, BLK, axis=0), BLK, axis=1)
    q = jnp.arange(row_count, dtype=jnp.int32)
    s = jnp.arange(key_count, dtype=jnp.int32)
    causal = s[None, :] <= q[:, None] + (key_count - row_count)
    return fine & causal


def body(queries, keys, values_in, teacher, gain, conv_weight, block_bits, mask_pos):
    row_count, channels = queries.shape
    tap_count = conv_weight.shape[0]
    rim_rows = tap_count - 1
    device = lax.axis_index("tm")
    even = device % 2 == 0
    score_scale = HD ** (-0.5)
    far_rows = row_count - BLK
    far_lead = 8
    key_count = REACH * row_count + (row_count - far_rows)

    def relay(own):
        second = from_behind(own, "tm", 2)
        first = chip_swap(jnp.where(even, own, second), "tm")
        third = from_behind(second[far_rows - far_lead :], "tm", 1)
        return jnp.concatenate([third, second, first, own], 0)

    key_win = relay(keys)[far_lead:]
    vin_win = relay(values_in).astype(jnp.float32)

    conv_sum = jnp.zeros((key_count, channels), jnp.float32)
    for tap_index in range(tap_count):
        conv_sum = conv_sum + conv_weight[tap_index] * vin_win[far_lead - tap_index : far_lead - tap_index + key_count]
    value_win = conv_sum.astype(jnp.bfloat16)

    allowed = window_mask(block_bits, device, row_count, key_count).astype(jnp.float32)
    flattened, row_peak, row_total = attention_forward(queries, key_win, value_win, allowed)

    squares = pair_sum(jnp.sum(flattened * flattened, axis=1), "head")
    inverse = lax.rsqrt(squares / D + NORM_EPS)
    prediction = flattened * inverse[:, None] * gain
    position = jnp.arange(row_count, dtype=jnp.int32) % BLK
    chosen = jnp.any(jnp.repeat(mask_pos, BLK, axis=0) == position[:, None], axis=1)
    residual = jnp.where(chosen[:, None], prediction - teacher.astype(jnp.float32), 0.0)
    scaled = residual * gain
    cross_term = pair_sum(jnp.sum(scaled * flattened, axis=1), "head")
    out_grad = (
        inverse[:, None] * scaled - flattened * (inverse**3 * cross_term / D)[:, None]
    ).astype(jnp.bfloat16)
    grad_f = out_grad.astype(jnp.float32)
    delta = jnp.sum(split_heads(grad_f * flattened), axis=2)
    delta_wide = jnp.repeat(delta, HD, axis=1)
    query_grad, key_part, value_part = attention_backward(
        queries, key_win, value_win, allowed, out_grad, row_peak, row_total, delta_wide
    )

    local_taps = jnp.stack(
        [
            jnp.sum(value_part * vin_win[far_lead - tap_index : far_lead - tap_index + key_count], axis=0)
            for tap_index in range(tap_count)
        ]
    )
    conv_grad = all_sum(local_taps, "tm")

    lead = jnp.zeros((far_lead, channels), jnp.float32)
    padded_value = jnp.concatenate([lead, value_part, jnp.zeros((rim_rows, channels), jnp.float32)], 0)
    value_sum = jnp.zeros((key_count + far_lead, channels), jnp.float32)
    for tap_index in range(tap_count):
        value_sum = value_sum + conv_weight[tap_index] * padded_value[tap_index : tap_index + key_count + far_lead]

    def relay_back(grads):
        cut_third = row_count - far_rows + far_lead
        grad_third = grads[:cut_third]
        grad_second = grads[cut_third : cut_third + row_count]
        grad_first = grads[cut_third + row_count : cut_third + 2 * row_count]
        grad_own = grads[cut_third + 2 * row_count :]
        back_third = from_behind(grad_third.astype(jnp.bfloat16), "tm", -1).astype(jnp.float32)
        back_first = chip_swap(grad_first.astype(jnp.bfloat16), "tm").astype(jnp.float32)
        grad_second = grad_second + jnp.concatenate(
            [jnp.zeros((far_rows - far_lead, grads.shape[1]), jnp.float32), back_third], 0
        )
        grad_second = grad_second + jnp.where(even, 0.0, back_first)
        back_second = from_behind(grad_second.astype(jnp.bfloat16), "tm", -2).astype(jnp.float32)
        return grad_own + jnp.where(even, back_first, 0.0) + back_second

    value_total = relay_back(value_sum)
    key_total = relay_back(jnp.concatenate([lead, key_part], 0))

    return (
        query_grad.astype(jnp.bfloat16),
        key_total.astype(jnp.bfloat16),
        value_total.astype(jnp.bfloat16),
        conv_grad,
    )


def solution(mesh):
    placed = (
        P("tm", "head"),
        P("tm", "head"),
        P("tm", "head"),
        P("tm", "head"),
        P("head"),
        P(None, "head"),
        P("tm", None),
        P("tm", None),
    )
    return jax.shard_map(
        body,
        mesh=mesh,
        in_specs=placed,
        out_specs=(P("tm", "head"), P("tm", "head"), P("tm", "head"), P(None, "head")),
        check_vma=False,
    )
```

time: 196 us -> 172 us (0.88)
  the two profiles are of different devices: /device:TPU:4 before, /device:TPU:28 now
where the time goes in v3:
time: 172 us; the launch traced here: 171 us
  waiting for transfers between devices  54.6 us (32%)
  starting transfers between devices  45.5 us (26%)
  other arithmetic  42.4 us (25%)
  Pallas kernels  22.9 us (13%)
  local copies, waits for them, and re-layouts  4.6 us (3%)
    ppermute x7, waiting for transfers between devices, all_sum(): lax.ppermute(block, axis, [(i, i ^ stride) for i in range(size)])  27.9 us
    ppermute x7, starting transfers between devices, all_sum(): lax.ppermute(block, axis, [(i, i ^ stride) for i in range(size)])  22.6 us
    ppermute x8, starting transfers between devices, from_behind(): return lax.ppermute(block, axis, route)  21.2 us
    broadcast_in_dim x1, other arithmetic, body(): delta_wide = jnp.repeat(delta, HD, axis=1)  19.5 us
    ppermute x8, waiting for transfers between devices, from_behind(): return lax.ppermute(block, axis, route)  17.6 us
    pallas_call x1, Pallas kernels, attention_backward(): pl.pallas_call(_backward_kernel, grid=(heads,), in_specs=[_head_spec(rows...  12.8 us
    pallas_call x1, Pallas kernels, attention_forward(): pl.pallas_call(_forward_kernel, grid=(heads,), in_specs=[_head_spec(rows)...  10.1 us
    ppermute x2, waiting for transfers between devices, pair_sum(): return block + lax.ppermute(block, axis, [(0, 1), (1, 0)])  8.98 us
  transfers between devices with their start and end apart: 21, of which 11 were waited for; matrix products, arithmetic and copies ran while one was open for 8% of the time, Pallas kernels for 0%

profile of v3, /device:TPU:28, one launch (start us, length us, event | category | flops | bytes accessed | tf_op | source)
XLA Modules:
  0.0 171.0 jit_solution(3175449996537748032)
XLA Ops:
  0.7 2.9 %collective-permute-start.3 = (bf16[256,1024]{1,0:T(8,128)(2,1)}, bf16[256,1024]{1,0:T(8,128)(2,1)S(1)}, u32[]{:S(2)}, u32[]{:S(2)}) collective-permute-start(bf16[256,1024]{1,0:T(8,128)(2,1)} %param.10), channel_id=1, source_target_pairs={{0,4},{2,6},{4,8},{6,10},{8,12},{10,14},{12,16},{14,18},{16,20},{1... | collective-permute-start | bytes 1572872 | tf_op jit(solution)/shard_map/ppermute | solution.py:21
  3.6 3.5 %collective-permute-start = (bf16[256,1024]{1,0:T(8,128)(2,1)}, bf16[256,1024]{1,0:T(8,128)(2,1)S(1)}, u32[]{:S(2)}, u32[]{:S(2)}) collective-permute-start(bf16[256,1024]{1,0:T(8,128)(2,1)} %param.9), channel_id=1, source_target_pairs={{0,4},{2,6},{4,8},{6,10},{8,12},{10,14},{12,16},{14,18},{16,20},{1... | collective-permute-start | bytes 1572872 | tf_op jit(solution)/shard_map/ppermute | solution.py:21
  9.8 7.9 %collective-permute-done.3 = bf16[256,1024]{1,0:T(8,128)(2,1)S(1)} collective-permute-done((bf16[256,1024]{1,0:T(8,128)(2,1)}, bf16[256,1024]{1,0:T(8,128)(2,1)S(1)}, u32[]{:S(2)}, u32[]{:S(2)}) %collective-permute-start.3) | collective-permute-done | bytes 524320 | tf_op jit(solution)/shard_map/ppermute | solution.py:21
  19.8 2.4 %collective-permute-start.4 = (bf16[136,1024]{1,0:T(8,128)(2,1)S(1)}, bf16[136,1024]{1,0:T(8,128)(2,1)S(1)}, u32[]{:S(2)}, u32[]{:S(2)}) collective-permute-start(bf16[136,1024]{1,0:T(8,128)(2,1)S(1)} %slice.103), channel_id=1, source_target_pairs={{0,2},{2,4},{4,6},{6,8},{8,10},{10,12},{12,14},{14,16},{16,18},{18... | collective-permute-start | bytes 835592 | tf_op jit(solution)/shard_map/ppermute | solution.py:21
  22.2 6.7 %collective-permute-done = bf16[256,1024]{1,0:T(8,128)(2,1)S(1)} collective-permute-done((bf16[256,1024]{1,0:T(8,128)(2,1)}, bf16[256,1024]{1,0:T(8,128)(2,1)S(1)}, u32[]{:S(2)}, u32[]{:S(2)}) %collective-permute-start) | collective-permute-done | bytes 524320 | tf_op jit(solution)/shard_map/ppermute | solution.py:21
  29.1 2.4 %collective-permute-start.1 = (bf16[136,1024]{1,0:T(8,128)(2,1)S(1)}, bf16[136,1024]{1,0:T(8,128)(2,1)S(1)}, u32[]{:S(2)}, u32[]{:S(2)}) collective-permute-start(bf16[136,1024]{1,0:T(8,128)(2,1)S(1)} %slice.102), channel_id=1, source_target_pairs={{0,2},{2,4},{4,6},{6,8},{8,10},{10,12},{12,14},{14,16},{16,18},{18... | collective-permute-start | bytes 835592 | tf_op jit(solution)/shard_map/ppermute | solution.py:21
  32.0 2.6 %add_convert_fusion.v_ref = bf16[896,1024]{1,0:T(8,128)(2,1)} fusion(f32[904,1024]{1,0:T(8,128)S(1)} %maximum_convert_fusion, f32[1024]{0:T(1024)S(1)} %bitcast.40, f32[1024]{0:T(1024)S(1)} %bitcast.42, f32[1024]{0:T(1024)S(1)} %bitcast.38, f32[1024]{0:T(1024)S(1)} %bitcast.36), kind=kLoop, calls=%fused_computation.12 | loop fusion | flops 7340032 | bytes 16531456 | tf_op jit(solution)/shard_map/convert_element_type | solution.py:166
  34.6 2.4 %collective-permute-done.1 = bf16[136,1024]{1,0:T(8,128)(2,1)S(1)} collective-permute-done((bf16[136,1024]{1,0:T(8,128)(2,1)S(1)}, bf16[136,1024]{1,0:T(8,128)(2,1)S(1)}, u32[]{:S(2)}, u32[]{:S(2)}) %collective-permute-start.1) | collective-permute-done | bytes 278560 | tf_op jit(solution)/shard_map/ppermute | solution.py:21
  37.0 1.4 pad_maximum_fusion.k_ref
  38.4 10.1 %shard_map.111 = (f32[256,1024]{1,0:T(8,128)}, f32[256,1024]{1,0:T(8,128)}, f32[256,1024]{1,0:T(8,128)}) custom-call(bf16[256,1024]{1,0:T(8,128)(2,1)} %q_ref.3, bf16[896,1024]{1,0:T(8,128)(2,1)} %pad_maximum_fusion.k_ref, bf16[896,1024]{1,0:T(8,128)(2,1)} %add_convert_fusion.v_ref, f32[256,896]{1,0:T(8,128)} %fusion.15.allowed_ref), custom_call_target="tpu_custom_call" | custom-call | tf_op jit(solution)/shard_map/pallas_call | solution.py:97
  48.5 1.4 multiply_reduce_fusion.5
  50.6 4.5 %collective-permute-done.6 = f32[256]{0:T(256)S(1)} collective-permute-done((f32[256]{0:T(256)S(1)}, f32[256]{0:T(256)S(1)}, u32[]{:S(2)}, u32[]{:S(2)}) %collective-permute-start.6) | collective-permute-done | bytes 1056 | tf_op jit(solution)/shard_map/ppermute | solution.py:43
  55.1 1.7 multiply_reduce_fusion.4
  57.4 4.5 %collective-permute-done.7 = f32[256]{0:T(256)S(1)} collective-permute-done((f32[256]{0:T(256)S(1)}, f32[256]{0:T(256)S(1)}, u32[]{:S(2)}, u32[]{:S(2)}) %collective-permute-start.7) | collective-permute-done | bytes 1056 | tf_op jit(solution)/shard_map/ppermute | solution.py:43
  61.9 2.5 %multiply_bitcast_fusion = (f32[32,8,8,128]{3,1,2,0:T(8,128)S(1)}, bf16[256,1024]{1,0:T(8,128)(2,1)}) fusion(f32[256,1024]{1,0:T(8,128)} %get-tuple-element.10, f32[256]{0:T(256)S(1)} %fusion.18, bf16[256,1024]{1,0:T(8,128)(2,1)S(1)} %copy-done.5, f32[1024]{0:T(1024)S(1)} %copy-done.8, pred[256]{0:T(512)(128)(4,1)S(1)} %bitcast.45, f32[256]{0:T(256)S(1)} %add_rsqrt_fusion), kind=kLoop, calls=%fused_computation.34 | loop fusion | flops 3145728 | bytes 3152128
  64.6 19.5 %fusion = f32[256,8,128]{2,1,0:T(8,128)S(1)} fusion(f32[256,8,128]{2,1,0:T(8,128)S(1)} %bitcast.21), kind=kOutput, calls=%fused_computation | output fusion | flops 2175 | bytes 2097152 | tf_op jit(solution)/shard_map/broadcast_in_dim | solution.py:184
  85.2 12.8 %shard_map.112 = (f32[256,1024]{1,0:T(8,128)}, f32[896,1024]{1,0:T(8,128)}, f32[896,1024]{1,0:T(8,128)}) custom-call(bf16[256,1024]{1,0:T(8,128)(2,1)} %q_ref.3, bf16[896,1024]{1,0:T(8,128)(2,1)} %pad_maximum_fusion.k_ref, bf16[896,1024]{1,0:T(8,128)(2,1)} %add_convert_fusion.v_ref, f32[256,896]{1,0:T(8,128)} %fusion.15.allowed_ref, ...), custom_call_target="tpu_custom_call" | custom-call | tf_op jit(solution)/shard_map/pallas_call | solution.py:112
  98.0 2.6 %maximum_maximum_fusion = f32[907,1024]{1,0:T(8,128)S(1)} fusion(f32[896,1024]{1,0:T(8,128)} %get-tuple-element.15, f32[907]{0:T(1024)S(1)} %pad.13.clone, f32[907]{0:T(1024)S(1)} %pad.11.clone), kind=kLoop, calls=%fused_computation.1 | loop fusion | flops 1857536 | bytes 7392344 | tf_op jit(solution)/shard_map/concatenate | solution.py:198
  101.2 1.7 fusion.20
  103.2 1.7 %multiply_reduce_fusion.3 = (f32[1024]{0:T(1024)S(1)}, f32[1024]{0:T(1024)S(1)}, f32[1024]{0:T(1024)S(1)}, f32[1024]{0:T(1024)S(1)}) fusion(f32[896,1024]{1,0:T(8,128)S(1)} %copy-done.2, f32[904,1024]{1,0:T(8,128)S(1)} %copy-done.1), kind=kLoop, calls=%fused_computation.11 | loop fusion | flops 7335936 | bytes 18366464 | tf_op jit(solution)/shard_map/reduce_sum | solution.py:191
  105.4 2.5 %collective-permute-start.12 = (bf16[136,1024]{1,0:T(8,128)(2,1)S(1)}, bf16[136,1024]{1,0:T(8,128)(2,1)S(1)}, u32[]{:S(2)}, u32[]{:S(2)}) collective-permute-start(bf16[136,1024]{1,0:T(8,128)(2,1)S(1)} %slice.115), channel_id=1, source_target_pairs={{2,0},{4,2},{6,4},{8,6},{10,8},{12,10},{14,12},{16,14},{18,16},{20... | collective-permute-start | bytes 835592 | tf_op jit(solution)/shard_map/ppermute | solution.py:21
  108.5 2.5 %collective-permute-start.9 = (bf16[136,1024]{1,0:T(8,128)(2,1)S(1)}, bf16[136,1024]{1,0:T(8,128)(2,1)S(1)}, u32[]{:S(2)}, u32[]{:S(2)}) collective-permute-start(bf16[136,1024]{1,0:T(8,128)(2,1)S(1)} %pad_slice_fusion), channel_id=1, source_target_pairs={{2,0},{4,2},{6,4},{8,6},{10,8},{12,10},{14,12},{16,14},{18,16},{20... | collective-permute-start | bytes 835592 | tf_op jit(solution)/shard_map/ppermute | solution.py:21
  112.1 3.1 %collective-permute-start.13 = (bf16[256,1024]{1,0:T(8,128)(2,1)S(1)}, bf16[256,1024]{1,0:T(8,128)(2,1)S(1)}, u32[]{:S(2)}, u32[]{:S(2)}) collective-permute-start(bf16[256,1024]{1,0:T(8,128)(2,1)S(1)} %fusion.13), channel_id=1, source_target_pairs={{4,0},{6,2},{8,4},{10,6},{12,8},{14,10},{16,12},{18,14},{20,16},{2... | collective-permute-start | bytes 1572872 | tf_op jit(solution)/shard_map/ppermute | solution.py:21
  115.5 2.0 %collective-permute-start.10 = (bf16[256,1024]{1,0:T(8,128)(2,1)S(1)}, bf16[256,1024]{1,0:T(8,128)(2,1)S(1)}, u32[]{:S(2)}, u32[]{:S(2)}) collective-permute-start(bf16[256,1024]{1,0:T(8,128)(2,1)S(1)} %fusion.8), channel_id=1, source_target_pairs={{4,0},{6,2},{8,4},{10,6},{12,8},{14,10},{16,12},{18,14},{20,16},{2... | collective-permute-start | bytes 1572872 | tf_op jit(solution)/shard_map/ppermute | solution.py:21
  118.2 21.9 %collective-permute-done.16 = f32[4,1024]{1,0:T(4,128)S(1)} collective-permute-done((f32[4,1024]{1,0:T(4,128)S(1)}, f32[4,1024]{1,0:T(4,128)S(1)}, u32[]{:S(2)}, u32[]{:S(2)}) %collective-permute-start.16) | collective-permute-done | bytes 16416 | tf_op jit(solution)/shard_map/ppermute | solution.py:35
  140.1 5.3 %collective-permute-start.17 = (f32[4,1024]{1,0:T(4,128)S(1)}, f32[4,1024]{1,0:T(4,128)S(1)}, u32[]{:S(2)}, u32[]{:S(2)}) collective-permute-start(f32[4,1024]{1,0:T(4,128)S(1)} %add.160), channel_id=1, source_target_pairs={{0,16},{2,18},{4,20},{6,22},{8,24},{10,26},{12,28},{14,30},{16,0},... | collective-permute-start | bytes 49160 | tf_op jit(solution)/shard_map/ppermute | solution.py:35
  145.4 1.7 %collective-permute-done.17 = f32[4,1024]{1,0:T(4,128)S(1)} collective-permute-done((f32[4,1024]{1,0:T(4,128)S(1)}, f32[4,1024]{1,0:T(4,128)S(1)}, u32[]{:S(2)}, u32[]{:S(2)}) %collective-permute-start.17) | collective-permute-done | bytes 16416 | tf_op jit(solution)/shard_map/ppermute | solution.py:35
  147.1 3.6 %collective-permute-start.18 = (f32[4,1024]{1,0:T(4,128)S(1)}, f32[4,1024]{1,0:T(4,128)S(1)}, u32[]{:S(2)}, u32[]{:S(2)}) collective-permute-start(f32[4,1024]{1,0:T(4,128)S(1)} %add.161), channel_id=1, source_target_pairs={{0,32},{2,34},{4,36},{6,38},{8,40},{10,42},{12,44},{14,46},{16,48}... | collective-permute-start | bytes 49160 | tf_op jit(solution)/shard_map/ppermute | solution.py:35
  150.7 1.7 %collective-permute-done.18 = f32[4,1024]{1,0:T(4,128)S(1)} collective-permute-done((f32[4,1024]{1,0:T(4,128)S(1)}, f32[4,1024]{1,0:T(4,128)S(1)}, u32[]{:S(2)}, u32[]{:S(2)}) %collective-permute-start.18) | collective-permute-done | bytes 16416 | tf_op jit(solution)/shard_map/ppermute | solution.py:35
  152.4 3.4 %collective-permute-start.19 = (f32[4,1024]{1,0:T(4,128)S(1)}, f32[4,1024]{1,0:T(4,128)S(1)}, u32[]{:S(2)}, u32[]{:S(2)}) collective-permute-start(f32[4,1024]{1,0:T(4,128)S(1)} %add.162), channel_id=1, source_target_pairs={{0,64},{2,66},{4,68},{6,70},{8,72},{10,74},{12,76},{14,78},{16,80}... | collective-permute-start | bytes 49160 | tf_op jit(solution)/shard_map/ppermute | solution.py:35
  155.8 1.7 %collective-permute-done.19 = f32[4,1024]{1,0:T(4,128)S(1)} collective-permute-done((f32[4,1024]{1,0:T(4,128)S(1)}, f32[4,1024]{1,0:T(4,128)S(1)}, u32[]{:S(2)}, u32[]{:S(2)}) %collective-permute-start.19) | collective-permute-done | bytes 16416 | tf_op jit(solution)/shard_map/ppermute | solution.py:35
  157.5 9.1 %collective-permute-start.20 = (f32[4,1024]{1,0:T(4,128)S(1)}, f32[4,1024]{1,0:T(4,128)S(1)}, u32[]{:S(2)}, u32[]{:S(2)}) collective-permute-start(f32[4,1024]{1,0:T(4,128)S(1)} %add.163), channel_id=1, source_target_pairs={{0,128},{2,130},{4,132},{6,134},{8,136},{10,138},{12,140},{14,142}... | collective-permute-start | bytes 49160 | tf_op jit(solution)/shard_map/ppermute | solution.py:35
  (86 shorter events, 16.5 us)
Async XLA Ops:
  0.6 30.9 %copy-start.6 = (bf16[256,1024]{1,0:T(8,128)(2,1)S(1)}, bf16[256,1024]{1,0:T(8,128)(2,1)}, u32[]{:S(2)}) copy-start(bf16[256,1024]{1,0:T(8,128)(2,1)} %param.10) | copy-start | bytes 1572868
  0.6 28.3 %copy-start.4 = (bf16[256,1024]{1,0:T(8,128)(2,1)S(1)}, bf16[256,1024]{1,0:T(8,128)(2,1)}, u32[]{:S(2)}) copy-start(bf16[256,1024]{1,0:T(8,128)(2,1)} %param.9) | copy-start | bytes 1572868
  0.7 17.0 %collective-permute-start.3 = (bf16[256,1024]{1,0:T(8,128)(2,1)}, bf16[256,1024]{1,0:T(8,128)(2,1)S(1)}, u32[]{:S(2)}, u32[]{:S(2)}) collective-permute-start(bf16[256,1024]{1,0:T(8,128)(2,1)} %param.10), channel_id=1, source_target_pairs={{0,4},{2,6},{4,8},{6,10},{8,12},{10,14},{12,16},{14,18},{16,20},{1... | collective-permute-start | bytes 1572872 | tf_op jit(solution)/shard_map/ppermute | solution.py:21
  3.6 25.4 %collective-permute-start = (bf16[256,1024]{1,0:T(8,128)(2,1)}, bf16[256,1024]{1,0:T(8,128)(2,1)S(1)}, u32[]{:S(2)}, u32[]{:S(2)}) collective-permute-start(bf16[256,1024]{1,0:T(8,128)(2,1)} %param.9), channel_id=1, source_target_pairs={{0,4},{2,6},{4,8},{6,10},{8,12},{10,14},{12,16},{14,18},{16,20},{1... | collective-permute-start | bytes 1572872 | tf_op jit(solution)/shard_map/ppermute | solution.py:21
  18.8 12.7 %collective-permute-start.5 = (bf16[256,1024]{1,0:T(8,128)(2,1)S(1)}, bf16[256,1024]{1,0:T(8,128)(2,1)S(1)}, u32[]{:S(2)}, u32[]{:S(2)}) collective-permute-start(bf16[256,1024]{1,0:T(8,128)(2,1)S(1)} %broadcast_select_fusion), channel_id=1, source_target_pairs={{0,2},{2,0},{4,6},{6,4},{8,10},{10,8},{12,14},{14,12},{16,18},{18,... | collective-permute-start | bytes 1572872 | tf_op jit(solution)/shard_map/ppermute | solution.py:26
  19.8 11.7 %collective-permute-start.4 = (bf16[136,1024]{1,0:T(8,128)(2,1)S(1)}, bf16[136,1024]{1,0:T(8,128)(2,1)S(1)}, u32[]{:S(2)}, u32[]{:S(2)}) collective-permute-start(bf16[136,1024]{1,0:T(8,128)(2,1)S(1)} %slice.103), channel_id=1, source_target_pairs={{0,2},{2,4},{4,6},{6,8},{8,10},{10,12},{12,14},{14,16},{16,18},{18... | collective-permute-start | bytes 835592 | tf_op jit(solution)/shard_map/ppermute | solution.py:21
  29.0 8.0 %collective-permute-start.2 = (bf16[256,1024]{1,0:T(8,128)(2,1)S(1)}, bf16[256,1024]{1,0:T(8,128)(2,1)S(1)}, u32[]{:S(2)}, u32[]{:S(2)}) collective-permute-start(bf16[256,1024]{1,0:T(8,128)(2,1)S(1)} %broadcast_select_fusion.1), channel_id=1, source_target_pairs={{0,2},{2,0},{4,6},{6,4},{8,10},{10,8},{12,14},{14,12},{16,18},{18,... | collective-permute-start | bytes 1572872 | tf_op jit(solution)/shard_map/ppermute | solution.py:26
  29.1 7.9 %collective-permute-start.1 = (bf16[136,1024]{1,0:T(8,128)(2,1)S(1)}, bf16[136,1024]{1,0:T(8,128)(2,1)S(1)}, u32[]{:S(2)}, u32[]{:S(2)}) collective-permute-start(bf16[136,1024]{1,0:T(8,128)(2,1)S(1)} %slice.102), channel_id=1, source_target_pairs={{0,2},{2,4},{4,6},{6,8},{8,10},{10,12},{12,14},{14,16},{16,18},{18... | collective-permute-start | bytes 835592 | tf_op jit(solution)/shard_map/ppermute | solution.py:21
  32.0 2.6 %copy-start = (f32[904,1024]{1,0:T(8,128)}, f32[904,1024]{1,0:T(8,128)S(1)}, u32[]{:S(2)}) copy-start(f32[904,1024]{1,0:T(8,128)S(1)} %maximum_convert_fusion) | copy-start | bytes 11108356
  38.4 12.0 %copy-start.9 = (s32[2,64]{1,0:T(2,128)S(1)}, s32[2,64]{1,0:T(2,128)}, u32[]{:S(2)}) copy-start(s32[2,64]{1,0:T(2,128)} %param.15) | copy-start | bytes 1540
  38.4 16.6 %copy-start.5 = (bf16[256,1024]{1,0:T(8,128)(2,1)S(1)}, bf16[256,1024]{1,0:T(8,128)(2,1)}, u32[]{:S(2)}) copy-start(bf16[256,1024]{1,0:T(8,128)(2,1)} %param.11) | copy-start | bytes 1572868
  38.4 16.6 %copy-start.8 = (f32[1024]{0:T(1024)S(1)}, f32[1024]{0:T(1024)}, u32[]{:S(2)}) copy-start(f32[1024]{0:T(1024)} %param.12) | copy-start | bytes 12292
  49.9 5.2 %collective-permute-start.6 = (f32[256]{0:T(256)S(1)}, f32[256]{0:T(256)S(1)}, u32[]{:S(2)}, u32[]{:S(2)}) collective-permute-start(f32[256]{0:T(256)S(1)} %multiply_reduce_fusion.5), channel_id=1, source_target_pairs={{0,1},{1,0},{2,3},{3,2},{4,5},{5,4},{6,7},{7,6},{8,9},{9,8},{10,11... | collective-permute-start | bytes 3080 | tf_op jit(solution)/shard_map/ppermute | solution.py:43
  56.7 5.2 %collective-permute-start.7 = (f32[256]{0:T(256)S(1)}, f32[256]{0:T(256)S(1)}, u32[]{:S(2)}, u32[]{:S(2)}) collective-permute-start(f32[256]{0:T(256)S(1)} %multiply_reduce_fusion.4), channel_id=1, source_target_pairs={{0,1},{1,0},{2,3},{3,2},{4,5},{5,4},{6,7},{7,6},{8,9},{9,8},{10,11... | collective-permute-start | bytes 3080 | tf_op jit(solution)/shard_map/ppermute | solution.py:43
  98.0 3.1 %copy-start.2 = (f32[896,1024]{1,0:T(8,128)S(1)}, f32[896,1024]{1,0:T(8,128)}, u32[]{:S(2)}) copy-start(f32[896,1024]{1,0:T(8,128)} %get-tuple-element.15) | copy-start | bytes 11010052
  101.2 2.0 %copy-start.1 = (f32[904,1024]{1,0:T(8,128)S(1)}, f32[904,1024]{1,0:T(8,128)}, u32[]{:S(2)}) copy-start(f32[904,1024]{1,0:T(8,128)} %copy-done) | copy-start | bytes 11108356
  102.9 5.0 %copy-start.3 = (f32[896,1024]{1,0:T(8,128)S(1)}, f32[896,1024]{1,0:T(8,128)}, u32[]{:S(2)}) copy-start(f32[896,1024]{1,0:T(8,128)} %get-tuple-element.14) | copy-start | bytes 11010052
  102.9 9.0 %collective-permute-start.11 = (bf16[256,1024]{1,0:T(8,128)(2,1)S(1)}, bf16[256,1024]{1,0:T(8,128)(2,1)S(1)}, u32[]{:S(2)}, u32[]{:S(2)}) collective-permute-start(bf16[256,1024]{1,0:T(8,128)(2,1)S(1)} %slice.113), channel_id=1, source_target_pairs={{0,2},{2,0},{4,6},{6,4},{8,10},{10,8},{12,14},{14,12},{16,18},{18,... | collective-permute-start | bytes 1572872 | tf_op jit(solution)/shard_map/ppermute | solution.py:26
  105.0 6.0 %collective-permute-start.14 = (f32[4,1024]{1,0:T(4,128)S(1)}, f32[4,1024]{1,0:T(4,128)S(1)}, u32[]{:S(2)}, u32[]{:S(2)}) collective-permute-start(f32[4,1024]{1,0:T(4,128)S(1)} %pad_maximum_fusion.3), channel_id=1, source_target_pairs={{0,2},{2,0},{4,6},{6,4},{8,10},{10,8},{12,14},{14,12},{16,18},{18,... | collective-permute-start | bytes 49160 | tf_op jit(solution)/shard_map/ppermute | solution.py:35
  105.4 6.5 %collective-permute-start.12 = (bf16[136,1024]{1,0:T(8,128)(2,1)S(1)}, bf16[136,1024]{1,0:T(8,128)(2,1)S(1)}, u32[]{:S(2)}, u32[]{:S(2)}) collective-permute-start(bf16[136,1024]{1,0:T(8,128)(2,1)S(1)} %slice.115), channel_id=1, source_target_pairs={{2,0},{4,2},{6,4},{8,6},{10,8},{12,10},{14,12},{16,14},{18,16},{20... | collective-permute-start | bytes 835592 | tf_op jit(solution)/shard_map/ppermute | solution.py:21
  108.2 58.4 %copy-start.7 = (f32[256,1024]{1,0:T(8,128)S(1)}, f32[256,1024]{1,0:T(8,128)}, u32[]{:S(2)}) copy-start(f32[256,1024]{1,0:T(8,128)} %get-tuple-element.13) | copy-start | bytes 3145732
  108.2 7.1 %collective-permute-start.8 = (bf16[256,1024]{1,0:T(8,128)(2,1)S(1)}, bf16[256,1024]{1,0:T(8,128)(2,1)S(1)}, u32[]{:S(2)}, u32[]{:S(2)}) collective-permute-start(bf16[256,1024]{1,0:T(8,128)(2,1)S(1)} %slice.108), channel_id=1, source_target_pairs={{0,2},{2,0},{4,6},{6,4},{8,10},{10,8},{12,14},{14,12},{16,18},{18,... | collective-permute-start | bytes 1572872 | tf_op jit(solution)/shard_map/ppermute | solution.py:26
  108.5 6.8 %collective-permute-start.9 = (bf16[136,1024]{1,0:T(8,128)(2,1)S(1)}, bf16[136,1024]{1,0:T(8,128)(2,1)S(1)}, u32[]{:S(2)}, u32[]{:S(2)}) collective-permute-start(bf16[136,1024]{1,0:T(8,128)(2,1)S(1)} %pad_slice_fusion), channel_id=1, source_target_pairs={{2,0},{4,2},{6,4},{8,6},{10,8},{12,10},{14,12},{16,14},{18,16},{20... | collective-permute-start | bytes 835592 | tf_op jit(solution)/shard_map/ppermute | solution.py:21
  111.0 6.5 %collective-permute-start.15 = (f32[4,1024]{1,0:T(4,128)S(1)}, f32[4,1024]{1,0:T(4,128)S(1)}, u32[]{:S(2)}, u32[]{:S(2)}) collective-permute-start(f32[4,1024]{1,0:T(4,128)S(1)} %fusion.19), channel_id=1, source_target_pairs={{0,4},{2,6},{4,0},{6,2},{8,12},{10,14},{12,8},{14,10},{16,20},{18,... | collective-permute-start | bytes 49160 | tf_op jit(solution)/shard_map/ppermute | solution.py:35
  112.1 56.8 %collective-permute-start.13 = (bf16[256,1024]{1,0:T(8,128)(2,1)S(1)}, bf16[256,1024]{1,0:T(8,128)(2,1)S(1)}, u32[]{:S(2)}, u32[]{:S(2)}) collective-permute-start(bf16[256,1024]{1,0:T(8,128)(2,1)S(1)} %fusion.13), channel_id=1, source_target_pairs={{4,0},{6,2},{8,4},{10,6},{12,8},{14,10},{16,12},{18,14},{20,16},{2... | collective-permute-start | bytes 1572872 | tf_op jit(solution)/shard_map/ppermute | solution.py:21
  115.5 54.5 %collective-permute-start.10 = (bf16[256,1024]{1,0:T(8,128)(2,1)S(1)}, bf16[256,1024]{1,0:T(8,128)(2,1)S(1)}, u32[]{:S(2)}, u32[]{:S(2)}) collective-permute-start(bf16[256,1024]{1,0:T(8,128)(2,1)S(1)} %fusion.8), channel_id=1, source_target_pairs={{4,0},{6,2},{8,4},{10,6},{12,8},{14,10},{16,12},{18,14},{20,16},{2... | collective-permute-start | bytes 1572872 | tf_op jit(solution)/shard_map/ppermute | solution.py:21
  117.5 22.6 %collective-permute-start.16 = (f32[4,1024]{1,0:T(4,128)S(1)}, f32[4,1024]{1,0:T(4,128)S(1)}, u32[]{:S(2)}, u32[]{:S(2)}) collective-permute-start(f32[4,1024]{1,0:T(4,128)S(1)} %fusion.24), channel_id=1, source_target_pairs={{0,8},{2,10},{4,12},{6,14},{8,0},{10,2},{12,4},{14,6},{16,24},{18,... | collective-permute-start | bytes 49160 | tf_op jit(solution)/shard_map/ppermute | solution.py:35
  140.1 7.0 %collective-permute-start.17 = (f32[4,1024]{1,0:T(4,128)S(1)}, f32[4,1024]{1,0:T(4,128)S(1)}, u32[]{:S(2)}, u32[]{:S(2)}) collective-permute-start(f32[4,1024]{1,0:T(4,128)S(1)} %add.160), channel_id=1, source_target_pairs={{0,16},{2,18},{4,20},{6,22},{8,24},{10,26},{12,28},{14,30},{16,0},... | collective-permute-start | bytes 49160 | tf_op jit(solution)/shard_map/ppermute | solution.py:35
  147.1 5.3 %collective-permute-start.18 = (f32[4,1024]{1,0:T(4,128)S(1)}, f32[4,1024]{1,0:T(4,128)S(1)}, u32[]{:S(2)}, u32[]{:S(2)}) collective-permute-start(f32[4,1024]{1,0:T(4,128)S(1)} %add.161), channel_id=1, source_target_pairs={{0,32},{2,34},{4,36},{6,38},{8,40},{10,42},{12,44},{14,46},{16,48}... | collective-permute-start | bytes 49160 | tf_op jit(solution)/shard_map/ppermute | solution.py:35
  152.4 5.1 %collective-permute-start.19 = (f32[4,1024]{1,0:T(4,128)S(1)}, f32[4,1024]{1,0:T(4,128)S(1)}, u32[]{:S(2)}, u32[]{:S(2)}) collective-permute-start(f32[4,1024]{1,0:T(4,128)S(1)} %add.162), channel_id=1, source_target_pairs={{0,64},{2,66},{4,68},{6,70},{8,72},{10,74},{12,76},{14,78},{16,80}... | collective-permute-start | bytes 49160 | tf_op jit(solution)/shard_map/ppermute | solution.py:35
  157.5 10.9 %collective-permute-start.20 = (f32[4,1024]{1,0:T(4,128)S(1)}, f32[4,1024]{1,0:T(4,128)S(1)}, u32[]{:S(2)}, u32[]{:S(2)}) collective-permute-start(f32[4,1024]{1,0:T(4,128)S(1)} %add.163), channel_id=1, source_target_pairs={{0,128},{2,130},{4,132},{6,134},{8,136},{10,138},{12,140},{14,142}... | collective-permute-start | bytes 49160 | tf_op jit(solution)/shard_map/ppermute | solution.py:35

commit v4 on v3

--- a/solution.py
+++ b/solution.py
@@ -55,7 +55,7 @@
     return jnp.where(allowed, raw, NEG_FILL), allowed
 
 
-def _forward_kernel(q_ref, k_ref, v_ref, allowed_ref, out_ref, peak_ref, total_ref):
+def _forward_kernel(q_ref, k_ref, v_ref, vin_ref, allowed_ref, out_ref, peak_ref, total_ref, mixed_ref):
     scores, allowed = _scores(q_ref, k_ref, allowed_ref)
     peak = jnp.max(scores, axis=1, keepdims=True)
     expo = jnp.where(allowed, jnp.exp(scores - peak), 0.0)
@@ -64,48 +64,78 @@
     out_ref[...] = jnp.dot(weights, v_ref[...], preferred_element_type=jnp.float32)
     peak_ref[...] = jnp.broadcast_to(peak, peak_ref.shape)
     total_ref[...] = jnp.broadcast_to(total, total_ref.shape)
-
-
-def _backward_kernel(q_ref, k_ref, v_ref, allowed_ref, g_ref, peak_ref, total_ref, delta_ref,
-                     dq_ref, dk_ref, dv_ref):
+    keys_n = k_ref.shape[0]
+    lead = vin_ref.shape[0] - keys_n
+    for tap_index in range(mixed_ref.shape[0]):
+        shifted = vin_ref[lead - tap_index : lead - tap_index + keys_n, :].astype(jnp.bfloat16)
+        mixed_ref[tap_index] = jnp.dot(weights, shifted, preferred_element_type=jnp.float32)
+
+
+def _probabilities(q_ref, k_ref, allowed_ref, peak_ref, total_ref):
     scores, allowed = _scores(q_ref, k_ref, allowed_ref)
     expo = jnp.where(allowed, jnp.exp(scores - peak_ref[:, :1]), 0.0)
-    prob = expo / total_ref[:, :1]
+    return expo / total_ref[:, :1]
+
+
+def _value_grad_kernel(q_ref, k_ref, allowed_ref, g_ref, peak_ref, total_ref, dv_ref):
+    prob = _probabilities(q_ref, k_ref, allowed_ref, peak_ref, total_ref)
+    dv_ref[...] = lax.dot_general(
+        prob.astype(jnp.bfloat16), g_ref[...], (((0,), (0,)), ((), ())), preferred_element_type=jnp.float32
+    )
+
+
+def _backward_kernel(q_ref, k_ref, v_ref, allowed_ref, g_ref, peak_ref, total_ref, att_ref,
+                     dq_ref, dk_ref):
+    prob = _probabilities(q_ref, k_ref, allowed_ref, peak_ref, total_ref)
     grad = g_ref[...]
+    delta = jnp.sum(grad.astype(jnp.float32) * att_ref[...], axis=1, keepdims=True)
     prob_grad = lax.dot_general(
         grad, v_ref[...], (((1,), (1,)), ((), ())), preferred_element_type=jnp.float32
     )
-    score_grad = (prob * (prob_grad - delta_ref[:, :1])).astype(jnp.bfloat16)
+    score_grad = (prob * (prob_grad - delta)).astype(jnp.bfloat16)
     scale = HD ** (-0.5)
     dq_ref[...] = jnp.dot(score_grad, k_ref[...], preferred_element_type=jnp.float32) * scale
     dk_ref[...] = lax.dot_general(
         score_grad, q_ref[...], (((0,), (0,)), ((), ())), preferred_element_type=jnp.float32
     ) * scale
-    dv_ref[...] = lax.dot_general(
-        prob.astype(jnp.bfloat16), grad, (((0,), (0,)), ((), ())), preferred_element_type=jnp.float32
-    )
 
 
 def _head_spec(rows):
     return pl.BlockSpec((rows, HD), lambda h: (0, h))
 
 
-def attention_forward(queries, key_win, value_win, allowed, interpret=False):
+def attention_forward(queries, key_win, value_win, vin_win, allowed, taps, interpret=False):
     rows, channels = queries.shape
     keys_n = key_win.shape[0]
     heads = channels // HD
     return pl.pallas_call(
         _forward_kernel,
         grid=(heads,),
-        in_specs=[_head_spec(rows), _head_spec(keys_n), _head_spec(keys_n),
+        in_specs=[_head_spec(rows), _head_spec(keys_n), _head_spec(keys_n), _head_spec(vin_win.shape[0]),
                   pl.BlockSpec((rows, keys_n), lambda h: (0, 0))],
-        out_specs=[_head_spec(rows), _head_spec(rows), _head_spec(rows)],
-        out_shape=[jax.ShapeDtypeStruct((rows, channels), jnp.float32)] * 3,
+        out_specs=[_head_spec(rows), _head_spec(rows), _head_spec(rows),
+                   pl.BlockSpec((taps, rows, HD), lambda h: (0, 0, h))],
+        out_shape=[jax.ShapeDtypeStruct((rows, channels), jnp.float32)] * 3
+        + [jax.ShapeDtypeStruct((taps, rows, channels), jnp.float32)],
         interpret=interpret,
-    )(queries, key_win, value_win, allowed)
-
-
-def attention_backward(queries, key_win, value_win, allowed, grad, peak, total, delta, interpret=False):
+    )(queries, key_win, value_win, vin_win, allowed)
+
+
+def value_grad(queries, key_win, allowed, grad, peak, total, interpret=False):
+    rows, channels = queries.shape
+    keys_n = key_win.shape[0]
+    return pl.pallas_call(
+        _value_grad_kernel,
+        grid=(channels // HD,),
+        in_specs=[_head_spec(rows), _head_spec(keys_n), pl.BlockSpec((rows, keys_n), lambda h: (0, 0)),
+                  _head_spec(rows), _head_spec(rows), _head_spec(rows)],
+        out_specs=_head_spec(keys_n),
+        out_shape=jax.ShapeDtypeStruct((keys_n, channels), jnp.float32),
+        interpret=interpret,
+    )(queries, key_win, allowed, grad, peak, total)
+
+
+def attention_backward(queries, key_win, value_win, allowed, grad, peak, total, attended, interpret=False):
     rows, channels = queries.shape
     keys_n = key_win.shape[0]
     heads = channels // HD
@@ -115,12 +145,11 @@
         in_specs=[_head_spec(rows), _head_spec(keys_n), _head_spec(keys_n),
                   pl.BlockSpec((rows, keys_n), lambda h: (0, 0)),
                   _head_spec(rows), _head_spec(rows), _head_spec(rows), _head_spec(rows)],
-        out_specs=[_head_spec(rows), _head_spec(keys_n), _head_spec(keys_n)],
+        out_specs=[_head_spec(rows), _head_spec(keys_n)],
         out_shape=[jax.ShapeDtypeStruct((rows, channels), jnp.float32),
-                   jax.ShapeDtypeStruct((keys_n, channels), jnp.float32),
                    jax.ShapeDtypeStruct((keys_n, channels), jnp.float32)],
         interpret=interpret,
-    )(queries, key_win, value_win, allowed, grad, peak, total, delta)
+    )(queries, key_win, value_win, allowed, grad, peak, total, attended)
 
 
 def window_mask(block_bits, device, row_count, key_count):
@@ -166,7 +195,9 @@
     value_win = conv_sum.astype(jnp.bfloat16)
 
     allowed = window_mask(block_bits, device, row_count, key_count).astype(jnp.float32)
-    flattened, row_peak, row_total = attention_forward(queries, key_win, value_win, allowed)
+    flattened, row_peak, row_total, mixed = attention_forward(
+        queries, key_win, value_win, vin_win, allowed, tap_count
+    )
 
     squares = pair_sum(jnp.sum(flattened * flattened, axis=1), "head")
     inverse = lax.rsqrt(squares / D + NORM_EPS)
@@ -179,19 +210,12 @@
     out_grad = (
         inverse[:, None] * scaled - flattened * (inverse**3 * cross_term / D)[:, None]
     ).astype(jnp.bfloat16)
-    grad_f = out_grad.astype(jnp.float32)
-    delta = jnp.sum(split_heads(grad_f * flattened), axis=2)
-    delta_wide = jnp.repeat(delta, HD, axis=1)
-    query_grad, key_part, value_part = attention_backward(
-        queries, key_win, value_win, allowed, out_grad, row_peak, row_total, delta_wide
-    )
-
-    local_taps = jnp.stack(
-        [
-            jnp.sum(value_part * vin_win[far_lead - tap_index : far_lead - tap_index + key_count], axis=0)
-            for tap_index in range(tap_count)
-        ]
-    )
+    value_part = value_grad(queries, key_win, allowed, out_grad, row_peak, row_total)
+    query_grad, key_part = attention_backward(
+        queries, key_win, value_win, allowed, out_grad, row_peak, row_total, flattened
+    )
+
+    local_taps = jnp.sum(out_grad.astype(jnp.float32)[None] * mixed, axis=1)
     conv_grad = all_sum(local_taps, "tm")
 
     lead = jnp.zeros((far_lead, channels), jnp.float32)

time: 172 us -> 171 us (level)
  the two profiles are of different devices: /device:TPU:28 before, /device:TPU:4 now
where the time goes in v4:
time: 171 us; the launch traced here: 170 us
  starting transfers between devices  56.4 us (33%)
  waiting for transfers between devices  52.9 us (31%)
  Pallas kernels  35.3 us (21%)
  other arithmetic  21.9 us (13%)
  local copies, waits for them, and re-layouts  2.44 us (1%)
    ppermute x7, starting transfers between devices, all_sum(): lax.ppermute(block, axis, [(i, i ^ stride) for i in range(size)])  34.1 us
    ppermute x7, waiting for transfers between devices, all_sum(): lax.ppermute(block, axis, [(i, i ^ stride) for i in range(size)])  27 us
    ppermute x8, starting transfers between devices, from_behind(): return lax.ppermute(block, axis, route)  19.2 us
    ppermute x8, waiting for transfers between devices, from_behind(): return lax.ppermute(block, axis, route)  16.9 us
    pallas_call x1, Pallas kernels, attention_forward(): pl.pallas_call(_forward_kernel, grid=(heads,), in_specs=[_head_spec(rows)...  13.9 us
    pallas_call x1, Pallas kernels, attention_backward(): pl.pallas_call(_backward_kernel, grid=(heads,), in_specs=[_head_spec(rows...  11.4 us
    pallas_call x1, Pallas kernels, value_grad(): pl.pallas_call(_value_grad_kernel, grid=(channels // HD,), in_specs=[_hea...  10 us
    ppermute x2, waiting for transfers between devices, pair_sum(): return block + lax.ppermute(block, axis, [(0, 1), (1, 0)])  8.98 us
  transfers between devices with their start and end apart: 21, of which 11 were waited for; matrix products, arithmetic and copies ran while one was open for 8% of the time, Pallas kernels for 0%

profile of v4, /device:TPU:4, one launch (start us, length us, event | category | flops | bytes accessed | tf_op | source)
XLA Modules:
  0.0 170.0 jit_solution(10168669951196562611)
XLA Ops:
  0.7 3.6 %collective-permute-start = (bf16[256,1024]{1,0:T(8,128)(2,1)}, bf16[256,1024]{1,0:T(8,128)(2,1)S(1)}, u32[]{:S(2)}, u32[]{:S(2)}) collective-permute-start(bf16[256,1024]{1,0:T(8,128)(2,1)} %param.9), channel_id=1, source_target_pairs={{0,4},{2,6},{4,8},{6,10},{8,12},{10,14},{12,16},{14,18},{16,20},{1... | collective-permute-start | bytes 1572872 | tf_op jit(solution)/shard_map/ppermute | solution.py:21
  4.3 3.5 %collective-permute-start.3 = (bf16[256,1024]{1,0:T(8,128)(2,1)}, bf16[256,1024]{1,0:T(8,128)(2,1)S(1)}, u32[]{:S(2)}, u32[]{:S(2)}) collective-permute-start(bf16[256,1024]{1,0:T(8,128)(2,1)} %param.10), channel_id=1, source_target_pairs={{0,4},{2,6},{4,8},{6,10},{8,12},{10,14},{12,16},{14,18},{16,20},{1... | collective-permute-start | bytes 1572872 | tf_op jit(solution)/shard_map/ppermute | solution.py:21
  10.5 16.4 %collective-permute-done.3 = bf16[256,1024]{1,0:T(8,128)(2,1)S(1)} collective-permute-done((bf16[256,1024]{1,0:T(8,128)(2,1)}, bf16[256,1024]{1,0:T(8,128)(2,1)S(1)}, u32[]{:S(2)}, u32[]{:S(2)}) %collective-permute-start.3) | collective-permute-done | bytes 524320 | tf_op jit(solution)/shard_map/ppermute | solution.py:21
  29.1 2.4 %collective-permute-start.4 = (bf16[136,1024]{1,0:T(8,128)(2,1)S(1)}, bf16[136,1024]{1,0:T(8,128)(2,1)S(1)}, u32[]{:S(2)}, u32[]{:S(2)}) collective-permute-start(bf16[136,1024]{1,0:T(8,128)(2,1)S(1)} %slice.99), channel_id=1, source_target_pairs={{0,2},{2,4},{4,6},{6,8},{8,10},{10,12},{12,14},{14,16},{16,18},{18... | collective-permute-start | bytes 835592 | tf_op jit(solution)/shard_map/ppermute | solution.py:21
  31.6 3.9 %collective-permute-start.1 = (bf16[136,1024]{1,0:T(8,128)(2,1)S(1)}, bf16[136,1024]{1,0:T(8,128)(2,1)S(1)}, u32[]{:S(2)}, u32[]{:S(2)}) collective-permute-start(bf16[136,1024]{1,0:T(8,128)(2,1)S(1)} %slice.98), channel_id=1, source_target_pairs={{0,2},{2,4},{4,6},{6,8},{8,10},{10,12},{12,14},{14,16},{16,18},{18... | collective-permute-start | bytes 835592 | tf_op jit(solution)/shard_map/ppermute | solution.py:21
  36.6 2.6 %fusion.4.v_ref = bf16[896,1024]{1,0:T(8,128)(2,1)} fusion(f32[904,1024]{1,0:T(8,128)S(1)} %maximum_convert_fusion.vin_ref, f32[1024]{0:T(1024)S(1)} %bitcast.13, f32[1024]{0:T(1024)S(1)} %bitcast.15, f32[1024]{0:T(1024)S(1)} %bitcast.11, f32[1024]{0:T(1024)S(1)} %bitcast.9), kind=kLoop, calls=%fused_computation.10 | loop fusion | flops 7340032 | bytes 16531456 | tf_op jit(solution)/shard_map/convert_element_type | solution.py:195
  39.2 1.5 pad_maximum_fusion.k_ref
  40.7 13.9 %shard_map.111 = (f32[256,1024]{1,0:T(8,128)}, f32[256,1024]{1,0:T(8,128)}, f32[256,1024]{1,0:T(8,128)}, f32[4,256,1024]{2,1,0:T(8,128)}) custom-call(bf16[256,1024]{1,0:T(8,128)(2,1)} %q_ref.5, bf16[896,1024]{1,0:T(8,128)(2,1)} %pad_maximum_fusion.k_ref, bf16[896,1024]{1,0:T(8,128)(2,1)} %fusion.4.v_ref, f32[904,1024]{1,0:T(8,128)} %copy-done, ...), custom_call_target="tpu_custom_call" | custom-call | tf_op jit(solution)/shard_map/pallas_call | solution.py:111
  54.6 1.4 multiply_reduce_fusion.2
  56.6 4.5 %collective-permute-done.6 = f32[256]{0:T(256)S(1)} collective-permute-done((f32[256]{0:T(256)S(1)}, f32[256]{0:T(256)S(1)}, u32[]{:S(2)}, u32[]{:S(2)}) %collective-permute-start.6) | collective-permute-done | bytes 1056 | tf_op jit(solution)/shard_map/ppermute | solution.py:43
  61.2 1.7 multiply_reduce_fusion.1
  63.5 4.5 %collective-permute-done.7 = f32[256]{0:T(256)S(1)} collective-permute-done((f32[256]{0:T(256)S(1)}, f32[256]{0:T(256)S(1)}, u32[]{:S(2)}, u32[]{:S(2)}) %collective-permute-start.7) | collective-permute-done | bytes 1056 | tf_op jit(solution)/shard_map/ppermute | solution.py:43
  68.0 2.4 %fusion.22 = (f32[256,1024]{1,0:T(8,128)S(1)}, bf16[256,1024]{1,0:T(8,128)(2,1)}) fusion(f32[256,1024]{1,0:T(8,128)} %get-tuple-element.10.att_ref, f32[256]{0:T(256)S(1)} %fusion.21, bf16[256,1024]{1,0:T(8,128)(2,1)S(1)} %copy-done.5, f32[1024]{0:T(1024)S(1)} %copy-done.8, pred[256]{0:T(512)(128)(4,1)S(1)} %bitcast.18, f32[256]{0:T(256)S(1)} %add_rsqrt_fusion), kind=kLoop, calls=%fused_computation.59 | loop fusion | flops 2883584 | bytes 3152128 | tf_op jit(solution)/shard_map/convert_element_type | solution.py:218
  70.4 11.4 %shard_map.112 = (f32[256,1024]{1,0:T(8,128)}, f32[896,1024]{1,0:T(8,128)}) custom-call(bf16[256,1024]{1,0:T(8,128)(2,1)} %q_ref.5, bf16[896,1024]{1,0:T(8,128)(2,1)} %pad_maximum_fusion.k_ref, bf16[896,1024]{1,0:T(8,128)(2,1)} %fusion.4.v_ref, f32[256,896]{1,0:T(8,128)} %fusion.18.allowed_ref, bf16[256,1024]{1,0:T(8,128)(2,1)} %get-tuple-element.17.g_ref, ...), custom_call_target="tpu_custom_call" | custom-call | tf_op jit(solution)/shard_map/pallas_call | solution.py:142
  81.8 10.0 %shard_map.113 = f32[896,1024]{1,0:T(8,128)} custom-call(bf16[256,1024]{1,0:T(8,128)(2,1)} %q_ref.5, bf16[896,1024]{1,0:T(8,128)(2,1)} %pad_maximum_fusion.k_ref, f32[256,896]{1,0:T(8,128)} %fusion.18.allowed_ref, bf16[256,1024]{1,0:T(8,128)(2,1)} %get-tuple-element.17.g_ref, f32[256,1024]{1,0:T(8,128)} %get-tuple-element.11.peak_ref, ...), custom_call_target="tpu_custom_call" | custom-call | tf_op jit(solution)/shard_map/pallas_call | solution.py:127
  91.9 2.5 %convert.14 = bf16[896,1024]{1,0:T(8,128)(2,1)S(1)} convert(f32[896,1024]{1,0:T(8,128)} %get-tuple-element.14) | non-fusion elementwise | flops 917504 | bytes 5505024 | tf_op jit(solution)/shard_map/convert.9
  97.3 1.7 fusion.23
  99.2 1.6 collective-permute-start.12
  101.0 1.5 collective-permute-start.10
  103.2 1.4 collective-permute-start.13
  105.3 6.5 %collective-permute-start.14 = (f32[4,1024]{1,0:T(4,128)S(1)}, f32[4,1024]{1,0:T(4,128)S(1)}, u32[]{:S(2)}, u32[]{:S(2)}) collective-permute-start(f32[4,1024]{1,0:T(4,128)S(1)} %multiply_reduce_fusion), channel_id=1, source_target_pairs={{0,2},{2,0},{4,6},{6,4},{8,10},{10,8},{12,14},{14,12},{16,18},{18,... | collective-permute-start | bytes 49160 | tf_op jit(solution)/shard_map/ppermute | solution.py:35
  112.6 3.0 %collective-permute-start.15 = (f32[4,1024]{1,0:T(4,128)S(1)}, f32[4,1024]{1,0:T(4,128)S(1)}, u32[]{:S(2)}, u32[]{:S(2)}) collective-permute-start(f32[4,1024]{1,0:T(4,128)S(1)} %add.158), channel_id=1, source_target_pairs={{0,4},{2,6},{4,0},{6,2},{8,12},{10,14},{12,8},{14,10},{16,20},{18,... | collective-permute-start | bytes 49160 | tf_op jit(solution)/shard_map/ppermute | solution.py:35
  115.6 16.3 %collective-permute-done.15 = f32[4,1024]{1,0:T(4,128)S(1)} collective-permute-done((f32[4,1024]{1,0:T(4,128)S(1)}, f32[4,1024]{1,0:T(4,128)S(1)}, u32[]{:S(2)}, u32[]{:S(2)}) %collective-permute-start.15) | collective-permute-done | bytes 16416 | tf_op jit(solution)/shard_map/ppermute | solution.py:35
  131.9 1.4 collective-permute-start.16
  133.3 3.8 %collective-permute-done.16 = f32[4,1024]{1,0:T(4,128)S(1)} collective-permute-done((f32[4,1024]{1,0:T(4,128)S(1)}, f32[4,1024]{1,0:T(4,128)S(1)}, u32[]{:S(2)}, u32[]{:S(2)}) %collective-permute-start.16) | collective-permute-done | bytes 16416 | tf_op jit(solution)/shard_map/ppermute | solution.py:35
  137.2 6.0 %collective-permute-start.17 = (f32[4,1024]{1,0:T(4,128)S(1)}, f32[4,1024]{1,0:T(4,128)S(1)}, u32[]{:S(2)}, u32[]{:S(2)}) collective-permute-start(f32[4,1024]{1,0:T(4,128)S(1)} %add.160), channel_id=1, source_target_pairs={{0,16},{2,18},{4,20},{6,22},{8,24},{10,26},{12,28},{14,30},{16,0},... | collective-permute-start | bytes 49160 | tf_op jit(solution)/shard_map/ppermute | solution.py:35
  143.2 1.7 %collective-permute-done.17 = f32[4,1024]{1,0:T(4,128)S(1)} collective-permute-done((f32[4,1024]{1,0:T(4,128)S(1)}, f32[4,1024]{1,0:T(4,128)S(1)}, u32[]{:S(2)}, u32[]{:S(2)}) %collective-permute-start.17) | collective-permute-done | bytes 16416 | tf_op jit(solution)/shard_map/ppermute | solution.py:35
  144.9 4.5 %collective-permute-start.18 = (f32[4,1024]{1,0:T(4,128)S(1)}, f32[4,1024]{1,0:T(4,128)S(1)}, u32[]{:S(2)}, u32[]{:S(2)}) collective-permute-start(f32[4,1024]{1,0:T(4,128)S(1)} %add.161), channel_id=1, source_target_pairs={{0,32},{2,34},{4,36},{6,38},{8,40},{10,42},{12,44},{14,46},{16,48}... | collective-permute-start | bytes 49160 | tf_op jit(solution)/shard_map/ppermute | solution.py:35
  149.4 1.8 %collective-permute-done.18 = f32[4,1024]{1,0:T(4,128)S(1)} collective-permute-done((f32[4,1024]{1,0:T(4,128)S(1)}, f32[4,1024]{1,0:T(4,128)S(1)}, u32[]{:S(2)}, u32[]{:S(2)}) %collective-permute-start.18) | collective-permute-done | bytes 16416 | tf_op jit(solution)/shard_map/ppermute | solution.py:35
  151.2 3.3 %collective-permute-start.19 = (f32[4,1024]{1,0:T(4,128)S(1)}, f32[4,1024]{1,0:T(4,128)S(1)}, u32[]{:S(2)}, u32[]{:S(2)}) collective-permute-start(f32[4,1024]{1,0:T(4,128)S(1)} %add.162), channel_id=1, source_target_pairs={{0,64},{2,66},{4,68},{6,70},{8,72},{10,74},{12,76},{14,78},{16,80}... | collective-permute-start | bytes 49160 | tf_op jit(solution)/shard_map/ppermute | solution.py:35
  154.6 1.7 %collective-permute-done.19 = f32[4,1024]{1,0:T(4,128)S(1)} collective-permute-done((f32[4,1024]{1,0:T(4,128)S(1)}, f32[4,1024]{1,0:T(4,128)S(1)}, u32[]{:S(2)}, u32[]{:S(2)}) %collective-permute-start.19) | collective-permute-done | bytes 16416 | tf_op jit(solution)/shard_map/ppermute | solution.py:35
  156.3 9.3 %collective-permute-start.20 = (f32[4,1024]{1,0:T(4,128)S(1)}, f32[4,1024]{1,0:T(4,128)S(1)}, u32[]{:S(2)}, u32[]{:S(2)}) collective-permute-start(f32[4,1024]{1,0:T(4,128)S(1)} %add.163), channel_id=1, source_target_pairs={{0,128},{2,130},{4,132},{6,134},{8,136},{10,138},{12,140},{14,142}... | collective-permute-start | bytes 49160 | tf_op jit(solution)/shard_map/ppermute | solution.py:35
  (83 shorter events, 17.1 us)
Async XLA Ops:
  0.6 34.9 %copy-start.4 = (bf16[256,1024]{1,0:T(8,128)(2,1)S(1)}, bf16[256,1024]{1,0:T(8,128)(2,1)}, u32[]{:S(2)}) copy-start(bf16[256,1024]{1,0:T(8,128)(2,1)} %param.9) | copy-start | bytes 1572868
  0.6 35.5 %copy-start.6 = (bf16[256,1024]{1,0:T(8,128)(2,1)S(1)}, bf16[256,1024]{1,0:T(8,128)(2,1)}, u32[]{:S(2)}) copy-start(bf16[256,1024]{1,0:T(8,128)(2,1)} %param.10) | copy-start | bytes 1572868
  0.7 30.9 %collective-permute-start = (bf16[256,1024]{1,0:T(8,128)(2,1)}, bf16[256,1024]{1,0:T(8,128)(2,1)S(1)}, u32[]{:S(2)}, u32[]{:S(2)}) collective-permute-start(bf16[256,1024]{1,0:T(8,128)(2,1)} %param.9), channel_id=1, source_target_pairs={{0,4},{2,6},{4,8},{6,10},{8,12},{10,14},{12,16},{14,18},{16,20},{1... | collective-permute-start | bytes 1572872 | tf_op jit(solution)/shard_map/ppermute | solution.py:21
  4.3 22.7 %collective-permute-start.3 = (bf16[256,1024]{1,0:T(8,128)(2,1)}, bf16[256,1024]{1,0:T(8,128)(2,1)S(1)}, u32[]{:S(2)}, u32[]{:S(2)}) collective-permute-start(bf16[256,1024]{1,0:T(8,128)(2,1)} %param.10), channel_id=1, source_target_pairs={{0,4},{2,6},{4,8},{6,10},{8,12},{10,14},{12,16},{14,18},{16,20},{1... | collective-permute-start | bytes 1572872 | tf_op jit(solution)/shard_map/ppermute | solution.py:21
  28.1 8.1 %collective-permute-start.5 = (bf16[256,1024]{1,0:T(8,128)(2,1)S(1)}, bf16[256,1024]{1,0:T(8,128)(2,1)S(1)}, u32[]{:S(2)}, u32[]{:S(2)}) collective-permute-start(bf16[256,1024]{1,0:T(8,128)(2,1)S(1)} %broadcast_select_fusion), channel_id=1, source_target_pairs={{0,2},{2,0},{4,6},{6,4},{8,10},{10,8},{12,14},{14,12},{16,18},{18,... | collective-permute-start | bytes 1572872 | tf_op jit(solution)/shard_map/ppermute | solution.py:26
  29.1 7.0 %collective-permute-start.4 = (bf16[136,1024]{1,0:T(8,128)(2,1)S(1)}, bf16[136,1024]{1,0:T(8,128)(2,1)S(1)}, u32[]{:S(2)}, u32[]{:S(2)}) collective-permute-start(bf16[136,1024]{1,0:T(8,128)(2,1)S(1)} %slice.99), channel_id=1, source_target_pairs={{0,2},{2,4},{4,6},{6,8},{8,10},{10,12},{12,14},{14,16},{16,18},{18... | collective-permute-start | bytes 835592 | tf_op jit(solution)/shard_map/ppermute | solution.py:21
  31.6 7.6 %collective-permute-start.1 = (bf16[136,1024]{1,0:T(8,128)(2,1)S(1)}, bf16[136,1024]{1,0:T(8,128)(2,1)S(1)}, u32[]{:S(2)}, u32[]{:S(2)}) collective-permute-start(bf16[136,1024]{1,0:T(8,128)(2,1)S(1)} %slice.98), channel_id=1, source_target_pairs={{0,2},{2,4},{4,6},{6,8},{8,10},{10,12},{12,14},{14,16},{16,18},{18... | collective-permute-start | bytes 835592 | tf_op jit(solution)/shard_map/ppermute | solution.py:21
  35.6 3.7 %collective-permute-start.2 = (bf16[256,1024]{1,0:T(8,128)(2,1)S(1)}, bf16[256,1024]{1,0:T(8,128)(2,1)S(1)}, u32[]{:S(2)}, u32[]{:S(2)}) collective-permute-start(bf16[256,1024]{1,0:T(8,128)(2,1)S(1)} %broadcast_select_fusion.1), channel_id=1, source_target_pairs={{0,2},{2,0},{4,6},{6,4},{8,10},{10,8},{12,14},{14,12},{16,18},{18,... | collective-permute-start | bytes 1572872 | tf_op jit(solution)/shard_map/ppermute | solution.py:26
  36.6 2.6 %copy-start = (f32[904,1024]{1,0:T(8,128)}, f32[904,1024]{1,0:T(8,128)S(1)}, u32[]{:S(2)}) copy-start(f32[904,1024]{1,0:T(8,128)S(1)} %maximum_convert_fusion.vin_ref) | copy-start | bytes 11108356
  40.7 15.9 %copy-start.9 = (s32[2,64]{1,0:T(2,128)S(1)}, s32[2,64]{1,0:T(2,128)}, u32[]{:S(2)}) copy-start(s32[2,64]{1,0:T(2,128)} %param.15) | copy-start | bytes 1540
  40.7 20.4 %copy-start.5 = (bf16[256,1024]{1,0:T(8,128)(2,1)S(1)}, bf16[256,1024]{1,0:T(8,128)(2,1)}, u32[]{:S(2)}) copy-start(bf16[256,1024]{1,0:T(8,128)(2,1)} %param.11) | copy-start | bytes 1572868
  40.7 20.4 %copy-start.8 = (f32[1024]{0:T(1024)S(1)}, f32[1024]{0:T(1024)}, u32[]{:S(2)}) copy-start(f32[1024]{0:T(1024)} %param.12) | copy-start | bytes 12292
  56.0 5.2 %collective-permute-start.6 = (f32[256]{0:T(256)S(1)}, f32[256]{0:T(256)S(1)}, u32[]{:S(2)}, u32[]{:S(2)}) collective-permute-start(f32[256]{0:T(256)S(1)} %multiply_reduce_fusion.2), channel_id=1, source_target_pairs={{0,1},{1,0},{2,3},{3,2},{4,5},{5,4},{6,7},{7,6},{8,9},{9,8},{10,11... | collective-permute-start | bytes 3080 | tf_op jit(solution)/shard_map/ppermute | solution.py:43
  62.8 5.2 %collective-permute-start.7 = (f32[256]{0:T(256)S(1)}, f32[256]{0:T(256)S(1)}, u32[]{:S(2)}, u32[]{:S(2)}) collective-permute-start(f32[256]{0:T(256)S(1)} %multiply_reduce_fusion.1), channel_id=1, source_target_pairs={{0,1},{1,0},{2,3},{3,2},{4,5},{5,4},{6,7},{7,6},{8,9},{9,8},{10,11... | collective-permute-start | bytes 3080 | tf_op jit(solution)/shard_map/ppermute | solution.py:43
  91.9 5.1 %copy-start.1 = (f32[896,1024]{1,0:T(8,128)S(1)}, f32[896,1024]{1,0:T(8,128)}, u32[]{:S(2)}) copy-start(f32[896,1024]{1,0:T(8,128)} %shard_map.113) | copy-start | bytes 11010052
  94.4 6.4 %collective-permute-start.9 = (bf16[136,1024]{1,0:T(8,128)(2,1)S(1)}, bf16[136,1024]{1,0:T(8,128)(2,1)S(1)}, u32[]{:S(2)}, u32[]{:S(2)}) collective-permute-start(bf16[136,1024]{1,0:T(8,128)(2,1)S(1)} %pad_slice_fusion), channel_id=1, source_target_pairs={{2,0},{4,2},{6,4},{8,6},{10,8},{12,10},{14,12},{16,14},{18,16},{20... | collective-permute-start | bytes 835592 | tf_op jit(solution)/shard_map/ppermute | solution.py:21
  95.7 5.1 %collective-permute-start.8 = (bf16[256,1024]{1,0:T(8,128)(2,1)S(1)}, bf16[256,1024]{1,0:T(8,128)(2,1)S(1)}, u32[]{:S(2)}, u32[]{:S(2)}) collective-permute-start(bf16[256,1024]{1,0:T(8,128)(2,1)S(1)} %slice.104), channel_id=1, source_target_pairs={{0,2},{2,0},{4,6},{6,4},{8,10},{10,8},{12,14},{14,12},{16,18},{18,... | collective-permute-start | bytes 1572872 | tf_op jit(solution)/shard_map/ppermute | solution.py:26
  97.3 3.5 %copy-start.2 = (f32[896,1024]{1,0:T(8,128)S(1)}, f32[896,1024]{1,0:T(8,128)}, u32[]{:S(2)}) copy-start(f32[896,1024]{1,0:T(8,128)} %get-tuple-element.14) | copy-start | bytes 11010052
  99.0 5.6 %copy-start.3 = (f32[4,256,1024]{2,1,0:T(8,128)S(1)}, f32[4,256,1024]{2,1,0:T(8,128)}, u32[]{:S(2)}) copy-start(f32[4,256,1024]{2,1,0:T(8,128)} %get-tuple-element.15) | copy-start | bytes 12582916
  99.1 3.9 %collective-permute-start.11 = (bf16[256,1024]{1,0:T(8,128)(2,1)S(1)}, bf16[256,1024]{1,0:T(8,128)(2,1)S(1)}, u32[]{:S(2)}, u32[]{:S(2)}) collective-permute-start(bf16[256,1024]{1,0:T(8,128)(2,1)S(1)} %slice.109), channel_id=1, source_target_pairs={{0,2},{2,0},{4,6},{6,4},{8,10},{10,8},{12,14},{14,12},{16,18},{18,... | collective-permute-start | bytes 1572872 | tf_op jit(solution)/shard_map/ppermute | solution.py:26
  99.2 3.7 %collective-permute-start.12 = (bf16[136,1024]{1,0:T(8,128)(2,1)S(1)}, bf16[136,1024]{1,0:T(8,128)(2,1)S(1)}, u32[]{:S(2)}, u32[]{:S(2)}) collective-permute-start(bf16[136,1024]{1,0:T(8,128)(2,1)S(1)} %slice.111), channel_id=1, source_target_pairs={{2,0},{4,2},{6,4},{8,6},{10,8},{12,10},{14,12},{16,14},{18,16},{20... | collective-permute-start | bytes 835592 | tf_op jit(solution)/shard_map/ppermute | solution.py:21
  101.0 66.9 %collective-permute-start.10 = (bf16[256,1024]{1,0:T(8,128)(2,1)S(1)}, bf16[256,1024]{1,0:T(8,128)(2,1)S(1)}, u32[]{:S(2)}, u32[]{:S(2)}) collective-permute-start(bf16[256,1024]{1,0:T(8,128)(2,1)S(1)} %fusion.11), channel_id=1, source_target_pairs={{4,0},{6,2},{8,4},{10,6},{12,8},{14,10},{16,12},{18,14},{20,16},{2... | collective-permute-start | bytes 1572872 | tf_op jit(solution)/shard_map/ppermute | solution.py:21
  102.9 62.6 %copy-start.7 = (f32[256,1024]{1,0:T(8,128)S(1)}, f32[256,1024]{1,0:T(8,128)}, u32[]{:S(2)}) copy-start(f32[256,1024]{1,0:T(8,128)} %get-tuple-element.13) | copy-start | bytes 3145732
  103.2 65.8 %collective-permute-start.13 = (bf16[256,1024]{1,0:T(8,128)(2,1)S(1)}, bf16[256,1024]{1,0:T(8,128)(2,1)S(1)}, u32[]{:S(2)}, u32[]{:S(2)}) collective-permute-start(bf16[256,1024]{1,0:T(8,128)(2,1)S(1)} %fusion.16), channel_id=1, source_target_pairs={{4,0},{6,2},{8,4},{10,6},{12,8},{14,10},{16,12},{18,14},{20,16},{2... | collective-permute-start | bytes 1572872 | tf_op jit(solution)/shard_map/ppermute | solution.py:21
  105.3 7.4 %collective-permute-start.14 = (f32[4,1024]{1,0:T(4,128)S(1)}, f32[4,1024]{1,0:T(4,128)S(1)}, u32[]{:S(2)}, u32[]{:S(2)}) collective-permute-start(f32[4,1024]{1,0:T(4,128)S(1)} %multiply_reduce_fusion), channel_id=1, source_target_pairs={{0,2},{2,0},{4,6},{6,4},{8,10},{10,8},{12,14},{14,12},{16,18},{18,... | collective-permute-start | bytes 49160 | tf_op jit(solution)/shard_map/ppermute | solution.py:35
  112.6 19.3 %collective-permute-start.15 = (f32[4,1024]{1,0:T(4,128)S(1)}, f32[4,1024]{1,0:T(4,128)S(1)}, u32[]{:S(2)}, u32[]{:S(2)}) collective-permute-start(f32[4,1024]{1,0:T(4,128)S(1)} %add.158), channel_id=1, source_target_pairs={{0,4},{2,6},{4,0},{6,2},{8,12},{10,14},{12,8},{14,10},{16,20},{18,... | collective-permute-start | bytes 49160 | tf_op jit(solution)/shard_map/ppermute | solution.py:35
  131.9 5.2 %collective-permute-start.16 = (f32[4,1024]{1,0:T(4,128)S(1)}, f32[4,1024]{1,0:T(4,128)S(1)}, u32[]{:S(2)}, u32[]{:S(2)}) collective-permute-start(f32[4,1024]{1,0:T(4,128)S(1)} %add.159), channel_id=1, source_target_pairs={{0,8},{2,10},{4,12},{6,14},{8,0},{10,2},{12,4},{14,6},{16,24},{18,... | collective-permute-start | bytes 49160 | tf_op jit(solution)/shard_map/ppermute | solution.py:35
  137.2 7.7 %collective-permute-start.17 = (f32[4,1024]{1,0:T(4,128)S(1)}, f32[4,1024]{1,0:T(4,128)S(1)}, u32[]{:S(2)}, u32[]{:S(2)}) collective-permute-start(f32[4,1024]{1,0:T(4,128)S(1)} %add.160), channel_id=1, source_target_pairs={{0,16},{2,18},{4,20},{6,22},{8,24},{10,26},{12,28},{14,30},{16,0},... | collective-permute-start | bytes 49160 | tf_op jit(solution)/shard_map/ppermute | solution.py:35
  144.9 6.3 %collective-permute-start.18 = (f32[4,1024]{1,0:T(4,128)S(1)}, f32[4,1024]{1,0:T(4,128)S(1)}, u32[]{:S(2)}, u32[]{:S(2)}) collective-permute-start(f32[4,1024]{1,0:T(4,128)S(1)} %add.161), channel_id=1, source_target_pairs={{0,32},{2,34},{4,36},{6,38},{8,40},{10,42},{12,44},{14,46},{16,48}... | collective-permute-start | bytes 49160 | tf_op jit(solution)/shard_map/ppermute | solution.py:35
  151.2 5.1 %collective-permute-start.19 = (f32[4,1024]{1,0:T(4,128)S(1)}, f32[4,1024]{1,0:T(4,128)S(1)}, u32[]{:S(2)}, u32[]{:S(2)}) collective-permute-start(f32[4,1024]{1,0:T(4,128)S(1)} %add.162), channel_id=1, source_target_pairs={{0,64},{2,66},{4,68},{6,70},{8,72},{10,74},{12,76},{14,78},{16,80}... | collective-permute-start | bytes 49160 | tf_op jit(solution)/shard_map/ppermute | solution.py:35
  156.3 11.0 %collective-permute-start.20 = (f32[4,1024]{1,0:T(4,128)S(1)}, f32[4,1024]{1,0:T(4,128)S(1)}, u32[]{:S(2)}, u32[]{:S(2)}) collective-permute-start(f32[4,1024]{1,0:T(4,128)S(1)} %add.163), channel_id=1, source_target_pairs={{0,128},{2,130},{4,132},{6,134},{8,136},{10,138},{12,140},{14,142}... | collective-permute-start | bytes 49160 | tf_op jit(solution)/shard_map/ppermute | solution.py:35

commit v5 on v2

--- a/solution.py
+++ b/solution.py
@@ -29,10 +29,10 @@
     size = lax.axis_size(axis)
     if size & (size - 1):
         return lax.psum(block, axis)
-    stride = 1
-    while stride < size:
+    stride = size // 2
+    while stride >= 1:
         block = block + lax.ppermute(block, axis, [(i, i ^ stride) for i in range(size)])
-        stride *= 2
+        stride //= 2
     return block
 
 
@@ -74,17 +74,20 @@
     far_lead = 8
     key_count = REACH * row_count + (row_count - far_rows)
 
-    own = jnp.concatenate([keys, values_in], 1)
-    second = from_behind(own, "tm", 2)
-    first = chip_swap(jnp.where(even, own, second), "tm")
-    third = from_behind(second[far_rows - far_lead :], "tm", 1)
-    window = jnp.concatenate([third, second, first, own], 0)
-    key_win = window[far_lead:, :channels]
-    vin_win = window[:, channels:].astype(jnp.float32)
+    def relay(own):
+        second = from_behind(own, "tm", 2)
+        first = chip_swap(jnp.where(even, own, second), "tm")
+        third = from_behind(second[far_rows - far_lead :], "tm", 1)
+        return jnp.concatenate([third, second, first, own], 0)
+
+    key_win = relay(keys)[far_lead:]
+    vin_win = relay(values_in)
 
     conv_sum = jnp.zeros((key_count, channels), jnp.float32)
     for tap_index in range(tap_count):
-        conv_sum = conv_sum + conv_weight[tap_index] * vin_win[far_lead - tap_index : far_lead - tap_index + key_count]
+        conv_sum = conv_sum + conv_weight[tap_index] * vin_win[
+            far_lead - tap_index : far_lead - tap_index + key_count
+        ].astype(jnp.float32)
     value_win = conv_sum.astype(jnp.bfloat16)
 
     heads_query = split_heads(queries)
@@ -105,14 +108,25 @@
     attended = jnp.einsum("htu,uhd->thd", weights, heads_value, preferred_element_type=jnp.float32)
 
     flattened = attended.reshape(row_count, channels)
-    squares = pair_sum(jnp.sum(flattened * flattened, axis=1), "head")
+    position = jnp.arange(row_count, dtype=jnp.int32) % BLK
+    chosen = jnp.any(jnp.repeat(mask_pos, BLK, axis=0) == position[:, None], axis=1)
+    weighted = flattened * gain
+    sums = pair_sum(
+        jnp.stack(
+            [
+                jnp.sum(flattened * flattened, axis=1),
+                jnp.sum(weighted * weighted, axis=1),
+                jnp.sum(teacher.astype(jnp.float32) * weighted, axis=1),
+            ]
+        ),
+        "head",
+    )
+    squares = sums[0]
     inverse = lax.rsqrt(squares / D + NORM_EPS)
     prediction = flattened * inverse[:, None] * gain
-    position = jnp.arange(row_count, dtype=jnp.int32) % BLK
-    chosen = jnp.any(jnp.repeat(mask_pos, BLK, axis=0) == position[:, None], axis=1)
     residual = jnp.where(chosen[:, None], prediction - teacher.astype(jnp.float32), 0.0)
     scaled = residual * gain
-    cross_term = pair_sum(jnp.sum(scaled * flattened, axis=1), "head")
+    cross_term = jnp.where(chosen, inverse * sums[1] - sums[2], 0.0)
     out_grad = (
         inverse[:, None] * scaled - flattened * (inverse**3 * cross_term / D)[:, None]
     ).astype(jnp.bfloat16)
@@ -135,7 +149,11 @@
 
     local_taps = jnp.stack(
         [
-            jnp.sum(value_part * vin_win[far_lead - tap_index : far_lead - tap_index + key_count], axis=0)
+            jnp.sum(
+                value_part
+                * vin_win[far_lead - tap_index : far_lead - tap_index + key_count].astype(jnp.float32),
+                axis=0,
+            )
             for tap_index in range(tap_count)
         ]
     )
@@ -146,27 +164,29 @@
     value_sum = jnp.zeros((key_count + far_lead, channels), jnp.float32)
     for tap_index in range(tap_count):
         value_sum = value_sum + conv_weight[tap_index] * padded_value[tap_index : tap_index + key_count + far_lead]
-    grads = jnp.concatenate([jnp.concatenate([lead, key_part], 0), value_sum], 1)
-
-    cut_third = row_count - far_rows + far_lead
-    grad_third = grads[:cut_third]
-    grad_second = grads[cut_third : cut_third + row_count]
-    grad_first = grads[cut_third + row_count : cut_third + 2 * row_count]
-    grad_own = grads[cut_third + 2 * row_count :]
-
-    back_third = from_behind(grad_third.astype(jnp.bfloat16), "tm", -1).astype(jnp.float32)
-    back_first = chip_swap(grad_first.astype(jnp.bfloat16), "tm").astype(jnp.float32)
-    grad_second = grad_second + jnp.concatenate(
-        [jnp.zeros((far_rows - far_lead, 2 * channels), jnp.float32), back_third], 0
-    )
-    grad_second = grad_second + jnp.where(even, 0.0, back_first)
-    back_second = from_behind(grad_second.astype(jnp.bfloat16), "tm", -2).astype(jnp.float32)
-    total = grad_own + jnp.where(even, back_first, 0.0) + back_second
+
+    def relay_back(grads):
+        cut_third = row_count - far_rows + far_lead
+        grad_third = grads[:cut_third]
+        grad_second = grads[cut_third : cut_third + row_count]
+        grad_first = grads[cut_third + row_count : cut_third + 2 * row_count]
+        grad_own = grads[cut_third + 2 * row_count :]
+        back_third = from_behind(grad_third.astype(jnp.bfloat16), "tm", -1).astype(jnp.float32)
+        back_first = chip_swap(grad_first.astype(jnp.bfloat16), "tm").astype(jnp.float32)
+        grad_second = grad_second + jnp.concatenate(
+            [jnp.zeros((far_rows - far_lead, grads.shape[1]), jnp.float32), back_third], 0
+        )
+        grad_second = grad_second + jnp.where(even, 0.0, back_first)
+        back_second = from_behind(grad_second.astype(jnp.bfloat16), "tm", -2).astype(jnp.float32)
+        return grad_own + jnp.where(even, back_first, 0.0) + back_second
+
+    value_total = relay_back(value_sum)
+    key_total = relay_back(jnp.concatenate([lead, key_part], 0))
 
     return (
         query_grad.reshape(row_count, channels).astype(jnp.bfloat16),
-        total[:, :channels].astype(jnp.bfloat16),
-        total[:, channels:].astype(jnp.bfloat16),
+        key_total.astype(jnp.bfloat16),
+        value_total.astype(jnp.bfloat16),
         conv_grad,
     )
 

time: 196 us -> 144 us (0.73)
  other arithmetic: 48.7 us -> 31.6 us
  starting transfers between devices: 48.9 us -> 34.7 us
  waiting for transfers between devices: 62.3 us -> 49.8 us
  matrix products: 19.6 us -> 12.7 us
    ppermute x7, starting transfers between devices: 32.8 us -> 14.8 us  [all_sum(): lax.ppermute(block, axis, [(i, i ^ stride) for i in range(size)])]
    ppermute x7, waiting for transfers between devices: 30.7 us -> 17.1 us  [all_sum(): lax.ppermute(block, axis, [(i, i ^ stride) for i in range(size)])]
    ppermute x4 -> x8, starting transfers between devices: 9.84 us -> 17.8 us  [from_behind(): return lax.ppermute(block, axis, route)]
    add x1, other arithmetic: 5.21 us -> 0.01 us  [pair_sum(): return block + lax.ppermute(block, axis, [(0, 1), (1, 0)])]
    ppermute x4 -> x8, waiting for transfers between devices: 23 us -> 28.2 us  [from_behind(): return lax.ppermute(block, axis, route)]
    concatenate x2, other arithmetic: 8.43 us -> 3.82 us  [relay(): return jnp.concatenate([third, second, first, own], 0)]
    dot_general x1, matrix products: 5.85 us -> 1.45 us  [body(): jnp.einsum('thd,uhd->htu', heads_grad, heads_value, preferred_element_typ...]
    ppermute x2 -> x1, waiting for transfers between devices: 8.6 us -> 4.41 us  [pair_sum(): return block + lax.ppermute(block, axis, [(0, 1), (1, 0)])]
  transfers between devices with their start and end apart: 15 -> 20, of which waited for: 10 -> 10; matrix products, arithmetic and copies ran while one was open for 12% -> 28% of each run, Pallas kernels for 0% -> 0%
where the time goes in v5:
time: 144 us; the launch traced here: 143 us
  waiting for transfers between devices  49.8 us (35%)
  starting transfers between devices  34.7 us (24%)
  other arithmetic  31.6 us (22%)
  local copies, waits for them, and re-layouts  13.2 us (9%)
  matrix products  12.7 us (9%)
    ppermute x8, waiting for transfers between devices, from_behind(): return lax.ppermute(block, axis, route)  28.2 us
    ppermute x8, starting transfers between devices, from_behind(): return lax.ppermute(block, axis, route)  17.8 us
    ppermute x7, waiting for transfers between devices, all_sum(): lax.ppermute(block, axis, [(i, i ^ stride) for i in range(size)])  17.1 us
    ppermute x7, starting transfers between devices, all_sum(): lax.ppermute(block, axis, [(i, i ^ stride) for i in range(size)])  14.8 us
    unnamed x37, local copies, waits for them, and re-layouts  8.42 us
    sub x1, matrix products, body(): expo = jnp.where(mask[None], jnp.exp(scores - row_peak[..., None]), 0.0)  7.3 us
    another operation x1, other arithmetic  5.2 us
    ppermute x1, waiting for transfers between devices, pair_sum(): return block + lax.ppermute(block, axis, [(0, 1), (1, 0)])  4.41 us
  transfers between devices with their start and end apart: 20, of which 10 were waited for; matrix products, arithmetic and copies ran while one was open for 28% of the time, Pallas kernels for 0%

profile of v5, /device:TPU:4, one launch (start us, length us, event | category | flops | bytes accessed | tf_op | source)
XLA Modules:
  0.0 143.1 jit_solution(3112991609077901278)
XLA Ops:
  0.6 1.3 copy.59
  1.9 3.5 %collective-permute-start = (bf16[256,1024]{0,1:T(8,128)(2,1)S(1)}, bf16[256,1024]{0,1:T(8,128)(2,1)S(1)}, u32[]{:S(2)}, u32[]{:S(2)}) collective-permute-start(bf16[256,1024]{0,1:T(8,128)(2,1)S(1)} %copy.59), channel_id=1, source_target_pairs={{0,4},{2,6},{4,8},{6,10},{8,12},{10,14},{12,16},{14,18},{16,20},{1... | collective-permute-start | bytes 1572872 | tf_op jit(solution)/shard_map/ppermute | solution.py:20
  5.5 1.2 copy.65
  6.7 3.5 %collective-permute-start.3 = (bf16[256,1024]{0,1:T(8,128)(2,1)S(1)}, bf16[256,1024]{0,1:T(8,128)(2,1)S(1)}, u32[]{:S(2)}, u32[]{:S(2)}) collective-permute-start(bf16[256,1024]{0,1:T(8,128)(2,1)S(1)} %copy.65), channel_id=1, source_target_pairs={{0,4},{2,6},{4,8},{6,10},{8,12},{10,14},{12,16},{14,18},{16,20},{1... | collective-permute-start | bytes 1572872 | tf_op jit(solution)/shard_map/ppermute | solution.py:20
  12.2 5.6 %collective-permute-done = bf16[256,1024]{0,1:T(8,128)(2,1)S(1)} collective-permute-done((bf16[256,1024]{0,1:T(8,128)(2,1)S(1)}, bf16[256,1024]{0,1:T(8,128)(2,1)S(1)}, u32[]{:S(2)}, u32[]{:S(2)}) %collective-permute-start) | collective-permute-done | bytes 524320 | tf_op jit(solution)/shard_map/ppermute | solution.py:20
  19.7 2.4 %collective-permute-start.1 = (bf16[136,1024]{0,1:T(8,128)(2,1)}, bf16[136,1024]{0,1:T(8,128)(2,1)S(1)}, u32[]{:S(2)}, u32[]{:S(2)}) collective-permute-start(bf16[136,1024]{0,1:T(8,128)(2,1)} %slice.123), channel_id=1, source_target_pairs={{0,2},{2,4},{4,6},{6,8},{8,10},{10,12},{12,14},{14,16},{16,18},{18... | collective-permute-start | bytes 835592 | tf_op jit(solution)/shard_map/ppermute | solution.py:20
  23.2 1.2 copy.69
  25.3 3.7 %collective-permute-done.3 = bf16[256,1024]{0,1:T(8,128)(2,1)S(1)} collective-permute-done((bf16[256,1024]{0,1:T(8,128)(2,1)S(1)}, bf16[256,1024]{0,1:T(8,128)(2,1)S(1)}, u32[]{:S(2)}, u32[]{:S(2)}) %collective-permute-start.3) | collective-permute-done | bytes 524320 | tf_op jit(solution)/shard_map/ppermute | solution.py:20
  31.0 3.2 %collective-permute-start.4 = (bf16[136,1024]{0,1:T(8,128)(2,1)}, bf16[136,1024]{0,1:T(8,128)(2,1)}, u32[]{:S(2)}, u32[]{:S(2)}) collective-permute-start(bf16[136,1024]{0,1:T(8,128)(2,1)} %slice.124), channel_id=1, source_target_pairs={{0,2},{2,4},{4,6},{6,8},{8,10},{10,12},{12,14},{14,16},{16,18},{18... | collective-permute-start | bytes 835592 | tf_op jit(solution)/shard_map/ppermute | solution.py:20
  35.0 1.6 %pad_maximum_fusion.1 = bf16[896,1024]{0,1:T(8,128)(2,1)S(1)} fusion(bf16[256,1024]{0,1:T(8,128)(2,1)S(1)} %copy.59, bf16[256,1024]{0,1:T(8,128)(2,1)} %collective-permute-done.2, bf16[256,1024]{0,1:T(8,128)(2,1)S(1)} %collective-permute-done, bf16[136,1024]{0,1:T(8,128)(2,1)} %copy-done.9), kind=kLoop, calls=%fused_computation.36 | loop fusion | flops 7340032 | bytes 3686400 | tf_op jit(solution)/shard_map/concatenate | solution.py:81
  36.6 7.3 %fusion.57 = (f32[8,256]{1,0:T(8,128)S(1)}, f32[8,256,896]{1,2,0:T(8,128)}) fusion(pred[256,896]{0,1:T(8,128)(4,1)} %fusion.39, bf16[896,8,128]{0,2,1:T(8,128)(2,1)S(1)} %bitcast.103, bf16[256,8,128]{0,2,1:T(8,128)(2,1)} %bitcast.107), kind=kOutput, calls=%fused_computation.107 | convolution fusion | flops 478937984 | bytes 9936896 | tf_op jit(solution)/shard_map/sub | solution.py:104
  43.9 3.8 %fusion.16 = bf16[8,256,896]{1,2,0:T(8,128)(2,1)S(1)} fusion(f32[8,256,896]{1,2,0:T(8,128)} %get-tuple-element.36, f32[8,256]{1,0:T(8,128)S(1)} %get-tuple-element.35), kind=kLoop, calls=%fused_computation.33 | loop fusion | flops 3670016 | bytes 11018240 | tf_op jit(solution)/shard_map/convert_element_type | solution.py:107
  47.8 2.2 %pad_maximum_fusion = bf16[904,1024]{0,1:T(8,128)(2,1)S(1)} fusion(bf16[256,1024]{0,1:T(8,128)(2,1)S(1)} %copy-done.2, bf16[256,1024]{0,1:T(8,128)(2,1)} %collective-permute-done.5, bf16[256,1024]{0,1:T(8,128)(2,1)S(1)} %copy-done.4, bf16[136,1024]{0,1:T(8,128)(2,1)} %collective-permute-done.4), kind=kLoop, calls=%fused_computation.34 | loop fusion | flops 7405568 | bytes 3702784 | tf_op jit(solution)/shard_map/concatenate | solution.py:81
  50.0 3.4 %fusion.8 = bf16[896,1024]{0,1:T(8,128)(2,1)S(1)} fusion(f32[1024]{0:T(1024)S(1)} %bitcast.129, f32[1024]{0:T(1024)S(1)} %bitcast.131, f32[1024]{0:T(1024)S(1)} %bitcast.127, f32[1024]{0:T(1024)S(1)} %bitcast.125, bf16[904,1024]{0,1:T(8,128)(2,1)S(1)} %pad_maximum_fusion), kind=kLoop, calls=%fused_computation.23 | loop fusion | flops 11010048 | bytes 9191424 | tf_op jit(solution)/shard_map/convert_element_type | solution.py:91
  55.5 4.4 %collective-permute-done.6 = f32[3,256]{1,0:T(4,128)S(1)} collective-permute-done((f32[3,256]{1,0:T(4,128)S(1)}, f32[3,256]{1,0:T(4,128)S(1)}, u32[]{:S(2)}, u32[]{:S(2)}) %collective-permute-start.6) | collective-permute-done | bytes 3104 | tf_op jit(solution)/shard_map/ppermute | solution.py:42
  61.6 3.9 %fusion.9 = (f32[1024]{0:T(1024)S(1)}, f32[1024]{0:T(1024)S(1)}, f32[1024]{0:T(1024)S(1)}, f32[1024]{0:T(1024)S(1)}) fusion(bf16[904,1024]{0,1:T(8,128)(2,1)S(1)} %pad_maximum_fusion, f32[8,128,896]{2,1,0:T(8,128)S(1)} %fusion.59), kind=kLoop, calls=%fused_computation.24 | loop fusion | flops 11005952 | bytes 11026432 | tf_op jit(solution)/shard_map/reduce_sum | solution.py:152
  65.6 12.8 %collective-permute-start.13 = (f32[4,1024]{1,0:T(4,128)S(1)}, f32[4,1024]{1,0:T(4,128)S(1)}, u32[]{:S(2)}, u32[]{:S(2)}) collective-permute-start(f32[4,1024]{1,0:T(4,128)S(1)} %pad_maximum_fusion.4), channel_id=1, source_target_pairs={{0,128},{2,130},{4,132},{6,134},{8,136},{10,138},{12,140},{14,142}... | collective-permute-start | bytes 49160 | tf_op jit(solution)/shard_map/ppermute | solution.py:34
  78.4 1.4 %multiply_convert_fusion = bf16[8,256,896]{1,2,0:T(8,128)(2,1)S(1)} fusion(f32[8,256]{1,0:T(8,128)S(1)} %bitcast.142, f32[8,256,896]{1,2,0:T(8,128)S(1)} %bitcast.102, f32[8,256]{1,0:T(8,128)S(1)} %get-tuple-element.35, bf16[256,8,128]{0,2,1:T(8,128)(2,1)S(1)} %bitcast.111, bf16[896,8,128]{0,2,1:T(8,128)(2,1)S(1)} %bitcast.106), kind=kOutput, calls=%fused_computation.2 | convolution fusion | flops 477102080 | bytes 13385728 | tf_op jit(solution)/shard_map/thd,uhd->htu/dot_general | solution.py:136
  81.6 3.3 %collective-permute-done.14 = f32[4,1024]{1,0:T(4,128)S(1)} collective-permute-done((f32[4,1024]{1,0:T(4,128)S(1)}, f32[4,1024]{1,0:T(4,128)S(1)}, u32[]{:S(2)}, u32[]{:S(2)}) %collective-permute-start.14) | collective-permute-done | bytes 16416 | tf_op jit(solution)/shard_map/ppermute | solution.py:34
  86.2 2.6 %collective-permute-done.15 = f32[4,1024]{1,0:T(4,128)S(1)} collective-permute-done((f32[4,1024]{1,0:T(4,128)S(1)}, f32[4,1024]{1,0:T(4,128)S(1)}, u32[]{:S(2)}, u32[]{:S(2)}) %collective-permute-start.15) | collective-permute-done | bytes 16416 | tf_op jit(solution)/shard_map/ppermute | solution.py:34
  88.8 5.2 %fusion.51 = (bf16[904,1024]{0,1:T(8,128)(2,1)S(1)}, f32[904,1024]{0,1:T(8,128)S(1)}) fusion(f32[907,1024]{0,1:T(8,128)S(1)} %maximum_maximum_fusion, f32[1024]{0:T(1024)S(1)} %bitcast.130, f32[1024]{0:T(1024)S(1)} %bitcast.132, f32[1024]{0:T(1024)S(1)} %bitcast.128, f32[896,1024]{0,1:T(8,128)S(1)} %bitcast.99, f32[1024]{0:T(1024)S(1)} %bitcast.126), kind=kLoop, calls=%fused_computation.103 | loop fusion | flops 7405568 | bytes 20348928 | tf_op jit(solution)/shard_map/convert.5
  94.9 1.3 collective-permute-start.8
  97.4 1.3 collective-permute-start.11
  99.6 1.5 %collective-permute-start.18 = (f32[4,1024]{1,0:T(4,128)S(1)}, f32[4,1024]{1,0:T(4,128)S(1)}, u32[]{:S(2)}, u32[]{:S(2)}) collective-permute-start(f32[4,1024]{1,0:T(4,128)S(1)} %add.166), channel_id=1, source_target_pairs={{0,4},{2,6},{4,0},{6,2},{8,12},{10,14},{12,8},{14,10},{16,20},{18,... | collective-permute-start | bytes 49160 | tf_op jit(solution)/shard_map/ppermute | solution.py:34
  101.2 10.1 %collective-permute-done.18 = f32[4,1024]{1,0:T(4,128)S(1)} collective-permute-done((f32[4,1024]{1,0:T(4,128)S(1)}, f32[4,1024]{1,0:T(4,128)S(1)}, u32[]{:S(2)}, u32[]{:S(2)}) %collective-permute-start.18) | collective-permute-done | bytes 16416 | tf_op jit(solution)/shard_map/ppermute | solution.py:34
  112.5 1.3 collective-permute-start.9
  113.8 1.3 fusion.33
  115.1 1.3 collective-permute-start.12
  118.9 10.6 %collective-permute-done.9 = bf16[256,1024]{0,1:T(8,128)(2,1)} collective-permute-done((bf16[256,1024]{0,1:T(8,128)(2,1)}, bf16[256,1024]{0,1:T(8,128)(2,1)}, u32[]{:S(2)}, u32[]{:S(2)}) %collective-permute-start.9) | collective-permute-done | bytes 524320 | tf_op jit(solution)/shard_map/ppermute | solution.py:20
  129.4 1.4 fusion.26
  131.8 8.4 %collective-permute-done.12 = bf16[256,1024]{0,1:T(8,128)(2,1)} collective-permute-done((bf16[256,1024]{0,1:T(8,128)(2,1)}, bf16[256,1024]{0,1:T(8,128)(2,1)}, u32[]{:S(2)}, u32[]{:S(2)}) %collective-permute-start.12) | collective-permute-done | bytes 524320 | tf_op jit(solution)/shard_map/ppermute | solution.py:20
  140.2 1.9 %fusion.31 = bf16[256,1024]{0,1:T(8,128)(2,1)S(1)} fusion(bf16[256,1024]{0,1:T(8,128)(2,1)S(1)} %copy-done.8, f32[904,1024]{0,1:T(8,128)} %copy-done, bf16[256,1024]{0,1:T(8,128)(2,1)} %collective-permute-done.12, pred[]{:T(512)S(6)} %eq.29), kind=kLoop, calls=%fused_computation.60 | loop fusion | flops 1572864 | bytes 2621441 | tf_op jit(solution)/shard_map/convert_element_type | solution.py:189
  (102 shorter events, 24.0 us)
Async XLA Ops:
  0.6 21.5 %copy-start.10 = (bf16[256,1024]{1,0:T(8,128)(2,1)S(1)}, bf16[256,1024]{1,0:T(8,128)(2,1)}, u32[]{:S(2)}) copy-start(bf16[256,1024]{1,0:T(8,128)(2,1)} %param.8) | copy-start | bytes 1572868
  1.9 15.8 %collective-permute-start = (bf16[256,1024]{0,1:T(8,128)(2,1)S(1)}, bf16[256,1024]{0,1:T(8,128)(2,1)S(1)}, u32[]{:S(2)}, u32[]{:S(2)}) collective-permute-start(bf16[256,1024]{0,1:T(8,128)(2,1)S(1)} %copy.59), channel_id=1, source_target_pairs={{0,4},{2,6},{4,8},{6,10},{8,12},{10,14},{12,16},{14,18},{16,20},{1... | collective-permute-start | bytes 1572872 | tf_op jit(solution)/shard_map/ppermute | solution.py:20
  6.7 24.3 %copy-start.1 = (bf16[256,1024]{0,1:T(8,128)(2,1)}, bf16[256,1024]{0,1:T(8,128)(2,1)S(1)}, u32[]{:S(2)}) copy-start(bf16[256,1024]{0,1:T(8,128)(2,1)S(1)} %copy.65) | copy-start | bytes 1572868
  6.7 22.3 %collective-permute-start.3 = (bf16[256,1024]{0,1:T(8,128)(2,1)S(1)}, bf16[256,1024]{0,1:T(8,128)(2,1)S(1)}, u32[]{:S(2)}, u32[]{:S(2)}) collective-permute-start(bf16[256,1024]{0,1:T(8,128)(2,1)S(1)} %copy.65), channel_id=1, source_target_pairs={{0,4},{2,6},{4,8},{6,10},{8,12},{10,14},{12,16},{14,18},{16,20},{1... | collective-permute-start | bytes 1572872 | tf_op jit(solution)/shard_map/ppermute | solution.py:20
  18.6 16.4 %collective-permute-start.2 = (bf16[256,1024]{0,1:T(8,128)(2,1)}, bf16[256,1024]{0,1:T(8,128)(2,1)}, u32[]{:S(2)}, u32[]{:S(2)}) collective-permute-start(bf16[256,1024]{0,1:T(8,128)(2,1)} %broadcast_select_fusion.1), channel_id=1, source_target_pairs={{0,2},{2,0},{4,6},{6,4},{8,10},{10,8},{12,14},{14,12},{16,18},{18,... | collective-permute-start | bytes 1572872 | tf_op jit(solution)/shard_map/ppermute | solution.py:25
  19.7 14.5 %collective-permute-start.1 = (bf16[136,1024]{0,1:T(8,128)(2,1)}, bf16[136,1024]{0,1:T(8,128)(2,1)S(1)}, u32[]{:S(2)}, u32[]{:S(2)}) collective-permute-start(bf16[136,1024]{0,1:T(8,128)(2,1)} %slice.123), channel_id=1, source_target_pairs={{0,2},{2,4},{4,6},{6,8},{8,10},{10,12},{12,14},{14,16},{16,18},{18... | collective-permute-start | bytes 835592 | tf_op jit(solution)/shard_map/ppermute | solution.py:20
  29.0 5.2 %copy-start.3 = (bf16[256,1024]{0,1:T(8,128)(2,1)}, bf16[256,1024]{0,1:T(8,128)(2,1)S(1)}, u32[]{:S(2)}) copy-start(bf16[256,1024]{0,1:T(8,128)(2,1)S(1)} %collective-permute-done.3) | copy-start | bytes 1572868
  29.9 17.8 %collective-permute-start.5 = (bf16[256,1024]{0,1:T(8,128)(2,1)}, bf16[256,1024]{0,1:T(8,128)(2,1)}, u32[]{:S(2)}, u32[]{:S(2)}) collective-permute-start(bf16[256,1024]{0,1:T(8,128)(2,1)} %broadcast_select_fusion), channel_id=1, source_target_pairs={{0,2},{2,0},{4,6},{6,4},{8,10},{10,8},{12,14},{14,12},{16,18},{18,... | collective-permute-start | bytes 1572872 | tf_op jit(solution)/shard_map/ppermute | solution.py:25
  31.0 16.7 %collective-permute-start.4 = (bf16[136,1024]{0,1:T(8,128)(2,1)}, bf16[136,1024]{0,1:T(8,128)(2,1)}, u32[]{:S(2)}, u32[]{:S(2)}) collective-permute-start(bf16[136,1024]{0,1:T(8,128)(2,1)} %slice.124), channel_id=1, source_target_pairs={{0,2},{2,4},{4,6},{6,8},{8,10},{10,12},{12,14},{14,16},{16,18},{18... | collective-permute-start | bytes 835592 | tf_op jit(solution)/shard_map/ppermute | solution.py:20
  43.9 3.8 %copy-start.2 = (bf16[256,1024]{0,1:T(8,128)(2,1)S(1)}, bf16[256,1024]{0,1:T(8,128)(2,1)}, u32[]{:S(2)}) copy-start(bf16[256,1024]{0,1:T(8,128)(2,1)} %copy-done.1) | copy-start | bytes 1572868
  43.9 3.8 %copy-start.4 = (bf16[256,1024]{0,1:T(8,128)(2,1)S(1)}, bf16[256,1024]{0,1:T(8,128)(2,1)}, u32[]{:S(2)}) copy-start(bf16[256,1024]{0,1:T(8,128)(2,1)} %copy-done.3) | copy-start | bytes 1572868
  50.0 3.4 %copy-start.11 = (f32[1024]{0:T(1024)S(1)}, f32[1024]{0:T(1024)}, u32[]{:S(2)}) copy-start(f32[1024]{0:T(1024)} %param.12) | copy-start | bytes 12292
  54.5 5.4 %collective-permute-start.6 = (f32[3,256]{1,0:T(4,128)S(1)}, f32[3,256]{1,0:T(4,128)S(1)}, u32[]{:S(2)}, u32[]{:S(2)}) collective-permute-start(f32[3,256]{1,0:T(4,128)S(1)} %pad_maximum_fusion.5), channel_id=1, source_target_pairs={{0,1},{1,0},{2,3},{3,2},{4,5},{5,4},{6,7},{7,6},{8,9},{9,8},{10,11... | collective-permute-start | bytes 9224 | tf_op jit(solution)/shard_map/ppermute | solution.py:42
  60.4 18.0 %slice-start = ((s8[7340032]{0:T(1024)(128)(4,1)}), s8[4194304]{0:T(1024)(128)(4,1)S(1)}, s32[]{:S(2)}) async-start(s8[7340032]{0:T(1024)(128)(4,1)} %bitcast.101), calls=%async_computation | async-start | bytes 8388608
  61.6 16.8 %slice-start.1 = ((s8[7340032]{0:T(1024)(128)(4,1)}), s8[3145728]{0:T(1024)(128)(4,1)S(1)}, s32[]{:S(2)}) async-start(s8[7340032]{0:T(1024)(128)(4,1)} %bitcast.101), calls=%async_computation.1 | async-start | bytes 6291456
  65.6 14.5 %collective-permute-start.13 = (f32[4,1024]{1,0:T(4,128)S(1)}, f32[4,1024]{1,0:T(4,128)S(1)}, u32[]{:S(2)}, u32[]{:S(2)}) collective-permute-start(f32[4,1024]{1,0:T(4,128)S(1)} %pad_maximum_fusion.4), channel_id=1, source_target_pairs={{0,128},{2,130},{4,132},{6,134},{8,136},{10,138},{12,140},{14,142}... | collective-permute-start | bytes 49160 | tf_op jit(solution)/shard_map/ppermute | solution.py:34
  80.2 4.7 %collective-permute-start.14 = (f32[4,1024]{1,0:T(4,128)S(1)}, f32[4,1024]{1,0:T(4,128)S(1)}, u32[]{:S(2)}, u32[]{:S(2)}) collective-permute-start(f32[4,1024]{1,0:T(4,128)S(1)} %fusion.50), channel_id=1, source_target_pairs={{0,64},{2,66},{4,68},{6,70},{8,72},{10,74},{12,76},{14,78},{16,80}... | collective-permute-start | bytes 49160 | tf_op jit(solution)/shard_map/ppermute | solution.py:34
  81.5 29.8 %collective-permute-start.7 = (bf16[256,1024]{0,1:T(8,128)(2,1)S(1)}, bf16[256,1024]{0,1:T(8,128)(2,1)S(1)}, u32[]{:S(2)}, u32[]{:S(2)}) collective-permute-start(bf16[256,1024]{0,1:T(8,128)(2,1)S(1)} %bitcast.112), channel_id=1, source_target_pairs={{0,2},{2,0},{4,6},{6,4},{8,10},{10,8},{12,14},{14,12},{16,18},{18,... | collective-permute-start | bytes 1572872 | tf_op jit(solution)/shard_map/ppermute | solution.py:25
  84.9 3.8 %collective-permute-start.15 = (f32[4,1024]{1,0:T(4,128)S(1)}, f32[4,1024]{1,0:T(4,128)S(1)}, u32[]{:S(2)}, u32[]{:S(2)}) collective-permute-start(f32[4,1024]{1,0:T(4,128)S(1)} %fusion.74), channel_id=1, source_target_pairs={{0,32},{2,34},{4,36},{6,38},{8,40},{10,42},{12,44},{14,46},{16,48}... | collective-permute-start | bytes 49160 | tf_op jit(solution)/shard_map/ppermute | solution.py:34
  88.8 5.2 %collective-permute-start.16 = (f32[4,1024]{1,0:T(4,128)S(1)}, f32[4,1024]{1,0:T(4,128)S(1)}, u32[]{:S(2)}, u32[]{:S(2)}) collective-permute-start(f32[4,1024]{1,0:T(4,128)S(1)} %add.164), channel_id=1, source_target_pairs={{0,16},{2,18},{4,20},{6,22},{8,24},{10,26},{12,28},{14,30},{16,0},... | collective-permute-start | bytes 49160 | tf_op jit(solution)/shard_map/ppermute | solution.py:34
  94.0 19.8 %copy-start = (f32[904,1024]{0,1:T(8,128)}, f32[904,1024]{0,1:T(8,128)S(1)}, u32[]{:S(2)}) copy-start(f32[904,1024]{0,1:T(8,128)S(1)} %get-tuple-element.23) | copy-start | bytes 11108356
  94.0 5.6 %collective-permute-start.17 = (f32[4,1024]{1,0:T(4,128)S(1)}, f32[4,1024]{1,0:T(4,128)S(1)}, u32[]{:S(2)}, u32[]{:S(2)}) collective-permute-start(f32[4,1024]{1,0:T(4,128)S(1)} %add.165), channel_id=1, source_target_pairs={{0,8},{2,10},{4,12},{6,14},{8,0},{10,2},{12,4},{14,6},{16,24},{18,... | collective-permute-start | bytes 49160 | tf_op jit(solution)/shard_map/ppermute | solution.py:34
  94.9 16.4 %collective-permute-start.8 = (bf16[136,1024]{0,1:T(8,128)(2,1)S(1)}, bf16[136,1024]{0,1:T(8,128)(2,1)S(1)}, u32[]{:S(2)}, u32[]{:S(2)}) collective-permute-start(bf16[136,1024]{0,1:T(8,128)(2,1)S(1)} %pad_slice_fusion), channel_id=1, source_target_pairs={{2,0},{4,2},{6,4},{8,6},{10,8},{12,10},{14,12},{16,14},{18,16},{20... | collective-permute-start | bytes 835592 | tf_op jit(solution)/shard_map/ppermute | solution.py:20
  96.2 17.6 %collective-permute-start.10 = (bf16[256,1024]{0,1:T(8,128)(2,1)S(1)}, bf16[256,1024]{0,1:T(8,128)(2,1)S(1)}, u32[]{:S(2)}, u32[]{:S(2)}) collective-permute-start(bf16[256,1024]{0,1:T(8,128)(2,1)S(1)} %slice.139), channel_id=1, source_target_pairs={{0,2},{2,0},{4,6},{6,4},{8,10},{10,8},{12,14},{14,12},{16,18},{18,... | collective-permute-start | bytes 1572872 | tf_op jit(solution)/shard_map/ppermute | solution.py:25
  97.4 16.4 %collective-permute-start.11 = (bf16[136,1024]{0,1:T(8,128)(2,1)S(1)}, bf16[136,1024]{0,1:T(8,128)(2,1)S(1)}, u32[]{:S(2)}, u32[]{:S(2)}) collective-permute-start(bf16[136,1024]{0,1:T(8,128)(2,1)S(1)} %slice.141), channel_id=1, source_target_pairs={{2,0},{4,2},{6,4},{8,6},{10,8},{12,10},{14,12},{16,14},{18,16},{20... | collective-permute-start | bytes 835592 | tf_op jit(solution)/shard_map/ppermute | solution.py:20
  99.6 11.7 %collective-permute-start.18 = (f32[4,1024]{1,0:T(4,128)S(1)}, f32[4,1024]{1,0:T(4,128)S(1)}, u32[]{:S(2)}, u32[]{:S(2)}) collective-permute-start(f32[4,1024]{1,0:T(4,128)S(1)} %add.166), channel_id=1, source_target_pairs={{0,4},{2,6},{4,0},{6,2},{8,12},{10,14},{12,8},{14,10},{16,20},{18,... | collective-permute-start | bytes 49160 | tf_op jit(solution)/shard_map/ppermute | solution.py:34
  111.3 6.9 %collective-permute-start.19 = (f32[4,1024]{1,0:T(4,128)S(1)}, f32[4,1024]{1,0:T(4,128)S(1)}, u32[]{:S(2)}, u32[]{:S(2)}) collective-permute-start(f32[4,1024]{1,0:T(4,128)S(1)} %add.167), channel_id=1, source_target_pairs={{0,2},{2,0},{4,6},{6,4},{8,10},{10,8},{12,14},{14,12},{16,18},{18,... | collective-permute-start | bytes 49160 | tf_op jit(solution)/shard_map/ppermute | solution.py:34
  111.3 5.9 %copy-start.6 = (bf16[256,1024]{0,1:T(8,128)(2,1)}, bf16[256,1024]{0,1:T(8,128)(2,1)S(1)}, u32[]{:S(2)}) copy-start(bf16[256,1024]{0,1:T(8,128)(2,1)S(1)} %collective-permute-done.7) | copy-start | bytes 1572868
  112.5 16.9 %collective-permute-start.9 = (bf16[256,1024]{0,1:T(8,128)(2,1)}, bf16[256,1024]{0,1:T(8,128)(2,1)}, u32[]{:S(2)}, u32[]{:S(2)}) collective-permute-start(bf16[256,1024]{0,1:T(8,128)(2,1)} %fusion.28), channel_id=1, source_target_pairs={{4,0},{6,2},{8,4},{10,6},{12,8},{14,10},{16,12},{18,14},{20,16},{2... | collective-permute-start | bytes 1572872 | tf_op jit(solution)/shard_map/ppermute | solution.py:20
  113.8 3.4 %copy-start.7 = (bf16[256,1024]{0,1:T(8,128)(2,1)}, bf16[256,1024]{0,1:T(8,128)(2,1)S(1)}, u32[]{:S(2)}) copy-start(bf16[256,1024]{0,1:T(8,128)(2,1)S(1)} %collective-permute-done.10) | copy-start | bytes 1572868
  115.1 25.1 %collective-permute-start.12 = (bf16[256,1024]{0,1:T(8,128)(2,1)}, bf16[256,1024]{0,1:T(8,128)(2,1)}, u32[]{:S(2)}, u32[]{:S(2)}) collective-permute-start(bf16[256,1024]{0,1:T(8,128)(2,1)} %fusion.33), channel_id=1, source_target_pairs={{4,0},{6,2},{8,4},{10,6},{12,8},{14,10},{16,12},{18,14},{20,16},{2... | collective-permute-start | bytes 1572872 | tf_op jit(solution)/shard_map/ppermute | solution.py:20
  117.2 23.0 %copy-start.8 = (bf16[256,1024]{0,1:T(8,128)(2,1)S(1)}, bf16[256,1024]{0,1:T(8,128)(2,1)}, u32[]{:S(2)}) copy-start(bf16[256,1024]{0,1:T(8,128)(2,1)} %copy-done.7) | copy-start | bytes 1572868
  (3 other events, 4.5 us)

commit v6 on v5

--- a/solution.py
+++ b/solution.py
@@ -29,10 +29,10 @@
     size = lax.axis_size(axis)
     if size & (size - 1):
         return lax.psum(block, axis)
-    stride = size // 2
-    while stride >= 1:
+    stride = 1
+    while stride < size:
         block = block + lax.ppermute(block, axis, [(i, i ^ stride) for i in range(size)])
-        stride //= 2
+        stride *= 2
     return block
 
 
@@ -165,23 +165,21 @@
     for tap_index in range(tap_count):
         value_sum = value_sum + conv_weight[tap_index] * padded_value[tap_index : tap_index + key_count + far_lead]
 
-    def relay_back(grads):
+    def send_back(grads):
         cut_third = row_count - far_rows + far_lead
         grad_third = grads[:cut_third]
         grad_second = grads[cut_third : cut_third + row_count]
         grad_first = grads[cut_third + row_count : cut_third + 2 * row_count]
         grad_own = grads[cut_third + 2 * row_count :]
-        back_third = from_behind(grad_third.astype(jnp.bfloat16), "tm", -1).astype(jnp.float32)
-        back_first = chip_swap(grad_first.astype(jnp.bfloat16), "tm").astype(jnp.float32)
-        grad_second = grad_second + jnp.concatenate(
-            [jnp.zeros((far_rows - far_lead, grads.shape[1]), jnp.float32), back_third], 0
-        )
-        grad_second = grad_second + jnp.where(even, 0.0, back_first)
-        back_second = from_behind(grad_second.astype(jnp.bfloat16), "tm", -2).astype(jnp.float32)
-        return grad_own + jnp.where(even, back_first, 0.0) + back_second
-
-    value_total = relay_back(value_sum)
-    key_total = relay_back(jnp.concatenate([lead, key_part], 0))
+        back = [
+            from_behind(part.astype(jnp.bfloat16), "tm", -distance).astype(jnp.float32)
+            for distance, part in ((1, grad_first), (2, grad_second), (3, grad_third))
+        ]
+        far = jnp.concatenate([jnp.zeros((far_rows - far_lead, grads.shape[1]), jnp.float32), back[2]], 0)
+        return grad_own + back[0] + back[1] + far
+
+    value_total = send_back(value_sum)
+    key_total = send_back(jnp.concatenate([lead, key_part], 0))
 
     return (
         query_grad.reshape(row_count, channels).astype(jnp.bfloat16),

time: 144 us -> 183 us (1.27)
  the two profiles are of different devices: /device:TPU:4 before, /device:TPU:23 now
where the time goes in v6:
time: 183 us
  waiting for transfers between devices  51.3 us (28%)
  starting transfers between devices  50.9 us (28%)
  other arithmetic  35.2 us (19%)
  local copies, waits for them, and re-layouts  22.9 us (13%)
  matrix products  21.1 us (12%)
    ppermute x10, waiting for transfers between devices, from_behind(): return lax.ppermute(block, axis, route)  45.4 us
    ppermute x10, starting transfers between devices, from_behind(): return lax.ppermute(block, axis, route)  28.2 us
    ppermute x7, starting transfers between devices, all_sum(): lax.ppermute(block, axis, [(i, i ^ stride) for i in range(size)])  15.9 us
    sub x1, matrix products, body(): expo = jnp.where(mask[None], jnp.exp(scores - row_peak[..., None]), 0.0)  7.96 us
    another operation x1, other arithmetic  6.39 us
    unnamed x37, local copies, waits for them, and re-layouts  6.17 us
    ppermute x2, starting transfers between devices, chip_swap(): return lax.ppermute(block, axis, [(i, i ^ 1) for i in range(size)])  5.39 us
    concatenate x2, other arithmetic, relay(): return jnp.concatenate([third, second, first, own], 0)  4.62 us
  transfers between devices with their start and end apart: 20, of which 7 were waited for; matrix products, arithmetic and copies ran while one was open for 29% of the time, Pallas kernels for 0%

profile of v6, /device:TPU:23, one launch (start us, length us, event | category | flops | bytes accessed | tf_op | source)
XLA Modules:
  0.0 182.5 jit_solution(17654568472067540870)
XLA Ops:
  1.9 2.9 %collective-permute-start = (bf16[256,1024]{0,1:T(8,128)(2,1)S(1)}, bf16[256,1024]{0,1:T(8,128)(2,1)S(1)}, u32[]{:S(2)}, u32[]{:S(2)}) collective-permute-start(bf16[256,1024]{0,1:T(8,128)(2,1)S(1)} %copy.65), channel_id=1, source_target_pairs={{0,4},{2,6},{4,8},{6,10},{8,12},{10,14},{12,16},{14,18},{16,20},{1... | collective-permute-start | bytes 1572872 | tf_op jit(solution)/shard_map/ppermute | solution.py:20
  6.1 3.5 %collective-permute-start.3 = (bf16[256,1024]{0,1:T(8,128)(2,1)S(1)}, bf16[256,1024]{0,1:T(8,128)(2,1)S(1)}, u32[]{:S(2)}, u32[]{:S(2)}) collective-permute-start(bf16[256,1024]{0,1:T(8,128)(2,1)S(1)} %copy.71), channel_id=1, source_target_pairs={{0,4},{2,6},{4,8},{6,10},{8,12},{10,14},{12,16},{14,18},{16,20},{1... | collective-permute-start | bytes 1572872 | tf_op jit(solution)/shard_map/ppermute | solution.py:20
  11.5 5.1 %collective-permute-done = bf16[256,1024]{0,1:T(8,128)(2,1)S(1)} collective-permute-done((bf16[256,1024]{0,1:T(8,128)(2,1)S(1)}, bf16[256,1024]{0,1:T(8,128)(2,1)S(1)}, u32[]{:S(2)}, u32[]{:S(2)}) %collective-permute-start) | collective-permute-done | bytes 524320 | tf_op jit(solution)/shard_map/ppermute | solution.py:20
  17.5 2.7 %collective-permute-start.2 = (bf16[256,1024]{0,1:T(8,128)(2,1)}, bf16[256,1024]{0,1:T(8,128)(2,1)}, u32[]{:S(2)}, u32[]{:S(2)}) collective-permute-start(bf16[256,1024]{0,1:T(8,128)(2,1)} %broadcast_select_fusion.1), channel_id=1, source_target_pairs={{0,2},{2,0},{4,6},{6,4},{8,10},{10,8},{12,14},{14,12},{16,18},{18,... | collective-permute-start | bytes 1572872 | tf_op jit(solution)/shard_map/ppermute | solution.py:25
  21.3 2.8 %collective-permute-start.1 = (bf16[136,1024]{0,1:T(8,128)(2,1)}, bf16[136,1024]{0,1:T(8,128)(2,1)S(1)}, u32[]{:S(2)}, u32[]{:S(2)}) collective-permute-start(bf16[136,1024]{0,1:T(8,128)(2,1)} %slice.122), channel_id=1, source_target_pairs={{0,2},{2,4},{4,6},{6,8},{8,10},{10,12},{12,14},{14,16},{16,18},{18... | collective-permute-start | bytes 835592 | tf_op jit(solution)/shard_map/ppermute | solution.py:20
  28.8 2.7 %collective-permute-start.5 = (bf16[256,1024]{0,1:T(8,128)(2,1)}, bf16[256,1024]{0,1:T(8,128)(2,1)}, u32[]{:S(2)}, u32[]{:S(2)}) collective-permute-start(bf16[256,1024]{0,1:T(8,128)(2,1)} %broadcast_select_fusion), channel_id=1, source_target_pairs={{0,2},{2,0},{4,6},{6,4},{8,10},{10,8},{12,14},{14,12},{16,18},{18,... | collective-permute-start | bytes 1572872 | tf_op jit(solution)/shard_map/ppermute | solution.py:25
  32.5 2.8 %collective-permute-start.4 = (bf16[136,1024]{0,1:T(8,128)(2,1)}, bf16[136,1024]{0,1:T(8,128)(2,1)}, u32[]{:S(2)}, u32[]{:S(2)}) collective-permute-start(bf16[136,1024]{0,1:T(8,128)(2,1)} %slice.123), channel_id=1, source_target_pairs={{0,2},{2,4},{4,6},{6,8},{8,10},{10,12},{12,14},{14,16},{16,18},{18... | collective-permute-start | bytes 835592 | tf_op jit(solution)/shard_map/ppermute | solution.py:20
  37.7 8.0 %fusion.49 = (f32[8,256]{1,0:T(8,128)S(1)}, f32[8,256,896]{1,2,0:T(8,128)}) fusion(pred[256,896]{0,1:T(8,128)(4,1)} %fusion.31, bf16[896,8,128]{0,2,1:T(8,128)(2,1)S(1)} %bitcast.88, bf16[256,8,128]{0,2,1:T(8,128)(2,1)} %bitcast.95), kind=kOutput, calls=%fused_computation.93 | convolution fusion | flops 478937984 | bytes 9936896 | tf_op jit(solution)/shard_map/sub | solution.py:104
  45.7 3.8 %fusion.16 = bf16[8,256,896]{1,2,0:T(8,128)(2,1)S(1)} fusion(f32[8,256,896]{1,2,0:T(8,128)} %get-tuple-element.36, f32[8,256]{1,0:T(8,128)S(1)} %get-tuple-element.35), kind=kLoop, calls=%fused_computation.33 | loop fusion | flops 3670016 | bytes 11018240 | tf_op jit(solution)/shard_map/convert_element_type | solution.py:107
  49.5 3.0 %pad_maximum_fusion = bf16[904,1024]{0,1:T(8,128)(2,1)S(1)} fusion(bf16[256,1024]{0,1:T(8,128)(2,1)S(1)} %copy.71, bf16[256,1024]{0,1:T(8,128)(2,1)} %collective-permute-done.5, bf16[256,1024]{0,1:T(8,128)(2,1)S(1)} %copy-done.7, bf16[136,1024]{0,1:T(8,128)(2,1)} %collective-permute-done.4), kind=kLoop, calls=%fused_computation.34 | loop fusion | flops 7405568 | bytes 3702784 | tf_op jit(solution)/shard_map/concatenate | solution.py:81
  52.6 3.4 %fusion.8 = bf16[896,1024]{0,1:T(8,128)(2,1)S(1)} fusion(f32[1024]{0:T(1024)S(1)} %bitcast.116, f32[1024]{0:T(1024)S(1)} %bitcast.118, f32[1024]{0:T(1024)S(1)} %bitcast.114, f32[1024]{0:T(1024)S(1)} %bitcast.112, bf16[904,1024]{0,1:T(8,128)(2,1)S(1)} %pad_maximum_fusion), kind=kLoop, calls=%fused_computation.23 | loop fusion | flops 11010048 | bytes 9191424 | tf_op jit(solution)/shard_map/convert_element_type | solution.py:91
  62.2 2.6 %collective-permute-done.6 = f32[3,256]{1,0:T(4,128)S(1)} collective-permute-done((f32[3,256]{1,0:T(4,128)S(1)}, f32[3,256]{1,0:T(4,128)S(1)}, u32[]{:S(2)}, u32[]{:S(2)}) %collective-permute-start.6) | collective-permute-done | bytes 3104 | tf_op jit(solution)/shard_map/ppermute | solution.py:42
  64.9 2.2 %fusion.23 = bf16[256,1024]{1,0:T(8,128)(2,1)} fusion(bf16[256,1024]{1,0:T(8,128)(2,1)} %param.11, f32[256,1024]{1,0:T(8,128)S(1)} %copy.75, f32[256]{0:T(256)S(1)} %fusion.36, f32[256]{0:T(256)S(1)} %bitcast.122, f32[1024]{0:T(1024)S(1)} %copy-done.12, pred[256]{0:T(512)(128)(4,1)S(1)} %bitcast.130), kind=kLoop, calls=%fused_computation.48 | loop fusion | flops 2621440 | bytes 2103552 | tf_op jit(solution)/shard_map/convert_element_type | solution.py:132
  68.4 3.4 %fusion.51 = f32[8,128,896]{2,1,0:T(8,128)S(1)} fusion(bf16[256,8,128]{0,2,1:T(8,128)(2,1)S(1)} %bitcast.92, bf16[8,256,896]{1,2,0:T(8,128)(2,1)} %copy-done), kind=kOutput, calls=%fused_computation.95 | convolution fusion | flops 469762048 | bytes 7864320 | tf_op jit(solution)/shard_map/htu,thd->uhd/dot_general | solution.py:146
  71.8 3.9 %fusion.9 = (f32[1024]{0:T(1024)S(1)}, f32[1024]{0:T(1024)S(1)}, f32[1024]{0:T(1024)S(1)}, f32[1024]{0:T(1024)S(1)}) fusion(bf16[904,1024]{0,1:T(8,128)(2,1)S(1)} %pad_maximum_fusion, f32[8,128,896]{2,1,0:T(8,128)S(1)} %fusion.51), kind=kLoop, calls=%fused_computation.24 | loop fusion | flops 11005952 | bytes 11026432 | tf_op jit(solution)/shard_map/reduce_sum | solution.py:152
  77.6 3.0 %collective-permute-start.14 = (f32[4,1024]{1,0:T(4,128)S(1)}, f32[4,1024]{1,0:T(4,128)S(1)}, u32[]{:S(2)}, u32[]{:S(2)}) collective-permute-start(f32[4,1024]{1,0:T(4,128)S(1)} %fusion.42), channel_id=1, source_target_pairs={{0,4},{2,6},{4,0},{6,2},{8,12},{10,14},{12,8},{14,10},{16,20},{18,... | collective-permute-start | bytes 49160 | tf_op jit(solution)/shard_map/ppermute | solution.py:34
  83.7 2.6 %collective-permute-done.15 = f32[4,1024]{1,0:T(4,128)S(1)} collective-permute-done((f32[4,1024]{1,0:T(4,128)S(1)}, f32[4,1024]{1,0:T(4,128)S(1)}, u32[]{:S(2)}, u32[]{:S(2)}) %collective-permute-start.15) | collective-permute-done | bytes 16416 | tf_op jit(solution)/shard_map/ppermute | solution.py:34
  86.4 6.4 %fusion.43 = (bf16[904,1024]{0,1:T(8,128)(2,1)S(1)}, f32[904,1024]{0,1:T(8,128)}) fusion(f32[907,1024]{0,1:T(8,128)S(1)} %maximum_maximum_fusion, f32[1024]{0:T(1024)S(1)} %bitcast.117, f32[1024]{0:T(1024)S(1)} %bitcast.119, f32[1024]{0:T(1024)S(1)} %bitcast.115, f32[896,1024]{0,1:T(8,128)S(1)} %bitcast.83, f32[1024]{0:T(1024)S(1)} %bitcast.113), kind=kLoop, calls=%fused_computation.88 | loop fusion | flops 7405568 | bytes 20348928 | tf_op jit(solution)/shard_map/convert.6
  92.8 1.9 %collective-permute-start.17 = (f32[4,1024]{1,0:T(4,128)S(1)}, f32[4,1024]{1,0:T(4,128)S(1)}, u32[]{:S(2)}, u32[]{:S(2)}) collective-permute-start(f32[4,1024]{1,0:T(4,128)S(1)} %add.157), channel_id=1, source_target_pairs={{0,32},{2,34},{4,36},{6,38},{8,40},{10,42},{12,44},{14,46},{16,48}... | collective-permute-start | bytes 49160 | tf_op jit(solution)/shard_map/ppermute | solution.py:34
  94.8 3.1 %fusion.50 = (bf16[896,8,128]{0,2,1:T(8,128)(2,1)S(1)}, f32[896,8,128]{0,2,1:T(8,128)}) fusion(bf16[8,256,896]{1,2,0:T(8,128)(2,1)S(1)} %multiply_convert_fusion, bf16[256,8,128]{0,2,1:T(8,128)(2,1)S(1)} %bitcast.96), kind=kOutput, calls=%fused_computation.94 | convolution fusion | flops 471597056 | bytes 9699328 | tf_op jit(solution)/shard_map/htu,thd->uhd/dot_general | solution.py:143
  97.9 5.5 %collective-permute-start.18 = (f32[4,1024]{1,0:T(4,128)S(1)}, f32[4,1024]{1,0:T(4,128)S(1)}, u32[]{:S(2)}, u32[]{:S(2)}) collective-permute-start(f32[4,1024]{1,0:T(4,128)S(1)} %add.158), channel_id=1, source_target_pairs={{0,64},{2,66},{4,68},{6,70},{8,72},{10,74},{12,76},{14,78},{16,80}... | collective-permute-start | bytes 49160 | tf_op jit(solution)/shard_map/ppermute | solution.py:34
  106.7 4.3 %collective-permute-start.10 = (bf16[256,1024]{0,1:T(8,128)(2,1)}, bf16[256,1024]{0,1:T(8,128)(2,1)}, u32[]{:S(2)}, u32[]{:S(2)}) collective-permute-start(bf16[256,1024]{0,1:T(8,128)(2,1)} %get-tuple-element.24), channel_id=1, source_target_pairs={{2,0},{4,2},{6,4},{8,6},{10,8},{12,10},{14,12},{16,14},{18,16},{20... | collective-permute-start | bytes 1572872 | tf_op jit(solution)/shard_map/ppermute | solution.py:20
  111.0 4.0 %collective-permute-start.19 = (f32[4,1024]{1,0:T(4,128)S(1)}, f32[4,1024]{1,0:T(4,128)S(1)}, u32[]{:S(2)}, u32[]{:S(2)}) collective-permute-start(f32[4,1024]{1,0:T(4,128)S(1)} %add.159), channel_id=1, source_target_pairs={{0,128},{2,130},{4,132},{6,134},{8,136},{10,138},{12,140},{14,142}... | collective-permute-start | bytes 49160 | tf_op jit(solution)/shard_map/ppermute | solution.py:34
  116.2 3.6 %collective-permute-start.8 = (bf16[256,1024]{1,0:T(8,128)(2,1)S(1)}, bf16[256,1024]{1,0:T(8,128)(2,1)}, u32[]{:S(2)}, u32[]{:S(2)}) collective-permute-start(bf16[256,1024]{1,0:T(8,128)(2,1)S(1)} %copy.87), channel_id=1, source_target_pairs={{4,0},{6,2},{8,4},{10,6},{12,8},{14,10},{16,12},{18,14},{20,16},{2... | collective-permute-start | bytes 1572872 | tf_op jit(solution)/shard_map/ppermute | solution.py:20
  120.9 2.5 %collective-permute-start.7 = (bf16[256,1024]{1,0:T(8,128)(2,1)}, bf16[256,1024]{1,0:T(8,128)(2,1)}, u32[]{:S(2)}, u32[]{:S(2)}) collective-permute-start(bf16[256,1024]{1,0:T(8,128)(2,1)} %copy.85), channel_id=1, source_target_pairs={{2,0},{4,2},{6,4},{8,6},{10,8},{12,10},{14,12},{16,14},{18,16},{20... | collective-permute-start | bytes 1572872 | tf_op jit(solution)/shard_map/ppermute | solution.py:20
  123.4 2.1 %collective-permute-start.12 = (bf16[136,1024]{0,1:T(8,128)(2,1)}, bf16[136,1024]{0,1:T(8,128)(2,1)}, u32[]{:S(2)}, u32[]{:S(2)}) collective-permute-start(bf16[136,1024]{0,1:T(8,128)(2,1)} %slice.140), channel_id=1, source_target_pairs={{6,0},{8,2},{10,4},{12,6},{14,8},{16,10},{18,12},{20,14},{22,16},{... | collective-permute-start | bytes 835592 | tf_op jit(solution)/shard_map/ppermute | solution.py:20
  125.5 3.3 %fusion.17 = bf16[8,128,256]{2,1,0:T(8,128)(2,1)S(1)} fusion(bf16[896,8,128]{0,2,1:T(8,128)(2,1)} %bitcast.89, bf16[8,256,896]{1,2,0:T(8,128)(2,1)} %copy-done.1), kind=kOutput, calls=%fused_computation.42 | convolution fusion | flops 470286336 | bytes 6029312 | tf_op jit(solution)/shard_map/htu,uhd->thd/dot_general | solution.py:139
  132.4 2.5 %copy.88 = bf16[896,1024]{1,0:T(8,128)(2,1)} copy(bf16[896,1024]{0,1:T(8,128)(2,1)S(1)} %bitcast.84) | data formatting | bytes 3670016 | tf_op jit(solution)/shard_map/reshape | solution.py:145
  136.6 32.5 %collective-permute-done.12 = bf16[136,1024]{0,1:T(8,128)(2,1)} collective-permute-done((bf16[136,1024]{0,1:T(8,128)(2,1)}, bf16[136,1024]{0,1:T(8,128)(2,1)}, u32[]{:S(2)}, u32[]{:S(2)}) %collective-permute-start.12) | collective-permute-done | bytes 278560 | tf_op jit(solution)/shard_map/ppermute | solution.py:20
  171.0 2.3 %fusion.26 = bf16[256,1024]{0,1:T(8,128)(2,1)S(1)} fusion(f32[904,1024]{0,1:T(8,128)} %get-tuple-element.23, bf16[256,1024]{0,1:T(8,128)(2,1)} %collective-permute-done.11, bf16[256,1024]{0,1:T(8,128)(2,1)} %collective-permute-done.10, bf16[136,1024]{0,1:T(8,128)(2,1)} %collective-permute-done.12), kind=kLoop, calls=%fused_computation.52 | loop fusion | flops 1835008 | bytes 2899968 | tf_op jit(solution)/shard_map/convert_element_type | solution.py:187
  174.4 5.9 %collective-permute-done.9 = bf16[136,1024]{1,0:T(8,128)(2,1)S(1)} collective-permute-done((bf16[136,1024]{1,0:T(8,128)(2,1)S(1)}, bf16[136,1024]{1,0:T(8,128)(2,1)S(1)}, u32[]{:S(2)}, u32[]{:S(2)}) %collective-permute-start.9) | collective-permute-done | bytes 278560 | tf_op jit(solution)/shard_map/ppermute | solution.py:20
  180.3 2.3 %add_convert_fusion = bf16[256,1024]{1,0:T(8,128)(2,1)} fusion(bf16[256,1024]{1,0:T(8,128)(2,1)} %collective-permute-done.8, f32[256,1024]{1,0:T(8,128)S(1)} %copy-done.8, bf16[256,1024]{1,0:T(8,128)(2,1)} %collective-permute-done.7, bf16[136,1024]{1,0:T(8,128)(2,1)S(1)} %collective-permute-done.9), kind=kLoop, calls=%fused_computation.60 | loop fusion | flops 1835008 | bytes 2899968 | tf_op jit(solution)/shard_map/convert_element_type | solution.py:186
  (107 shorter events, 40.8 us)
Async XLA Ops:
  0.6 23.5 %copy-start.11 = (bf16[256,1024]{1,0:T(8,128)(2,1)S(1)}, bf16[256,1024]{1,0:T(8,128)(2,1)}, u32[]{:S(2)}) copy-start(bf16[256,1024]{1,0:T(8,128)(2,1)} %param.8) | copy-start | bytes 1572868
  1.9 14.7 %collective-permute-start = (bf16[256,1024]{0,1:T(8,128)(2,1)S(1)}, bf16[256,1024]{0,1:T(8,128)(2,1)S(1)}, u32[]{:S(2)}, u32[]{:S(2)}) collective-permute-start(bf16[256,1024]{0,1:T(8,128)(2,1)S(1)} %copy.65), channel_id=1, source_target_pairs={{0,4},{2,6},{4,8},{6,10},{8,12},{10,14},{12,16},{14,18},{16,20},{1... | collective-permute-start | bytes 1572872 | tf_op jit(solution)/shard_map/ppermute | solution.py:20
  6.1 21.8 %collective-permute-start.3 = (bf16[256,1024]{0,1:T(8,128)(2,1)S(1)}, bf16[256,1024]{0,1:T(8,128)(2,1)S(1)}, u32[]{:S(2)}, u32[]{:S(2)}) collective-permute-start(bf16[256,1024]{0,1:T(8,128)(2,1)S(1)} %copy.71), channel_id=1, source_target_pairs={{0,4},{2,6},{4,8},{6,10},{8,12},{10,14},{12,16},{14,18},{16,20},{1... | collective-permute-start | bytes 1572872 | tf_op jit(solution)/shard_map/ppermute | solution.py:20
  17.5 18.6 %collective-permute-start.2 = (bf16[256,1024]{0,1:T(8,128)(2,1)}, bf16[256,1024]{0,1:T(8,128)(2,1)}, u32[]{:S(2)}, u32[]{:S(2)}) collective-permute-start(bf16[256,1024]{0,1:T(8,128)(2,1)} %broadcast_select_fusion.1), channel_id=1, source_target_pairs={{0,2},{2,0},{4,6},{6,4},{8,10},{10,8},{12,14},{14,12},{16,18},{18,... | collective-permute-start | bytes 1572872 | tf_op jit(solution)/shard_map/ppermute | solution.py:25
  21.3 14.0 %collective-permute-start.1 = (bf16[136,1024]{0,1:T(8,128)(2,1)}, bf16[136,1024]{0,1:T(8,128)(2,1)S(1)}, u32[]{:S(2)}, u32[]{:S(2)}) collective-permute-start(bf16[136,1024]{0,1:T(8,128)(2,1)} %slice.122), channel_id=1, source_target_pairs={{0,2},{2,4},{4,6},{6,8},{8,10},{10,12},{12,14},{14,16},{16,18},{18... | collective-permute-start | bytes 835592 | tf_op jit(solution)/shard_map/ppermute | solution.py:20
  27.9 7.5 %copy-start.6 = (bf16[256,1024]{0,1:T(8,128)(2,1)}, bf16[256,1024]{0,1:T(8,128)(2,1)S(1)}, u32[]{:S(2)}) copy-start(bf16[256,1024]{0,1:T(8,128)(2,1)S(1)} %collective-permute-done.3) | copy-start | bytes 1572868
  28.8 20.7 %collective-permute-start.5 = (bf16[256,1024]{0,1:T(8,128)(2,1)}, bf16[256,1024]{0,1:T(8,128)(2,1)}, u32[]{:S(2)}, u32[]{:S(2)}) collective-permute-start(bf16[256,1024]{0,1:T(8,128)(2,1)} %broadcast_select_fusion), channel_id=1, source_target_pairs={{0,2},{2,0},{4,6},{6,4},{8,10},{10,8},{12,14},{14,12},{16,18},{18,... | collective-permute-start | bytes 1572872 | tf_op jit(solution)/shard_map/ppermute | solution.py:25
  32.5 17.0 %collective-permute-start.4 = (bf16[136,1024]{0,1:T(8,128)(2,1)}, bf16[136,1024]{0,1:T(8,128)(2,1)}, u32[]{:S(2)}, u32[]{:S(2)}) collective-permute-start(bf16[136,1024]{0,1:T(8,128)(2,1)} %slice.123), channel_id=1, source_target_pairs={{0,2},{2,4},{4,6},{6,8},{8,10},{10,12},{12,14},{14,16},{16,18},{18... | collective-permute-start | bytes 835592 | tf_op jit(solution)/shard_map/ppermute | solution.py:20
  37.7 8.0 %copy-start.3 = (bf16[896,1024]{0,1:T(8,128)(2,1)}, bf16[896,1024]{0,1:T(8,128)(2,1)S(1)}, u32[]{:S(2)}) copy-start(bf16[896,1024]{0,1:T(8,128)(2,1)S(1)} %pad_maximum_fusion.1) | copy-start | bytes 5505028
  49.5 6.5 %copy-start = (bf16[8,256,896]{1,2,0:T(8,128)(2,1)}, bf16[8,256,896]{1,2,0:T(8,128)(2,1)S(1)}, u32[]{:S(2)}) copy-start(bf16[8,256,896]{1,2,0:T(8,128)(2,1)S(1)} %fusion.16) | copy-start | bytes 11010052
  56.0 6.1 %copy-start.13 = (s32[2,64]{1,0:T(2,128)S(1)}, s32[2,64]{1,0:T(2,128)}, u32[]{:S(2)}) copy-start(s32[2,64]{1,0:T(2,128)} %param.15) | copy-start | bytes 1540
  60.7 4.2 %collective-permute-start.6 = (f32[3,256]{1,0:T(4,128)S(1)}, f32[3,256]{1,0:T(4,128)S(1)}, u32[]{:S(2)}, u32[]{:S(2)}) collective-permute-start(f32[3,256]{1,0:T(4,128)S(1)} %pad_maximum_fusion.5), channel_id=1, source_target_pairs={{0,1},{1,0},{2,3},{3,2},{4,5},{5,4},{6,7},{7,6},{8,9},{9,8},{10,11... | collective-permute-start | bytes 9224 | tf_op jit(solution)/shard_map/ppermute | solution.py:42
  68.4 12.2 %slice-start = ((s8[7340032]{0:T(1024)(128)(4,1)}), s8[4194304]{0:T(1024)(128)(4,1)S(1)}, s32[]{:S(2)}) async-start(s8[7340032]{0:T(1024)(128)(4,1)} %bitcast.86), calls=%async_computation | async-start | bytes 8388608
  71.8 4.9 %copy-start.2 = (f32[8,128,256]{2,1,0:T(8,128)S(1)}, f32[8,128,256]{2,1,0:T(8,128)}, u32[]{:S(2)}) copy-start(f32[8,128,256]{2,1,0:T(8,128)} %get-tuple-element.37) | copy-start | bytes 3145732
  71.8 8.8 %slice-start.1 = ((s8[7340032]{0:T(1024)(128)(4,1)}), s8[3145728]{0:T(1024)(128)(4,1)S(1)}, s32[]{:S(2)}) async-start(s8[7340032]{0:T(1024)(128)(4,1)} %bitcast.86), calls=%async_computation.1 | async-start | bytes 6291456
  71.8 8.8 %copy-start.5 = (bf16[896,1024]{0,1:T(8,128)(2,1)S(1)}, bf16[896,1024]{0,1:T(8,128)(2,1)}, u32[]{:S(2)}) copy-start(bf16[896,1024]{0,1:T(8,128)(2,1)} %copy-done.4) | copy-start | bytes 5505028
  75.8 1.8 collective-permute-start.13
  77.6 4.5 %collective-permute-start.14 = (f32[4,1024]{1,0:T(4,128)S(1)}, f32[4,1024]{1,0:T(4,128)S(1)}, u32[]{:S(2)}, u32[]{:S(2)}) collective-permute-start(f32[4,1024]{1,0:T(4,128)S(1)} %fusion.42), channel_id=1, source_target_pairs={{0,4},{2,6},{4,0},{6,2},{8,12},{10,14},{12,8},{14,10},{16,20},{18,... | collective-permute-start | bytes 49160 | tf_op jit(solution)/shard_map/ppermute | solution.py:34
  82.1 12.7 %copy-start.1 = (bf16[8,256,896]{1,2,0:T(8,128)(2,1)}, bf16[8,256,896]{1,2,0:T(8,128)(2,1)S(1)}, u32[]{:S(2)}) copy-start(bf16[8,256,896]{1,2,0:T(8,128)(2,1)S(1)} %multiply_convert_fusion) | copy-start | bytes 11010052
  82.2 4.2 %collective-permute-start.15 = (f32[4,1024]{1,0:T(4,128)S(1)}, f32[4,1024]{1,0:T(4,128)S(1)}, u32[]{:S(2)}, u32[]{:S(2)}) collective-permute-start(f32[4,1024]{1,0:T(4,128)S(1)} %fusion.66), channel_id=1, source_target_pairs={{0,8},{2,10},{4,12},{6,14},{8,0},{10,2},{12,4},{14,6},{16,24},{18,... | collective-permute-start | bytes 49160 | tf_op jit(solution)/shard_map/ppermute | solution.py:34
  86.3 8.5 %copy-start.9 = (bf16[256,1024]{0,1:T(8,128)(2,1)S(1)}, bf16[256,1024]{0,1:T(8,128)(2,1)}, u32[]{:S(2)}) copy-start(bf16[256,1024]{0,1:T(8,128)(2,1)} %copy.100) | copy-start | bytes 1572868
  86.3 6.5 %collective-permute-start.16 = (f32[4,1024]{1,0:T(4,128)S(1)}, f32[4,1024]{1,0:T(4,128)S(1)}, u32[]{:S(2)}, u32[]{:S(2)}) collective-permute-start(f32[4,1024]{1,0:T(4,128)S(1)} %add.156), channel_id=1, source_target_pairs={{0,16},{2,18},{4,20},{6,22},{8,24},{10,26},{12,28},{14,30},{16,0},... | collective-permute-start | bytes 49160 | tf_op jit(solution)/shard_map/ppermute | solution.py:34
  92.8 5.1 %collective-permute-start.17 = (f32[4,1024]{1,0:T(4,128)S(1)}, f32[4,1024]{1,0:T(4,128)S(1)}, u32[]{:S(2)}, u32[]{:S(2)}) collective-permute-start(f32[4,1024]{1,0:T(4,128)S(1)} %add.157), channel_id=1, source_target_pairs={{0,32},{2,34},{4,36},{6,38},{8,40},{10,42},{12,44},{14,46},{16,48}... | collective-permute-start | bytes 49160 | tf_op jit(solution)/shard_map/ppermute | solution.py:34
  97.9 13.1 %collective-permute-start.18 = (f32[4,1024]{1,0:T(4,128)S(1)}, f32[4,1024]{1,0:T(4,128)S(1)}, u32[]{:S(2)}, u32[]{:S(2)}) collective-permute-start(f32[4,1024]{1,0:T(4,128)S(1)} %add.158), channel_id=1, source_target_pairs={{0,64},{2,66},{4,68},{6,70},{8,72},{10,74},{12,76},{14,78},{16,80}... | collective-permute-start | bytes 49160 | tf_op jit(solution)/shard_map/ppermute | solution.py:34
  104.8 66.2 %collective-permute-start.11 = (bf16[256,1024]{0,1:T(8,128)(2,1)}, bf16[256,1024]{0,1:T(8,128)(2,1)}, u32[]{:S(2)}, u32[]{:S(2)}) collective-permute-start(bf16[256,1024]{0,1:T(8,128)(2,1)} %get-tuple-element.25), channel_id=1, source_target_pairs={{4,0},{6,2},{8,4},{10,6},{12,8},{14,10},{16,12},{18,14},{20,16},{2... | collective-permute-start | bytes 1572872 | tf_op jit(solution)/shard_map/ppermute | solution.py:20
  106.7 64.3 %collective-permute-start.10 = (bf16[256,1024]{0,1:T(8,128)(2,1)}, bf16[256,1024]{0,1:T(8,128)(2,1)}, u32[]{:S(2)}, u32[]{:S(2)}) collective-permute-start(bf16[256,1024]{0,1:T(8,128)(2,1)} %get-tuple-element.24), channel_id=1, source_target_pairs={{2,0},{4,2},{6,4},{8,6},{10,8},{12,10},{14,12},{16,14},{18,16},{20... | collective-permute-start | bytes 1572872 | tf_op jit(solution)/shard_map/ppermute | solution.py:20
  111.0 12.3 %collective-permute-start.19 = (f32[4,1024]{1,0:T(4,128)S(1)}, f32[4,1024]{1,0:T(4,128)S(1)}, u32[]{:S(2)}, u32[]{:S(2)}) collective-permute-start(f32[4,1024]{1,0:T(4,128)S(1)} %add.159), channel_id=1, source_target_pairs={{0,128},{2,130},{4,132},{6,134},{8,136},{10,138},{12,140},{14,142}... | collective-permute-start | bytes 49160 | tf_op jit(solution)/shard_map/ppermute | solution.py:34
  116.2 64.0 %collective-permute-start.8 = (bf16[256,1024]{1,0:T(8,128)(2,1)S(1)}, bf16[256,1024]{1,0:T(8,128)(2,1)}, u32[]{:S(2)}, u32[]{:S(2)}) collective-permute-start(bf16[256,1024]{1,0:T(8,128)(2,1)S(1)} %copy.87), channel_id=1, source_target_pairs={{4,0},{6,2},{8,4},{10,6},{12,8},{14,10},{16,12},{18,14},{20,16},{2... | collective-permute-start | bytes 1572872 | tf_op jit(solution)/shard_map/ppermute | solution.py:20
  120.9 59.3 %collective-permute-start.7 = (bf16[256,1024]{1,0:T(8,128)(2,1)}, bf16[256,1024]{1,0:T(8,128)(2,1)}, u32[]{:S(2)}, u32[]{:S(2)}) collective-permute-start(bf16[256,1024]{1,0:T(8,128)(2,1)} %copy.85), channel_id=1, source_target_pairs={{2,0},{4,2},{6,4},{8,6},{10,8},{12,10},{14,12},{16,14},{18,16},{20... | collective-permute-start | bytes 1572872 | tf_op jit(solution)/shard_map/ppermute | solution.py:20
  123.4 45.7 %collective-permute-start.12 = (bf16[136,1024]{0,1:T(8,128)(2,1)}, bf16[136,1024]{0,1:T(8,128)(2,1)}, u32[]{:S(2)}, u32[]{:S(2)}) collective-permute-start(bf16[136,1024]{0,1:T(8,128)(2,1)} %slice.140), channel_id=1, source_target_pairs={{6,0},{8,2},{10,4},{12,6},{14,8},{16,10},{18,12},{20,14},{22,16},{... | collective-permute-start | bytes 835592 | tf_op jit(solution)/shard_map/ppermute | solution.py:20
  134.9 45.3 %copy-start.8 = (f32[256,1024]{1,0:T(8,128)S(1)}, f32[256,1024]{1,0:T(8,128)}, u32[]{:S(2)}) copy-start(f32[256,1024]{1,0:T(8,128)} %copy.86) | copy-start | bytes 3145732
  169.1 11.2 %collective-permute-start.9 = (bf16[136,1024]{1,0:T(8,128)(2,1)S(1)}, bf16[136,1024]{1,0:T(8,128)(2,1)S(1)}, u32[]{:S(2)}, u32[]{:S(2)}) collective-permute-start(bf16[136,1024]{1,0:T(8,128)(2,1)S(1)} %pad_slice_fusion), channel_id=1, source_target_pairs={{6,0},{8,2},{10,4},{12,6},{14,8},{16,10},{18,12},{20,14},{22,16},{... | collective-permute-start | bytes 835592 | tf_op jit(solution)/shard_map/ppermute | solution.py:20
  (4 other events, 9.9 us)

commit v7 on v5

--- a/solution.py
+++ b/solution.py
@@ -29,10 +29,10 @@
     size = lax.axis_size(axis)
     if size & (size - 1):
         return lax.psum(block, axis)
-    stride = size // 2
-    while stride >= 1:
+    stride = 1
+    while stride < size:
         block = block + lax.ppermute(block, axis, [(i, i ^ stride) for i in range(size)])
-        stride //= 2
+        stride *= 2
     return block
 
 
@@ -74,35 +74,37 @@
     far_lead = 8
     key_count = REACH * row_count + (row_count - far_rows)
 
-    def relay(own):
-        second = from_behind(own, "tm", 2)
+    def relay(own, second):
         first = chip_swap(jnp.where(even, own, second), "tm")
         third = from_behind(second[far_rows - far_lead :], "tm", 1)
         return jnp.concatenate([third, second, first, own], 0)
 
-    key_win = relay(keys)[far_lead:]
-    vin_win = relay(values_in)
-
+    key_second = from_behind(keys, "tm", 2)
+    key_second, values_in = lax.optimization_barrier((key_second, values_in))
+    key_win = relay(keys, key_second)[far_lead:]
+    value_second = from_behind(values_in, "tm", 2)
+
+    heads_query = split_heads(queries)
+    heads_key = split_heads(key_win)
+    mask = window_mask(block_bits, device, row_count, key_count)
+
+    raw_scores = (
+        jnp.einsum("thd,uhd->htu", heads_query, heads_key, preferred_element_type=jnp.float32)
+        * score_scale
+    )
+    scores = jnp.where(mask[None], raw_scores, NEG_FILL)
+    row_peak = jnp.max(scores, axis=2)
+    expo = jnp.where(mask[None], jnp.exp(scores - row_peak[..., None]), 0.0)
+    row_total = jnp.sum(expo, axis=2)
+    value_second, row_total = lax.optimization_barrier((value_second, row_total))
+    vin_win = relay(values_in, value_second)
     conv_sum = jnp.zeros((key_count, channels), jnp.float32)
     for tap_index in range(tap_count):
         conv_sum = conv_sum + conv_weight[tap_index] * vin_win[
             far_lead - tap_index : far_lead - tap_index + key_count
         ].astype(jnp.float32)
     value_win = conv_sum.astype(jnp.bfloat16)
-
-    heads_query = split_heads(queries)
-    heads_key = split_heads(key_win)
     heads_value = split_heads(value_win)
-    mask = window_mask(block_bits, device, row_count, key_count)
-
-    raw_scores = (
-        jnp.einsum("thd,uhd->htu", heads_query, heads_key, preferred_element_type=jnp.float32)
-        * score_scale
-    )
-    scores = jnp.where(mask[None], raw_scores, NEG_FILL)
-    row_peak = jnp.max(scores, axis=2)
-    expo = jnp.where(mask[None], jnp.exp(scores - row_peak[..., None]), 0.0)
-    row_total = jnp.sum(expo, axis=2)
     prob = expo / row_total[..., None]
     weights = prob.astype(jnp.bfloat16)
     attended = jnp.einsum("htu,uhd->thd", weights, heads_value, preferred_element_type=jnp.float32)

time: 144 us -> 150 us (1.042)
  starting transfers between devices: 34.7 us -> 55.4 us
  waiting for transfers between devices: 49.8 us -> 36.8 us
  local copies, waits for them, and re-layouts: 13.2 us -> 11.4 us
    ppermute x7, starting transfers between devices: 14.8 us -> 34.3 us  [all_sum(): lax.ppermute(block, axis, [(i, i ^ stride) for i in range(size)])]
    ppermute x8, waiting for transfers between devices: 28.2 us -> 21.1 us  [from_behind(): return lax.ppermute(block, axis, route)]
    ppermute x7, waiting for transfers between devices: 17.1 us -> 11.3 us  [all_sum(): lax.ppermute(block, axis, [(i, i ^ stride) for i in range(size)])]
    unnamed x37 -> x34, local copies, waits for them, and re-layouts: 8.42 us -> 6.19 us
  transfers between devices with their start and end apart: 20 -> 20, of which waited for: 10 -> 8; matrix products, arithmetic and copies ran while one was open for 28% -> 23% of each run, Pallas kernels for 0% -> 0%
where the time goes in v7:
time: 150 us; the launch traced here: 149 us
  starting transfers between devices  55.4 us (37%)
  waiting for transfers between devices  36.8 us (25%)
  other arithmetic  31.6 us (21%)
  matrix products  12.7 us (8%)
  local copies, waits for them, and re-layouts  11.4 us (8%)
    ppermute x7, starting transfers between devices, all_sum(): lax.ppermute(block, axis, [(i, i ^ stride) for i in range(size)])  34.3 us
    ppermute x8, waiting for transfers between devices, from_behind(): return lax.ppermute(block, axis, route)  21.1 us
    ppermute x8, starting transfers between devices, from_behind(): return lax.ppermute(block, axis, route)  18.4 us
    ppermute x7, waiting for transfers between devices, all_sum(): lax.ppermute(block, axis, [(i, i ^ stride) for i in range(size)])  11.3 us
    sub x1, matrix products, body(): expo = jnp.where(mask[None], jnp.exp(scores - row_peak[..., None]), 0.0)  7.31 us
    unnamed x34, local copies, waits for them, and re-layouts  6.19 us
    another operation x1, other arithmetic  5.18 us
    ppermute x1, waiting for transfers between devices, pair_sum(): return block + lax.ppermute(block, axis, [(0, 1), (1, 0)])  4.41 us
  transfers between devices with their start and end apart: 20, of which 8 were waited for; matrix products, arithmetic and copies ran while one was open for 23% of the time, Pallas kernels for 0%

profile of v7, /device:TPU:4, one launch (start us, length us, event | category | flops | bytes accessed | tf_op | source)
XLA Modules:
  0.0 149.1 jit_solution(1228801704663841169)
XLA Ops:
  0.7 1.4 copy.59
  2.0 3.5 %collective-permute-start = (bf16[256,1024]{0,1:T(8,128)(2,1)S(1)}, bf16[256,1024]{0,1:T(8,128)(2,1)S(1)}, u32[]{:S(2)}, u32[]{:S(2)}) collective-permute-start(bf16[256,1024]{0,1:T(8,128)(2,1)S(1)} %copy.59), channel_id=1, source_target_pairs={{0,4},{2,6},{4,8},{6,10},{8,12},{10,14},{12,16},{14,18},{16,20},{1... | collective-permute-start | bytes 1572872 | tf_op jit(solution)/shard_map/ppermute | solution.py:20
  6.6 10.1 %collective-permute-done = bf16[256,1024]{0,1:T(8,128)(2,1)S(1)} collective-permute-done((bf16[256,1024]{0,1:T(8,128)(2,1)S(1)}, bf16[256,1024]{0,1:T(8,128)(2,1)S(1)}, u32[]{:S(2)}, u32[]{:S(2)}) %collective-permute-start) | collective-permute-done | bytes 524320 | tf_op jit(solution)/shard_map/ppermute | solution.py:20
  18.7 2.4 %collective-permute-start.1 = (bf16[136,1024]{0,1:T(8,128)(2,1)}, bf16[136,1024]{0,1:T(8,128)(2,1)S(1)}, u32[]{:S(2)}, u32[]{:S(2)}) collective-permute-start(bf16[136,1024]{0,1:T(8,128)(2,1)} %slice.96), channel_id=1, source_target_pairs={{0,2},{2,4},{4,6},{6,8},{8,10},{10,12},{12,14},{14,16},{16,18},{18... | collective-permute-start | bytes 835592 | tf_op jit(solution)/shard_map/ppermute | solution.py:20
  24.2 5.2 %collective-permute-start.3 = (bf16[256,1024]{0,1:T(8,128)(2,1)}, bf16[256,1024]{0,1:T(8,128)(2,1)}, u32[]{:S(2)}, u32[]{:S(2)}) collective-permute-start(bf16[256,1024]{0,1:T(8,128)(2,1)} %copy.65), channel_id=1, source_target_pairs={{0,4},{2,6},{4,8},{6,10},{8,12},{10,14},{12,16},{14,18},{16,20},{1... | collective-permute-start | bytes 1572872 | tf_op jit(solution)/shard_map/ppermute | solution.py:20
  30.2 1.6 %pad_maximum_fusion.1 = bf16[896,1024]{0,1:T(8,128)(2,1)S(1)} fusion(bf16[256,1024]{0,1:T(8,128)(2,1)S(1)} %copy.59, bf16[256,1024]{0,1:T(8,128)(2,1)} %collective-permute-done.2, bf16[256,1024]{0,1:T(8,128)(2,1)S(1)} %collective-permute-done, bf16[136,1024]{0,1:T(8,128)(2,1)} %copy-done.5), kind=kLoop, calls=%fused_computation.36 | loop fusion | flops 7340032 | bytes 3686400 | tf_op jit(solution)/shard_map/concatenate | solution.py:80
  31.8 7.3 %fusion.57 = (f32[8,256]{1,0:T(8,128)S(1)}, f32[8,256,896]{1,2,0:T(8,128)}) fusion(pred[256,896]{0,1:T(8,128)(4,1)} %fusion.39, bf16[896,8,128]{0,2,1:T(8,128)(2,1)S(1)} %bitcast.103, bf16[256,8,128]{0,2,1:T(8,128)(2,1)} %bitcast.107), kind=kOutput, calls=%fused_computation.107 | convolution fusion | flops 478937984 | bytes 9936896 | tf_op jit(solution)/shard_map/sub | solution.py:97
  39.1 1.9 %collective-permute-done.3 = bf16[256,1024]{0,1:T(8,128)(2,1)} collective-permute-done((bf16[256,1024]{0,1:T(8,128)(2,1)}, bf16[256,1024]{0,1:T(8,128)(2,1)}, u32[]{:S(2)}, u32[]{:S(2)}) %collective-permute-start.3) | collective-permute-done | bytes 524320 | tf_op jit(solution)/shard_map/ppermute | solution.py:20
  42.1 1.3 slice.99
  43.8 2.1 %collective-permute-start.4 = (bf16[136,1024]{0,1:T(8,128)(2,1)S(1)}, bf16[136,1024]{0,1:T(8,128)(2,1)S(1)}, u32[]{:S(2)}, u32[]{:S(2)}) collective-permute-start(bf16[136,1024]{0,1:T(8,128)(2,1)S(1)} %slice.99), channel_id=1, source_target_pairs={{0,2},{2,4},{4,6},{6,8},{8,10},{10,12},{12,14},{14,16},{16,18},{18... | collective-permute-start | bytes 835592 | tf_op jit(solution)/shard_map/ppermute | solution.py:20
  45.9 3.7 %fusion.16 = bf16[8,256,896]{1,2,0:T(8,128)(2,1)S(1)} fusion(f32[8,256,896]{1,2,0:T(8,128)} %get-tuple-element.44, f32[8,256]{1,0:T(8,128)S(1)} %get-tuple-element.10), kind=kLoop, calls=%fused_computation.33 | loop fusion | flops 3670016 | bytes 11018240 | tf_op jit(solution)/shard_map/convert_element_type | solution.py:109
  49.7 2.3 %pad_maximum_fusion = bf16[904,1024]{0,1:T(8,128)(2,1)S(1)} fusion(bf16[256,1024]{0,1:T(8,128)(2,1)} %copy.65, bf16[256,1024]{0,1:T(8,128)(2,1)S(1)} %collective-permute-done.5, bf16[256,1024]{0,1:T(8,128)(2,1)} %collective-permute-done.3, bf16[136,1024]{0,1:T(8,128)(2,1)S(1)} %collective-permute-done.4), kind=kLoop, calls=%fused_computation.34 | loop fusion | flops 7405568 | bytes 3702784 | tf_op jit(solution)/shard_map/concatenate | solution.py:80
  51.9 3.4 %fusion.8 = bf16[896,1024]{0,1:T(8,128)(2,1)S(1)} fusion(f32[1024]{0:T(1024)S(1)} %bitcast.129, f32[1024]{0:T(1024)S(1)} %bitcast.131, f32[1024]{0:T(1024)S(1)} %bitcast.127, f32[1024]{0:T(1024)S(1)} %bitcast.125, bf16[904,1024]{0,1:T(8,128)(2,1)S(1)} %pad_maximum_fusion), kind=kLoop, calls=%fused_computation.23 | loop fusion | flops 11010048 | bytes 9191424 | tf_op jit(solution)/shard_map/convert_element_type | solution.py:106
  57.4 4.4 %collective-permute-done.6 = f32[3,256]{1,0:T(4,128)S(1)} collective-permute-done((f32[3,256]{1,0:T(4,128)S(1)}, f32[3,256]{1,0:T(4,128)S(1)}, u32[]{:S(2)}, u32[]{:S(2)}) %collective-permute-start.6) | collective-permute-done | bytes 3104 | tf_op jit(solution)/shard_map/ppermute | solution.py:42
  63.6 3.9 %fusion.9 = (f32[1024]{0:T(1024)S(1)}, f32[1024]{0:T(1024)S(1)}, f32[1024]{0:T(1024)S(1)}, f32[1024]{0:T(1024)S(1)}) fusion(bf16[904,1024]{0,1:T(8,128)(2,1)S(1)} %pad_maximum_fusion, f32[8,128,896]{2,1,0:T(8,128)S(1)} %fusion.59), kind=kLoop, calls=%fused_computation.24 | loop fusion | flops 11005952 | bytes 11026432 | tf_op jit(solution)/shard_map/reduce_sum | solution.py:154
  67.5 3.5 %collective-permute-start.13 = (f32[4,1024]{1,0:T(4,128)S(1)}, f32[4,1024]{1,0:T(4,128)S(1)}, u32[]{:S(2)}, u32[]{:S(2)}) collective-permute-start(f32[4,1024]{1,0:T(4,128)S(1)} %pad_maximum_fusion.4), channel_id=1, source_target_pairs={{0,2},{2,0},{4,6},{6,4},{8,10},{10,8},{12,14},{14,12},{16,18},{18,... | collective-permute-start | bytes 49160 | tf_op jit(solution)/shard_map/ppermute | solution.py:34
  71.0 1.4 multiply_convert_fusion
  72.5 3.6 %collective-permute-start.14 = (f32[4,1024]{1,0:T(4,128)S(1)}, f32[4,1024]{1,0:T(4,128)S(1)}, u32[]{:S(2)}, u32[]{:S(2)}) collective-permute-start(f32[4,1024]{1,0:T(4,128)S(1)} %fusion.50), channel_id=1, source_target_pairs={{0,4},{2,6},{4,0},{6,2},{8,12},{10,14},{12,8},{14,10},{16,20},{18,... | collective-permute-start | bytes 49160 | tf_op jit(solution)/shard_map/ppermute | solution.py:34
  77.9 4.1 %collective-permute-start.15 = (f32[4,1024]{1,0:T(4,128)S(1)}, f32[4,1024]{1,0:T(4,128)S(1)}, u32[]{:S(2)}, u32[]{:S(2)}) collective-permute-start(f32[4,1024]{1,0:T(4,128)S(1)} %fusion.74), channel_id=1, source_target_pairs={{0,8},{2,10},{4,12},{6,14},{8,0},{10,2},{12,4},{14,6},{16,24},{18,... | collective-permute-start | bytes 49160 | tf_op jit(solution)/shard_map/ppermute | solution.py:34
  83.7 7.1 %collective-permute-start.16 = (f32[4,1024]{1,0:T(4,128)S(1)}, f32[4,1024]{1,0:T(4,128)S(1)}, u32[]{:S(2)}, u32[]{:S(2)}) collective-permute-start(f32[4,1024]{1,0:T(4,128)S(1)} %add.164), channel_id=1, source_target_pairs={{0,16},{2,18},{4,20},{6,22},{8,24},{10,26},{12,28},{14,30},{16,0},... | collective-permute-start | bytes 49160 | tf_op jit(solution)/shard_map/ppermute | solution.py:34
  90.8 5.2 %fusion.51 = (bf16[904,1024]{0,1:T(8,128)(2,1)S(1)}, f32[904,1024]{0,1:T(8,128)S(1)}) fusion(f32[907,1024]{0,1:T(8,128)S(1)} %maximum_maximum_fusion, f32[1024]{0:T(1024)S(1)} %bitcast.130, f32[1024]{0:T(1024)S(1)} %bitcast.132, f32[1024]{0:T(1024)S(1)} %bitcast.128, f32[896,1024]{0,1:T(8,128)S(1)} %bitcast.99, f32[1024]{0:T(1024)S(1)} %bitcast.126), kind=kLoop, calls=%fused_computation.103 | loop fusion | flops 7405568 | bytes 20348928 | tf_op jit(solution)/shard_map/convert.5
  96.0 3.8 %collective-permute-start.17 = (f32[4,1024]{1,0:T(4,128)S(1)}, f32[4,1024]{1,0:T(4,128)S(1)}, u32[]{:S(2)}, u32[]{:S(2)}) collective-permute-start(f32[4,1024]{1,0:T(4,128)S(1)} %add.165), channel_id=1, source_target_pairs={{0,32},{2,34},{4,36},{6,38},{8,40},{10,42},{12,44},{14,46},{16,48}... | collective-permute-start | bytes 49160 | tf_op jit(solution)/shard_map/ppermute | solution.py:34
  100.3 1.3 collective-permute-start.8
  102.8 1.3 collective-permute-start.11
  104.2 4.0 %collective-permute-start.18 = (f32[4,1024]{1,0:T(4,128)S(1)}, f32[4,1024]{1,0:T(4,128)S(1)}, u32[]{:S(2)}, u32[]{:S(2)}) collective-permute-start(f32[4,1024]{1,0:T(4,128)S(1)} %add.166), channel_id=1, source_target_pairs={{0,64},{2,66},{4,68},{6,70},{8,72},{10,74},{12,76},{14,78},{16,80}... | collective-permute-start | bytes 49160 | tf_op jit(solution)/shard_map/ppermute | solution.py:34
  108.3 10.5 %collective-permute-done.18 = f32[4,1024]{1,0:T(4,128)S(1)} collective-permute-done((f32[4,1024]{1,0:T(4,128)S(1)}, f32[4,1024]{1,0:T(4,128)S(1)}, u32[]{:S(2)}, u32[]{:S(2)}) %collective-permute-start.18) | collective-permute-done | bytes 16416 | tf_op jit(solution)/shard_map/ppermute | solution.py:34
  118.8 8.3 %collective-permute-start.19 = (f32[4,1024]{1,0:T(4,128)S(1)}, f32[4,1024]{1,0:T(4,128)S(1)}, u32[]{:S(2)}, u32[]{:S(2)}) collective-permute-start(f32[4,1024]{1,0:T(4,128)S(1)} %add.167), channel_id=1, source_target_pairs={{0,128},{2,130},{4,132},{6,134},{8,136},{10,138},{12,140},{14,142}... | collective-permute-start | bytes 49160 | tf_op jit(solution)/shard_map/ppermute | solution.py:34
  129.6 1.3 fusion.33
  134.6 6.0 %collective-permute-done.9 = bf16[256,1024]{0,1:T(8,128)(2,1)} collective-permute-done((bf16[256,1024]{0,1:T(8,128)(2,1)}, bf16[256,1024]{0,1:T(8,128)(2,1)}, u32[]{:S(2)}, u32[]{:S(2)}) %collective-permute-start.9) | collective-permute-done | bytes 524320 | tf_op jit(solution)/shard_map/ppermute | solution.py:20
  140.5 1.4 fusion.26
  143.0 3.2 %collective-permute-done.12 = bf16[256,1024]{0,1:T(8,128)(2,1)} collective-permute-done((bf16[256,1024]{0,1:T(8,128)(2,1)}, bf16[256,1024]{0,1:T(8,128)(2,1)}, u32[]{:S(2)}, u32[]{:S(2)}) %collective-permute-start.12) | collective-permute-done | bytes 524320 | tf_op jit(solution)/shard_map/ppermute | solution.py:20
  146.2 1.9 %fusion.31 = bf16[256,1024]{0,1:T(8,128)(2,1)S(1)} fusion(bf16[256,1024]{0,1:T(8,128)(2,1)S(1)} %copy-done.4, f32[904,1024]{0,1:T(8,128)} %copy-done, bf16[256,1024]{0,1:T(8,128)(2,1)} %collective-permute-done.12, pred[]{:T(512)S(6)} %eq.29), kind=kLoop, calls=%fused_computation.60 | loop fusion | flops 1572864 | bytes 2621441 | tf_op jit(solution)/shard_map/convert_element_type | solution.py:191
  (100 shorter events, 25.7 us)
Async XLA Ops:
  0.6 22.6 %copy-start.8 = (bf16[256,1024]{1,0:T(8,128)(2,1)S(1)}, bf16[256,1024]{1,0:T(8,128)(2,1)}, u32[]{:S(2)}) copy-start(bf16[256,1024]{1,0:T(8,128)(2,1)} %param.10) | copy-start | bytes 1572868
  0.6 20.5 %copy-start.6 = (bf16[256,1024]{1,0:T(8,128)(2,1)S(1)}, bf16[256,1024]{1,0:T(8,128)(2,1)}, u32[]{:S(2)}) copy-start(bf16[256,1024]{1,0:T(8,128)(2,1)} %param.8) | copy-start | bytes 1572868
  0.7 21.5 %copy-start.7 = (bf16[256,1024]{1,0:T(8,128)(2,1)S(1)}, bf16[256,1024]{1,0:T(8,128)(2,1)}, u32[]{:S(2)}) copy-start(bf16[256,1024]{1,0:T(8,128)(2,1)} %param.11) | copy-start | bytes 1572868
  0.7 22.6 %copy-start.10 = (f32[4,1024]{1,0:T(4,128)S(1)}, f32[4,1024]{1,0:T(4,128)}, u32[]{:S(2)}) copy-start(f32[4,1024]{1,0:T(4,128)} %param.13) | copy-start | bytes 49156
  2.0 14.7 %collective-permute-start = (bf16[256,1024]{0,1:T(8,128)(2,1)S(1)}, bf16[256,1024]{0,1:T(8,128)(2,1)S(1)}, u32[]{:S(2)}, u32[]{:S(2)}) collective-permute-start(bf16[256,1024]{0,1:T(8,128)(2,1)S(1)} %copy.59), channel_id=1, source_target_pairs={{0,4},{2,6},{4,8},{6,10},{8,12},{10,14},{12,16},{14,18},{16,20},{1... | collective-permute-start | bytes 1572872 | tf_op jit(solution)/shard_map/ppermute | solution.py:20
  17.5 12.7 %collective-permute-start.2 = (bf16[256,1024]{0,1:T(8,128)(2,1)}, bf16[256,1024]{0,1:T(8,128)(2,1)}, u32[]{:S(2)}, u32[]{:S(2)}) collective-permute-start(bf16[256,1024]{0,1:T(8,128)(2,1)} %broadcast_select_fusion.1), channel_id=1, source_target_pairs={{0,2},{2,0},{4,6},{6,4},{8,10},{10,8},{12,14},{14,12},{16,18},{18,... | collective-permute-start | bytes 1572872 | tf_op jit(solution)/shard_map/ppermute | solution.py:25
  18.7 10.8 %collective-permute-start.1 = (bf16[136,1024]{0,1:T(8,128)(2,1)}, bf16[136,1024]{0,1:T(8,128)(2,1)S(1)}, u32[]{:S(2)}, u32[]{:S(2)}) collective-permute-start(bf16[136,1024]{0,1:T(8,128)(2,1)} %slice.96), channel_id=1, source_target_pairs={{0,2},{2,4},{4,6},{6,8},{8,10},{10,12},{12,14},{14,16},{16,18},{18... | collective-permute-start | bytes 835592 | tf_op jit(solution)/shard_map/ppermute | solution.py:20
  24.2 16.8 %collective-permute-start.3 = (bf16[256,1024]{0,1:T(8,128)(2,1)}, bf16[256,1024]{0,1:T(8,128)(2,1)}, u32[]{:S(2)}, u32[]{:S(2)}) collective-permute-start(bf16[256,1024]{0,1:T(8,128)(2,1)} %copy.65), channel_id=1, source_target_pairs={{0,4},{2,6},{4,8},{6,10},{8,12},{10,14},{12,16},{14,18},{16,20},{1... | collective-permute-start | bytes 1572872 | tf_op jit(solution)/shard_map/ppermute | solution.py:20
  43.4 6.3 %collective-permute-start.5 = (bf16[256,1024]{0,1:T(8,128)(2,1)S(1)}, bf16[256,1024]{0,1:T(8,128)(2,1)S(1)}, u32[]{:S(2)}, u32[]{:S(2)}) collective-permute-start(bf16[256,1024]{0,1:T(8,128)(2,1)S(1)} %broadcast_select_fusion), channel_id=1, source_target_pairs={{0,2},{2,0},{4,6},{6,4},{8,10},{10,8},{12,14},{14,12},{16,18},{18,... | collective-permute-start | bytes 1572872 | tf_op jit(solution)/shard_map/ppermute | solution.py:25
  43.8 5.8 %collective-permute-start.4 = (bf16[136,1024]{0,1:T(8,128)(2,1)S(1)}, bf16[136,1024]{0,1:T(8,128)(2,1)S(1)}, u32[]{:S(2)}, u32[]{:S(2)}) collective-permute-start(bf16[136,1024]{0,1:T(8,128)(2,1)S(1)} %slice.99), channel_id=1, source_target_pairs={{0,2},{2,4},{4,6},{6,8},{8,10},{10,12},{12,14},{14,16},{16,18},{18... | collective-permute-start | bytes 835592 | tf_op jit(solution)/shard_map/ppermute | solution.py:20
  51.9 3.4 %copy-start.9 = (f32[1024]{0:T(1024)S(1)}, f32[1024]{0:T(1024)}, u32[]{:S(2)}) copy-start(f32[1024]{0:T(1024)} %param.12) | copy-start | bytes 12292
  56.4 5.4 %collective-permute-start.6 = (f32[3,256]{1,0:T(4,128)S(1)}, f32[3,256]{1,0:T(4,128)S(1)}, u32[]{:S(2)}, u32[]{:S(2)}) collective-permute-start(f32[3,256]{1,0:T(4,128)S(1)} %pad_maximum_fusion.5), channel_id=1, source_target_pairs={{0,1},{1,0},{2,3},{3,2},{4,5},{5,4},{6,7},{7,6},{8,9},{9,8},{10,11... | collective-permute-start | bytes 9224 | tf_op jit(solution)/shard_map/ppermute | solution.py:42
  62.4 8.6 %slice-start = ((s8[7340032]{0:T(1024)(128)(4,1)}), s8[4194304]{0:T(1024)(128)(4,1)S(1)}, s32[]{:S(2)}) async-start(s8[7340032]{0:T(1024)(128)(4,1)} %bitcast.101), calls=%async_computation | async-start | bytes 8388608
  63.6 7.5 %slice-start.1 = ((s8[7340032]{0:T(1024)(128)(4,1)}), s8[3145728]{0:T(1024)(128)(4,1)S(1)}, s32[]{:S(2)}) async-start(s8[7340032]{0:T(1024)(128)(4,1)} %bitcast.101), calls=%async_computation.1 | async-start | bytes 6291456
  67.5 4.9 %collective-permute-start.13 = (f32[4,1024]{1,0:T(4,128)S(1)}, f32[4,1024]{1,0:T(4,128)S(1)}, u32[]{:S(2)}, u32[]{:S(2)}) collective-permute-start(f32[4,1024]{1,0:T(4,128)S(1)} %pad_maximum_fusion.4), channel_id=1, source_target_pairs={{0,2},{2,0},{4,6},{6,4},{8,10},{10,8},{12,14},{14,12},{16,18},{18,... | collective-permute-start | bytes 49160 | tf_op jit(solution)/shard_map/ppermute | solution.py:34
  71.0 5.1 %copy-start.1 = (bf16[256,1024]{0,1:T(8,128)(2,1)S(1)}, bf16[256,1024]{0,1:T(8,128)(2,1)}, u32[]{:S(2)}) copy-start(bf16[256,1024]{0,1:T(8,128)(2,1)} %copy.88) | copy-start | bytes 1572868
  72.5 5.4 %collective-permute-start.14 = (f32[4,1024]{1,0:T(4,128)S(1)}, f32[4,1024]{1,0:T(4,128)S(1)}, u32[]{:S(2)}, u32[]{:S(2)}) collective-permute-start(f32[4,1024]{1,0:T(4,128)S(1)} %fusion.50), channel_id=1, source_target_pairs={{0,4},{2,6},{4,0},{6,2},{8,12},{10,14},{12,8},{14,10},{16,20},{18,... | collective-permute-start | bytes 49160 | tf_op jit(solution)/shard_map/ppermute | solution.py:34
  77.4 49.7 %collective-permute-start.7 = (bf16[256,1024]{0,1:T(8,128)(2,1)S(1)}, bf16[256,1024]{0,1:T(8,128)(2,1)S(1)}, u32[]{:S(2)}, u32[]{:S(2)}) collective-permute-start(bf16[256,1024]{0,1:T(8,128)(2,1)S(1)} %bitcast.112), channel_id=1, source_target_pairs={{0,2},{2,0},{4,6},{6,4},{8,10},{10,8},{12,14},{14,12},{16,18},{18,... | collective-permute-start | bytes 1572872 | tf_op jit(solution)/shard_map/ppermute | solution.py:25
  77.9 5.8 %collective-permute-start.15 = (f32[4,1024]{1,0:T(4,128)S(1)}, f32[4,1024]{1,0:T(4,128)S(1)}, u32[]{:S(2)}, u32[]{:S(2)}) collective-permute-start(f32[4,1024]{1,0:T(4,128)S(1)} %fusion.74), channel_id=1, source_target_pairs={{0,8},{2,10},{4,12},{6,14},{8,0},{10,2},{12,4},{14,6},{16,24},{18,... | collective-permute-start | bytes 49160 | tf_op jit(solution)/shard_map/ppermute | solution.py:34
  83.7 12.3 %collective-permute-start.16 = (f32[4,1024]{1,0:T(4,128)S(1)}, f32[4,1024]{1,0:T(4,128)S(1)}, u32[]{:S(2)}, u32[]{:S(2)}) collective-permute-start(f32[4,1024]{1,0:T(4,128)S(1)} %add.164), channel_id=1, source_target_pairs={{0,16},{2,18},{4,20},{6,22},{8,24},{10,26},{12,28},{14,30},{16,0},... | collective-permute-start | bytes 49160 | tf_op jit(solution)/shard_map/ppermute | solution.py:34
  96.0 33.5 %copy-start = (f32[904,1024]{0,1:T(8,128)}, f32[904,1024]{0,1:T(8,128)S(1)}, u32[]{:S(2)}) copy-start(f32[904,1024]{0,1:T(8,128)S(1)} %get-tuple-element.31) | copy-start | bytes 11108356
  96.0 8.1 %collective-permute-start.17 = (f32[4,1024]{1,0:T(4,128)S(1)}, f32[4,1024]{1,0:T(4,128)S(1)}, u32[]{:S(2)}, u32[]{:S(2)}) collective-permute-start(f32[4,1024]{1,0:T(4,128)S(1)} %add.165), channel_id=1, source_target_pairs={{0,32},{2,34},{4,36},{6,38},{8,40},{10,42},{12,44},{14,46},{16,48}... | collective-permute-start | bytes 49160 | tf_op jit(solution)/shard_map/ppermute | solution.py:34
  100.3 26.7 %collective-permute-start.8 = (bf16[136,1024]{0,1:T(8,128)(2,1)S(1)}, bf16[136,1024]{0,1:T(8,128)(2,1)S(1)}, u32[]{:S(2)}, u32[]{:S(2)}) collective-permute-start(bf16[136,1024]{0,1:T(8,128)(2,1)S(1)} %pad_slice_fusion), channel_id=1, source_target_pairs={{2,0},{4,2},{6,4},{8,6},{10,8},{12,10},{14,12},{16,14},{18,16},{20... | collective-permute-start | bytes 835592 | tf_op jit(solution)/shard_map/ppermute | solution.py:20
  101.6 27.9 %collective-permute-start.10 = (bf16[256,1024]{0,1:T(8,128)(2,1)S(1)}, bf16[256,1024]{0,1:T(8,128)(2,1)S(1)}, u32[]{:S(2)}, u32[]{:S(2)}) collective-permute-start(bf16[256,1024]{0,1:T(8,128)(2,1)S(1)} %slice.137), channel_id=1, source_target_pairs={{0,2},{2,0},{4,6},{6,4},{8,10},{10,8},{12,14},{14,12},{16,18},{18,... | collective-permute-start | bytes 1572872 | tf_op jit(solution)/shard_map/ppermute | solution.py:25
  102.8 26.7 %collective-permute-start.11 = (bf16[136,1024]{0,1:T(8,128)(2,1)S(1)}, bf16[136,1024]{0,1:T(8,128)(2,1)S(1)}, u32[]{:S(2)}, u32[]{:S(2)}) collective-permute-start(bf16[136,1024]{0,1:T(8,128)(2,1)S(1)} %slice.139), channel_id=1, source_target_pairs={{2,0},{4,2},{6,4},{8,6},{10,8},{12,10},{14,12},{16,14},{18,16},{20... | collective-permute-start | bytes 835592 | tf_op jit(solution)/shard_map/ppermute | solution.py:20
  104.2 14.6 %collective-permute-start.18 = (f32[4,1024]{1,0:T(4,128)S(1)}, f32[4,1024]{1,0:T(4,128)S(1)}, u32[]{:S(2)}, u32[]{:S(2)}) collective-permute-start(f32[4,1024]{1,0:T(4,128)S(1)} %add.166), channel_id=1, source_target_pairs={{0,64},{2,66},{4,68},{6,70},{8,72},{10,74},{12,76},{14,78},{16,80}... | collective-permute-start | bytes 49160 | tf_op jit(solution)/shard_map/ppermute | solution.py:34
  118.8 15.1 %collective-permute-start.19 = (f32[4,1024]{1,0:T(4,128)S(1)}, f32[4,1024]{1,0:T(4,128)S(1)}, u32[]{:S(2)}, u32[]{:S(2)}) collective-permute-start(f32[4,1024]{1,0:T(4,128)S(1)} %add.167), channel_id=1, source_target_pairs={{0,128},{2,130},{4,132},{6,134},{8,136},{10,138},{12,140},{14,142}... | collective-permute-start | bytes 49160 | tf_op jit(solution)/shard_map/ppermute | solution.py:34
  127.1 5.8 %copy-start.2 = (bf16[256,1024]{0,1:T(8,128)(2,1)}, bf16[256,1024]{0,1:T(8,128)(2,1)S(1)}, u32[]{:S(2)}) copy-start(bf16[256,1024]{0,1:T(8,128)(2,1)S(1)} %collective-permute-done.7) | copy-start | bytes 1572868
  128.2 12.3 %collective-permute-start.9 = (bf16[256,1024]{0,1:T(8,128)(2,1)}, bf16[256,1024]{0,1:T(8,128)(2,1)}, u32[]{:S(2)}, u32[]{:S(2)}) collective-permute-start(bf16[256,1024]{0,1:T(8,128)(2,1)} %fusion.28), channel_id=1, source_target_pairs={{4,0},{6,2},{8,4},{10,6},{12,8},{14,10},{16,12},{18,14},{20,16},{2... | collective-permute-start | bytes 1572872 | tf_op jit(solution)/shard_map/ppermute | solution.py:20
  129.5 3.4 %copy-start.3 = (bf16[256,1024]{0,1:T(8,128)(2,1)}, bf16[256,1024]{0,1:T(8,128)(2,1)S(1)}, u32[]{:S(2)}) copy-start(bf16[256,1024]{0,1:T(8,128)(2,1)S(1)} %collective-permute-done.10) | copy-start | bytes 1572868
  130.9 15.3 %collective-permute-start.12 = (bf16[256,1024]{0,1:T(8,128)(2,1)}, bf16[256,1024]{0,1:T(8,128)(2,1)}, u32[]{:S(2)}, u32[]{:S(2)}) collective-permute-start(bf16[256,1024]{0,1:T(8,128)(2,1)} %fusion.33), channel_id=1, source_target_pairs={{4,0},{6,2},{8,4},{10,6},{12,8},{14,10},{16,12},{18,14},{20,16},{2... | collective-permute-start | bytes 1572872 | tf_op jit(solution)/shard_map/ppermute | solution.py:20
  132.9 13.2 %copy-start.4 = (bf16[256,1024]{0,1:T(8,128)(2,1)S(1)}, bf16[256,1024]{0,1:T(8,128)(2,1)}, u32[]{:S(2)}) copy-start(bf16[256,1024]{0,1:T(8,128)(2,1)} %copy-done.3) | copy-start | bytes 1572868
  (2 other events, 2.7 us)

commit v8 on v5

--- a/solution.py
+++ b/solution.py
@@ -25,14 +25,12 @@
     return lax.ppermute(block, axis, [(i, i ^ 1) for i in range(size)])
 
 
-def all_sum(block, axis):
+def exchange_rounds(block, axis, first, last):
     size = lax.axis_size(axis)
-    if size & (size - 1):
-        return lax.psum(block, axis)
-    stride = size // 2
-    while stride >= 1:
+    stride = first
+    while stride < min(last, size):
         block = block + lax.ppermute(block, axis, [(i, i ^ stride) for i in range(size)])
-        stride //= 2
+        stride *= 2
     return block
 
 
@@ -157,7 +155,6 @@
             for tap_index in range(tap_count)
         ]
     )
-    conv_grad = all_sum(local_taps, "tm")
 
     lead = jnp.zeros((far_lead, channels), jnp.float32)
     padded_value = jnp.concatenate([lead, value_part, jnp.zeros((rim_rows, channels), jnp.float32)], 0)
@@ -165,7 +162,7 @@
     for tap_index in range(tap_count):
         value_sum = value_sum + conv_weight[tap_index] * padded_value[tap_index : tap_index + key_count + far_lead]
 
-    def relay_back(grads):
+    def relay_back_first(grads):
         cut_third = row_count - far_rows + far_lead
         grad_third = grads[:cut_third]
         grad_second = grads[cut_third : cut_third + row_count]
@@ -177,11 +174,21 @@
             [jnp.zeros((far_rows - far_lead, grads.shape[1]), jnp.float32), back_third], 0
         )
         grad_second = grad_second + jnp.where(even, 0.0, back_first)
-        back_second = from_behind(grad_second.astype(jnp.bfloat16), "tm", -2).astype(jnp.float32)
-        return grad_own + jnp.where(even, back_first, 0.0) + back_second
-
-    value_total = relay_back(value_sum)
-    key_total = relay_back(jnp.concatenate([lead, key_part], 0))
+        return grad_own + jnp.where(even, back_first, 0.0), grad_second.astype(jnp.bfloat16)
+
+    value_near, value_second = relay_back_first(value_sum)
+    key_near, key_second = relay_back_first(jnp.concatenate([lead, key_part], 0))
+
+    size = lax.axis_size("tm")
+    if size & (size - 1):
+        conv_grad = lax.psum(local_taps, "tm")
+    else:
+        split = max(1, size // 4)
+        taps_near = exchange_rounds(local_taps, "tm", 1, split)
+        taps_near, value_second, key_second = lax.optimization_barrier((taps_near, value_second, key_second))
+        conv_grad = exchange_rounds(taps_near, "tm", split, size)
+    value_total = value_near + from_behind(value_second, "tm", -2).astype(jnp.float32)
+    key_total = key_near + from_behind(key_second, "tm", -2).astype(jnp.float32)
 
     return (
         query_grad.reshape(row_count, channels).astype(jnp.bfloat16),

time: 144 us -> 143 us (level)
  the two profiles are of different devices: /device:TPU:4 before, /device:TPU:37 now
where the time goes in v8:
time: 143 us; the launch traced here: 142 us
  starting transfers between devices  45.2 us (32%)
  waiting for transfers between devices  37.8 us (26%)
  other arithmetic  31.7 us (22%)
  local copies, waits for them, and re-layouts  13.4 us (9%)
  matrix products  12.7 us (9%)
    ppermute x8, starting transfers between devices, from_behind(): return lax.ppermute(block, axis, route)  24 us
    ppermute x7, waiting for transfers between devices, exchange_rounds(): lax.ppermute(block, axis, [(i, i ^ stride) for i in range(size)])  20.4 us
    ppermute x7, starting transfers between devices, exchange_rounds(): lax.ppermute(block, axis, [(i, i ^ stride) for i in range(size)])  15.7 us
    ppermute x8, waiting for transfers between devices, from_behind(): return lax.ppermute(block, axis, route)  13.8 us
    unnamed x37, local copies, waits for them, and re-layouts  8.61 us
    sub x1, matrix products, body(): expo = jnp.where(mask[None], jnp.exp(scores - row_peak[..., None]), 0.0)  7.3 us
    another operation x1, other arithmetic  5.2 us
    ppermute x4, starting transfers between devices, chip_swap(): return lax.ppermute(block, axis, [(i, i ^ 1) for i in range(size)])  4.96 us
  transfers between devices with their start and end apart: 20, of which 7 were waited for; matrix products, arithmetic and copies ran while one was open for 26% of the time, Pallas kernels for 0%

profile of v8, /device:TPU:37, one launch (start us, length us, event | category | flops | bytes accessed | tf_op | source)
XLA Modules:
  0.0 142.1 jit_solution(14866243789758403743)
XLA Ops:
  1.9 3.2 %collective-permute-start = (bf16[256,1024]{0,1:T(8,128)(2,1)S(1)}, bf16[256,1024]{0,1:T(8,128)(2,1)S(1)}, u32[]{:S(2)}, u32[]{:S(2)}) collective-permute-start(bf16[256,1024]{0,1:T(8,128)(2,1)S(1)} %copy.59), channel_id=1, source_target_pairs={{0,4},{2,6},{4,8},{6,10},{8,12},{10,14},{12,16},{14,18},{16,20},{1... | collective-permute-start | bytes 1572872 | tf_op jit(solution)/shard_map/ppermute | solution.py:20
  6.4 3.2 %collective-permute-start.3 = (bf16[256,1024]{0,1:T(8,128)(2,1)S(1)}, bf16[256,1024]{0,1:T(8,128)(2,1)S(1)}, u32[]{:S(2)}, u32[]{:S(2)}) collective-permute-start(bf16[256,1024]{0,1:T(8,128)(2,1)S(1)} %copy.65), channel_id=1, source_target_pairs={{0,4},{2,6},{4,8},{6,10},{8,12},{10,14},{12,16},{14,18},{16,20},{1... | collective-permute-start | bytes 1572872 | tf_op jit(solution)/shard_map/ppermute | solution.py:20
  11.6 8.1 %collective-permute-done = bf16[256,1024]{0,1:T(8,128)(2,1)S(1)} collective-permute-done((bf16[256,1024]{0,1:T(8,128)(2,1)S(1)}, bf16[256,1024]{0,1:T(8,128)(2,1)S(1)}, u32[]{:S(2)}, u32[]{:S(2)}) %collective-permute-start) | collective-permute-done | bytes 524320 | tf_op jit(solution)/shard_map/ppermute | solution.py:20
  20.5 2.7 %collective-permute-start.2 = (bf16[256,1024]{0,1:T(8,128)(2,1)}, bf16[256,1024]{0,1:T(8,128)(2,1)}, u32[]{:S(2)}, u32[]{:S(2)}) collective-permute-start(bf16[256,1024]{0,1:T(8,128)(2,1)} %broadcast_select_fusion.1), channel_id=1, source_target_pairs={{0,2},{2,0},{4,6},{6,4},{8,10},{10,8},{12,14},{14,12},{16,18},{18,... | collective-permute-start | bytes 1572872 | tf_op jit(solution)/shard_map/ppermute | solution.py:25
  24.3 1.9 %collective-permute-start.1 = (bf16[136,1024]{0,1:T(8,128)(2,1)}, bf16[136,1024]{0,1:T(8,128)(2,1)S(1)}, u32[]{:S(2)}, u32[]{:S(2)}) collective-permute-start(bf16[136,1024]{0,1:T(8,128)(2,1)} %slice.123), channel_id=1, source_target_pairs={{0,2},{2,4},{4,6},{6,8},{8,10},{10,12},{12,14},{14,16},{16,18},{18... | collective-permute-start | bytes 835592 | tf_op jit(solution)/shard_map/ppermute | solution.py:20
  29.4 1.5 %collective-permute-done.3 = bf16[256,1024]{0,1:T(8,128)(2,1)S(1)} collective-permute-done((bf16[256,1024]{0,1:T(8,128)(2,1)S(1)}, bf16[256,1024]{0,1:T(8,128)(2,1)S(1)}, u32[]{:S(2)}, u32[]{:S(2)}) %collective-permute-start.3) | collective-permute-done | bytes 524320 | tf_op jit(solution)/shard_map/ppermute | solution.py:20
  31.8 1.5 %collective-permute-start.5 = (bf16[256,1024]{0,1:T(8,128)(2,1)}, bf16[256,1024]{0,1:T(8,128)(2,1)}, u32[]{:S(2)}, u32[]{:S(2)}) collective-permute-start(bf16[256,1024]{0,1:T(8,128)(2,1)} %broadcast_select_fusion), channel_id=1, source_target_pairs={{0,2},{2,0},{4,6},{6,4},{8,10},{10,8},{12,14},{14,12},{16,18},{18,... | collective-permute-start | bytes 1572872 | tf_op jit(solution)/shard_map/ppermute | solution.py:25
  34.4 1.9 %collective-permute-start.4 = (bf16[136,1024]{0,1:T(8,128)(2,1)}, bf16[136,1024]{0,1:T(8,128)(2,1)}, u32[]{:S(2)}, u32[]{:S(2)}) collective-permute-start(bf16[136,1024]{0,1:T(8,128)(2,1)} %slice.124), channel_id=1, source_target_pairs={{0,2},{2,4},{4,6},{6,8},{8,10},{10,12},{12,14},{14,16},{16,18},{18... | collective-permute-start | bytes 835592 | tf_op jit(solution)/shard_map/ppermute | solution.py:20
  37.2 1.6 %pad_maximum_fusion.1 = bf16[896,1024]{0,1:T(8,128)(2,1)S(1)} fusion(bf16[256,1024]{0,1:T(8,128)(2,1)S(1)} %copy.59, bf16[256,1024]{0,1:T(8,128)(2,1)} %collective-permute-done.2, bf16[256,1024]{0,1:T(8,128)(2,1)S(1)} %collective-permute-done, bf16[136,1024]{0,1:T(8,128)(2,1)} %copy-done.9), kind=kLoop, calls=%fused_computation.36 | loop fusion | flops 7340032 | bytes 3686400 | tf_op jit(solution)/shard_map/concatenate | solution.py:79
  38.8 7.3 %fusion.57 = (f32[8,256]{1,0:T(8,128)S(1)}, f32[8,256,896]{1,2,0:T(8,128)}) fusion(pred[256,896]{0,1:T(8,128)(4,1)} %fusion.39, bf16[896,8,128]{0,2,1:T(8,128)(2,1)S(1)} %bitcast.103, bf16[256,8,128]{0,2,1:T(8,128)(2,1)} %bitcast.107), kind=kOutput, calls=%fused_computation.107 | convolution fusion | flops 478937984 | bytes 9936896 | tf_op jit(solution)/shard_map/sub | solution.py:102
  46.1 3.8 %fusion.16 = bf16[8,256,896]{1,2,0:T(8,128)(2,1)S(1)} fusion(f32[8,256,896]{1,2,0:T(8,128)} %get-tuple-element.42, f32[8,256]{1,0:T(8,128)S(1)} %get-tuple-element.41), kind=kLoop, calls=%fused_computation.33 | loop fusion | flops 3670016 | bytes 11018240 | tf_op jit(solution)/shard_map/convert_element_type | solution.py:105
  49.9 2.2 %pad_maximum_fusion = bf16[904,1024]{0,1:T(8,128)(2,1)S(1)} fusion(bf16[256,1024]{0,1:T(8,128)(2,1)S(1)} %copy-done.2, bf16[256,1024]{0,1:T(8,128)(2,1)} %collective-permute-done.5, bf16[256,1024]{0,1:T(8,128)(2,1)S(1)} %copy-done.4, bf16[136,1024]{0,1:T(8,128)(2,1)} %collective-permute-done.4), kind=kLoop, calls=%fused_computation.34 | loop fusion | flops 7405568 | bytes 3702784 | tf_op jit(solution)/shard_map/concatenate | solution.py:79
  52.2 3.4 %fusion.8 = bf16[896,1024]{0,1:T(8,128)(2,1)S(1)} fusion(f32[1024]{0:T(1024)S(1)} %bitcast.129, f32[1024]{0:T(1024)S(1)} %bitcast.131, f32[1024]{0:T(1024)S(1)} %bitcast.127, f32[1024]{0:T(1024)S(1)} %bitcast.125, bf16[904,1024]{0,1:T(8,128)(2,1)S(1)} %pad_maximum_fusion), kind=kLoop, calls=%fused_computation.23 | loop fusion | flops 11010048 | bytes 9191424 | tf_op jit(solution)/shard_map/convert_element_type | solution.py:89
  57.4 3.5 %collective-permute-done.6 = f32[3,256]{1,0:T(4,128)S(1)} collective-permute-done((f32[3,256]{1,0:T(4,128)S(1)}, f32[3,256]{1,0:T(4,128)S(1)}, u32[]{:S(2)}, u32[]{:S(2)}) %collective-permute-start.6) | collective-permute-done | bytes 3104 | tf_op jit(solution)/shard_map/ppermute | solution.py:40
  62.9 1.4 %multiply_convert_fusion = bf16[8,256,896]{1,2,0:T(8,128)(2,1)S(1)} fusion(f32[8,256]{1,0:T(8,128)S(1)} %bitcast.142, f32[8,256,896]{1,2,0:T(8,128)S(1)} %bitcast.102, f32[8,256]{1,0:T(8,128)S(1)} %get-tuple-element.41, bf16[256,8,128]{0,2,1:T(8,128)(2,1)S(1)} %bitcast.111, bf16[896,8,128]{0,2,1:T(8,128)(2,1)S(1)} %bitcast.106), kind=kOutput, calls=%fused_computation.2 | convolution fusion | flops 477102080 | bytes 13385728 | tf_op jit(solution)/shard_map/thd,uhd->htu/dot_general | solution.py:134
  64.3 4.0 %fusion.9 = (f32[1024]{0:T(1024)S(1)}, f32[1024]{0:T(1024)S(1)}, f32[1024]{0:T(1024)S(1)}, f32[1024]{0:T(1024)S(1)}) fusion(bf16[904,1024]{0,1:T(8,128)(2,1)S(1)} %pad_maximum_fusion, f32[8,128,896]{2,1,0:T(8,128)S(1)} %fusion.59), kind=kLoop, calls=%fused_computation.24 | loop fusion | flops 11005952 | bytes 11026432 | tf_op jit(solution)/shard_map/reduce_sum | solution.py:150
  68.4 2.9 %collective-permute-start.8 = (f32[4,1024]{1,0:T(4,128)S(1)}, f32[4,1024]{1,0:T(4,128)S(1)}, u32[]{:S(2)}, u32[]{:S(2)}) collective-permute-start(f32[4,1024]{1,0:T(4,128)S(1)} %pad_maximum_fusion.4), channel_id=1, source_target_pairs={{0,2},{2,0},{4,6},{6,4},{8,10},{10,8},{12,14},{14,12},{16,18},{18,... | collective-permute-start | bytes 49160 | tf_op jit(solution)/shard_map/ppermute | solution.py:32
  72.6 5.2 %fusion.51 = (bf16[904,1024]{0,1:T(8,128)(2,1)S(1)}, f32[904,1024]{0,1:T(8,128)S(1)}) fusion(f32[907,1024]{0,1:T(8,128)S(1)} %maximum_maximum_fusion, f32[1024]{0:T(1024)S(1)} %bitcast.130, f32[1024]{0:T(1024)S(1)} %bitcast.132, f32[1024]{0:T(1024)S(1)} %bitcast.128, f32[896,1024]{0,1:T(8,128)S(1)} %bitcast.99, f32[1024]{0:T(1024)S(1)} %bitcast.126), kind=kLoop, calls=%fused_computation.103 | loop fusion | flops 7405568 | bytes 20348928 | tf_op jit(solution)/shard_map/convert.9
  78.2 2.3 %collective-permute-start.10 = (f32[4,1024]{1,0:T(4,128)S(1)}, f32[4,1024]{1,0:T(4,128)S(1)}, u32[]{:S(2)}, u32[]{:S(2)}) collective-permute-start(f32[4,1024]{1,0:T(4,128)S(1)} %fusion.74), channel_id=1, source_target_pairs={{0,8},{2,10},{4,12},{6,14},{8,0},{10,2},{12,4},{14,6},{16,24},{18,... | collective-permute-start | bytes 49160 | tf_op jit(solution)/shard_map/ppermute | solution.py:32
  82.4 2.1 %collective-permute-start.13 = (bf16[136,1024]{0,1:T(8,128)(2,1)S(1)}, bf16[136,1024]{0,1:T(8,128)(2,1)S(1)}, u32[]{:S(2)}, u32[]{:S(2)}) collective-permute-start(bf16[136,1024]{0,1:T(8,128)(2,1)S(1)} %slice.138), channel_id=1, source_target_pairs={{2,0},{4,2},{6,4},{8,6},{10,8},{12,10},{14,12},{16,14},{18,16},{20... | collective-permute-start | bytes 835592 | tf_op jit(solution)/shard_map/ppermute | solution.py:20
  84.6 2.0 %collective-permute-start.11 = (f32[4,1024]{1,0:T(4,128)S(1)}, f32[4,1024]{1,0:T(4,128)S(1)}, u32[]{:S(2)}, u32[]{:S(2)}) collective-permute-start(f32[4,1024]{1,0:T(4,128)S(1)} %add.154), channel_id=1, source_target_pairs={{0,16},{2,18},{4,20},{6,22},{8,24},{10,26},{12,28},{14,30},{16,0},... | collective-permute-start | bytes 49160 | tf_op jit(solution)/shard_map/ppermute | solution.py:32
  86.8 3.7 %collective-permute-start.15 = (bf16[136,1024]{0,1:T(8,128)(2,1)S(1)}, bf16[136,1024]{0,1:T(8,128)(2,1)S(1)}, u32[]{:S(2)}, u32[]{:S(2)}) collective-permute-start(bf16[136,1024]{0,1:T(8,128)(2,1)S(1)} %pad_slice_fusion), channel_id=1, source_target_pairs={{2,0},{4,2},{6,4},{8,6},{10,8},{12,10},{14,12},{16,14},{18,16},{20... | collective-permute-start | bytes 835592 | tf_op jit(solution)/shard_map/ppermute | solution.py:20
  90.8 2.4 %collective-permute-done.12 = f32[4,1024]{1,0:T(4,128)S(1)} collective-permute-done((f32[4,1024]{1,0:T(4,128)S(1)}, f32[4,1024]{1,0:T(4,128)S(1)}, u32[]{:S(2)}, u32[]{:S(2)}) %collective-permute-start.12) | collective-permute-done | bytes 16416 | tf_op jit(solution)/shard_map/ppermute | solution.py:32
  94.6 4.2 %collective-permute-done.15 = bf16[136,1024]{0,1:T(8,128)(2,1)S(1)} collective-permute-done((bf16[136,1024]{0,1:T(8,128)(2,1)S(1)}, bf16[136,1024]{0,1:T(8,128)(2,1)S(1)}, u32[]{:S(2)}, u32[]{:S(2)}) %collective-permute-start.15) | collective-permute-done | bytes 278560 | tf_op jit(solution)/shard_map/ppermute | solution.py:20
  100.0 6.1 %collective-permute-start.16 = (bf16[256,1024]{0,1:T(8,128)(2,1)}, bf16[256,1024]{0,1:T(8,128)(2,1)}, u32[]{:S(2)}, u32[]{:S(2)}) collective-permute-start(bf16[256,1024]{0,1:T(8,128)(2,1)} %fusion.28), channel_id=1, source_target_pairs={{4,0},{6,2},{8,4},{10,6},{12,8},{14,10},{16,12},{18,14},{20,16},{2... | collective-permute-start | bytes 1572872 | tf_op jit(solution)/shard_map/ppermute | solution.py:20
  106.1 3.1 %collective-permute-start.18 = (f32[4,1024]{1,0:T(4,128)S(1)}, f32[4,1024]{1,0:T(4,128)S(1)}, u32[]{:S(2)}, u32[]{:S(2)}) collective-permute-start(f32[4,1024]{1,0:T(4,128)S(1)} %add.156), channel_id=1, source_target_pairs={{0,64},{2,66},{4,68},{6,70},{8,72},{10,74},{12,76},{14,78},{16,80}... | collective-permute-start | bytes 49160 | tf_op jit(solution)/shard_map/ppermute | solution.py:32
  109.2 1.9 %collective-permute-start.17 = (bf16[256,1024]{0,1:T(8,128)(2,1)}, bf16[256,1024]{0,1:T(8,128)(2,1)}, u32[]{:S(2)}, u32[]{:S(2)}) collective-permute-start(bf16[256,1024]{0,1:T(8,128)(2,1)} %fusion.30), channel_id=1, source_target_pairs={{4,0},{6,2},{8,4},{10,6},{12,8},{14,10},{16,12},{18,14},{20,16},{2... | collective-permute-start | bytes 1572872 | tf_op jit(solution)/shard_map/ppermute | solution.py:20
  111.1 10.7 %collective-permute-done.18 = f32[4,1024]{1,0:T(4,128)S(1)} collective-permute-done((f32[4,1024]{1,0:T(4,128)S(1)}, f32[4,1024]{1,0:T(4,128)S(1)}, u32[]{:S(2)}, u32[]{:S(2)}) %collective-permute-start.18) | collective-permute-done | bytes 16416 | tf_op jit(solution)/shard_map/ppermute | solution.py:32
  121.9 5.2 %collective-permute-start.19 = (f32[4,1024]{1,0:T(4,128)S(1)}, f32[4,1024]{1,0:T(4,128)S(1)}, u32[]{:S(2)}, u32[]{:S(2)}) collective-permute-start(f32[4,1024]{1,0:T(4,128)S(1)} %add.167), channel_id=1, source_target_pairs={{0,128},{2,130},{4,132},{6,134},{8,136},{10,138},{12,140},{14,142}... | collective-permute-start | bytes 49160 | tf_op jit(solution)/shard_map/ppermute | solution.py:32
  128.9 7.3 %collective-permute-done.19 = f32[4,1024]{1,0:T(4,128)S(1)} collective-permute-done((f32[4,1024]{1,0:T(4,128)S(1)}, f32[4,1024]{1,0:T(4,128)S(1)}, u32[]{:S(2)}, u32[]{:S(2)}) %collective-permute-start.19) | collective-permute-done | bytes 16416 | tf_op jit(solution)/shard_map/ppermute | solution.py:32
  136.7 1.4 %fusion.26 = bf16[256,1024]{0,1:T(8,128)(2,1)S(1)} fusion(bf16[256,1024]{0,1:T(8,128)(2,1)} %copy-done.8, f32[256,8,128]{0,2,1:T(8,128)S(1)} %get-tuple-element.33, bf16[256,1024]{0,1:T(8,128)(2,1)} %collective-permute-done.16, pred[]{:T(512)S(6)} %eq.29), kind=kLoop, calls=%fused_computation.55 | loop fusion | flops 1572864 | bytes 2621441 | tf_op jit(solution)/shard_map/convert_element_type | solution.py:195
  139.2 1.9 %fusion.33 = bf16[256,1024]{0,1:T(8,128)(2,1)S(1)} fusion(bf16[256,1024]{0,1:T(8,128)(2,1)S(1)} %copy-done.7, f32[904,1024]{0,1:T(8,128)} %copy-done, bf16[256,1024]{0,1:T(8,128)(2,1)} %collective-permute-done.17, pred[]{:T(512)S(6)} %eq.29), kind=kLoop, calls=%fused_computation.62 | loop fusion | flops 1572864 | bytes 2621441 | tf_op jit(solution)/shard_map/convert_element_type | solution.py:196
  (102 shorter events, 27.0 us)
Async XLA Ops:
  0.6 25.6 %copy-start.10 = (bf16[256,1024]{1,0:T(8,128)(2,1)S(1)}, bf16[256,1024]{1,0:T(8,128)(2,1)}, u32[]{:S(2)}) copy-start(bf16[256,1024]{1,0:T(8,128)(2,1)} %param.8) | copy-start | bytes 1572868
  1.9 17.7 %collective-permute-start = (bf16[256,1024]{0,1:T(8,128)(2,1)S(1)}, bf16[256,1024]{0,1:T(8,128)(2,1)S(1)}, u32[]{:S(2)}, u32[]{:S(2)}) collective-permute-start(bf16[256,1024]{0,1:T(8,128)(2,1)S(1)} %copy.59), channel_id=1, source_target_pairs={{0,4},{2,6},{4,8},{6,10},{8,12},{10,14},{12,16},{14,18},{16,20},{1... | collective-permute-start | bytes 1572872 | tf_op jit(solution)/shard_map/ppermute | solution.py:20
  6.4 28.0 %copy-start.1 = (bf16[256,1024]{0,1:T(8,128)(2,1)}, bf16[256,1024]{0,1:T(8,128)(2,1)S(1)}, u32[]{:S(2)}) copy-start(bf16[256,1024]{0,1:T(8,128)(2,1)S(1)} %copy.65) | copy-start | bytes 1572868
  6.4 24.5 %collective-permute-start.3 = (bf16[256,1024]{0,1:T(8,128)(2,1)S(1)}, bf16[256,1024]{0,1:T(8,128)(2,1)S(1)}, u32[]{:S(2)}, u32[]{:S(2)}) collective-permute-start(bf16[256,1024]{0,1:T(8,128)(2,1)S(1)} %copy.65), channel_id=1, source_target_pairs={{0,4},{2,6},{4,8},{6,10},{8,12},{10,14},{12,16},{14,18},{16,20},{1... | collective-permute-start | bytes 1572872 | tf_op jit(solution)/shard_map/ppermute | solution.py:20
  20.5 16.7 %collective-permute-start.2 = (bf16[256,1024]{0,1:T(8,128)(2,1)}, bf16[256,1024]{0,1:T(8,128)(2,1)}, u32[]{:S(2)}, u32[]{:S(2)}) collective-permute-start(bf16[256,1024]{0,1:T(8,128)(2,1)} %broadcast_select_fusion.1), channel_id=1, source_target_pairs={{0,2},{2,0},{4,6},{6,4},{8,10},{10,8},{12,14},{14,12},{16,18},{18,... | collective-permute-start | bytes 1572872 | tf_op jit(solution)/shard_map/ppermute | solution.py:25
  24.3 12.0 %collective-permute-start.1 = (bf16[136,1024]{0,1:T(8,128)(2,1)}, bf16[136,1024]{0,1:T(8,128)(2,1)S(1)}, u32[]{:S(2)}, u32[]{:S(2)}) collective-permute-start(bf16[136,1024]{0,1:T(8,128)(2,1)} %slice.123), channel_id=1, source_target_pairs={{0,2},{2,4},{4,6},{6,8},{8,10},{10,12},{12,14},{14,16},{16,18},{18... | collective-permute-start | bytes 835592 | tf_op jit(solution)/shard_map/ppermute | solution.py:20
  30.9 5.5 %copy-start.3 = (bf16[256,1024]{0,1:T(8,128)(2,1)}, bf16[256,1024]{0,1:T(8,128)(2,1)S(1)}, u32[]{:S(2)}) copy-start(bf16[256,1024]{0,1:T(8,128)(2,1)S(1)} %collective-permute-done.3) | copy-start | bytes 1572868
  31.8 18.1 %collective-permute-start.5 = (bf16[256,1024]{0,1:T(8,128)(2,1)}, bf16[256,1024]{0,1:T(8,128)(2,1)}, u32[]{:S(2)}, u32[]{:S(2)}) collective-permute-start(bf16[256,1024]{0,1:T(8,128)(2,1)} %broadcast_select_fusion), channel_id=1, source_target_pairs={{0,2},{2,0},{4,6},{6,4},{8,10},{10,8},{12,14},{14,12},{16,18},{18,... | collective-permute-start | bytes 1572872 | tf_op jit(solution)/shard_map/ppermute | solution.py:25
  34.4 15.4 %collective-permute-start.4 = (bf16[136,1024]{0,1:T(8,128)(2,1)}, bf16[136,1024]{0,1:T(8,128)(2,1)}, u32[]{:S(2)}, u32[]{:S(2)}) collective-permute-start(bf16[136,1024]{0,1:T(8,128)(2,1)} %slice.124), channel_id=1, source_target_pairs={{0,2},{2,4},{4,6},{6,8},{8,10},{10,12},{12,14},{14,16},{16,18},{18... | collective-permute-start | bytes 835592 | tf_op jit(solution)/shard_map/ppermute | solution.py:20
  46.1 3.8 %copy-start.2 = (bf16[256,1024]{0,1:T(8,128)(2,1)S(1)}, bf16[256,1024]{0,1:T(8,128)(2,1)}, u32[]{:S(2)}) copy-start(bf16[256,1024]{0,1:T(8,128)(2,1)} %copy-done.1) | copy-start | bytes 1572868
  46.1 3.8 %copy-start.4 = (bf16[256,1024]{0,1:T(8,128)(2,1)S(1)}, bf16[256,1024]{0,1:T(8,128)(2,1)}, u32[]{:S(2)}) copy-start(bf16[256,1024]{0,1:T(8,128)(2,1)} %copy-done.3) | copy-start | bytes 1572868
  52.2 3.4 %copy-start.11 = (f32[1024]{0:T(1024)S(1)}, f32[1024]{0:T(1024)}, u32[]{:S(2)}) copy-start(f32[1024]{0:T(1024)} %param.12) | copy-start | bytes 12292
  55.6 7.1 %slice-start = ((s8[7340032]{0:T(1024)(128)(4,1)}), s8[4194304]{0:T(1024)(128)(4,1)S(1)}, s32[]{:S(2)}) async-start(s8[7340032]{0:T(1024)(128)(4,1)} %bitcast.101), calls=%async_computation | async-start | bytes 8388608
  56.7 4.2 %collective-permute-start.6 = (f32[3,256]{1,0:T(4,128)S(1)}, f32[3,256]{1,0:T(4,128)S(1)}, u32[]{:S(2)}, u32[]{:S(2)}) collective-permute-start(f32[3,256]{1,0:T(4,128)S(1)} %pad_maximum_fusion.5), channel_id=1, source_target_pairs={{0,1},{1,0},{2,3},{3,2},{4,5},{5,4},{6,7},{7,6},{8,9},{9,8},{10,11... | collective-permute-start | bytes 9224 | tf_op jit(solution)/shard_map/ppermute | solution.py:40
  68.4 4.1 %collective-permute-start.8 = (f32[4,1024]{1,0:T(4,128)S(1)}, f32[4,1024]{1,0:T(4,128)S(1)}, u32[]{:S(2)}, u32[]{:S(2)}) collective-permute-start(f32[4,1024]{1,0:T(4,128)S(1)} %pad_maximum_fusion.4), channel_id=1, source_target_pairs={{0,2},{2,0},{4,6},{6,4},{8,10},{10,8},{12,14},{14,12},{16,18},{18,... | collective-permute-start | bytes 49160 | tf_op jit(solution)/shard_map/ppermute | solution.py:32
  72.5 8.0 %copy-start.5 = (bf16[256,1024]{0,1:T(8,128)(2,1)S(1)}, bf16[256,1024]{0,1:T(8,128)(2,1)}, u32[]{:S(2)}) copy-start(bf16[256,1024]{0,1:T(8,128)(2,1)} %copy.88) | copy-start | bytes 1572868
  72.5 5.7 %collective-permute-start.9 = (f32[4,1024]{1,0:T(4,128)S(1)}, f32[4,1024]{1,0:T(4,128)S(1)}, u32[]{:S(2)}, u32[]{:S(2)}) collective-permute-start(f32[4,1024]{1,0:T(4,128)S(1)} %fusion.50), channel_id=1, source_target_pairs={{0,4},{2,6},{4,0},{6,2},{8,12},{10,14},{12,8},{14,10},{16,20},{18,... | collective-permute-start | bytes 49160 | tf_op jit(solution)/shard_map/ppermute | solution.py:32
  77.8 15.4 %copy-start = (f32[904,1024]{0,1:T(8,128)}, f32[904,1024]{0,1:T(8,128)S(1)}, u32[]{:S(2)}) copy-start(f32[904,1024]{0,1:T(8,128)S(1)} %get-tuple-element.29) | copy-start | bytes 11108356
  78.0 15.2 %collective-permute-start.14 = (bf16[256,1024]{0,1:T(8,128)(2,1)S(1)}, bf16[256,1024]{0,1:T(8,128)(2,1)S(1)}, u32[]{:S(2)}, u32[]{:S(2)}) collective-permute-start(bf16[256,1024]{0,1:T(8,128)(2,1)S(1)} %slice.139), channel_id=1, source_target_pairs={{0,2},{2,0},{4,6},{6,4},{8,10},{10,8},{12,14},{14,12},{16,18},{18,... | collective-permute-start | bytes 1572872 | tf_op jit(solution)/shard_map/ppermute | solution.py:25
  78.2 6.4 %collective-permute-start.10 = (f32[4,1024]{1,0:T(4,128)S(1)}, f32[4,1024]{1,0:T(4,128)S(1)}, u32[]{:S(2)}, u32[]{:S(2)}) collective-permute-start(f32[4,1024]{1,0:T(4,128)S(1)} %fusion.74), channel_id=1, source_target_pairs={{0,8},{2,10},{4,12},{6,14},{8,0},{10,2},{12,4},{14,6},{16,24},{18,... | collective-permute-start | bytes 49160 | tf_op jit(solution)/shard_map/ppermute | solution.py:32
  81.8 17.0 %collective-permute-start.7 = (bf16[256,1024]{0,1:T(8,128)(2,1)S(1)}, bf16[256,1024]{0,1:T(8,128)(2,1)S(1)}, u32[]{:S(2)}, u32[]{:S(2)}) collective-permute-start(bf16[256,1024]{0,1:T(8,128)(2,1)S(1)} %bitcast.112), channel_id=1, source_target_pairs={{0,2},{2,0},{4,6},{6,4},{8,10},{10,8},{12,14},{14,12},{16,18},{18,... | collective-permute-start | bytes 1572872 | tf_op jit(solution)/shard_map/ppermute | solution.py:25
  82.4 10.8 %collective-permute-start.13 = (bf16[136,1024]{0,1:T(8,128)(2,1)S(1)}, bf16[136,1024]{0,1:T(8,128)(2,1)S(1)}, u32[]{:S(2)}, u32[]{:S(2)}) collective-permute-start(bf16[136,1024]{0,1:T(8,128)(2,1)S(1)} %slice.138), channel_id=1, source_target_pairs={{2,0},{4,2},{6,4},{8,6},{10,8},{12,10},{14,12},{16,14},{18,16},{20... | collective-permute-start | bytes 835592 | tf_op jit(solution)/shard_map/ppermute | solution.py:20
  84.6 5.9 %collective-permute-start.11 = (f32[4,1024]{1,0:T(4,128)S(1)}, f32[4,1024]{1,0:T(4,128)S(1)}, u32[]{:S(2)}, u32[]{:S(2)}) collective-permute-start(f32[4,1024]{1,0:T(4,128)S(1)} %add.154), channel_id=1, source_target_pairs={{0,16},{2,18},{4,20},{6,22},{8,24},{10,26},{12,28},{14,30},{16,0},... | collective-permute-start | bytes 49160 | tf_op jit(solution)/shard_map/ppermute | solution.py:32
  86.8 12.0 %collective-permute-start.15 = (bf16[136,1024]{0,1:T(8,128)(2,1)S(1)}, bf16[136,1024]{0,1:T(8,128)(2,1)S(1)}, u32[]{:S(2)}, u32[]{:S(2)}) collective-permute-start(bf16[136,1024]{0,1:T(8,128)(2,1)S(1)} %pad_slice_fusion), channel_id=1, source_target_pairs={{2,0},{4,2},{6,4},{8,6},{10,8},{12,10},{14,12},{16,14},{18,16},{20... | collective-permute-start | bytes 835592 | tf_op jit(solution)/shard_map/ppermute | solution.py:20
  90.5 2.7 %collective-permute-start.12 = (f32[4,1024]{1,0:T(4,128)S(1)}, f32[4,1024]{1,0:T(4,128)S(1)}, u32[]{:S(2)}, u32[]{:S(2)}) collective-permute-start(f32[4,1024]{1,0:T(4,128)S(1)} %add.155), channel_id=1, source_target_pairs={{0,32},{2,34},{4,36},{6,38},{8,40},{10,42},{12,44},{14,46},{16,48}... | collective-permute-start | bytes 49160 | tf_op jit(solution)/shard_map/ppermute | solution.py:32
  93.2 34.6 %copy-start.6 = (bf16[256,1024]{0,1:T(8,128)(2,1)}, bf16[256,1024]{0,1:T(8,128)(2,1)S(1)}, u32[]{:S(2)}) copy-start(bf16[256,1024]{0,1:T(8,128)(2,1)S(1)} %collective-permute-done.14) | copy-start | bytes 1572868
  98.8 29.0 %copy-start.8 = (bf16[256,1024]{0,1:T(8,128)(2,1)}, bf16[256,1024]{0,1:T(8,128)(2,1)S(1)}, u32[]{:S(2)}) copy-start(bf16[256,1024]{0,1:T(8,128)(2,1)S(1)} %collective-permute-done.7) | copy-start | bytes 1572868
  100.0 36.7 %collective-permute-start.16 = (bf16[256,1024]{0,1:T(8,128)(2,1)}, bf16[256,1024]{0,1:T(8,128)(2,1)}, u32[]{:S(2)}, u32[]{:S(2)}) collective-permute-start(bf16[256,1024]{0,1:T(8,128)(2,1)} %fusion.28), channel_id=1, source_target_pairs={{4,0},{6,2},{8,4},{10,6},{12,8},{14,10},{16,12},{18,14},{20,16},{2... | collective-permute-start | bytes 1572872 | tf_op jit(solution)/shard_map/ppermute | solution.py:20
  106.1 15.8 %collective-permute-start.18 = (f32[4,1024]{1,0:T(4,128)S(1)}, f32[4,1024]{1,0:T(4,128)S(1)}, u32[]{:S(2)}, u32[]{:S(2)}) collective-permute-start(f32[4,1024]{1,0:T(4,128)S(1)} %add.156), channel_id=1, source_target_pairs={{0,64},{2,66},{4,68},{6,70},{8,72},{10,74},{12,76},{14,78},{16,80}... | collective-permute-start | bytes 49160 | tf_op jit(solution)/shard_map/ppermute | solution.py:32
  109.2 29.9 %collective-permute-start.17 = (bf16[256,1024]{0,1:T(8,128)(2,1)}, bf16[256,1024]{0,1:T(8,128)(2,1)}, u32[]{:S(2)}, u32[]{:S(2)}) collective-permute-start(bf16[256,1024]{0,1:T(8,128)(2,1)} %fusion.30), channel_id=1, source_target_pairs={{4,0},{6,2},{8,4},{10,6},{12,8},{14,10},{16,12},{18,14},{20,16},{2... | collective-permute-start | bytes 1572872 | tf_op jit(solution)/shard_map/ppermute | solution.py:20
  121.9 14.2 %collective-permute-start.19 = (f32[4,1024]{1,0:T(4,128)S(1)}, f32[4,1024]{1,0:T(4,128)S(1)}, u32[]{:S(2)}, u32[]{:S(2)}) collective-permute-start(f32[4,1024]{1,0:T(4,128)S(1)} %add.167), channel_id=1, source_target_pairs={{0,128},{2,130},{4,132},{6,134},{8,136},{10,138},{12,140},{14,142}... | collective-permute-start | bytes 49160 | tf_op jit(solution)/shard_map/ppermute | solution.py:32
  127.8 11.3 %copy-start.7 = (bf16[256,1024]{0,1:T(8,128)(2,1)S(1)}, bf16[256,1024]{0,1:T(8,128)(2,1)}, u32[]{:S(2)}) copy-start(bf16[256,1024]{0,1:T(8,128)(2,1)} %copy-done.6) | copy-start | bytes 1572868
  (3 other events, 4.3 us)

commit v9 on v5

--- a/solution.py
+++ b/solution.py
@@ -29,10 +29,10 @@
     size = lax.axis_size(axis)
     if size & (size - 1):
         return lax.psum(block, axis)
-    stride = size // 2
-    while stride >= 1:
+    stride = 1
+    while stride < size:
         block = block + lax.ppermute(block, axis, [(i, i ^ stride) for i in range(size)])
-        stride //= 2
+        stride *= 2
     return block
 
 
@@ -160,12 +160,8 @@
     conv_grad = all_sum(local_taps, "tm")
 
     lead = jnp.zeros((far_lead, channels), jnp.float32)
-    padded_value = jnp.concatenate([lead, value_part, jnp.zeros((rim_rows, channels), jnp.float32)], 0)
-    value_sum = jnp.zeros((key_count + far_lead, channels), jnp.float32)
-    for tap_index in range(tap_count):
-        value_sum = value_sum + conv_weight[tap_index] * padded_value[tap_index : tap_index + key_count + far_lead]
-
-    def relay_back(grads):
+
+    def relay_back_first(grads):
         cut_third = row_count - far_rows + far_lead
         grad_third = grads[:cut_third]
         grad_second = grads[cut_third : cut_third + row_count]
@@ -177,11 +173,21 @@
             [jnp.zeros((far_rows - far_lead, grads.shape[1]), jnp.float32), back_third], 0
         )
         grad_second = grad_second + jnp.where(even, 0.0, back_first)
-        back_second = from_behind(grad_second.astype(jnp.bfloat16), "tm", -2).astype(jnp.float32)
-        return grad_own + jnp.where(even, back_first, 0.0) + back_second
-
+        return grad_own + jnp.where(even, back_first, 0.0), grad_second.astype(jnp.bfloat16)
+
+    def relay_back(grads):
+        near, second = relay_back_first(grads)
+        return near + from_behind(second, "tm", -2).astype(jnp.float32)
+
+    key_near, key_second = relay_back_first(jnp.concatenate([lead, key_part], 0))
+    key_near, key_second, value_part = lax.optimization_barrier((key_near, key_second, value_part))
+    key_total = key_near + from_behind(key_second, "tm", -2).astype(jnp.float32)
+
+    padded_value = jnp.concatenate([lead, value_part, jnp.zeros((rim_rows, channels), jnp.float32)], 0)
+    value_sum = jnp.zeros((key_count + far_lead, channels), jnp.float32)
+    for tap_index in range(tap_count):
+        value_sum = value_sum + conv_weight[tap_index] * padded_value[tap_index : tap_index + key_count + far_lead]
     value_total = relay_back(value_sum)
-    key_total = relay_back(jnp.concatenate([lead, key_part], 0))
 
     return (
         query_grad.reshape(row_count, channels).astype(jnp.bfloat16),

time: 144 us -> 146 us (1.014)
  the two profiles are of different devices: /device:TPU:4 before, /device:TPU:230 now
where the time goes in v9:
time: 146 us
  starting transfers between devices  44 us (30%)
  waiting for transfers between devices  42.9 us (29%)
  other arithmetic  31.5 us (22%)
  local copies, waits for them, and re-layouts  13.4 us (9%)
  matrix products  12.7 us (9%)
    ppermute x8, waiting for transfers between devices, from_behind(): return lax.ppermute(block, axis, route)  28.8 us
    ppermute x8, starting transfers between devices, from_behind(): return lax.ppermute(block, axis, route)  25.7 us
    ppermute x7, starting transfers between devices, all_sum(): lax.ppermute(block, axis, [(i, i ^ stride) for i in range(size)])  16 us
    ppermute x7, waiting for transfers between devices, all_sum(): lax.ppermute(block, axis, [(i, i ^ stride) for i in range(size)])  10.6 us
    unnamed x35, local copies, waits for them, and re-layouts  8.6 us
    sub x1, matrix products, body(): expo = jnp.where(mask[None], jnp.exp(scores - row_peak[..., None]), 0.0)  7.3 us
    another operation x1, other arithmetic  5.2 us
    reduce_sum x1, other arithmetic, body(): jnp.sum(value_part * vin_win[far_lead - tap_index:far_lead - tap_index +...  4 us
  transfers between devices with their start and end apart: 20, of which 11 were waited for; matrix products, arithmetic and copies ran while one was open for 28% of the time, Pallas kernels for 0%

profile of v9, /device:TPU:230, one launch (start us, length us, event | category | flops | bytes accessed | tf_op | source)
XLA Modules:
  0.0 145.7 jit_solution(11054250409511282464)
XLA Ops:
  1.9 3.5 %collective-permute-start = (bf16[256,1024]{0,1:T(8,128)(2,1)S(1)}, bf16[256,1024]{0,1:T(8,128)(2,1)S(1)}, u32[]{:S(2)}, u32[]{:S(2)}) collective-permute-start(bf16[256,1024]{0,1:T(8,128)(2,1)S(1)} %copy.59), channel_id=1, source_target_pairs={{0,4},{2,6},{4,8},{6,10},{8,12},{10,14},{12,16},{14,18},{16,20},{1... | collective-permute-start | bytes 1572872 | tf_op jit(solution)/shard_map/ppermute | solution.py:20
  6.7 3.5 %collective-permute-start.3 = (bf16[256,1024]{0,1:T(8,128)(2,1)S(1)}, bf16[256,1024]{0,1:T(8,128)(2,1)S(1)}, u32[]{:S(2)}, u32[]{:S(2)}) collective-permute-start(bf16[256,1024]{0,1:T(8,128)(2,1)S(1)} %copy.65), channel_id=1, source_target_pairs={{0,4},{2,6},{4,8},{6,10},{8,12},{10,14},{12,16},{14,18},{16,20},{1... | collective-permute-start | bytes 1572872 | tf_op jit(solution)/shard_map/ppermute | solution.py:20
  12.1 8.6 %collective-permute-done = bf16[256,1024]{0,1:T(8,128)(2,1)S(1)} collective-permute-done((bf16[256,1024]{0,1:T(8,128)(2,1)S(1)}, bf16[256,1024]{0,1:T(8,128)(2,1)S(1)}, u32[]{:S(2)}, u32[]{:S(2)}) %collective-permute-start) | collective-permute-done | bytes 524320 | tf_op jit(solution)/shard_map/ppermute | solution.py:20
  22.7 2.4 %collective-permute-start.1 = (bf16[136,1024]{0,1:T(8,128)(2,1)}, bf16[136,1024]{0,1:T(8,128)(2,1)S(1)}, u32[]{:S(2)}, u32[]{:S(2)}) collective-permute-start(bf16[136,1024]{0,1:T(8,128)(2,1)} %slice.123), channel_id=1, source_target_pairs={{0,2},{2,4},{4,6},{6,8},{8,10},{10,12},{12,14},{14,16},{16,18},{18... | collective-permute-start | bytes 835592 | tf_op jit(solution)/shard_map/ppermute | solution.py:20
  28.3 3.4 %collective-permute-done.3 = bf16[256,1024]{0,1:T(8,128)(2,1)S(1)} collective-permute-done((bf16[256,1024]{0,1:T(8,128)(2,1)S(1)}, bf16[256,1024]{0,1:T(8,128)(2,1)S(1)}, u32[]{:S(2)}, u32[]{:S(2)}) %collective-permute-start.3) | collective-permute-done | bytes 524320 | tf_op jit(solution)/shard_map/ppermute | solution.py:20
  33.7 2.4 %collective-permute-start.4 = (bf16[136,1024]{0,1:T(8,128)(2,1)}, bf16[136,1024]{0,1:T(8,128)(2,1)}, u32[]{:S(2)}, u32[]{:S(2)}) collective-permute-start(bf16[136,1024]{0,1:T(8,128)(2,1)} %slice.124), channel_id=1, source_target_pairs={{0,2},{2,4},{4,6},{6,8},{8,10},{10,12},{12,14},{14,16},{16,18},{18... | collective-permute-start | bytes 835592 | tf_op jit(solution)/shard_map/ppermute | solution.py:20
  37.3 1.6 %pad_maximum_fusion.1 = bf16[896,1024]{0,1:T(8,128)(2,1)S(1)} fusion(bf16[256,1024]{0,1:T(8,128)(2,1)S(1)} %copy.59, bf16[256,1024]{0,1:T(8,128)(2,1)} %collective-permute-done.2, bf16[256,1024]{0,1:T(8,128)(2,1)S(1)} %collective-permute-done, bf16[136,1024]{0,1:T(8,128)(2,1)} %copy-done.8), kind=kLoop, calls=%fused_computation.36 | loop fusion | flops 7340032 | bytes 3686400 | tf_op jit(solution)/shard_map/concatenate | solution.py:81
  38.9 7.3 %fusion.55 = (f32[8,256]{1,0:T(8,128)S(1)}, f32[8,256,896]{1,2,0:T(8,128)}) fusion(pred[256,896]{0,1:T(8,128)(4,1)} %fusion.37, bf16[896,8,128]{0,2,1:T(8,128)(2,1)S(1)} %bitcast.103, bf16[256,8,128]{0,2,1:T(8,128)(2,1)} %bitcast.107), kind=kOutput, calls=%fused_computation.106 | convolution fusion | flops 478937984 | bytes 9936896 | tf_op jit(solution)/shard_map/sub | solution.py:104
  46.2 3.8 %fusion.16 = bf16[8,256,896]{1,2,0:T(8,128)(2,1)S(1)} fusion(f32[8,256,896]{1,2,0:T(8,128)} %get-tuple-element.44, f32[8,256]{1,0:T(8,128)S(1)} %get-tuple-element.43), kind=kLoop, calls=%fused_computation.33 | loop fusion | flops 3670016 | bytes 11018240 | tf_op jit(solution)/shard_map/convert_element_type | solution.py:107
  50.0 2.2 %pad_maximum_fusion = bf16[904,1024]{0,1:T(8,128)(2,1)S(1)} fusion(bf16[256,1024]{0,1:T(8,128)(2,1)S(1)} %copy-done.2, bf16[256,1024]{0,1:T(8,128)(2,1)} %collective-permute-done.5, bf16[256,1024]{0,1:T(8,128)(2,1)S(1)} %copy-done.4, bf16[136,1024]{0,1:T(8,128)(2,1)} %collective-permute-done.4), kind=kLoop, calls=%fused_computation.34 | loop fusion | flops 7405568 | bytes 3702784 | tf_op jit(solution)/shard_map/concatenate | solution.py:81
  52.3 3.4 %fusion.8 = bf16[896,1024]{0,1:T(8,128)(2,1)S(1)} fusion(f32[1024]{0:T(1024)S(1)} %bitcast.129, f32[1024]{0:T(1024)S(1)} %bitcast.131, f32[1024]{0:T(1024)S(1)} %bitcast.127, f32[1024]{0:T(1024)S(1)} %bitcast.125, bf16[904,1024]{0,1:T(8,128)(2,1)S(1)} %pad_maximum_fusion), kind=kLoop, calls=%fused_computation.23 | loop fusion | flops 11010048 | bytes 9191424 | tf_op jit(solution)/shard_map/convert_element_type | solution.py:91
  56.8 1.7 %collective-permute-start.6 = (f32[3,256]{1,0:T(4,128)S(1)}, f32[3,256]{1,0:T(4,128)S(1)}, u32[]{:S(2)}, u32[]{:S(2)}) collective-permute-start(f32[3,256]{1,0:T(4,128)S(1)} %pad_maximum_fusion.5), channel_id=1, source_target_pairs={{0,1},{1,0},{2,3},{3,2},{4,5},{5,4},{6,7},{7,6},{8,9},{9,8},{10,11... | collective-permute-start | bytes 9224 | tf_op jit(solution)/shard_map/ppermute | solution.py:42
  58.7 3.5 %collective-permute-done.6 = f32[3,256]{1,0:T(4,128)S(1)} collective-permute-done((f32[3,256]{1,0:T(4,128)S(1)}, f32[3,256]{1,0:T(4,128)S(1)}, u32[]{:S(2)}, u32[]{:S(2)}) %collective-permute-start.6) | collective-permute-done | bytes 3104 | tf_op jit(solution)/shard_map/ppermute | solution.py:42
  64.1 1.5 multiply_convert_fusion
  67.1 3.8 %collective-permute-start.8 = (bf16[136,1024]{0,1:T(8,128)(2,1)S(1)}, bf16[136,1024]{0,1:T(8,128)(2,1)S(1)}, u32[]{:S(2)}, u32[]{:S(2)}) collective-permute-start(bf16[136,1024]{0,1:T(8,128)(2,1)S(1)} %pad_slice_fusion), channel_id=1, source_target_pairs={{2,0},{4,2},{6,4},{8,6},{10,8},{12,10},{14,12},{16,14},{18,16},{20... | collective-permute-start | bytes 835592 | tf_op jit(solution)/shard_map/ppermute | solution.py:20
  70.9 4.0 %fusion.9 = (f32[1024]{0:T(1024)S(1)}, f32[1024]{0:T(1024)S(1)}, f32[1024]{0:T(1024)S(1)}, f32[1024]{0:T(1024)S(1)}) fusion(bf16[904,1024]{0,1:T(8,128)(2,1)S(1)} %pad_maximum_fusion, f32[8,128,896]{2,1,0:T(8,128)S(1)} %fusion.57), kind=kLoop, calls=%fused_computation.24 | loop fusion | flops 11005952 | bytes 11026432 | tf_op jit(solution)/shard_map/reduce_sum | solution.py:152
  75.3 2.4 %collective-permute-done.8 = bf16[136,1024]{0,1:T(8,128)(2,1)S(1)} collective-permute-done((bf16[136,1024]{0,1:T(8,128)(2,1)S(1)}, bf16[136,1024]{0,1:T(8,128)(2,1)S(1)}, u32[]{:S(2)}, u32[]{:S(2)}) %collective-permute-start.8) | collective-permute-done | bytes 278560 | tf_op jit(solution)/shard_map/ppermute | solution.py:20
  80.0 5.2 %fusion.49 = (bf16[904,1024]{0,1:T(8,128)(2,1)S(1)}, f32[904,1024]{0,1:T(8,128)S(1)}) fusion(f32[907,1024]{0,1:T(8,128)S(1)} %maximum_maximum_fusion, f32[1024]{0:T(1024)S(1)} %bitcast.130, f32[1024]{0:T(1024)S(1)} %bitcast.132, f32[1024]{0:T(1024)S(1)} %bitcast.128, f32[896,1024]{0,1:T(8,128)S(1)} %bitcast.99, f32[1024]{0:T(1024)S(1)} %bitcast.126), kind=kLoop, calls=%fused_computation.102 | loop fusion | flops 7405568 | bytes 20348928 | tf_op jit(solution)/shard_map/convert.5
  86.5 5.4 %collective-permute-start.11 = (bf16[136,1024]{0,1:T(8,128)(2,1)S(1)}, bf16[136,1024]{0,1:T(8,128)(2,1)S(1)}, u32[]{:S(2)}, u32[]{:S(2)}) collective-permute-start(bf16[136,1024]{0,1:T(8,128)(2,1)S(1)} %slice.141), channel_id=1, source_target_pairs={{2,0},{4,2},{6,4},{8,6},{10,8},{12,10},{14,12},{16,14},{18,16},{20... | collective-permute-start | bytes 835592 | tf_op jit(solution)/shard_map/ppermute | solution.py:20
  92.1 5.2 %collective-permute-done.15 = f32[4,1024]{1,0:T(4,128)S(1)} collective-permute-done((f32[4,1024]{1,0:T(4,128)S(1)}, f32[4,1024]{1,0:T(4,128)S(1)}, u32[]{:S(2)}, u32[]{:S(2)}) %collective-permute-start.15) | collective-permute-done | bytes 16416 | tf_op jit(solution)/shard_map/ppermute | solution.py:34
  97.3 2.7 %collective-permute-start.16 = (f32[4,1024]{1,0:T(4,128)S(1)}, f32[4,1024]{1,0:T(4,128)S(1)}, u32[]{:S(2)}, u32[]{:S(2)}) collective-permute-start(f32[4,1024]{1,0:T(4,128)S(1)} %add.164), channel_id=1, source_target_pairs={{0,16},{2,18},{4,20},{6,22},{8,24},{10,26},{12,28},{14,30},{16,0},... | collective-permute-start | bytes 49160 | tf_op jit(solution)/shard_map/ppermute | solution.py:34
  100.0 1.7 %collective-permute-done.16 = f32[4,1024]{1,0:T(4,128)S(1)} collective-permute-done((f32[4,1024]{1,0:T(4,128)S(1)}, f32[4,1024]{1,0:T(4,128)S(1)}, u32[]{:S(2)}, u32[]{:S(2)}) %collective-permute-start.16) | collective-permute-done | bytes 16416 | tf_op jit(solution)/shard_map/ppermute | solution.py:34
  101.7 1.8 %collective-permute-start.17 = (f32[4,1024]{1,0:T(4,128)S(1)}, f32[4,1024]{1,0:T(4,128)S(1)}, u32[]{:S(2)}, u32[]{:S(2)}) collective-permute-start(f32[4,1024]{1,0:T(4,128)S(1)} %add.165), channel_id=1, source_target_pairs={{0,32},{2,34},{4,36},{6,38},{8,40},{10,42},{12,44},{14,46},{16,48}... | collective-permute-start | bytes 49160 | tf_op jit(solution)/shard_map/ppermute | solution.py:34
  103.6 1.9 %collective-permute-done.17 = f32[4,1024]{1,0:T(4,128)S(1)} collective-permute-done((f32[4,1024]{1,0:T(4,128)S(1)}, f32[4,1024]{1,0:T(4,128)S(1)}, u32[]{:S(2)}, u32[]{:S(2)}) %collective-permute-start.17) | collective-permute-done | bytes 16416 | tf_op jit(solution)/shard_map/ppermute | solution.py:34
  105.5 4.1 %collective-permute-start.18 = (f32[4,1024]{1,0:T(4,128)S(1)}, f32[4,1024]{1,0:T(4,128)S(1)}, u32[]{:S(2)}, u32[]{:S(2)}) collective-permute-start(f32[4,1024]{1,0:T(4,128)S(1)} %add.166), channel_id=1, source_target_pairs={{0,64},{2,66},{4,68},{6,70},{8,72},{10,74},{12,76},{14,78},{16,80}... | collective-permute-start | bytes 49160 | tf_op jit(solution)/shard_map/ppermute | solution.py:34
  109.5 1.7 %collective-permute-done.18 = f32[4,1024]{1,0:T(4,128)S(1)} collective-permute-done((f32[4,1024]{1,0:T(4,128)S(1)}, f32[4,1024]{1,0:T(4,128)S(1)}, u32[]{:S(2)}, u32[]{:S(2)}) %collective-permute-start.18) | collective-permute-done | bytes 16416 | tf_op jit(solution)/shard_map/ppermute | solution.py:34
  111.3 6.9 %collective-permute-start.19 = (f32[4,1024]{1,0:T(4,128)S(1)}, f32[4,1024]{1,0:T(4,128)S(1)}, u32[]{:S(2)}, u32[]{:S(2)}) collective-permute-start(f32[4,1024]{1,0:T(4,128)S(1)} %add.167), channel_id=1, source_target_pairs={{0,128},{2,130},{4,132},{6,134},{8,136},{10,138},{12,140},{14,142}... | collective-permute-start | bytes 49160 | tf_op jit(solution)/shard_map/ppermute | solution.py:34
  118.1 2.7 %collective-permute-start.9 = (bf16[256,1024]{0,1:T(8,128)(2,1)}, bf16[256,1024]{0,1:T(8,128)(2,1)}, u32[]{:S(2)}, u32[]{:S(2)}) collective-permute-start(bf16[256,1024]{0,1:T(8,128)(2,1)} %get-tuple-element.8), channel_id=1, source_target_pairs={{4,0},{6,2},{8,4},{10,6},{12,8},{14,10},{16,12},{18,14},{20,16},{2... | collective-permute-start | bytes 1572872 | tf_op jit(solution)/shard_map/ppermute | solution.py:20
  122.3 1.9 %collective-permute-start.12 = (bf16[256,1024]{0,1:T(8,128)(2,1)}, bf16[256,1024]{0,1:T(8,128)(2,1)}, u32[]{:S(2)}, u32[]{:S(2)}) collective-permute-start(bf16[256,1024]{0,1:T(8,128)(2,1)} %fusion.31), channel_id=1, source_target_pairs={{4,0},{6,2},{8,4},{10,6},{12,8},{14,10},{16,12},{18,14},{20,16},{2... | collective-permute-start | bytes 1572872 | tf_op jit(solution)/shard_map/ppermute | solution.py:20
  126.6 9.2 %collective-permute-done.9 = bf16[256,1024]{0,1:T(8,128)(2,1)} collective-permute-done((bf16[256,1024]{0,1:T(8,128)(2,1)}, bf16[256,1024]{0,1:T(8,128)(2,1)}, u32[]{:S(2)}, u32[]{:S(2)}) %collective-permute-start.9) | collective-permute-done | bytes 524320 | tf_op jit(solution)/shard_map/ppermute | solution.py:20
  137.9 4.9 %collective-permute-done.12 = bf16[256,1024]{0,1:T(8,128)(2,1)} collective-permute-done((bf16[256,1024]{0,1:T(8,128)(2,1)}, bf16[256,1024]{0,1:T(8,128)(2,1)}, u32[]{:S(2)}, u32[]{:S(2)}) %collective-permute-start.12) | collective-permute-done | bytes 524320 | tf_op jit(solution)/shard_map/ppermute | solution.py:20
  142.8 1.9 %fusion.29 = bf16[256,1024]{0,1:T(8,128)(2,1)S(1)} fusion(bf16[256,1024]{0,1:T(8,128)(2,1)S(1)} %copy-done.7, f32[904,1024]{0,1:T(8,128)} %copy-done, bf16[256,1024]{0,1:T(8,128)(2,1)} %collective-permute-done.12, pred[]{:T(512)S(6)} %eq.29), kind=kLoop, calls=%fused_computation.58 | loop fusion | flops 1572864 | bytes 2621441 | tf_op jit(solution)/shard_map/convert_element_type | solution.py:195
  (100 shorter events, 28.4 us)
Async XLA Ops:
  0.6 24.5 %copy-start.9 = (bf16[256,1024]{1,0:T(8,128)(2,1)S(1)}, bf16[256,1024]{1,0:T(8,128)(2,1)}, u32[]{:S(2)}) copy-start(bf16[256,1024]{1,0:T(8,128)(2,1)} %param.8) | copy-start | bytes 1572868
  1.9 18.8 %collective-permute-start = (bf16[256,1024]{0,1:T(8,128)(2,1)S(1)}, bf16[256,1024]{0,1:T(8,128)(2,1)S(1)}, u32[]{:S(2)}, u32[]{:S(2)}) collective-permute-start(bf16[256,1024]{0,1:T(8,128)(2,1)S(1)} %copy.59), channel_id=1, source_target_pairs={{0,4},{2,6},{4,8},{6,10},{8,12},{10,14},{12,16},{14,18},{16,20},{1... | collective-permute-start | bytes 1572872 | tf_op jit(solution)/shard_map/ppermute | solution.py:20
  6.7 27.0 %copy-start.1 = (bf16[256,1024]{0,1:T(8,128)(2,1)}, bf16[256,1024]{0,1:T(8,128)(2,1)S(1)}, u32[]{:S(2)}) copy-start(bf16[256,1024]{0,1:T(8,128)(2,1)S(1)} %copy.65) | copy-start | bytes 1572868
  6.7 25.0 %collective-permute-start.3 = (bf16[256,1024]{0,1:T(8,128)(2,1)S(1)}, bf16[256,1024]{0,1:T(8,128)(2,1)S(1)}, u32[]{:S(2)}, u32[]{:S(2)}) collective-permute-start(bf16[256,1024]{0,1:T(8,128)(2,1)S(1)} %copy.65), channel_id=1, source_target_pairs={{0,4},{2,6},{4,8},{6,10},{8,12},{10,14},{12,16},{14,18},{16,20},{1... | collective-permute-start | bytes 1572872 | tf_op jit(solution)/shard_map/ppermute | solution.py:20
  21.6 15.7 %collective-permute-start.2 = (bf16[256,1024]{0,1:T(8,128)(2,1)}, bf16[256,1024]{0,1:T(8,128)(2,1)}, u32[]{:S(2)}, u32[]{:S(2)}) collective-permute-start(bf16[256,1024]{0,1:T(8,128)(2,1)} %broadcast_select_fusion.1), channel_id=1, source_target_pairs={{0,2},{2,0},{4,6},{6,4},{8,10},{10,8},{12,14},{14,12},{16,18},{18,... | collective-permute-start | bytes 1572872 | tf_op jit(solution)/shard_map/ppermute | solution.py:25
  22.7 13.7 %collective-permute-start.1 = (bf16[136,1024]{0,1:T(8,128)(2,1)}, bf16[136,1024]{0,1:T(8,128)(2,1)S(1)}, u32[]{:S(2)}, u32[]{:S(2)}) collective-permute-start(bf16[136,1024]{0,1:T(8,128)(2,1)} %slice.123), channel_id=1, source_target_pairs={{0,2},{2,4},{4,6},{6,8},{8,10},{10,12},{12,14},{14,16},{16,18},{18... | collective-permute-start | bytes 835592 | tf_op jit(solution)/shard_map/ppermute | solution.py:20
  31.7 4.8 %copy-start.3 = (bf16[256,1024]{0,1:T(8,128)(2,1)}, bf16[256,1024]{0,1:T(8,128)(2,1)S(1)}, u32[]{:S(2)}) copy-start(bf16[256,1024]{0,1:T(8,128)(2,1)S(1)} %collective-permute-done.3) | copy-start | bytes 1572868
  32.7 17.3 %collective-permute-start.5 = (bf16[256,1024]{0,1:T(8,128)(2,1)}, bf16[256,1024]{0,1:T(8,128)(2,1)}, u32[]{:S(2)}, u32[]{:S(2)}) collective-permute-start(bf16[256,1024]{0,1:T(8,128)(2,1)} %broadcast_select_fusion), channel_id=1, source_target_pairs={{0,2},{2,0},{4,6},{6,4},{8,10},{10,8},{12,14},{14,12},{16,18},{18,... | collective-permute-start | bytes 1572872 | tf_op jit(solution)/shard_map/ppermute | solution.py:25
  33.7 16.3 %collective-permute-start.4 = (bf16[136,1024]{0,1:T(8,128)(2,1)}, bf16[136,1024]{0,1:T(8,128)(2,1)}, u32[]{:S(2)}, u32[]{:S(2)}) collective-permute-start(bf16[136,1024]{0,1:T(8,128)(2,1)} %slice.124), channel_id=1, source_target_pairs={{0,2},{2,4},{4,6},{6,8},{8,10},{10,12},{12,14},{14,16},{16,18},{18... | collective-permute-start | bytes 835592 | tf_op jit(solution)/shard_map/ppermute | solution.py:20
  46.2 3.8 %copy-start.2 = (bf16[256,1024]{0,1:T(8,128)(2,1)S(1)}, bf16[256,1024]{0,1:T(8,128)(2,1)}, u32[]{:S(2)}) copy-start(bf16[256,1024]{0,1:T(8,128)(2,1)} %copy-done.1) | copy-start | bytes 1572868
  46.2 3.8 %copy-start.4 = (bf16[256,1024]{0,1:T(8,128)(2,1)S(1)}, bf16[256,1024]{0,1:T(8,128)(2,1)}, u32[]{:S(2)}) copy-start(bf16[256,1024]{0,1:T(8,128)(2,1)} %copy-done.3) | copy-start | bytes 1572868
  52.3 3.4 %copy-start.10 = (f32[1024]{0:T(1024)S(1)}, f32[1024]{0:T(1024)}, u32[]{:S(2)}) copy-start(f32[1024]{0:T(1024)} %param.12) | copy-start | bytes 12292
  55.7 2.8 %copy-start.11 = (s32[2,64]{1,0:T(2,128)S(1)}, s32[2,64]{1,0:T(2,128)}, u32[]{:S(2)}) copy-start(s32[2,64]{1,0:T(2,128)} %param.15) | copy-start | bytes 1540
  55.7 8.2 %slice-start = ((s8[7340032]{0:T(1024)(128)(4,1)}), s8[4194304]{0:T(1024)(128)(4,1)S(1)}, s32[]{:S(2)}) async-start(s8[7340032]{0:T(1024)(128)(4,1)} %bitcast.101), calls=%async_computation | async-start | bytes 8388608
  56.8 5.4 %collective-permute-start.6 = (f32[3,256]{1,0:T(4,128)S(1)}, f32[3,256]{1,0:T(4,128)S(1)}, u32[]{:S(2)}, u32[]{:S(2)}) collective-permute-start(f32[3,256]{1,0:T(4,128)S(1)} %pad_maximum_fusion.5), channel_id=1, source_target_pairs={{0,1},{1,0},{2,3},{3,2},{4,5},{5,4},{6,7},{7,6},{8,9},{9,8},{10,11... | collective-permute-start | bytes 9224 | tf_op jit(solution)/shard_map/ppermute | solution.py:42
  62.2 1.9 %slice-start.1 = ((s8[7340032]{0:T(1024)(128)(4,1)}), s8[3145728]{0:T(1024)(128)(4,1)S(1)}, s32[]{:S(2)}) async-start(s8[7340032]{0:T(1024)(128)(4,1)} %bitcast.101), calls=%async_computation.1 | async-start | bytes 6291456
  66.8 10.8 %collective-permute-start.7 = (bf16[256,1024]{0,1:T(8,128)(2,1)S(1)}, bf16[256,1024]{0,1:T(8,128)(2,1)S(1)}, u32[]{:S(2)}, u32[]{:S(2)}) collective-permute-start(bf16[256,1024]{0,1:T(8,128)(2,1)S(1)} %bitcast.112), channel_id=1, source_target_pairs={{0,2},{2,0},{4,6},{6,4},{8,10},{10,8},{12,14},{14,12},{16,18},{18,... | collective-permute-start | bytes 1572872 | tf_op jit(solution)/shard_map/ppermute | solution.py:25
  67.1 10.5 %collective-permute-start.8 = (bf16[136,1024]{0,1:T(8,128)(2,1)S(1)}, bf16[136,1024]{0,1:T(8,128)(2,1)S(1)}, u32[]{:S(2)}, u32[]{:S(2)}) collective-permute-start(bf16[136,1024]{0,1:T(8,128)(2,1)S(1)} %pad_slice_fusion), channel_id=1, source_target_pairs={{2,0},{4,2},{6,4},{8,6},{10,8},{12,10},{14,12},{16,14},{18,16},{20... | collective-permute-start | bytes 835592 | tf_op jit(solution)/shard_map/ppermute | solution.py:20
  75.0 11.1 %collective-permute-start.13 = (f32[4,1024]{1,0:T(4,128)S(1)}, f32[4,1024]{1,0:T(4,128)S(1)}, u32[]{:S(2)}, u32[]{:S(2)}) collective-permute-start(f32[4,1024]{1,0:T(4,128)S(1)} %pad_maximum_fusion.4), channel_id=1, source_target_pairs={{0,2},{2,0},{4,6},{6,4},{8,10},{10,8},{12,14},{14,12},{16,18},{18,... | collective-permute-start | bytes 49160 | tf_op jit(solution)/shard_map/ppermute | solution.py:34
  85.2 39.7 %copy-start = (f32[904,1024]{0,1:T(8,128)}, f32[904,1024]{0,1:T(8,128)S(1)}, u32[]{:S(2)}) copy-start(f32[904,1024]{0,1:T(8,128)S(1)} %get-tuple-element.29) | copy-start | bytes 11108356
  85.5 35.4 %collective-permute-start.10 = (bf16[256,1024]{0,1:T(8,128)(2,1)S(1)}, bf16[256,1024]{0,1:T(8,128)(2,1)S(1)}, u32[]{:S(2)}, u32[]{:S(2)}) collective-permute-start(bf16[256,1024]{0,1:T(8,128)(2,1)S(1)} %slice.139), channel_id=1, source_target_pairs={{0,2},{2,0},{4,6},{6,4},{8,10},{10,8},{12,14},{14,12},{16,18},{18,... | collective-permute-start | bytes 1572872 | tf_op jit(solution)/shard_map/ppermute | solution.py:25
  86.1 5.8 %collective-permute-start.14 = (f32[4,1024]{1,0:T(4,128)S(1)}, f32[4,1024]{1,0:T(4,128)S(1)}, u32[]{:S(2)}, u32[]{:S(2)}) collective-permute-start(f32[4,1024]{1,0:T(4,128)S(1)} %fusion.48), channel_id=1, source_target_pairs={{0,4},{2,6},{4,0},{6,2},{8,12},{10,14},{12,8},{14,10},{16,20},{18,... | collective-permute-start | bytes 49160 | tf_op jit(solution)/shard_map/ppermute | solution.py:34
  86.5 34.4 %collective-permute-start.11 = (bf16[136,1024]{0,1:T(8,128)(2,1)S(1)}, bf16[136,1024]{0,1:T(8,128)(2,1)S(1)}, u32[]{:S(2)}, u32[]{:S(2)}) collective-permute-start(bf16[136,1024]{0,1:T(8,128)(2,1)S(1)} %slice.141), channel_id=1, source_target_pairs={{2,0},{4,2},{6,4},{8,6},{10,8},{12,10},{14,12},{16,14},{18,16},{20... | collective-permute-start | bytes 835592 | tf_op jit(solution)/shard_map/ppermute | solution.py:20
  92.0 5.3 %collective-permute-start.15 = (f32[4,1024]{1,0:T(4,128)S(1)}, f32[4,1024]{1,0:T(4,128)S(1)}, u32[]{:S(2)}, u32[]{:S(2)}) collective-permute-start(f32[4,1024]{1,0:T(4,128)S(1)} %fusion.72), channel_id=1, source_target_pairs={{0,8},{2,10},{4,12},{6,14},{8,0},{10,2},{12,4},{14,6},{16,24},{18,... | collective-permute-start | bytes 49160 | tf_op jit(solution)/shard_map/ppermute | solution.py:34
  97.3 4.4 %collective-permute-start.16 = (f32[4,1024]{1,0:T(4,128)S(1)}, f32[4,1024]{1,0:T(4,128)S(1)}, u32[]{:S(2)}, u32[]{:S(2)}) collective-permute-start(f32[4,1024]{1,0:T(4,128)S(1)} %add.164), channel_id=1, source_target_pairs={{0,16},{2,18},{4,20},{6,22},{8,24},{10,26},{12,28},{14,30},{16,0},... | collective-permute-start | bytes 49160 | tf_op jit(solution)/shard_map/ppermute | solution.py:34
  101.7 3.7 %collective-permute-start.17 = (f32[4,1024]{1,0:T(4,128)S(1)}, f32[4,1024]{1,0:T(4,128)S(1)}, u32[]{:S(2)}, u32[]{:S(2)}) collective-permute-start(f32[4,1024]{1,0:T(4,128)S(1)} %add.165), channel_id=1, source_target_pairs={{0,32},{2,34},{4,36},{6,38},{8,40},{10,42},{12,44},{14,46},{16,48}... | collective-permute-start | bytes 49160 | tf_op jit(solution)/shard_map/ppermute | solution.py:34
  105.5 5.8 %collective-permute-start.18 = (f32[4,1024]{1,0:T(4,128)S(1)}, f32[4,1024]{1,0:T(4,128)S(1)}, u32[]{:S(2)}, u32[]{:S(2)}) collective-permute-start(f32[4,1024]{1,0:T(4,128)S(1)} %add.166), channel_id=1, source_target_pairs={{0,64},{2,66},{4,68},{6,70},{8,72},{10,74},{12,76},{14,78},{16,80}... | collective-permute-start | bytes 49160 | tf_op jit(solution)/shard_map/ppermute | solution.py:34
  111.3 14.7 %collective-permute-start.19 = (f32[4,1024]{1,0:T(4,128)S(1)}, f32[4,1024]{1,0:T(4,128)S(1)}, u32[]{:S(2)}, u32[]{:S(2)}) collective-permute-start(f32[4,1024]{1,0:T(4,128)S(1)} %add.167), channel_id=1, source_target_pairs={{0,128},{2,130},{4,132},{6,134},{8,136},{10,138},{12,140},{14,142}... | collective-permute-start | bytes 49160 | tf_op jit(solution)/shard_map/ppermute | solution.py:34
  118.1 17.6 %collective-permute-start.9 = (bf16[256,1024]{0,1:T(8,128)(2,1)}, bf16[256,1024]{0,1:T(8,128)(2,1)}, u32[]{:S(2)}, u32[]{:S(2)}) collective-permute-start(bf16[256,1024]{0,1:T(8,128)(2,1)} %get-tuple-element.8), channel_id=1, source_target_pairs={{4,0},{6,2},{8,4},{10,6},{12,8},{14,10},{16,12},{18,14},{20,16},{2... | collective-permute-start | bytes 1572872 | tf_op jit(solution)/shard_map/ppermute | solution.py:20
  120.9 4.0 %copy-start.6 = (bf16[256,1024]{0,1:T(8,128)(2,1)}, bf16[256,1024]{0,1:T(8,128)(2,1)S(1)}, u32[]{:S(2)}) copy-start(bf16[256,1024]{0,1:T(8,128)(2,1)S(1)} %collective-permute-done.10) | copy-start | bytes 1572868
  122.3 20.6 %collective-permute-start.12 = (bf16[256,1024]{0,1:T(8,128)(2,1)}, bf16[256,1024]{0,1:T(8,128)(2,1)}, u32[]{:S(2)}, u32[]{:S(2)}) collective-permute-start(bf16[256,1024]{0,1:T(8,128)(2,1)} %fusion.31), channel_id=1, source_target_pairs={{4,0},{6,2},{8,4},{10,6},{12,8},{14,10},{16,12},{18,14},{20,16},{2... | collective-permute-start | bytes 1572872 | tf_op jit(solution)/shard_map/ppermute | solution.py:20
  125.0 17.9 %copy-start.7 = (bf16[256,1024]{0,1:T(8,128)(2,1)S(1)}, bf16[256,1024]{0,1:T(8,128)(2,1)}, u32[]{:S(2)}) copy-start(bf16[256,1024]{0,1:T(8,128)(2,1)} %copy-done.6) | copy-start | bytes 1572868
  (2 other events, 2.3 us)

commit v10 on v6

--- a/solution.py
+++ b/solution.py
@@ -165,21 +165,33 @@
     for tap_index in range(tap_count):
         value_sum = value_sum + conv_weight[tap_index] * padded_value[tap_index : tap_index + key_count + far_lead]
 
-    def send_back(grads):
+    def parts(grads):
         cut_third = row_count - far_rows + far_lead
-        grad_third = grads[:cut_third]
-        grad_second = grads[cut_third : cut_third + row_count]
-        grad_first = grads[cut_third + row_count : cut_third + 2 * row_count]
-        grad_own = grads[cut_third + 2 * row_count :]
-        back = [
-            from_behind(part.astype(jnp.bfloat16), "tm", -distance).astype(jnp.float32)
-            for distance, part in ((1, grad_first), (2, grad_second), (3, grad_third))
-        ]
-        far = jnp.concatenate([jnp.zeros((far_rows - far_lead, grads.shape[1]), jnp.float32), back[2]], 0)
-        return grad_own + back[0] + back[1] + far
-
-    value_total = send_back(value_sum)
-    key_total = send_back(jnp.concatenate([lead, key_part], 0))
+        return (
+            grads[:cut_third],
+            grads[cut_third : cut_third + row_count],
+            grads[cut_third + row_count : cut_third + 2 * row_count],
+            grads[cut_third + 2 * row_count :],
+        )
+
+    key_grads = jnp.concatenate([lead, key_part], 0)
+    value_third, value_second, value_first, value_own = parts(value_sum)
+    key_third, key_second, key_first, key_own = parts(key_grads)
+    value_back_first = chip_swap(value_first.astype(jnp.bfloat16), "tm").astype(jnp.float32)
+    key_back_first = chip_swap(key_first.astype(jnp.bfloat16), "tm").astype(jnp.float32)
+    back_third = from_behind(
+        jnp.concatenate([value_third, key_third], 1).astype(jnp.bfloat16), "tm", -1
+    ).astype(jnp.float32)
+    spacer = jnp.zeros((far_rows - far_lead, 2 * channels), jnp.float32)
+    both_second = jnp.concatenate([value_second, key_second], 1) + jnp.concatenate([spacer, back_third], 0)
+    both_first = jnp.concatenate([value_back_first, key_back_first], 1)
+    both_second = both_second + jnp.where(even, 0.0, both_first)
+    back_second = from_behind(both_second.astype(jnp.bfloat16), "tm", -2).astype(jnp.float32)
+    both_total = (
+        jnp.concatenate([value_own, key_own], 1) + jnp.where(even, both_first, 0.0) + back_second
+    )
+    value_total = both_total[:, :channels]
+    key_total = both_total[:, channels:]
 
     return (
         query_grad.reshape(row_count, channels).astype(jnp.bfloat16),

time: 183 us -> 180 us (0.984)
  the two profiles are of different devices: /device:TPU:23 before, /device:TPU:4 now
where the time goes in v10:
time: 180 us; the launch traced here: 179 us
  starting transfers between devices  45.5 us (25%)
  waiting for transfers between devices  45.4 us (25%)
  other arithmetic  37.7 us (21%)
  local copies, waits for them, and re-layouts  28.4 us (16%)
  matrix products  20.9 us (12%)
    ppermute x7, waiting for transfers between devices, all_sum(): lax.ppermute(block, axis, [(i, i ^ stride) for i in range(size)])  30.5 us
    ppermute x7, starting transfers between devices, all_sum(): lax.ppermute(block, axis, [(i, i ^ stride) for i in range(size)])  28.1 us
    ppermute x6, starting transfers between devices, from_behind(): return lax.ppermute(block, axis, route)  15.5 us
    ppermute x6, waiting for transfers between devices, from_behind(): return lax.ppermute(block, axis, route)  10.5 us
    unnamed x46, local copies, waits for them, and re-layouts  9.02 us
    another operation x2, other arithmetic  8.6 us
    sub x1, matrix products, body(): expo = jnp.where(mask[None], jnp.exp(scores - row_peak[..., None]), 0.0)  7.96 us
    dot_general x1, matrix products, body(): jnp.einsum('thd,uhd->htu', heads_grad, heads_value, preferred_element_typ...  5.85 us
  transfers between devices with their start and end apart: 18, of which 9 were waited for; matrix products, arithmetic and copies ran while one was open for 21% of the time, Pallas kernels for 0%

profile of v10, /device:TPU:4, one launch (start us, length us, event | category | flops | bytes accessed | tf_op | source)
XLA Modules:
  0.0 179.0 jit_solution(16592696513467453726)
XLA Ops:
  1.9 3.5 %collective-permute-start = (bf16[256,1024]{0,1:T(8,128)(2,1)S(1)}, bf16[256,1024]{0,1:T(8,128)(2,1)S(1)}, u32[]{:S(2)}, u32[]{:S(2)}) collective-permute-start(bf16[256,1024]{0,1:T(8,128)(2,1)S(1)} %copy.87), channel_id=1, source_target_pairs={{0,4},{2,6},{4,8},{6,10},{8,12},{10,14},{12,16},{14,18},{16,20},{1... | collective-permute-start | bytes 1572872 | tf_op jit(solution)/shard_map/ppermute | solution.py:20
  6.7 3.5 %collective-permute-start.3 = (bf16[256,1024]{0,1:T(8,128)(2,1)S(1)}, bf16[256,1024]{0,1:T(8,128)(2,1)S(1)}, u32[]{:S(2)}, u32[]{:S(2)}) collective-permute-start(bf16[256,1024]{0,1:T(8,128)(2,1)S(1)} %copy.93), channel_id=1, source_target_pairs={{0,4},{2,6},{4,8},{6,10},{8,12},{10,14},{12,16},{14,18},{16,20},{1... | collective-permute-start | bytes 1572872 | tf_op jit(solution)/shard_map/ppermute | solution.py:20
  12.1 5.6 %collective-permute-done = bf16[256,1024]{0,1:T(8,128)(2,1)S(1)} collective-permute-done((bf16[256,1024]{0,1:T(8,128)(2,1)S(1)}, bf16[256,1024]{0,1:T(8,128)(2,1)S(1)}, u32[]{:S(2)}, u32[]{:S(2)}) %collective-permute-start) | collective-permute-done | bytes 524320 | tf_op jit(solution)/shard_map/ppermute | solution.py:20
  19.7 2.4 %collective-permute-start.1 = (bf16[136,1024]{0,1:T(8,128)(2,1)}, bf16[136,1024]{0,1:T(8,128)(2,1)S(1)}, u32[]{:S(2)}, u32[]{:S(2)}) collective-permute-start(bf16[136,1024]{0,1:T(8,128)(2,1)} %slice.133), channel_id=1, source_target_pairs={{0,2},{2,4},{4,6},{6,8},{8,10},{10,12},{12,14},{14,16},{16,18},{18... | collective-permute-start | bytes 835592 | tf_op jit(solution)/shard_map/ppermute | solution.py:20
  24.1 4.9 %collective-permute-done.3 = bf16[256,1024]{0,1:T(8,128)(2,1)S(1)} collective-permute-done((bf16[256,1024]{0,1:T(8,128)(2,1)S(1)}, bf16[256,1024]{0,1:T(8,128)(2,1)S(1)}, u32[]{:S(2)}, u32[]{:S(2)}) %collective-permute-start.3) | collective-permute-done | bytes 524320 | tf_op jit(solution)/shard_map/ppermute | solution.py:20
  30.9 3.2 %collective-permute-start.4 = (bf16[136,1024]{0,1:T(8,128)(2,1)}, bf16[136,1024]{0,1:T(8,128)(2,1)}, u32[]{:S(2)}, u32[]{:S(2)}) collective-permute-start(bf16[136,1024]{0,1:T(8,128)(2,1)} %slice.134), channel_id=1, source_target_pairs={{0,2},{2,4},{4,6},{6,8},{8,10},{10,12},{12,14},{14,16},{16,18},{18... | collective-permute-start | bytes 835592 | tf_op jit(solution)/shard_map/ppermute | solution.py:20
  36.6 8.0 %fusion.52 = (f32[8,256]{1,0:T(8,128)S(1)}, f32[8,256,896]{1,2,0:T(8,128)}) fusion(pred[256,896]{0,1:T(8,128)(4,1)} %fusion.33, bf16[896,8,128]{0,2,1:T(8,128)(2,1)S(1)} %bitcast.86, bf16[256,8,128]{0,2,1:T(8,128)(2,1)} %bitcast.94), kind=kOutput, calls=%fused_computation.99 | convolution fusion | flops 478937984 | bytes 9936896 | tf_op jit(solution)/shard_map/sub | solution.py:104
  44.5 3.8 %fusion.16 = bf16[8,256,896]{1,2,0:T(8,128)(2,1)S(1)} fusion(f32[8,256,896]{1,2,0:T(8,128)} %get-tuple-element.42, f32[8,256]{1,0:T(8,128)S(1)} %get-tuple-element.41), kind=kLoop, calls=%fused_computation.33 | loop fusion | flops 3670016 | bytes 11018240 | tf_op jit(solution)/shard_map/convert_element_type | solution.py:107
  48.3 3.0 %pad_maximum_fusion = bf16[904,1024]{0,1:T(8,128)(2,1)S(1)} fusion(bf16[256,1024]{0,1:T(8,128)(2,1)S(1)} %copy.93, bf16[256,1024]{0,1:T(8,128)(2,1)} %collective-permute-done.5, bf16[256,1024]{0,1:T(8,128)(2,1)S(1)} %copy-done.12, bf16[136,1024]{0,1:T(8,128)(2,1)} %collective-permute-done.4), kind=kLoop, calls=%fused_computation.41 | loop fusion | flops 7405568 | bytes 3702784 | tf_op jit(solution)/shard_map/concatenate | solution.py:81
  51.4 3.4 %fusion.8 = bf16[896,1024]{0,1:T(8,128)(2,1)S(1)} fusion(f32[1024]{0:T(1024)S(1)} %bitcast.113, f32[1024]{0:T(1024)S(1)} %bitcast.115, f32[1024]{0:T(1024)S(1)} %bitcast.111, f32[1024]{0:T(1024)S(1)} %bitcast.109, bf16[904,1024]{0,1:T(8,128)(2,1)S(1)} %pad_maximum_fusion), kind=kLoop, calls=%fused_computation.23 | loop fusion | flops 11010048 | bytes 9191424 | tf_op jit(solution)/shard_map/convert_element_type | solution.py:91
  54.8 1.8 %fusion.29 = (f32[256]{0:T(256)S(1)}, f32[256]{0:T(256)S(1)}, f32[8,128,256]{2,1,0:T(8,128)}) fusion(f32[8,128]{1,0:T(8,128)S(1)} %bitcast.117, bf16[896,8,128]{0,2,1:T(8,128)(2,1)S(1)} %bitcast.88, bf16[8,256,896]{1,2,0:T(8,128)(2,1)S(1)} %fusion.16), kind=kOutput, calls=%fused_computation.62 | convolution fusion | flops 471072256 | bytes 6559744 | tf_op jit(solution)/shard_map/htu,uhd->thd/dot_general | solution.py:108
  60.5 4.4 %collective-permute-done.6 = f32[3,256]{1,0:T(4,128)S(1)} collective-permute-done((f32[3,256]{1,0:T(4,128)S(1)}, f32[3,256]{1,0:T(4,128)S(1)}, u32[]{:S(2)}, u32[]{:S(2)}) %collective-permute-start.6) | collective-permute-done | bytes 3104 | tf_op jit(solution)/shard_map/ppermute | solution.py:42
  64.9 2.2 %fusion.28 = bf16[256,1024]{1,0:T(8,128)(2,1)} fusion(bf16[256,1024]{1,0:T(8,128)(2,1)} %param.11, f32[256,1024]{1,0:T(8,128)S(1)} %copy.97, f32[256]{0:T(256)S(1)} %fusion.38, f32[256]{0:T(256)S(1)} %bitcast.119, f32[1024]{0:T(1024)S(1)} %copy-done.18, pred[256]{0:T(512)(128)(4,1)S(1)} %bitcast.127), kind=kLoop, calls=%fused_computation.56 | loop fusion | flops 2621440 | bytes 2103552 | tf_op jit(solution)/shard_map/convert_element_type | solution.py:132
  69.7 3.4 %fusion.54 = f32[8,128,896]{2,1,0:T(8,128)S(1)} fusion(bf16[256,8,128]{0,2,1:T(8,128)(2,1)S(1)} %bitcast.90, bf16[8,256,896]{1,2,0:T(8,128)(2,1)} %copy-done.2), kind=kOutput, calls=%fused_computation.101 | convolution fusion | flops 469762048 | bytes 7864320 | tf_op jit(solution)/shard_map/htu,thd->uhd/dot_general | solution.py:146
  73.1 5.8 %multiply_convert_fusion = bf16[8,256,896]{1,2,0:T(8,128)(2,1)S(1)} fusion(f32[8,256]{1,0:T(8,128)S(1)} %bitcast.126, f32[8,256,896]{1,2,0:T(8,128)} %get-tuple-element.42, f32[8,256]{1,0:T(8,128)S(1)} %get-tuple-element.41, bf16[256,8,128]{0,2,1:T(8,128)(2,1)S(1)} %bitcast.91, bf16[896,8,128]{0,2,1:T(8,128)(2,1)S(1)} %bitcast.89), kind=kOutput, calls=%fused_computation.2 | convolution fusion | flops 477102080 | bytes 13385728 | tf_op jit(solution)/shard_map/thd,uhd->htu/dot_general | solution.py:136
  83.6 6.4 %fusion.45 = (bf16[904,1024]{0,1:T(8,128)(2,1)S(1)}, f32[904,1024]{0,1:T(8,128)}) fusion(f32[907,1024]{0,1:T(8,128)S(1)} %maximum_maximum_fusion, f32[1024]{0:T(1024)S(1)} %bitcast.114, f32[1024]{0:T(1024)S(1)} %bitcast.116, f32[1024]{0:T(1024)S(1)} %bitcast.112, f32[896,1024]{0,1:T(8,128)S(1)} %bitcast.83, f32[1024]{0:T(1024)S(1)} %bitcast.110), kind=kLoop, calls=%fused_computation.93 | loop fusion | flops 7405568 | bytes 20348928 | tf_op jit(solution)/shard_map/convert.13
  94.4 3.8 %fusion.47 = (f32[256,1024]{0,1:T(8,128)}, f32[256,1024]{0,1:T(8,128)}) fusion(f32[904,1024]{0,1:T(8,128)} %get-tuple-element.27), kind=kLoop, calls=%fused_computation.94 | loop fusion | bytes 4194304 | tf_op jit(solution)/shard_map/slice | solution.py:172
  98.2 1.9 %slice.148 = bf16[256,8,128]{0,2,1:T(8,128)(2,1)} slice(bf16[896,8,128]{0,2,1:T(8,128)(2,1)} %copy-done.5), slice={[384:640], [0:8], [0:128]} | slice | bytes 1048576 | tf_op jit(solution)/shard_map/slice | solution.py:173
  100.1 2.2 %slice.147 = bf16[256,1024]{0,1:T(8,128)(2,1)} slice(bf16[904,1024]{0,1:T(8,128)(2,1)} %copy-done.10), slice={[392:648], [0:1024]} | slice | bytes 1048576 | tf_op jit(solution)/shard_map/slice | solution.py:173
  103.3 3.9 %fusion.9 = (f32[1024]{0:T(1024)S(1)}, f32[1024]{0:T(1024)S(1)}, f32[1024]{0:T(1024)S(1)}, f32[1024]{0:T(1024)S(1)}) fusion(bf16[904,1024]{0,1:T(8,128)(2,1)S(1)} %pad_maximum_fusion, f32[8,128,896]{2,1,0:T(8,128)S(1)} %copy-done.1), kind=kLoop, calls=%fused_computation.24 | loop fusion | flops 11005952 | bytes 11026432 | tf_op jit(solution)/shard_map/reduce_sum | solution.py:152
  108.9 3.5 %fusion.21 = bf16[256,2048]{0,1:T(8,128)(2,1)} fusion(f32[256,1024]{0,1:T(8,128)} %bitcast.93, f32[256,1024]{0,1:T(8,128)} %get-tuple-element.28, bf16[136,2048]{0,1:T(8,128)(2,1)S(1)} %copy.109, pred[]{:T(512)S(6)} %eq.29, bf16[256,1024]{0,1:T(8,128)(2,1)S(1)} %collective-permute-done.8, bf16[256,1024]{0,1:T(8,128)(2,1)} %collective-permute-done.7), kind=kLoop, calls=%fused_computation.40 | loop fusion | flops 5242880 | bytes 4751361 | tf_op jit(solution)/shard_map/convert_element_type | solution.py:189
  115.2 2.6 %collective-permute-start.12 = (f32[4,1024]{1,0:T(4,128)S(1)}, f32[4,1024]{1,0:T(4,128)S(1)}, u32[]{:S(2)}, u32[]{:S(2)}) collective-permute-start(f32[4,1024]{1,0:T(4,128)S(1)} %fusion.44), channel_id=1, source_target_pairs={{0,4},{2,6},{4,0},{6,2},{8,12},{10,14},{12,8},{14,10},{16,20},{18,... | collective-permute-start | bytes 49160 | tf_op jit(solution)/shard_map/ppermute | solution.py:34
  117.7 22.7 %collective-permute-done.12 = f32[4,1024]{1,0:T(4,128)S(1)} collective-permute-done((f32[4,1024]{1,0:T(4,128)S(1)}, f32[4,1024]{1,0:T(4,128)S(1)}, u32[]{:S(2)}, u32[]{:S(2)}) %collective-permute-start.12) | collective-permute-done | bytes 16416 | tf_op jit(solution)/shard_map/ppermute | solution.py:34
  140.5 3.6 %collective-permute-start.13 = (f32[4,1024]{1,0:T(4,128)S(1)}, f32[4,1024]{1,0:T(4,128)S(1)}, u32[]{:S(2)}, u32[]{:S(2)}) collective-permute-start(f32[4,1024]{1,0:T(4,128)S(1)} %fusion.69), channel_id=1, source_target_pairs={{0,8},{2,10},{4,12},{6,14},{8,0},{10,2},{12,4},{14,6},{16,24},{18,... | collective-permute-start | bytes 49160 | tf_op jit(solution)/shard_map/ppermute | solution.py:34
  144.1 1.8 collective-permute-done.13
  145.8 4.8 %collective-permute-start.14 = (f32[4,1024]{1,0:T(4,128)S(1)}, f32[4,1024]{1,0:T(4,128)S(1)}, u32[]{:S(2)}, u32[]{:S(2)}) collective-permute-start(f32[4,1024]{1,0:T(4,128)S(1)} %add.146), channel_id=1, source_target_pairs={{0,16},{2,18},{4,20},{6,22},{8,24},{10,26},{12,28},{14,30},{16,0},... | collective-permute-start | bytes 49160 | tf_op jit(solution)/shard_map/ppermute | solution.py:34
  150.6 1.7 collective-permute-done.14
  152.4 3.9 %collective-permute-start.15 = (f32[4,1024]{1,0:T(4,128)S(1)}, f32[4,1024]{1,0:T(4,128)S(1)}, u32[]{:S(2)}, u32[]{:S(2)}) collective-permute-start(f32[4,1024]{1,0:T(4,128)S(1)} %add.147), channel_id=1, source_target_pairs={{0,32},{2,34},{4,36},{6,38},{8,40},{10,42},{12,44},{14,46},{16,48}... | collective-permute-start | bytes 49160 | tf_op jit(solution)/shard_map/ppermute | solution.py:34
  156.2 1.7 collective-permute-done.15
  157.9 3.4 %collective-permute-start.16 = (f32[4,1024]{1,0:T(4,128)S(1)}, f32[4,1024]{1,0:T(4,128)S(1)}, u32[]{:S(2)}, u32[]{:S(2)}) collective-permute-start(f32[4,1024]{1,0:T(4,128)S(1)} %add.148), channel_id=1, source_target_pairs={{0,64},{2,66},{4,68},{6,70},{8,72},{10,74},{12,76},{14,78},{16,80}... | collective-permute-start | bytes 49160 | tf_op jit(solution)/shard_map/ppermute | solution.py:34
  163.0 9.3 %collective-permute-start.17 = (f32[4,1024]{1,0:T(4,128)S(1)}, f32[4,1024]{1,0:T(4,128)S(1)}, u32[]{:S(2)}, u32[]{:S(2)}) collective-permute-start(f32[4,1024]{1,0:T(4,128)S(1)} %add.149), channel_id=1, source_target_pairs={{0,128},{2,130},{4,132},{6,134},{8,136},{10,138},{12,140},{14,142}... | collective-permute-start | bytes 49160 | tf_op jit(solution)/shard_map/ppermute | solution.py:34
  174.7 2.2 %fusion.19 = bf16[256,2048]{0,1:T(8,128)(2,1)S(1)} fusion(f32[256,1024]{0,1:T(8,128)S(1)} %bitcast.92, f32[256,1024]{0,1:T(8,128)} %get-tuple-element.29, bf16[256,2048]{0,1:T(8,128)(2,1)} %collective-permute-done.10, pred[]{:T(512)S(6)} %eq.29, bf16[256,1024]{0,1:T(8,128)(2,1)} %copy-done.15, bf16[256,1024]{0,1:T(8,128)(2,1)} %collective-permute-done.7), kind=kLoop, calls=%fused_computation.38 | loop fusion | flops 5242880 | bytes 5242881 | tf_op jit(solution)/shard_map/convert.4
  (112 shorter events, 39.6 us)
Async XLA Ops:
  0.6 21.5 %copy-start.17 = (bf16[256,1024]{1,0:T(8,128)(2,1)S(1)}, bf16[256,1024]{1,0:T(8,128)(2,1)}, u32[]{:S(2)}) copy-start(bf16[256,1024]{1,0:T(8,128)(2,1)} %param.8) | copy-start | bytes 1572868
  1.9 15.8 %collective-permute-start = (bf16[256,1024]{0,1:T(8,128)(2,1)S(1)}, bf16[256,1024]{0,1:T(8,128)(2,1)S(1)}, u32[]{:S(2)}, u32[]{:S(2)}) collective-permute-start(bf16[256,1024]{0,1:T(8,128)(2,1)S(1)} %copy.87), channel_id=1, source_target_pairs={{0,4},{2,6},{4,8},{6,10},{8,12},{10,14},{12,16},{14,18},{16,20},{1... | collective-permute-start | bytes 1572872 | tf_op jit(solution)/shard_map/ppermute | solution.py:20
  6.7 22.3 %collective-permute-start.3 = (bf16[256,1024]{0,1:T(8,128)(2,1)S(1)}, bf16[256,1024]{0,1:T(8,128)(2,1)S(1)}, u32[]{:S(2)}, u32[]{:S(2)}) collective-permute-start(bf16[256,1024]{0,1:T(8,128)(2,1)S(1)} %copy.93), channel_id=1, source_target_pairs={{0,4},{2,6},{4,8},{6,10},{8,12},{10,14},{12,16},{14,18},{16,20},{1... | collective-permute-start | bytes 1572872 | tf_op jit(solution)/shard_map/ppermute | solution.py:20
  18.6 16.4 %collective-permute-start.2 = (bf16[256,1024]{0,1:T(8,128)(2,1)}, bf16[256,1024]{0,1:T(8,128)(2,1)}, u32[]{:S(2)}, u32[]{:S(2)}) collective-permute-start(bf16[256,1024]{0,1:T(8,128)(2,1)} %broadcast_select_fusion.1), channel_id=1, source_target_pairs={{0,2},{2,0},{4,6},{6,4},{8,10},{10,8},{12,14},{14,12},{16,18},{18,... | collective-permute-start | bytes 1572872 | tf_op jit(solution)/shard_map/ppermute | solution.py:25
  19.7 14.4 %collective-permute-start.1 = (bf16[136,1024]{0,1:T(8,128)(2,1)}, bf16[136,1024]{0,1:T(8,128)(2,1)S(1)}, u32[]{:S(2)}, u32[]{:S(2)}) collective-permute-start(bf16[136,1024]{0,1:T(8,128)(2,1)} %slice.133), channel_id=1, source_target_pairs={{0,2},{2,4},{4,6},{6,8},{8,10},{10,12},{12,14},{14,16},{16,18},{18... | collective-permute-start | bytes 835592 | tf_op jit(solution)/shard_map/ppermute | solution.py:20
  29.0 5.2 %copy-start.11 = (bf16[256,1024]{0,1:T(8,128)(2,1)}, bf16[256,1024]{0,1:T(8,128)(2,1)S(1)}, u32[]{:S(2)}) copy-start(bf16[256,1024]{0,1:T(8,128)(2,1)S(1)} %collective-permute-done.3) | copy-start | bytes 1572868
  29.9 18.4 %collective-permute-start.5 = (bf16[256,1024]{0,1:T(8,128)(2,1)}, bf16[256,1024]{0,1:T(8,128)(2,1)}, u32[]{:S(2)}, u32[]{:S(2)}) collective-permute-start(bf16[256,1024]{0,1:T(8,128)(2,1)} %broadcast_select_fusion), channel_id=1, source_target_pairs={{0,2},{2,0},{4,6},{6,4},{8,10},{10,8},{12,14},{14,12},{16,18},{18,... | collective-permute-start | bytes 1572872 | tf_op jit(solution)/shard_map/ppermute | solution.py:25
  30.9 17.4 %collective-permute-start.4 = (bf16[136,1024]{0,1:T(8,128)(2,1)}, bf16[136,1024]{0,1:T(8,128)(2,1)}, u32[]{:S(2)}, u32[]{:S(2)}) collective-permute-start(bf16[136,1024]{0,1:T(8,128)(2,1)} %slice.134), channel_id=1, source_target_pairs={{0,2},{2,4},{4,6},{6,8},{8,10},{10,12},{12,14},{14,16},{16,18},{18... | collective-permute-start | bytes 835592 | tf_op jit(solution)/shard_map/ppermute | solution.py:20
  36.5 8.0 %copy-start.6 = (bf16[896,1024]{0,1:T(8,128)(2,1)}, bf16[896,1024]{0,1:T(8,128)(2,1)S(1)}, u32[]{:S(2)}) copy-start(bf16[896,1024]{0,1:T(8,128)(2,1)S(1)} %pad_maximum_fusion.1) | copy-start | bytes 5505028
  44.5 3.8 %copy-start.12 = (bf16[256,1024]{0,1:T(8,128)(2,1)S(1)}, bf16[256,1024]{0,1:T(8,128)(2,1)}, u32[]{:S(2)}) copy-start(bf16[256,1024]{0,1:T(8,128)(2,1)} %copy-done.11) | copy-start | bytes 1572868
  48.3 6.5 %copy-start.2 = (bf16[8,256,896]{1,2,0:T(8,128)(2,1)}, bf16[8,256,896]{1,2,0:T(8,128)(2,1)S(1)}, u32[]{:S(2)}) copy-start(bf16[8,256,896]{1,2,0:T(8,128)(2,1)S(1)} %fusion.16) | copy-start | bytes 11010052
  54.8 5.5 %copy-start.19 = (s32[2,64]{1,0:T(2,128)S(1)}, s32[2,64]{1,0:T(2,128)}, u32[]{:S(2)}) copy-start(s32[2,64]{1,0:T(2,128)} %param.15) | copy-start | bytes 1540
  59.5 5.4 %collective-permute-start.6 = (f32[3,256]{1,0:T(4,128)S(1)}, f32[3,256]{1,0:T(4,128)S(1)}, u32[]{:S(2)}, u32[]{:S(2)}) collective-permute-start(f32[3,256]{1,0:T(4,128)S(1)} %pad_maximum_fusion.7), channel_id=1, source_target_pairs={{0,1},{1,0},{2,3},{3,2},{4,5},{5,4},{6,7},{7,6},{8,9},{9,8},{10,11... | collective-permute-start | bytes 9224 | tf_op jit(solution)/shard_map/ppermute | solution.py:42
  73.1 10.5 %copy-start = (f32[8,128,896]{2,1,0:T(8,128)}, f32[8,128,896]{2,1,0:T(8,128)S(1)}, u32[]{:S(2)}) copy-start(f32[8,128,896]{2,1,0:T(8,128)S(1)} %fusion.54) | copy-start | bytes 11010052
  73.1 5.9 %copy-start.14 = (bf16[256,1024]{0,1:T(8,128)(2,1)S(1)}, bf16[256,1024]{0,1:T(8,128)(2,1)}, u32[]{:S(2)}) copy-start(bf16[256,1024]{0,1:T(8,128)(2,1)} %copy.121) | copy-start | bytes 1572868
  80.8 9.2 %copy-start.5 = (bf16[896,8,128]{0,2,1:T(8,128)(2,1)}, bf16[896,8,128]{0,2,1:T(8,128)(2,1)S(1)}, u32[]{:S(2)}) copy-start(bf16[896,8,128]{0,2,1:T(8,128)(2,1)S(1)} %get-tuple-element.44) | copy-start | bytes 5505028
  92.8 10.5 %copy-start.1 = (f32[8,128,896]{2,1,0:T(8,128)S(1)}, f32[8,128,896]{2,1,0:T(8,128)}, u32[]{:S(2)}) copy-start(f32[8,128,896]{2,1,0:T(8,128)} %copy-done) | copy-start | bytes 11010052
  92.8 14.5 %collective-permute-start.9 = (bf16[136,2048]{1,0:T(8,128)(2,1)}, bf16[136,2048]{1,0:T(8,128)(2,1)}, u32[]{:S(2)}, u32[]{:S(2)}) collective-permute-start(bf16[136,2048]{1,0:T(8,128)(2,1)} %copy.108), channel_id=1, source_target_pairs={{2,0},{4,2},{6,4},{8,6},{10,8},{12,10},{14,12},{16,14},{18,16},{20... | collective-permute-start | bytes 1671176 | tf_op jit(solution)/shard_map/ppermute | solution.py:20
  102.2 6.6 %collective-permute-start.8 = (bf16[256,1024]{0,1:T(8,128)(2,1)}, bf16[256,1024]{0,1:T(8,128)(2,1)S(1)}, u32[]{:S(2)}, u32[]{:S(2)}) collective-permute-start(bf16[256,1024]{0,1:T(8,128)(2,1)} %bitcast.29), channel_id=1, source_target_pairs={{0,2},{2,0},{4,6},{6,4},{8,10},{10,8},{12,14},{14,12},{16,18},{18,... | collective-permute-start | bytes 1572872 | tf_op jit(solution)/shard_map/ppermute | solution.py:25
  103.3 5.5 %collective-permute-start.7 = (bf16[256,1024]{0,1:T(8,128)(2,1)}, bf16[256,1024]{0,1:T(8,128)(2,1)}, u32[]{:S(2)}, u32[]{:S(2)}) collective-permute-start(bf16[256,1024]{0,1:T(8,128)(2,1)} %slice.147), channel_id=1, source_target_pairs={{0,2},{2,0},{4,6},{6,4},{8,10},{10,8},{12,14},{14,12},{16,18},{18,... | collective-permute-start | bytes 1572872 | tf_op jit(solution)/shard_map/ppermute | solution.py:25
  107.3 65.1 %copy-start.7 = (bf16[896,1024]{0,1:T(8,128)(2,1)S(1)}, bf16[896,1024]{0,1:T(8,128)(2,1)}, u32[]{:S(2)}) copy-start(bf16[896,1024]{0,1:T(8,128)(2,1)} %copy-done.6) | copy-start | bytes 5505028
  108.8 63.6 %copy-start.4 = (bf16[8,256,896]{1,2,0:T(8,128)(2,1)S(1)}, bf16[8,256,896]{1,2,0:T(8,128)(2,1)}, u32[]{:S(2)}) copy-start(bf16[8,256,896]{1,2,0:T(8,128)(2,1)} %copy-done.3) | copy-start | bytes 11010052
  108.9 54.2 %copy-start.15 = (bf16[256,1024]{0,1:T(8,128)(2,1)}, bf16[256,1024]{0,1:T(8,128)(2,1)S(1)}, u32[]{:S(2)}) copy-start(bf16[256,1024]{0,1:T(8,128)(2,1)S(1)} %collective-permute-done.8) | copy-start | bytes 1572868
  112.4 62.3 %collective-permute-start.10 = (bf16[256,2048]{0,1:T(8,128)(2,1)}, bf16[256,2048]{0,1:T(8,128)(2,1)}, u32[]{:S(2)}, u32[]{:S(2)}) collective-permute-start(bf16[256,2048]{0,1:T(8,128)(2,1)} %fusion.21), channel_id=1, source_target_pairs={{4,0},{6,2},{8,4},{10,6},{12,8},{14,10},{16,12},{18,14},{20,16},{2... | collective-permute-start | bytes 3145736 | tf_op jit(solution)/shard_map/ppermute | solution.py:20
  113.7 1.4 collective-permute-start.11
  115.2 25.3 %collective-permute-start.12 = (f32[4,1024]{1,0:T(4,128)S(1)}, f32[4,1024]{1,0:T(4,128)S(1)}, u32[]{:S(2)}, u32[]{:S(2)}) collective-permute-start(f32[4,1024]{1,0:T(4,128)S(1)} %fusion.44), channel_id=1, source_target_pairs={{0,4},{2,6},{4,0},{6,2},{8,12},{10,14},{12,8},{14,10},{16,20},{18,... | collective-permute-start | bytes 49160 | tf_op jit(solution)/shard_map/ppermute | solution.py:34
  140.5 34.3 %copy-start.13 = (f32[256,8,128]{0,2,1:T(8,128)S(1)}, f32[256,8,128]{0,2,1:T(8,128)}, u32[]{:S(2)}) copy-start(f32[256,8,128]{0,2,1:T(8,128)} %get-tuple-element.31) | copy-start | bytes 3145732
  140.5 5.3 %collective-permute-start.13 = (f32[4,1024]{1,0:T(4,128)S(1)}, f32[4,1024]{1,0:T(4,128)S(1)}, u32[]{:S(2)}, u32[]{:S(2)}) collective-permute-start(f32[4,1024]{1,0:T(4,128)S(1)} %fusion.69), channel_id=1, source_target_pairs={{0,8},{2,10},{4,12},{6,14},{8,0},{10,2},{12,4},{14,6},{16,24},{18,... | collective-permute-start | bytes 49160 | tf_op jit(solution)/shard_map/ppermute | solution.py:34
  145.8 6.5 %collective-permute-start.14 = (f32[4,1024]{1,0:T(4,128)S(1)}, f32[4,1024]{1,0:T(4,128)S(1)}, u32[]{:S(2)}, u32[]{:S(2)}) collective-permute-start(f32[4,1024]{1,0:T(4,128)S(1)} %add.146), channel_id=1, source_target_pairs={{0,16},{2,18},{4,20},{6,22},{8,24},{10,26},{12,28},{14,30},{16,0},... | collective-permute-start | bytes 49160 | tf_op jit(solution)/shard_map/ppermute | solution.py:34
  152.4 5.6 %collective-permute-start.15 = (f32[4,1024]{1,0:T(4,128)S(1)}, f32[4,1024]{1,0:T(4,128)S(1)}, u32[]{:S(2)}, u32[]{:S(2)}) collective-permute-start(f32[4,1024]{1,0:T(4,128)S(1)} %add.147), channel_id=1, source_target_pairs={{0,32},{2,34},{4,36},{6,38},{8,40},{10,42},{12,44},{14,46},{16,48}... | collective-permute-start | bytes 49160 | tf_op jit(solution)/shard_map/ppermute | solution.py:34
  157.9 5.1 %collective-permute-start.16 = (f32[4,1024]{1,0:T(4,128)S(1)}, f32[4,1024]{1,0:T(4,128)S(1)}, u32[]{:S(2)}, u32[]{:S(2)}) collective-permute-start(f32[4,1024]{1,0:T(4,128)S(1)} %add.148), channel_id=1, source_target_pairs={{0,64},{2,66},{4,68},{6,70},{8,72},{10,74},{12,76},{14,78},{16,80}... | collective-permute-start | bytes 49160 | tf_op jit(solution)/shard_map/ppermute | solution.py:34
  163.0 11.1 %collective-permute-start.17 = (f32[4,1024]{1,0:T(4,128)S(1)}, f32[4,1024]{1,0:T(4,128)S(1)}, u32[]{:S(2)}, u32[]{:S(2)}) collective-permute-start(f32[4,1024]{1,0:T(4,128)S(1)} %add.149), channel_id=1, source_target_pairs={{0,128},{2,130},{4,132},{6,134},{8,136},{10,138},{12,140},{14,142}... | collective-permute-start | bytes 49160 | tf_op jit(solution)/shard_map/ppermute | solution.py:34
  (6 other events, 12.7 us)

commit v11 on v5

--- a/solution.py
+++ b/solution.py
@@ -25,14 +25,29 @@
     return lax.ppermute(block, axis, [(i, i ^ 1) for i in range(size)])
 
 
-def all_sum(block, axis):
+def all_sum(block, axis, radix=4):
     size = lax.axis_size(axis)
     if size & (size - 1):
         return lax.psum(block, axis)
-    stride = size // 2
-    while stride >= 1:
-        block = block + lax.ppermute(block, axis, [(i, i ^ stride) for i in range(size)])
-        stride //= 2
+    index = lax.axis_index(axis)
+    stride = 1
+    while stride < size:
+        group = min(radix, size // stride)
+        digit = (index // stride) % group
+        received = [block]
+        for step in range(1, group):
+            route = []
+            for i in range(size):
+                own = (i // stride) % group
+                route.append((i, i + ((own + step) % group - own) * stride))
+            received.append(lax.ppermute(block, axis, route))
+        stacked = jnp.stack(received)
+        total = None
+        for source in range(group):
+            term = lax.dynamic_index_in_dim(stacked, (digit - source) % group, 0, keepdims=False)
+            total = term if total is None else total + term
+        block = total
+        stride *= group
     return block
 
 

time: 144 us -> 159 us (1.10)
  the two profiles are of different devices: /device:TPU:4 before, /device:TPU:33 now
where the time goes in v11:
time: 159 us; the launch traced here: 158 us
  starting transfers between devices  60 us (38%)
  other arithmetic  35.5 us (22%)
  waiting for transfers between devices  25.4 us (16%)
  local copies, waits for them, and re-layouts  19 us (12%)
  matrix products  17.1 us (11%)
    ppermute x8, starting transfers between devices, from_behind(): return lax.ppermute(block, axis, route)  28.1 us
    ppermute x10, starting transfers between devices, all_sum(): received.append(lax.ppermute(block, axis, route))  21.7 us
    ppermute x10, waiting for transfers between devices, all_sum(): received.append(lax.ppermute(block, axis, route))  13.3 us
    ppermute x8, waiting for transfers between devices, from_behind(): return lax.ppermute(block, axis, route)  11 us
    unnamed x39, local copies, waits for them, and re-layouts  10.7 us
    ppermute x4, starting transfers between devices, chip_swap(): return lax.ppermute(block, axis, [(i, i ^ 1) for i in range(size)])  7.18 us
    sub x1, matrix products, body(): expo = jnp.where(mask[None], jnp.exp(scores - row_peak[..., None]), 0.0)  7.1 us
    another operation x1, other arithmetic  6.38 us
  transfers between devices with their start and end apart: 23, of which 6 were waited for; matrix products, arithmetic and copies ran while one was open for 27% of the time, Pallas kernels for 0%

profile of v11, /device:TPU:33, one launch (start us, length us, event | category | flops | bytes accessed | tf_op | source)
XLA Modules:
  0.0 158.5 jit_solution(15751586401003155559)
XLA Ops:
  1.9 3.2 %collective-permute-start = (bf16[256,1024]{0,1:T(8,128)(2,1)S(1)}, bf16[256,1024]{0,1:T(8,128)(2,1)S(1)}, u32[]{:S(2)}, u32[]{:S(2)}) collective-permute-start(bf16[256,1024]{0,1:T(8,128)(2,1)S(1)} %copy.59), channel_id=1, source_target_pairs={{0,4},{2,6},{4,8},{6,10},{8,12},{10,14},{12,16},{14,18},{16,20},{1... | collective-permute-start | bytes 1572872 | tf_op jit(solution)/shard_map/ppermute | solution.py:20
  6.4 3.2 %collective-permute-start.3 = (bf16[256,1024]{0,1:T(8,128)(2,1)S(1)}, bf16[256,1024]{0,1:T(8,128)(2,1)S(1)}, u32[]{:S(2)}, u32[]{:S(2)}) collective-permute-start(bf16[256,1024]{0,1:T(8,128)(2,1)S(1)} %copy.65), channel_id=1, source_target_pairs={{0,4},{2,6},{4,8},{6,10},{8,12},{10,14},{12,16},{14,18},{16,20},{1... | collective-permute-start | bytes 1572872 | tf_op jit(solution)/shard_map/ppermute | solution.py:20
  11.6 8.0 %collective-permute-done = bf16[256,1024]{0,1:T(8,128)(2,1)S(1)} collective-permute-done((bf16[256,1024]{0,1:T(8,128)(2,1)S(1)}, bf16[256,1024]{0,1:T(8,128)(2,1)S(1)}, u32[]{:S(2)}, u32[]{:S(2)}) %collective-permute-start) | collective-permute-done | bytes 524320 | tf_op jit(solution)/shard_map/ppermute | solution.py:20
  20.4 2.7 %collective-permute-start.2 = (bf16[256,1024]{0,1:T(8,128)(2,1)}, bf16[256,1024]{0,1:T(8,128)(2,1)}, u32[]{:S(2)}, u32[]{:S(2)}) collective-permute-start(bf16[256,1024]{0,1:T(8,128)(2,1)} %broadcast_select_fusion.1), channel_id=1, source_target_pairs={{0,2},{2,0},{4,6},{6,4},{8,10},{10,8},{12,14},{14,12},{16,18},{18,... | collective-permute-start | bytes 1572872 | tf_op jit(solution)/shard_map/ppermute | solution.py:25
  24.3 1.9 %collective-permute-start.1 = (bf16[136,1024]{0,1:T(8,128)(2,1)}, bf16[136,1024]{0,1:T(8,128)(2,1)S(1)}, u32[]{:S(2)}, u32[]{:S(2)}) collective-permute-start(bf16[136,1024]{0,1:T(8,128)(2,1)} %slice.123), channel_id=1, source_target_pairs={{0,2},{2,4},{4,6},{6,8},{8,10},{10,12},{12,14},{14,16},{16,18},{18... | collective-permute-start | bytes 835592 | tf_op jit(solution)/shard_map/ppermute | solution.py:20
  27.7 2.3 %copy.69 = bf16[256,1024]{0,1:T(8,128)(2,1)} copy(bf16[256,1024]{1,0:T(8,128)(2,1)} %param.11) | data formatting | bytes 1048576 | tf_op args[3]
  34.3 1.9 %collective-permute-start.4 = (bf16[136,1024]{0,1:T(8,128)(2,1)}, bf16[136,1024]{0,1:T(8,128)(2,1)}, u32[]{:S(2)}, u32[]{:S(2)}) collective-permute-start(bf16[136,1024]{0,1:T(8,128)(2,1)} %slice.124), channel_id=1, source_target_pairs={{0,2},{2,4},{4,6},{6,8},{8,10},{10,12},{12,14},{14,16},{16,18},{18... | collective-permute-start | bytes 835592 | tf_op jit(solution)/shard_map/ppermute | solution.py:20
  37.1 1.6 %pad_maximum_fusion.1 = bf16[896,1024]{0,1:T(8,128)(2,1)S(1)} fusion(bf16[256,1024]{0,1:T(8,128)(2,1)S(1)} %copy.59, bf16[256,1024]{0,1:T(8,128)(2,1)} %collective-permute-done.2, bf16[256,1024]{0,1:T(8,128)(2,1)S(1)} %collective-permute-done, bf16[136,1024]{0,1:T(8,128)(2,1)} %copy-done.13), kind=kLoop, calls=%fused_computation.36 | loop fusion | flops 7340032 | bytes 3686400 | tf_op jit(solution)/shard_map/concatenate | solution.py:96
  38.7 7.1 %fusion.61 = (f32[8,256]{1,0:T(8,128)S(1)}, f32[8,256,896]{1,2,0:T(8,128)}) fusion(pred[256,896]{0,1:T(8,128)(4,1)} %fusion.39, bf16[896,8,128]{0,2,1:T(8,128)(2,1)S(1)} %bitcast.121, bf16[256,8,128]{0,2,1:T(8,128)(2,1)S(1)} %bitcast.125), kind=kOutput, calls=%fused_computation.121 | convolution fusion | flops 478937984 | bytes 9936896 | tf_op jit(solution)/shard_map/sub | solution.py:119
  45.8 3.8 %fusion.16 = bf16[8,256,896]{1,2,0:T(8,128)(2,1)S(1)} fusion(f32[8,256,896]{1,2,0:T(8,128)} %get-tuple-element.38, f32[8,256]{1,0:T(8,128)S(1)} %get-tuple-element.37), kind=kLoop, calls=%fused_computation.33 | loop fusion | flops 3670016 | bytes 11018240 | tf_op jit(solution)/shard_map/convert_element_type | solution.py:122
  49.7 3.0 %pad_maximum_fusion = bf16[904,1024]{0,1:T(8,128)(2,1)S(1)} fusion(bf16[256,1024]{0,1:T(8,128)(2,1)S(1)} %copy-done.7, bf16[256,1024]{0,1:T(8,128)(2,1)} %collective-permute-done.5, bf16[256,1024]{0,1:T(8,128)(2,1)S(1)} %copy-done.9, bf16[136,1024]{0,1:T(8,128)(2,1)} %collective-permute-done.4), kind=kLoop, calls=%fused_computation.34 | loop fusion | flops 7405568 | bytes 3702784 | tf_op jit(solution)/shard_map/concatenate | solution.py:96
  52.7 3.4 %fusion.8 = bf16[896,1024]{0,1:T(8,128)(2,1)S(1)} fusion(f32[1024]{0:T(1024)S(1)} %bitcast.134, f32[1024]{0:T(1024)S(1)} %bitcast.136, f32[1024]{0:T(1024)S(1)} %bitcast.132, f32[1024]{0:T(1024)S(1)} %bitcast.130, bf16[904,1024]{0,1:T(8,128)(2,1)S(1)} %pad_maximum_fusion), kind=kLoop, calls=%fused_computation.23 | loop fusion | flops 11010048 | bytes 9191424 | tf_op jit(solution)/shard_map/convert_element_type | solution.py:106
  57.8 3.0 %collective-permute-start.6 = (f32[3,256]{1,0:T(4,128)S(1)}, f32[3,256]{1,0:T(4,128)S(1)}, u32[]{:S(2)}, u32[]{:S(2)}) collective-permute-start(f32[3,256]{1,0:T(4,128)S(1)} %pad_maximum_fusion.8), channel_id=1, source_target_pairs={{0,1},{1,0},{2,3},{3,2},{4,5},{5,4},{6,7},{7,6},{8,9},{9,8},{10,11... | collective-permute-start | bytes 9224 | tf_op jit(solution)/shard_map/ppermute | solution.py:57
  62.1 1.6 %fusion.38 = (f32[256,8]{0,1:T(8,128)S(1)}, bf16[256,1024]{0,1:T(8,128)(2,1)S(1)}) fusion(f32[8,128,256]{2,1,0:T(8,128)S(1)} %get-tuple-element.39, f32[256]{0:T(256)S(1)} %fusion.48, bf16[256,1024]{0,1:T(8,128)(2,1)} %copy.69, f32[1024]{0:T(1024)S(1)} %copy-done.14, pred[256]{0:T(512)(128)(4,1)S(1)} %bitcast.162, f32[256]{0:T(256)S(1)} %bitcast.154), kind=kLoop, calls=%fused_computation.75 | loop fusion | flops 3405824 | bytes 2111744 | tf_op jit(solution)/shard_map/reduce_sum | solution.py:149
  63.7 5.2 %multiply_convert_fusion = bf16[8,256,896]{1,2,0:T(8,128)(2,1)S(1)} fusion(f32[8,256]{1,0:T(8,128)S(1)} %bitcast.161, f32[8,256,896]{1,2,0:T(8,128)} %get-tuple-element.38, f32[8,256]{1,0:T(8,128)S(1)} %get-tuple-element.37, bf16[256,8,128]{0,2,1:T(8,128)(2,1)S(1)} %bitcast.128, bf16[896,8,128]{0,2,1:T(8,128)(2,1)} %bitcast.124), kind=kOutput, calls=%fused_computation.2 | convolution fusion | flops 477102080 | bytes 13385728 | tf_op jit(solution)/shard_map/thd,uhd->htu/dot_general | solution.py:151
  73.7 3.9 %fusion.9 = (f32[1024]{0:T(1024)S(1)}, f32[1024]{0:T(1024)S(1)}, f32[1024]{0:T(1024)S(1)}, f32[1024]{0:T(1024)S(1)}) fusion(bf16[904,1024]{0,1:T(8,128)(2,1)S(1)} %pad_maximum_fusion, f32[8,128,896]{2,1,0:T(8,128)S(1)} %fusion.63), kind=kLoop, calls=%fused_computation.24 | loop fusion | flops 11005952 | bytes 11026432 | tf_op jit(solution)/shard_map/reduce_sum | solution.py:167
  77.6 2.9 %collective-permute-start.15 = (f32[4,1024]{1,0:T(4,128)S(1)}, f32[4,1024]{1,0:T(4,128)S(1)}, u32[]{:S(2)}, u32[]{:S(2)}) collective-permute-start(f32[4,1024]{1,0:T(4,128)S(1)} %get-tuple-element.29), channel_id=1, source_target_pairs={{0,6},{2,0},{4,2},{6,4},{8,14},{10,8},{12,10},{14,12},{16,22},{18,... | collective-permute-start | bytes 49160 | tf_op jit(solution)/shard_map/ppermute | solution.py:43
  80.6 1.7 %collective-permute-start.13 = (f32[4,1024]{1,0:T(4,128)S(1)}, f32[4,1024]{1,0:T(4,128)S(1)}, u32[]{:S(2)}, u32[]{:S(2)}) collective-permute-start(f32[4,1024]{1,0:T(4,128)S(1)} %get-tuple-element.29), channel_id=1, source_target_pairs={{0,2},{2,4},{4,6},{6,0},{8,10},{10,12},{12,14},{14,8},{16,18},{18,... | collective-permute-start | bytes 49160 | tf_op jit(solution)/shard_map/ppermute | solution.py:43
  84.2 2.6 %collective-permute-start.8 = (bf16[136,1024]{0,1:T(8,128)(2,1)}, bf16[136,1024]{0,1:T(8,128)(2,1)}, u32[]{:S(2)}, u32[]{:S(2)}) collective-permute-start(bf16[136,1024]{0,1:T(8,128)(2,1)} %pad_slice_fusion), channel_id=1, source_target_pairs={{2,0},{4,2},{6,4},{8,6},{10,8},{12,10},{14,12},{16,14},{18,16},{20... | collective-permute-start | bytes 835592 | tf_op jit(solution)/shard_map/ppermute | solution.py:20
  87.9 6.4 %fusion.55 = (bf16[904,1024]{0,1:T(8,128)(2,1)S(1)}, f32[904,1024]{0,1:T(8,128)}) fusion(f32[907,1024]{0,1:T(8,128)S(1)} %maximum_maximum_fusion, f32[1024]{0:T(1024)S(1)} %bitcast.135, f32[1024]{0:T(1024)S(1)} %bitcast.137, f32[1024]{0:T(1024)S(1)} %bitcast.133, f32[896,1024]{0,1:T(8,128)S(1)} %bitcast.119, f32[1024]{0:T(1024)S(1)} %bitcast.131), kind=kLoop, calls=%fused_computation.117 | loop fusion | flops 7405568 | bytes 20348928 | tf_op jit(solution)/shard_map/convert.5
  95.4 3.5 %collective-permute-start.18 = (f32[4,1024]{1,0:T(4,128)S(1)}, f32[4,1024]{1,0:T(4,128)S(1)}, u32[]{:S(2)}, u32[]{:S(2)}) collective-permute-start(f32[4,1024]{1,0:T(4,128)S(1)} %fusion.80), channel_id=1, source_target_pairs={{0,24},{2,26},{4,28},{6,30},{8,0},{10,2},{12,4},{14,6},{16,8},{18,... | collective-permute-start | bytes 49160 | tf_op jit(solution)/shard_map/ppermute | solution.py:43
  99.8 3.0 %collective-permute-start.10 = (bf16[256,1024]{0,1:T(8,128)(2,1)}, bf16[256,1024]{0,1:T(8,128)(2,1)}, u32[]{:S(2)}, u32[]{:S(2)}) collective-permute-start(bf16[256,1024]{0,1:T(8,128)(2,1)} %slice.139), channel_id=1, source_target_pairs={{0,2},{2,0},{4,6},{6,4},{8,10},{10,8},{12,14},{14,12},{16,18},{18,... | collective-permute-start | bytes 1572872 | tf_op jit(solution)/shard_map/ppermute | solution.py:25
  106.1 5.4 %collective-permute-start.20 = (f32[4,1024]{1,0:T(4,128)S(1)}, f32[4,1024]{1,0:T(4,128)S(1)}, u32[]{:S(2)}, u32[]{:S(2)}) collective-permute-start(f32[4,1024]{1,0:T(4,128)S(1)} %fusion.79), channel_id=1, source_target_pairs={{0,64},{2,66},{4,68},{6,70},{8,72},{10,74},{12,76},{14,78},{16,80}... | collective-permute-start | bytes 49160 | tf_op jit(solution)/shard_map/ppermute | solution.py:43
  111.5 2.4 %collective-permute-start.19 = (f32[4,1024]{1,0:T(4,128)S(1)}, f32[4,1024]{1,0:T(4,128)S(1)}, u32[]{:S(2)}, u32[]{:S(2)}) collective-permute-start(f32[4,1024]{1,0:T(4,128)S(1)} %fusion.79), channel_id=1, source_target_pairs={{0,32},{2,34},{4,36},{6,38},{8,40},{10,42},{12,44},{14,46},{16,48}... | collective-permute-start | bytes 49160 | tf_op jit(solution)/shard_map/ppermute | solution.py:43
  113.9 4.2 %collective-permute-start.11 = (bf16[136,1024]{0,1:T(8,128)(2,1)}, bf16[136,1024]{0,1:T(8,128)(2,1)S(1)}, u32[]{:S(2)}, u32[]{:S(2)}) collective-permute-start(bf16[136,1024]{0,1:T(8,128)(2,1)} %slice.141), channel_id=1, source_target_pairs={{2,0},{4,2},{6,4},{8,6},{10,8},{12,10},{14,12},{16,14},{18,16},{20... | collective-permute-start | bytes 835592 | tf_op jit(solution)/shard_map/ppermute | solution.py:20
  119.6 4.9 %collective-permute-start.9 = (bf16[256,1024]{0,1:T(8,128)(2,1)S(1)}, bf16[256,1024]{0,1:T(8,128)(2,1)S(1)}, u32[]{:S(2)}, u32[]{:S(2)}) collective-permute-start(bf16[256,1024]{0,1:T(8,128)(2,1)S(1)} %fusion.28), channel_id=1, source_target_pairs={{4,0},{6,2},{8,4},{10,6},{12,8},{14,10},{16,12},{18,14},{20,16},{2... | collective-permute-start | bytes 1572872 | tf_op jit(solution)/shard_map/ppermute | solution.py:20
  124.5 3.0 %collective-permute-done.11 = bf16[136,1024]{0,1:T(8,128)(2,1)S(1)} collective-permute-done((bf16[136,1024]{0,1:T(8,128)(2,1)}, bf16[136,1024]{0,1:T(8,128)(2,1)S(1)}, u32[]{:S(2)}, u32[]{:S(2)}) %collective-permute-start.11) | collective-permute-done | bytes 278560 | tf_op jit(solution)/shard_map/ppermute | solution.py:20
  127.5 2.9 %fusion.33 = bf16[256,1024]{0,1:T(8,128)(2,1)} fusion(bf16[256,1024]{0,1:T(8,128)(2,1)} %collective-permute-done.10, f32[904,1024]{0,1:T(8,128)} %get-tuple-element.23, bf16[136,1024]{0,1:T(8,128)(2,1)S(1)} %collective-permute-done.11, pred[]{:T(512)S(6)} %eq.47), kind=kLoop, calls=%fused_computation.62 | loop fusion | flops 1572864 | bytes 2375681 | tf_op jit(solution)/shard_map/convert_element_type | solution.py:195
  130.4 6.2 %collective-permute-start.12 = (bf16[256,1024]{0,1:T(8,128)(2,1)}, bf16[256,1024]{0,1:T(8,128)(2,1)}, u32[]{:S(2)}, u32[]{:S(2)}) collective-permute-start(bf16[256,1024]{0,1:T(8,128)(2,1)} %fusion.33), channel_id=1, source_target_pairs={{4,0},{6,2},{8,4},{10,6},{12,8},{14,10},{16,12},{18,14},{20,16},{2... | collective-permute-start | bytes 1572872 | tf_op jit(solution)/shard_map/ppermute | solution.py:20
  136.6 5.3 %collective-permute-start.22 = (f32[4,1024]{1,0:T(4,128)S(1)}, f32[4,1024]{1,0:T(4,128)S(1)}, u32[]{:S(2)}, u32[]{:S(2)}) collective-permute-start(f32[4,1024]{1,0:T(4,128)S(1)} %fusion.78), channel_id=1, source_target_pairs={{0,128},{2,130},{4,132},{6,134},{8,136},{10,138},{12,140},{14,142}... | collective-permute-start | bytes 49160 | tf_op jit(solution)/shard_map/ppermute | solution.py:43
  142.0 11.6 %collective-permute-done.22 = f32[4,1024]{1,0:T(4,128)S(1)} collective-permute-done((f32[4,1024]{1,0:T(4,128)S(1)}, f32[4,1024]{1,0:T(4,128)S(1)}, u32[]{:S(2)}, u32[]{:S(2)}) %collective-permute-start.22) | collective-permute-done | bytes 16416 | tf_op jit(solution)/shard_map/ppermute | solution.py:43
  155.4 2.0 %fusion.31 = bf16[256,1024]{0,1:T(8,128)(2,1)S(1)} fusion(bf16[256,1024]{0,1:T(8,128)(2,1)} %collective-permute-done.10, f32[904,1024]{0,1:T(8,128)} %get-tuple-element.23, bf16[256,1024]{0,1:T(8,128)(2,1)} %collective-permute-done.12, pred[]{:T(512)S(6)} %eq.47), kind=kLoop, calls=%fused_computation.60 | loop fusion | flops 1572864 | bytes 2621441 | tf_op jit(solution)/shard_map/convert_element_type | solution.py:204
  (112 shorter events, 33.2 us)
Async XLA Ops:
  0.6 22.5 %copy-start.15 = (s32[2,64]{1,0:T(2,128)S(1)}, s32[2,64]{1,0:T(2,128)}, u32[]{:S(2)}) copy-start(s32[2,64]{1,0:T(2,128)} %param.15) | copy-start | bytes 1540
  1.9 17.7 %collective-permute-start = (bf16[256,1024]{0,1:T(8,128)(2,1)S(1)}, bf16[256,1024]{0,1:T(8,128)(2,1)S(1)}, u32[]{:S(2)}, u32[]{:S(2)}) collective-permute-start(bf16[256,1024]{0,1:T(8,128)(2,1)S(1)} %copy.59), channel_id=1, source_target_pairs={{0,4},{2,6},{4,8},{6,10},{8,12},{10,14},{12,16},{14,18},{16,20},{1... | collective-permute-start | bytes 1572872 | tf_op jit(solution)/shard_map/ppermute | solution.py:20
  6.4 28.0 %copy-start.6 = (bf16[256,1024]{0,1:T(8,128)(2,1)}, bf16[256,1024]{0,1:T(8,128)(2,1)S(1)}, u32[]{:S(2)}) copy-start(bf16[256,1024]{0,1:T(8,128)(2,1)S(1)} %copy.65) | copy-start | bytes 1572868
  6.4 24.5 %collective-permute-start.3 = (bf16[256,1024]{0,1:T(8,128)(2,1)S(1)}, bf16[256,1024]{0,1:T(8,128)(2,1)S(1)}, u32[]{:S(2)}, u32[]{:S(2)}) collective-permute-start(bf16[256,1024]{0,1:T(8,128)(2,1)S(1)} %copy.65), channel_id=1, source_target_pairs={{0,4},{2,6},{4,8},{6,10},{8,12},{10,14},{12,16},{14,18},{16,20},{1... | collective-permute-start | bytes 1572872 | tf_op jit(solution)/shard_map/ppermute | solution.py:20
  20.4 16.6 %collective-permute-start.2 = (bf16[256,1024]{0,1:T(8,128)(2,1)}, bf16[256,1024]{0,1:T(8,128)(2,1)}, u32[]{:S(2)}, u32[]{:S(2)}) collective-permute-start(bf16[256,1024]{0,1:T(8,128)(2,1)} %broadcast_select_fusion.1), channel_id=1, source_target_pairs={{0,2},{2,0},{4,6},{6,4},{8,10},{10,8},{12,14},{14,12},{16,18},{18,... | collective-permute-start | bytes 1572872 | tf_op jit(solution)/shard_map/ppermute | solution.py:25
  24.3 12.0 %collective-permute-start.1 = (bf16[136,1024]{0,1:T(8,128)(2,1)}, bf16[136,1024]{0,1:T(8,128)(2,1)S(1)}, u32[]{:S(2)}, u32[]{:S(2)}) collective-permute-start(bf16[136,1024]{0,1:T(8,128)(2,1)} %slice.123), channel_id=1, source_target_pairs={{0,2},{2,4},{4,6},{6,8},{8,10},{10,12},{12,14},{14,16},{16,18},{18... | collective-permute-start | bytes 835592 | tf_op jit(solution)/shard_map/ppermute | solution.py:20
  27.7 11.0 %copy-start.10 = (bf16[256,1024]{0,1:T(8,128)(2,1)}, bf16[256,1024]{0,1:T(8,128)(2,1)S(1)}, u32[]{:S(2)}) copy-start(bf16[256,1024]{0,1:T(8,128)(2,1)S(1)} %copy.88) | copy-start | bytes 1572868
  30.9 5.4 %copy-start.8 = (bf16[256,1024]{0,1:T(8,128)(2,1)}, bf16[256,1024]{0,1:T(8,128)(2,1)S(1)}, u32[]{:S(2)}) copy-start(bf16[256,1024]{0,1:T(8,128)(2,1)S(1)} %collective-permute-done.3) | copy-start | bytes 1572868
  31.8 17.8 %collective-permute-start.5 = (bf16[256,1024]{0,1:T(8,128)(2,1)}, bf16[256,1024]{0,1:T(8,128)(2,1)}, u32[]{:S(2)}, u32[]{:S(2)}) collective-permute-start(bf16[256,1024]{0,1:T(8,128)(2,1)} %broadcast_select_fusion), channel_id=1, source_target_pairs={{0,2},{2,0},{4,6},{6,4},{8,10},{10,8},{12,14},{14,12},{16,18},{18,... | collective-permute-start | bytes 1572872 | tf_op jit(solution)/shard_map/ppermute | solution.py:25
  34.3 15.3 %collective-permute-start.4 = (bf16[136,1024]{0,1:T(8,128)(2,1)}, bf16[136,1024]{0,1:T(8,128)(2,1)}, u32[]{:S(2)}, u32[]{:S(2)}) collective-permute-start(bf16[136,1024]{0,1:T(8,128)(2,1)} %slice.124), channel_id=1, source_target_pairs={{0,2},{2,4},{4,6},{6,8},{8,10},{10,12},{12,14},{14,16},{16,18},{18... | collective-permute-start | bytes 835592 | tf_op jit(solution)/shard_map/ppermute | solution.py:20
  38.7 7.1 %copy-start.2 = (bf16[896,1024]{0,1:T(8,128)(2,1)}, bf16[896,1024]{0,1:T(8,128)(2,1)S(1)}, u32[]{:S(2)}) copy-start(bf16[896,1024]{0,1:T(8,128)(2,1)S(1)} %pad_maximum_fusion.1) | copy-start | bytes 5505028
  45.8 3.9 %copy-start.9 = (bf16[256,1024]{0,1:T(8,128)(2,1)S(1)}, bf16[256,1024]{0,1:T(8,128)(2,1)}, u32[]{:S(2)}) copy-start(bf16[256,1024]{0,1:T(8,128)(2,1)} %copy-done.8) | copy-start | bytes 1572868
  49.6 6.5 %copy-start = (bf16[8,256,896]{1,2,0:T(8,128)(2,1)}, bf16[8,256,896]{1,2,0:T(8,128)(2,1)S(1)}, u32[]{:S(2)}) copy-start(bf16[8,256,896]{1,2,0:T(8,128)(2,1)S(1)} %fusion.16) | copy-start | bytes 11010052
  57.8 4.2 %collective-permute-start.6 = (f32[3,256]{1,0:T(4,128)S(1)}, f32[3,256]{1,0:T(4,128)S(1)}, u32[]{:S(2)}, u32[]{:S(2)}) collective-permute-start(f32[3,256]{1,0:T(4,128)S(1)} %pad_maximum_fusion.8), channel_id=1, source_target_pairs={{0,1},{1,0},{2,3},{3,2},{4,5},{5,4},{6,7},{7,6},{8,9},{9,8},{10,11... | collective-permute-start | bytes 9224 | tf_op jit(solution)/shard_map/ppermute | solution.py:57
  63.7 5.2 %copy-start.3 = (bf16[896,1024]{0,1:T(8,128)(2,1)S(1)}, bf16[896,1024]{0,1:T(8,128)(2,1)}, u32[]{:S(2)}) copy-start(bf16[896,1024]{0,1:T(8,128)(2,1)} %copy-done.2) | copy-start | bytes 5505028
  77.6 17.7 %collective-permute-start.15 = (f32[4,1024]{1,0:T(4,128)S(1)}, f32[4,1024]{1,0:T(4,128)S(1)}, u32[]{:S(2)}, u32[]{:S(2)}) collective-permute-start(f32[4,1024]{1,0:T(4,128)S(1)} %get-tuple-element.29), channel_id=1, source_target_pairs={{0,6},{2,0},{4,2},{6,4},{8,14},{10,8},{12,10},{14,12},{16,22},{18,... | collective-permute-start | bytes 49160 | tf_op jit(solution)/shard_map/ppermute | solution.py:43
  80.6 14.8 %collective-permute-start.14 = (f32[4,1024]{1,0:T(4,128)S(1)}, f32[4,1024]{1,0:T(4,128)S(1)}, u32[]{:S(2)}, u32[]{:S(2)}) collective-permute-start(f32[4,1024]{1,0:T(4,128)S(1)} %get-tuple-element.29), channel_id=1, source_target_pairs={{0,4},{2,6},{4,0},{6,2},{8,12},{10,14},{12,8},{14,10},{16,20},{18,... | collective-permute-start | bytes 49160 | tf_op jit(solution)/shard_map/ppermute | solution.py:43
  80.6 14.8 %collective-permute-start.13 = (f32[4,1024]{1,0:T(4,128)S(1)}, f32[4,1024]{1,0:T(4,128)S(1)}, u32[]{:S(2)}, u32[]{:S(2)}) collective-permute-start(f32[4,1024]{1,0:T(4,128)S(1)} %get-tuple-element.29), channel_id=1, source_target_pairs={{0,2},{2,4},{4,6},{6,0},{8,10},{10,12},{12,14},{14,8},{16,18},{18,... | collective-permute-start | bytes 49160 | tf_op jit(solution)/shard_map/ppermute | solution.py:43
  83.1 35.0 %collective-permute-start.7 = (bf16[256,1024]{0,1:T(8,128)(2,1)}, bf16[256,1024]{0,1:T(8,128)(2,1)S(1)}, u32[]{:S(2)}, u32[]{:S(2)}) collective-permute-start(bf16[256,1024]{0,1:T(8,128)(2,1)} %bitcast.26), channel_id=1, source_target_pairs={{0,2},{2,0},{4,6},{6,4},{8,10},{10,8},{12,14},{14,12},{16,18},{18,... | collective-permute-start | bytes 1572872 | tf_op jit(solution)/shard_map/ppermute | solution.py:25
  84.2 34.0 %collective-permute-start.8 = (bf16[136,1024]{0,1:T(8,128)(2,1)}, bf16[136,1024]{0,1:T(8,128)(2,1)}, u32[]{:S(2)}, u32[]{:S(2)}) collective-permute-start(bf16[136,1024]{0,1:T(8,128)(2,1)} %pad_slice_fusion), channel_id=1, source_target_pairs={{2,0},{4,2},{6,4},{8,6},{10,8},{12,10},{14,12},{16,14},{18,16},{20... | collective-permute-start | bytes 835592 | tf_op jit(solution)/shard_map/ppermute | solution.py:20
  94.3 10.8 %copy-start.12 = (bf16[8,128,256]{2,1,0:T(8,128)(2,1)S(1)}, bf16[8,128,256]{2,1,0:T(8,128)(2,1)}, u32[]{:S(2)}) copy-start(bf16[8,128,256]{2,1,0:T(8,128)(2,1)} %fusion.17) | copy-start | bytes 1572868
  95.4 4.4 %collective-permute-start.18 = (f32[4,1024]{1,0:T(4,128)S(1)}, f32[4,1024]{1,0:T(4,128)S(1)}, u32[]{:S(2)}, u32[]{:S(2)}) collective-permute-start(f32[4,1024]{1,0:T(4,128)S(1)} %fusion.80), channel_id=1, source_target_pairs={{0,24},{2,26},{4,28},{6,30},{8,0},{10,2},{12,4},{14,6},{16,8},{18,... | collective-permute-start | bytes 49160 | tf_op jit(solution)/shard_map/ppermute | solution.py:43
  98.9 3.9 %collective-permute-start.17 = (f32[4,1024]{1,0:T(4,128)S(1)}, f32[4,1024]{1,0:T(4,128)S(1)}, u32[]{:S(2)}, u32[]{:S(2)}) collective-permute-start(f32[4,1024]{1,0:T(4,128)S(1)} %fusion.80), channel_id=1, source_target_pairs={{0,16},{2,18},{4,20},{6,22},{8,24},{10,26},{12,28},{14,30},{16,0},... | collective-permute-start | bytes 49160 | tf_op jit(solution)/shard_map/ppermute | solution.py:43
  98.9 5.0 %collective-permute-start.16 = (f32[4,1024]{1,0:T(4,128)S(1)}, f32[4,1024]{1,0:T(4,128)S(1)}, u32[]{:S(2)}, u32[]{:S(2)}) collective-permute-start(f32[4,1024]{1,0:T(4,128)S(1)} %fusion.80), channel_id=1, source_target_pairs={{0,8},{2,10},{4,12},{6,14},{8,16},{10,18},{12,20},{14,22},{16,24},... | collective-permute-start | bytes 49160 | tf_op jit(solution)/shard_map/ppermute | solution.py:43
  99.8 27.7 %collective-permute-start.10 = (bf16[256,1024]{0,1:T(8,128)(2,1)}, bf16[256,1024]{0,1:T(8,128)(2,1)}, u32[]{:S(2)}, u32[]{:S(2)}) collective-permute-start(bf16[256,1024]{0,1:T(8,128)(2,1)} %slice.139), channel_id=1, source_target_pairs={{0,2},{2,0},{4,6},{6,4},{8,10},{10,8},{12,14},{14,12},{16,18},{18,... | collective-permute-start | bytes 1572872 | tf_op jit(solution)/shard_map/ppermute | solution.py:25
  104.0 7.5 %collective-permute-start.21 = (f32[4,1024]{1,0:T(4,128)S(1)}, f32[4,1024]{1,0:T(4,128)S(1)}, u32[]{:S(2)}, u32[]{:S(2)}) collective-permute-start(f32[4,1024]{1,0:T(4,128)S(1)} %fusion.79), channel_id=1, source_target_pairs={{0,96},{2,98},{4,100},{6,102},{8,104},{10,106},{12,108},{14,110},{... | collective-permute-start | bytes 49160 | tf_op jit(solution)/shard_map/ppermute | solution.py:43
  106.1 7.8 %collective-permute-start.20 = (f32[4,1024]{1,0:T(4,128)S(1)}, f32[4,1024]{1,0:T(4,128)S(1)}, u32[]{:S(2)}, u32[]{:S(2)}) collective-permute-start(f32[4,1024]{1,0:T(4,128)S(1)} %fusion.79), channel_id=1, source_target_pairs={{0,64},{2,66},{4,68},{6,70},{8,72},{10,74},{12,76},{14,78},{16,80}... | collective-permute-start | bytes 49160 | tf_op jit(solution)/shard_map/ppermute | solution.py:43
  111.5 6.6 %collective-permute-start.19 = (f32[4,1024]{1,0:T(4,128)S(1)}, f32[4,1024]{1,0:T(4,128)S(1)}, u32[]{:S(2)}, u32[]{:S(2)}) collective-permute-start(f32[4,1024]{1,0:T(4,128)S(1)} %fusion.79), channel_id=1, source_target_pairs={{0,32},{2,34},{4,36},{6,38},{8,40},{10,42},{12,44},{14,46},{16,48}... | collective-permute-start | bytes 49160 | tf_op jit(solution)/shard_map/ppermute | solution.py:43
  113.9 13.7 %collective-permute-start.11 = (bf16[136,1024]{0,1:T(8,128)(2,1)}, bf16[136,1024]{0,1:T(8,128)(2,1)S(1)}, u32[]{:S(2)}, u32[]{:S(2)}) collective-permute-start(bf16[136,1024]{0,1:T(8,128)(2,1)} %slice.141), channel_id=1, source_target_pairs={{2,0},{4,2},{6,4},{8,6},{10,8},{12,10},{14,12},{16,14},{18,16},{20... | collective-permute-start | bytes 835592 | tf_op jit(solution)/shard_map/ppermute | solution.py:20
  119.6 34.6 %collective-permute-start.9 = (bf16[256,1024]{0,1:T(8,128)(2,1)S(1)}, bf16[256,1024]{0,1:T(8,128)(2,1)S(1)}, u32[]{:S(2)}, u32[]{:S(2)}) collective-permute-start(bf16[256,1024]{0,1:T(8,128)(2,1)S(1)} %fusion.28), channel_id=1, source_target_pairs={{4,0},{6,2},{8,4},{10,6},{12,8},{14,10},{16,12},{18,14},{20,16},{2... | collective-permute-start | bytes 1572872 | tf_op jit(solution)/shard_map/ppermute | solution.py:20
  130.4 25.0 %collective-permute-start.12 = (bf16[256,1024]{0,1:T(8,128)(2,1)}, bf16[256,1024]{0,1:T(8,128)(2,1)}, u32[]{:S(2)}, u32[]{:S(2)}) collective-permute-start(bf16[256,1024]{0,1:T(8,128)(2,1)} %fusion.33), channel_id=1, source_target_pairs={{4,0},{6,2},{8,4},{10,6},{12,8},{14,10},{16,12},{18,14},{20,16},{2... | collective-permute-start | bytes 1572872 | tf_op jit(solution)/shard_map/ppermute | solution.py:20
  136.6 17.0 %collective-permute-start.22 = (f32[4,1024]{1,0:T(4,128)S(1)}, f32[4,1024]{1,0:T(4,128)S(1)}, u32[]{:S(2)}, u32[]{:S(2)}) collective-permute-start(f32[4,1024]{1,0:T(4,128)S(1)} %fusion.78), channel_id=1, source_target_pairs={{0,128},{2,130},{4,132},{6,134},{8,136},{10,138},{12,140},{14,142}... | collective-permute-start | bytes 49160 | tf_op jit(solution)/shard_map/ppermute | solution.py:43
  (7 other events, 14.8 us)

commit v12 on v5

--- a/solution.py
+++ b/solution.py
@@ -29,10 +29,10 @@
     size = lax.axis_size(axis)
     if size & (size - 1):
         return lax.psum(block, axis)
-    stride = size // 2
-    while stride >= 1:
+    stride = 1
+    while stride < size:
         block = block + lax.ppermute(block, axis, [(i, i ^ stride) for i in range(size)])
-        stride //= 2
+        stride *= 2
     return block
 
 
@@ -74,13 +74,16 @@
     far_lead = 8
     key_count = REACH * row_count + (row_count - far_rows)
 
-    def relay(own):
+    def relay(own, direct_third=False):
         second = from_behind(own, "tm", 2)
         first = chip_swap(jnp.where(even, own, second), "tm")
-        third = from_behind(second[far_rows - far_lead :], "tm", 1)
+        if direct_third:
+            third = from_behind(own[far_rows - far_lead :], "tm", REACH)
+        else:
+            third = from_behind(second[far_rows - far_lead :], "tm", 1)
         return jnp.concatenate([third, second, first, own], 0)
 
-    key_win = relay(keys)[far_lead:]
+    key_win = relay(keys, direct_third=True)[far_lead:]
     vin_win = relay(values_in)
 
     conv_sum = jnp.zeros((key_count, channels), jnp.float32)

time: 144 us -> 152 us (1.056)
  starting transfers between devices: 34.7 us -> 44.2 us
  waiting for transfers between devices: 49.8 us -> 46.9 us
    ppermute x7, starting transfers between devices: 14.8 us -> 24.3 us  [all_sum(): lax.ppermute(block, axis, [(i, i ^ stride) for i in range(size)])]
    ppermute x7, waiting for transfers between devices: 17.1 us -> 12.1 us  [all_sum(): lax.ppermute(block, axis, [(i, i ^ stride) for i in range(size)])]
    ppermute x8, waiting for transfers between devices: 28.2 us -> 30.4 us  [from_behind(): return lax.ppermute(block, axis, route)]
    unnamed x37 -> x35, local copies, waits for them, and re-layouts: 8.42 us -> 8.42 us
  transfers between devices with their start and end apart: 20 -> 20, of which waited for: 10 -> 8; matrix products, arithmetic and copies ran while one was open for 28% -> 27% of each run, Pallas kernels for 0% -> 0%
where the time goes in v12:
time: 152 us; the launch traced here: 150 us
  waiting for transfers between devices  46.9 us (31%)
  starting transfers between devices  44.2 us (29%)
  other arithmetic  31.7 us (21%)
  local copies, waits for them, and re-layouts  13.2 us (9%)
  matrix products  12.7 us (8%)
    ppermute x8, waiting for transfers between devices, from_behind(): return lax.ppermute(block, axis, route)  30.4 us
    ppermute x7, starting transfers between devices, all_sum(): lax.ppermute(block, axis, [(i, i ^ stride) for i in range(size)])  24.3 us
    ppermute x8, starting transfers between devices, from_behind(): return lax.ppermute(block, axis, route)  17.7 us
    ppermute x7, waiting for transfers between devices, all_sum(): lax.ppermute(block, axis, [(i, i ^ stride) for i in range(size)])  12.1 us
    unnamed x35, local copies, waits for them, and re-layouts  8.42 us
    sub x1, matrix products, body(): expo = jnp.where(mask[None], jnp.exp(scores - row_peak[..., None]), 0.0)  7.3 us
    another operation x1, other arithmetic  5.18 us
    ppermute x1, waiting for transfers between devices, pair_sum(): return block + lax.ppermute(block, axis, [(0, 1), (1, 0)])  4.41 us
  transfers between devices with their start and end apart: 20, of which 8 were waited for; matrix products, arithmetic and copies ran while one was open for 27% of the time, Pallas kernels for 0%

profile of v12, /device:TPU:4, one launch (start us, length us, event | category | flops | bytes accessed | tf_op | source)
XLA Modules:
  0.0 149.9 jit_solution(4395523279662961004)
XLA Ops:
  0.6 1.3 copy.60
  1.9 3.5 %collective-permute-start.1 = (bf16[256,1024]{0,1:T(8,128)(2,1)S(1)}, bf16[256,1024]{0,1:T(8,128)(2,1)S(1)}, u32[]{:S(2)}, u32[]{:S(2)}) collective-permute-start(bf16[256,1024]{0,1:T(8,128)(2,1)S(1)} %copy.60), channel_id=1, source_target_pairs={{0,4},{2,6},{4,8},{6,10},{8,12},{10,14},{12,16},{14,18},{16,20},{1... | collective-permute-start | bytes 1572872 | tf_op jit(solution)/shard_map/ppermute | solution.py:20
  6.5 2.6 %collective-permute-start = (bf16[136,1024]{0,1:T(8,128)(2,1)}, bf16[136,1024]{0,1:T(8,128)(2,1)S(1)}, u32[]{:S(2)}, u32[]{:S(2)}) collective-permute-start(bf16[136,1024]{0,1:T(8,128)(2,1)} %slice.123), channel_id=1, source_target_pairs={{0,6},{2,8},{4,10},{6,12},{8,14},{10,16},{12,18},{14,20},{16,22},{... | collective-permute-start | bytes 835592 | tf_op jit(solution)/shard_map/ppermute | solution.py:20
  10.4 3.2 %collective-permute-start.3 = (bf16[256,1024]{0,1:T(8,128)(2,1)S(1)}, bf16[256,1024]{0,1:T(8,128)(2,1)S(1)}, u32[]{:S(2)}, u32[]{:S(2)}) collective-permute-start(bf16[256,1024]{0,1:T(8,128)(2,1)S(1)} %copy.67), channel_id=1, source_target_pairs={{0,4},{2,6},{4,8},{6,10},{8,12},{10,14},{12,16},{14,18},{16,20},{1... | collective-permute-start | bytes 1572872 | tf_op jit(solution)/shard_map/ppermute | solution.py:20
  15.6 2.2 %collective-permute-done.1 = bf16[256,1024]{0,1:T(8,128)(2,1)S(1)} collective-permute-done((bf16[256,1024]{0,1:T(8,128)(2,1)S(1)}, bf16[256,1024]{0,1:T(8,128)(2,1)S(1)}, u32[]{:S(2)}, u32[]{:S(2)}) %collective-permute-start.1) | collective-permute-done | bytes 524320 | tf_op jit(solution)/shard_map/ppermute | solution.py:20
  21.9 17.2 %collective-permute-done.3 = bf16[256,1024]{0,1:T(8,128)(2,1)S(1)} collective-permute-done((bf16[256,1024]{0,1:T(8,128)(2,1)S(1)}, bf16[256,1024]{0,1:T(8,128)(2,1)S(1)}, u32[]{:S(2)}, u32[]{:S(2)}) %collective-permute-start.3) | collective-permute-done | bytes 524320 | tf_op jit(solution)/shard_map/ppermute | solution.py:20
  41.0 3.2 %collective-permute-start.4 = (bf16[136,1024]{0,1:T(8,128)(2,1)}, bf16[136,1024]{0,1:T(8,128)(2,1)}, u32[]{:S(2)}, u32[]{:S(2)}) collective-permute-start(bf16[136,1024]{0,1:T(8,128)(2,1)} %slice.124), channel_id=1, source_target_pairs={{0,2},{2,4},{4,6},{6,8},{8,10},{10,12},{12,14},{14,16},{16,18},{18... | collective-permute-start | bytes 835592 | tf_op jit(solution)/shard_map/ppermute | solution.py:20
  45.1 1.7 %pad_maximum_fusion.1 = bf16[896,1024]{0,1:T(8,128)(2,1)S(1)} fusion(bf16[256,1024]{0,1:T(8,128)(2,1)S(1)} %copy.60, bf16[256,1024]{0,1:T(8,128)(2,1)} %collective-permute-done.2, bf16[256,1024]{0,1:T(8,128)(2,1)} %copy-done.4, bf16[136,1024]{0,1:T(8,128)(2,1)} %copy-done.8), kind=kLoop, calls=%fused_computation.36 | loop fusion | flops 7340032 | bytes 3686400 | tf_op jit(solution)/shard_map/concatenate | solution.py:84
  46.8 7.3 %fusion.57 = (f32[8,256]{1,0:T(8,128)S(1)}, f32[8,256,896]{1,2,0:T(8,128)}) fusion(pred[256,896]{0,1:T(8,128)(4,1)} %fusion.39, bf16[896,8,128]{0,2,1:T(8,128)(2,1)S(1)} %bitcast.103, bf16[256,8,128]{0,2,1:T(8,128)(2,1)} %bitcast.107), kind=kOutput, calls=%fused_computation.107 | convolution fusion | flops 478937984 | bytes 9936896 | tf_op jit(solution)/shard_map/sub | solution.py:107
  54.1 3.8 %fusion.16 = bf16[8,256,896]{1,2,0:T(8,128)(2,1)S(1)} fusion(f32[8,256,896]{1,2,0:T(8,128)} %get-tuple-element.36, f32[8,256]{1,0:T(8,128)S(1)} %get-tuple-element.35), kind=kLoop, calls=%fused_computation.33 | loop fusion | flops 3670016 | bytes 11018240 | tf_op jit(solution)/shard_map/convert_element_type | solution.py:110
  57.9 2.2 %pad_maximum_fusion = bf16[904,1024]{0,1:T(8,128)(2,1)S(1)} fusion(bf16[256,1024]{0,1:T(8,128)(2,1)S(1)} %copy.67, bf16[256,1024]{0,1:T(8,128)(2,1)} %collective-permute-done.5, bf16[256,1024]{0,1:T(8,128)(2,1)S(1)} %copy-done.2, bf16[136,1024]{0,1:T(8,128)(2,1)} %collective-permute-done.4), kind=kLoop, calls=%fused_computation.34 | loop fusion | flops 7405568 | bytes 3702784 | tf_op jit(solution)/shard_map/concatenate | solution.py:84
  60.2 3.4 %fusion.8 = bf16[896,1024]{0,1:T(8,128)(2,1)S(1)} fusion(f32[1024]{0:T(1024)S(1)} %bitcast.129, f32[1024]{0:T(1024)S(1)} %bitcast.131, f32[1024]{0:T(1024)S(1)} %bitcast.127, f32[1024]{0:T(1024)S(1)} %bitcast.125, bf16[904,1024]{0,1:T(8,128)(2,1)S(1)} %pad_maximum_fusion), kind=kLoop, calls=%fused_computation.23 | loop fusion | flops 11010048 | bytes 9191424 | tf_op jit(solution)/shard_map/convert_element_type | solution.py:94
  65.6 4.4 %collective-permute-done.6 = f32[3,256]{1,0:T(4,128)S(1)} collective-permute-done((f32[3,256]{1,0:T(4,128)S(1)}, f32[3,256]{1,0:T(4,128)S(1)}, u32[]{:S(2)}, u32[]{:S(2)}) %collective-permute-start.6) | collective-permute-done | bytes 3104 | tf_op jit(solution)/shard_map/ppermute | solution.py:42
  71.8 3.9 %fusion.9 = (f32[1024]{0:T(1024)S(1)}, f32[1024]{0:T(1024)S(1)}, f32[1024]{0:T(1024)S(1)}, f32[1024]{0:T(1024)S(1)}) fusion(bf16[904,1024]{0,1:T(8,128)(2,1)S(1)} %pad_maximum_fusion, f32[8,128,896]{2,1,0:T(8,128)S(1)} %fusion.59), kind=kLoop, calls=%fused_computation.24 | loop fusion | flops 11005952 | bytes 11026432 | tf_op jit(solution)/shard_map/reduce_sum | solution.py:155
  76.0 1.5 multiply_convert_fusion
  77.5 1.7 %collective-permute-start.14 = (f32[4,1024]{1,0:T(4,128)S(1)}, f32[4,1024]{1,0:T(4,128)S(1)}, u32[]{:S(2)}, u32[]{:S(2)}) collective-permute-start(f32[4,1024]{1,0:T(4,128)S(1)} %fusion.50), channel_id=1, source_target_pairs={{0,4},{2,6},{4,0},{6,2},{8,12},{10,14},{12,8},{14,10},{16,20},{18,... | collective-permute-start | bytes 49160 | tf_op jit(solution)/shard_map/ppermute | solution.py:34
  81.4 8.3 %collective-permute-start.15 = (f32[4,1024]{1,0:T(4,128)S(1)}, f32[4,1024]{1,0:T(4,128)S(1)}, u32[]{:S(2)}, u32[]{:S(2)}) collective-permute-start(f32[4,1024]{1,0:T(4,128)S(1)} %fusion.74), channel_id=1, source_target_pairs={{0,8},{2,10},{4,12},{6,14},{8,0},{10,2},{12,4},{14,6},{16,24},{18,... | collective-permute-start | bytes 49160 | tf_op jit(solution)/shard_map/ppermute | solution.py:34
  91.4 3.0 %collective-permute-start.16 = (f32[4,1024]{1,0:T(4,128)S(1)}, f32[4,1024]{1,0:T(4,128)S(1)}, u32[]{:S(2)}, u32[]{:S(2)}) collective-permute-start(f32[4,1024]{1,0:T(4,128)S(1)} %add.164), channel_id=1, source_target_pairs={{0,16},{2,18},{4,20},{6,22},{8,24},{10,26},{12,28},{14,30},{16,0},... | collective-permute-start | bytes 49160 | tf_op jit(solution)/shard_map/ppermute | solution.py:34
  94.4 5.2 %fusion.51 = (bf16[904,1024]{0,1:T(8,128)(2,1)S(1)}, f32[904,1024]{0,1:T(8,128)S(1)}) fusion(f32[907,1024]{0,1:T(8,128)S(1)} %maximum_maximum_fusion, f32[1024]{0:T(1024)S(1)} %bitcast.130, f32[1024]{0:T(1024)S(1)} %bitcast.132, f32[1024]{0:T(1024)S(1)} %bitcast.128, f32[896,1024]{0,1:T(8,128)S(1)} %bitcast.99, f32[1024]{0:T(1024)S(1)} %bitcast.126), kind=kLoop, calls=%fused_computation.103 | loop fusion | flops 7405568 | bytes 20348928 | tf_op jit(solution)/shard_map/convert.5
  99.6 2.2 %collective-permute-start.17 = (f32[4,1024]{1,0:T(4,128)S(1)}, f32[4,1024]{1,0:T(4,128)S(1)}, u32[]{:S(2)}, u32[]{:S(2)}) collective-permute-start(f32[4,1024]{1,0:T(4,128)S(1)} %add.165), channel_id=1, source_target_pairs={{0,32},{2,34},{4,36},{6,38},{8,40},{10,42},{12,44},{14,46},{16,48}... | collective-permute-start | bytes 49160 | tf_op jit(solution)/shard_map/ppermute | solution.py:34
  102.4 1.3 collective-permute-start.8
  104.9 1.3 collective-permute-start.11
  106.2 6.2 %collective-permute-start.18 = (f32[4,1024]{1,0:T(4,128)S(1)}, f32[4,1024]{1,0:T(4,128)S(1)}, u32[]{:S(2)}, u32[]{:S(2)}) collective-permute-start(f32[4,1024]{1,0:T(4,128)S(1)} %add.166), channel_id=1, source_target_pairs={{0,64},{2,66},{4,68},{6,70},{8,72},{10,74},{12,76},{14,78},{16,80}... | collective-permute-start | bytes 49160 | tf_op jit(solution)/shard_map/ppermute | solution.py:34
  112.6 10.9 %collective-permute-done.18 = f32[4,1024]{1,0:T(4,128)S(1)} collective-permute-done((f32[4,1024]{1,0:T(4,128)S(1)}, f32[4,1024]{1,0:T(4,128)S(1)}, u32[]{:S(2)}, u32[]{:S(2)}) %collective-permute-start.18) | collective-permute-done | bytes 16416 | tf_op jit(solution)/shard_map/ppermute | solution.py:34
  123.5 2.5 %collective-permute-start.19 = (f32[4,1024]{1,0:T(4,128)S(1)}, f32[4,1024]{1,0:T(4,128)S(1)}, u32[]{:S(2)}, u32[]{:S(2)}) collective-permute-start(f32[4,1024]{1,0:T(4,128)S(1)} %add.167), channel_id=1, source_target_pairs={{0,128},{2,130},{4,132},{6,134},{8,136},{10,138},{12,140},{14,142}... | collective-permute-start | bytes 49160 | tf_op jit(solution)/shard_map/ppermute | solution.py:34
  127.2 1.3 collective-permute-start.9
  128.5 1.3 fusion.33
  129.8 1.3 collective-permute-start.12
  133.5 7.8 %collective-permute-done.9 = bf16[256,1024]{0,1:T(8,128)(2,1)} collective-permute-done((bf16[256,1024]{0,1:T(8,128)(2,1)}, bf16[256,1024]{0,1:T(8,128)(2,1)}, u32[]{:S(2)}, u32[]{:S(2)}) %collective-permute-start.9) | collective-permute-done | bytes 524320 | tf_op jit(solution)/shard_map/ppermute | solution.py:20
  141.3 1.4 fusion.26
  143.8 3.2 %collective-permute-done.12 = bf16[256,1024]{0,1:T(8,128)(2,1)} collective-permute-done((bf16[256,1024]{0,1:T(8,128)(2,1)}, bf16[256,1024]{0,1:T(8,128)(2,1)}, u32[]{:S(2)}, u32[]{:S(2)}) %collective-permute-start.12) | collective-permute-done | bytes 524320 | tf_op jit(solution)/shard_map/ppermute | solution.py:20
  147.0 1.9 %fusion.31 = bf16[256,1024]{0,1:T(8,128)(2,1)S(1)} fusion(bf16[256,1024]{0,1:T(8,128)(2,1)S(1)} %copy-done.7, f32[904,1024]{0,1:T(8,128)} %copy-done, bf16[256,1024]{0,1:T(8,128)(2,1)} %collective-permute-done.12, pred[]{:T(512)S(6)} %eq.29), kind=kLoop, calls=%fused_computation.60 | loop fusion | flops 1572864 | bytes 2621441 | tf_op jit(solution)/shard_map/convert_element_type | solution.py:192
  (100 shorter events, 26.4 us)
Async XLA Ops:
  0.6 18.1 %copy-start.9 = (bf16[256,1024]{1,0:T(8,128)(2,1)S(1)}, bf16[256,1024]{1,0:T(8,128)(2,1)}, u32[]{:S(2)}) copy-start(bf16[256,1024]{1,0:T(8,128)(2,1)} %param.8) | copy-start | bytes 1572868
  1.9 15.8 %collective-permute-start.1 = (bf16[256,1024]{0,1:T(8,128)(2,1)S(1)}, bf16[256,1024]{0,1:T(8,128)(2,1)S(1)}, u32[]{:S(2)}, u32[]{:S(2)}) collective-permute-start(bf16[256,1024]{0,1:T(8,128)(2,1)S(1)} %copy.60), channel_id=1, source_target_pairs={{0,4},{2,6},{4,8},{6,10},{8,12},{10,14},{12,16},{14,18},{16,20},{1... | collective-permute-start | bytes 1572872 | tf_op jit(solution)/shard_map/ppermute | solution.py:20
  6.5 37.8 %collective-permute-start = (bf16[136,1024]{0,1:T(8,128)(2,1)}, bf16[136,1024]{0,1:T(8,128)(2,1)S(1)}, u32[]{:S(2)}, u32[]{:S(2)}) collective-permute-start(bf16[136,1024]{0,1:T(8,128)(2,1)} %slice.123), channel_id=1, source_target_pairs={{0,6},{2,8},{4,10},{6,12},{8,14},{10,16},{12,18},{14,20},{16,22},{... | collective-permute-start | bytes 835592 | tf_op jit(solution)/shard_map/ppermute | solution.py:20
  10.4 28.7 %collective-permute-start.3 = (bf16[256,1024]{0,1:T(8,128)(2,1)S(1)}, bf16[256,1024]{0,1:T(8,128)(2,1)S(1)}, u32[]{:S(2)}, u32[]{:S(2)}) collective-permute-start(bf16[256,1024]{0,1:T(8,128)(2,1)S(1)} %copy.67), channel_id=1, source_target_pairs={{0,4},{2,6},{4,8},{6,10},{8,12},{10,14},{12,16},{14,18},{16,20},{1... | collective-permute-start | bytes 1572872 | tf_op jit(solution)/shard_map/ppermute | solution.py:20
  18.7 26.4 %collective-permute-start.2 = (bf16[256,1024]{0,1:T(8,128)(2,1)}, bf16[256,1024]{0,1:T(8,128)(2,1)}, u32[]{:S(2)}, u32[]{:S(2)}) collective-permute-start(bf16[256,1024]{0,1:T(8,128)(2,1)} %broadcast_select_fusion.1), channel_id=1, source_target_pairs={{0,2},{2,0},{4,6},{6,4},{8,10},{10,8},{12,14},{14,12},{16,18},{18,... | collective-permute-start | bytes 1572872 | tf_op jit(solution)/shard_map/ppermute | solution.py:25
  39.1 5.2 %copy-start.1 = (bf16[256,1024]{0,1:T(8,128)(2,1)}, bf16[256,1024]{0,1:T(8,128)(2,1)S(1)}, u32[]{:S(2)}) copy-start(bf16[256,1024]{0,1:T(8,128)(2,1)S(1)} %collective-permute-done.3) | copy-start | bytes 1572868
  40.0 17.9 %collective-permute-start.5 = (bf16[256,1024]{0,1:T(8,128)(2,1)}, bf16[256,1024]{0,1:T(8,128)(2,1)}, u32[]{:S(2)}, u32[]{:S(2)}) collective-permute-start(bf16[256,1024]{0,1:T(8,128)(2,1)} %broadcast_select_fusion), channel_id=1, source_target_pairs={{0,2},{2,0},{4,6},{6,4},{8,10},{10,8},{12,14},{14,12},{16,18},{18,... | collective-permute-start | bytes 1572872 | tf_op jit(solution)/shard_map/ppermute | solution.py:25
  41.0 16.8 %collective-permute-start.4 = (bf16[136,1024]{0,1:T(8,128)(2,1)}, bf16[136,1024]{0,1:T(8,128)(2,1)}, u32[]{:S(2)}, u32[]{:S(2)}) collective-permute-start(bf16[136,1024]{0,1:T(8,128)(2,1)} %slice.124), channel_id=1, source_target_pairs={{0,2},{2,4},{4,6},{6,8},{8,10},{10,12},{12,14},{14,16},{16,18},{18... | collective-permute-start | bytes 835592 | tf_op jit(solution)/shard_map/ppermute | solution.py:20
  54.1 3.8 %copy-start.2 = (bf16[256,1024]{0,1:T(8,128)(2,1)S(1)}, bf16[256,1024]{0,1:T(8,128)(2,1)}, u32[]{:S(2)}) copy-start(bf16[256,1024]{0,1:T(8,128)(2,1)} %copy-done.1) | copy-start | bytes 1572868
  60.2 3.4 %copy-start.10 = (f32[1024]{0:T(1024)S(1)}, f32[1024]{0:T(1024)}, u32[]{:S(2)}) copy-start(f32[1024]{0:T(1024)} %param.12) | copy-start | bytes 12292
  63.6 1.9 %copy-start.11 = (s32[2,64]{1,0:T(2,128)S(1)}, s32[2,64]{1,0:T(2,128)}, u32[]{:S(2)}) copy-start(s32[2,64]{1,0:T(2,128)} %param.15) | copy-start | bytes 1540
  64.7 5.4 %collective-permute-start.6 = (f32[3,256]{1,0:T(4,128)S(1)}, f32[3,256]{1,0:T(4,128)S(1)}, u32[]{:S(2)}, u32[]{:S(2)}) collective-permute-start(f32[3,256]{1,0:T(4,128)S(1)} %pad_maximum_fusion.5), channel_id=1, source_target_pairs={{0,1},{1,0},{2,3},{3,2},{4,5},{5,4},{6,7},{7,6},{8,9},{9,8},{10,11... | collective-permute-start | bytes 9224 | tf_op jit(solution)/shard_map/ppermute | solution.py:42
  70.6 5.4 %slice-start = ((s8[7340032]{0:T(1024)(128)(4,1)}), s8[4194304]{0:T(1024)(128)(4,1)S(1)}, s32[]{:S(2)}) async-start(s8[7340032]{0:T(1024)(128)(4,1)} %bitcast.101), calls=%async_computation | async-start | bytes 8388608
  71.8 4.2 %slice-start.1 = ((s8[7340032]{0:T(1024)(128)(4,1)}), s8[3145728]{0:T(1024)(128)(4,1)S(1)}, s32[]{:S(2)}) async-start(s8[7340032]{0:T(1024)(128)(4,1)} %bitcast.101), calls=%async_computation.1 | async-start | bytes 6291456
  75.8 1.7 %collective-permute-start.13 = (f32[4,1024]{1,0:T(4,128)S(1)}, f32[4,1024]{1,0:T(4,128)S(1)}, u32[]{:S(2)}, u32[]{:S(2)}) collective-permute-start(f32[4,1024]{1,0:T(4,128)S(1)} %pad_maximum_fusion.4), channel_id=1, source_target_pairs={{0,2},{2,0},{4,6},{6,4},{8,10},{10,8},{12,14},{14,12},{16,18},{18,... | collective-permute-start | bytes 49160 | tf_op jit(solution)/shard_map/ppermute | solution.py:34
  76.0 3.3 %copy-start.3 = (bf16[256,1024]{0,1:T(8,128)(2,1)S(1)}, bf16[256,1024]{0,1:T(8,128)(2,1)}, u32[]{:S(2)}) copy-start(bf16[256,1024]{0,1:T(8,128)(2,1)} %copy.90) | copy-start | bytes 1572868
  77.5 3.8 %collective-permute-start.14 = (f32[4,1024]{1,0:T(4,128)S(1)}, f32[4,1024]{1,0:T(4,128)S(1)}, u32[]{:S(2)}, u32[]{:S(2)}) collective-permute-start(f32[4,1024]{1,0:T(4,128)S(1)} %fusion.50), channel_id=1, source_target_pairs={{0,4},{2,6},{4,0},{6,2},{8,12},{10,14},{12,8},{14,10},{16,20},{18,... | collective-permute-start | bytes 49160 | tf_op jit(solution)/shard_map/ppermute | solution.py:34
  80.5 45.5 %collective-permute-start.7 = (bf16[256,1024]{0,1:T(8,128)(2,1)S(1)}, bf16[256,1024]{0,1:T(8,128)(2,1)S(1)}, u32[]{:S(2)}, u32[]{:S(2)}) collective-permute-start(bf16[256,1024]{0,1:T(8,128)(2,1)S(1)} %bitcast.112), channel_id=1, source_target_pairs={{0,2},{2,0},{4,6},{6,4},{8,10},{10,8},{12,14},{14,12},{16,18},{18,... | collective-permute-start | bytes 1572872 | tf_op jit(solution)/shard_map/ppermute | solution.py:25
  81.4 10.0 %collective-permute-start.15 = (f32[4,1024]{1,0:T(4,128)S(1)}, f32[4,1024]{1,0:T(4,128)S(1)}, u32[]{:S(2)}, u32[]{:S(2)}) collective-permute-start(f32[4,1024]{1,0:T(4,128)S(1)} %fusion.74), channel_id=1, source_target_pairs={{0,8},{2,10},{4,12},{6,14},{8,0},{10,2},{12,4},{14,6},{16,24},{18,... | collective-permute-start | bytes 49160 | tf_op jit(solution)/shard_map/ppermute | solution.py:34
  91.4 8.2 %collective-permute-start.16 = (f32[4,1024]{1,0:T(4,128)S(1)}, f32[4,1024]{1,0:T(4,128)S(1)}, u32[]{:S(2)}, u32[]{:S(2)}) collective-permute-start(f32[4,1024]{1,0:T(4,128)S(1)} %add.164), channel_id=1, source_target_pairs={{0,16},{2,18},{4,20},{6,22},{8,24},{10,26},{12,28},{14,30},{16,0},... | collective-permute-start | bytes 49160 | tf_op jit(solution)/shard_map/ppermute | solution.py:34
  99.6 28.9 %copy-start = (f32[904,1024]{0,1:T(8,128)}, f32[904,1024]{0,1:T(8,128)S(1)}, u32[]{:S(2)}) copy-start(f32[904,1024]{0,1:T(8,128)S(1)} %get-tuple-element.23) | copy-start | bytes 11108356
  99.6 6.6 %collective-permute-start.17 = (f32[4,1024]{1,0:T(4,128)S(1)}, f32[4,1024]{1,0:T(4,128)S(1)}, u32[]{:S(2)}, u32[]{:S(2)}) collective-permute-start(f32[4,1024]{1,0:T(4,128)S(1)} %add.165), channel_id=1, source_target_pairs={{0,32},{2,34},{4,36},{6,38},{8,40},{10,42},{12,44},{14,46},{16,48}... | collective-permute-start | bytes 49160 | tf_op jit(solution)/shard_map/ppermute | solution.py:34
  102.4 23.6 %collective-permute-start.8 = (bf16[136,1024]{0,1:T(8,128)(2,1)S(1)}, bf16[136,1024]{0,1:T(8,128)(2,1)S(1)}, u32[]{:S(2)}, u32[]{:S(2)}) collective-permute-start(bf16[136,1024]{0,1:T(8,128)(2,1)S(1)} %pad_slice_fusion), channel_id=1, source_target_pairs={{2,0},{4,2},{6,4},{8,6},{10,8},{12,10},{14,12},{16,14},{18,16},{20... | collective-permute-start | bytes 835592 | tf_op jit(solution)/shard_map/ppermute | solution.py:20
  103.7 24.8 %collective-permute-start.10 = (bf16[256,1024]{0,1:T(8,128)(2,1)S(1)}, bf16[256,1024]{0,1:T(8,128)(2,1)S(1)}, u32[]{:S(2)}, u32[]{:S(2)}) collective-permute-start(bf16[256,1024]{0,1:T(8,128)(2,1)S(1)} %slice.139), channel_id=1, source_target_pairs={{0,2},{2,0},{4,6},{6,4},{8,10},{10,8},{12,14},{14,12},{16,18},{18,... | collective-permute-start | bytes 1572872 | tf_op jit(solution)/shard_map/ppermute | solution.py:25
  104.9 23.6 %collective-permute-start.11 = (bf16[136,1024]{0,1:T(8,128)(2,1)S(1)}, bf16[136,1024]{0,1:T(8,128)(2,1)S(1)}, u32[]{:S(2)}, u32[]{:S(2)}) collective-permute-start(bf16[136,1024]{0,1:T(8,128)(2,1)S(1)} %slice.141), channel_id=1, source_target_pairs={{2,0},{4,2},{6,4},{8,6},{10,8},{12,10},{14,12},{16,14},{18,16},{20... | collective-permute-start | bytes 835592 | tf_op jit(solution)/shard_map/ppermute | solution.py:20
  106.2 17.2 %collective-permute-start.18 = (f32[4,1024]{1,0:T(4,128)S(1)}, f32[4,1024]{1,0:T(4,128)S(1)}, u32[]{:S(2)}, u32[]{:S(2)}) collective-permute-start(f32[4,1024]{1,0:T(4,128)S(1)} %add.166), channel_id=1, source_target_pairs={{0,64},{2,66},{4,68},{6,70},{8,72},{10,74},{12,76},{14,78},{16,80}... | collective-permute-start | bytes 49160 | tf_op jit(solution)/shard_map/ppermute | solution.py:34
  123.5 9.4 %collective-permute-start.19 = (f32[4,1024]{1,0:T(4,128)S(1)}, f32[4,1024]{1,0:T(4,128)S(1)}, u32[]{:S(2)}, u32[]{:S(2)}) collective-permute-start(f32[4,1024]{1,0:T(4,128)S(1)} %add.167), channel_id=1, source_target_pairs={{0,128},{2,130},{4,132},{6,134},{8,136},{10,138},{12,140},{14,142}... | collective-permute-start | bytes 49160 | tf_op jit(solution)/shard_map/ppermute | solution.py:34
  126.0 5.8 %copy-start.5 = (bf16[256,1024]{0,1:T(8,128)(2,1)}, bf16[256,1024]{0,1:T(8,128)(2,1)S(1)}, u32[]{:S(2)}) copy-start(bf16[256,1024]{0,1:T(8,128)(2,1)S(1)} %collective-permute-done.7) | copy-start | bytes 1572868
  127.2 14.2 %collective-permute-start.9 = (bf16[256,1024]{0,1:T(8,128)(2,1)}, bf16[256,1024]{0,1:T(8,128)(2,1)}, u32[]{:S(2)}, u32[]{:S(2)}) collective-permute-start(bf16[256,1024]{0,1:T(8,128)(2,1)} %fusion.28), channel_id=1, source_target_pairs={{4,0},{6,2},{8,4},{10,6},{12,8},{14,10},{16,12},{18,14},{20,16},{2... | collective-permute-start | bytes 1572872 | tf_op jit(solution)/shard_map/ppermute | solution.py:20
  128.5 3.4 %copy-start.6 = (bf16[256,1024]{0,1:T(8,128)(2,1)}, bf16[256,1024]{0,1:T(8,128)(2,1)S(1)}, u32[]{:S(2)}) copy-start(bf16[256,1024]{0,1:T(8,128)(2,1)S(1)} %collective-permute-done.10) | copy-start | bytes 1572868
  129.8 17.2 %collective-permute-start.12 = (bf16[256,1024]{0,1:T(8,128)(2,1)}, bf16[256,1024]{0,1:T(8,128)(2,1)}, u32[]{:S(2)}, u32[]{:S(2)}) collective-permute-start(bf16[256,1024]{0,1:T(8,128)(2,1)} %fusion.33), channel_id=1, source_target_pairs={{4,0},{6,2},{8,4},{10,6},{12,8},{14,10},{16,12},{18,14},{20,16},{2... | collective-permute-start | bytes 1572872 | tf_op jit(solution)/shard_map/ppermute | solution.py:20
  131.9 15.1 %copy-start.7 = (bf16[256,1024]{0,1:T(8,128)(2,1)S(1)}, bf16[256,1024]{0,1:T(8,128)(2,1)}, u32[]{:S(2)}) copy-start(bf16[256,1024]{0,1:T(8,128)(2,1)} %copy-done.6) | copy-start | bytes 1572868
  (2 other events, 1.8 us)

commit v13 on v12

--- a/solution.py
+++ b/solution.py
@@ -74,17 +74,14 @@
     far_lead = 8
     key_count = REACH * row_count + (row_count - far_rows)
 
-    def relay(own, direct_third=False):
+    def relay(own, lead_rows):
         second = from_behind(own, "tm", 2)
         first = chip_swap(jnp.where(even, own, second), "tm")
-        if direct_third:
-            third = from_behind(own[far_rows - far_lead :], "tm", REACH)
-        else:
-            third = from_behind(second[far_rows - far_lead :], "tm", 1)
+        third = from_behind(second[far_rows - lead_rows :], "tm", 1)
         return jnp.concatenate([third, second, first, own], 0)
 
-    key_win = relay(keys, direct_third=True)[far_lead:]
-    vin_win = relay(values_in)
+    key_win = relay(keys, 0)
+    vin_win = relay(values_in, far_lead)
 
     conv_sum = jnp.zeros((key_count, channels), jnp.float32)
     for tap_index in range(tap_count):

time: 152 us -> 135 us (0.89)
  waiting for transfers between devices: 46.9 us -> 39.3 us
  starting transfers between devices: 44.2 us -> 39.2 us
  local copies, waits for them, and re-layouts: 13.2 us -> 9.55 us
    ppermute x8, waiting for transfers between devices: 30.4 us -> 22.5 us  [from_behind(): return lax.ppermute(block, axis, route)]
    ppermute x7, starting transfers between devices: 24.3 us -> 19.1 us  [all_sum(): lax.ppermute(block, axis, [(i, i ^ stride) for i in range(size)])]
    unnamed x35 -> x37, local copies, waits for them, and re-layouts: 8.42 us -> 6.62 us
  transfers between devices with their start and end apart: 20 -> 20, of which waited for: 8 -> 8; matrix products, arithmetic and copies ran while one was open for 27% -> 28% of each run, Pallas kernels for 0% -> 0%
where the time goes in v13:
time: 135 us; the launch traced here: 133 us
  waiting for transfers between devices  39.3 us (29%)
  starting transfers between devices  39.2 us (29%)
  other arithmetic  31.4 us (23%)
  matrix products  12.7 us (9%)
  local copies, waits for them, and re-layouts  9.55 us (7%)
    ppermute x8, waiting for transfers between devices, from_behind(): return lax.ppermute(block, axis, route)  22.5 us
    ppermute x7, starting transfers between devices, all_sum(): lax.ppermute(block, axis, [(i, i ^ stride) for i in range(size)])  19.1 us
    ppermute x8, starting transfers between devices, from_behind(): return lax.ppermute(block, axis, route)  17.8 us
    ppermute x7, waiting for transfers between devices, all_sum(): lax.ppermute(block, axis, [(i, i ^ stride) for i in range(size)])  12.4 us
    sub x1, matrix products, body(): expo = jnp.where(mask[None], jnp.exp(scores - row_peak[..., None]), 0.0)  7.3 us
    unnamed x37, local copies, waits for them, and re-layouts  6.62 us
    another operation x1, other arithmetic  5.18 us
    ppermute x1, waiting for transfers between devices, pair_sum(): return block + lax.ppermute(block, axis, [(0, 1), (1, 0)])  4.41 us
  transfers between devices with their start and end apart: 20, of which 8 were waited for; matrix products, arithmetic and copies ran while one was open for 28% of the time, Pallas kernels for 0%

profile of v13, /device:TPU:4, one launch (start us, length us, event | category | flops | bytes accessed | tf_op | source)
XLA Modules:
  0.0 133.3 jit_solution(12239064121826943157)
XLA Ops:
  0.7 1.3 copy.59
  2.0 3.5 %collective-permute-start = (bf16[256,1024]{0,1:T(8,128)(2,1)S(1)}, bf16[256,1024]{0,1:T(8,128)(2,1)S(1)}, u32[]{:S(2)}, u32[]{:S(2)}) collective-permute-start(bf16[256,1024]{0,1:T(8,128)(2,1)S(1)} %copy.59), channel_id=1, source_target_pairs={{0,4},{2,6},{4,8},{6,10},{8,12},{10,14},{12,16},{14,18},{16,20},{1... | collective-permute-start | bytes 1572872 | tf_op jit(solution)/shard_map/ppermute | solution.py:20
  6.8 3.5 %collective-permute-start.3 = (bf16[256,1024]{0,1:T(8,128)(2,1)S(1)}, bf16[256,1024]{0,1:T(8,128)(2,1)S(1)}, u32[]{:S(2)}, u32[]{:S(2)}) collective-permute-start(bf16[256,1024]{0,1:T(8,128)(2,1)S(1)} %copy.65), channel_id=1, source_target_pairs={{0,4},{2,6},{4,8},{6,10},{8,12},{10,14},{12,16},{14,18},{16,20},{1... | collective-permute-start | bytes 1572872 | tf_op jit(solution)/shard_map/ppermute | solution.py:20
  11.4 6.4 %collective-permute-done = bf16[256,1024]{0,1:T(8,128)(2,1)S(1)} collective-permute-done((bf16[256,1024]{0,1:T(8,128)(2,1)S(1)}, bf16[256,1024]{0,1:T(8,128)(2,1)S(1)}, u32[]{:S(2)}, u32[]{:S(2)}) %collective-permute-start) | collective-permute-done | bytes 524320 | tf_op jit(solution)/shard_map/ppermute | solution.py:20
  20.9 2.4 %collective-permute-start.1 = (bf16[128,1024]{0,1:T(8,128)(2,1)S(1)}, bf16[128,1024]{0,1:T(8,128)(2,1)S(1)}, u32[]{:S(2)}, u32[]{:S(2)}) collective-permute-start(bf16[128,1024]{0,1:T(8,128)(2,1)S(1)} %slice.119), channel_id=1, source_target_pairs={{0,2},{2,4},{4,6},{6,8},{8,10},{10,12},{12,14},{14,16},{16,18},{18... | collective-permute-start | bytes 786440 | tf_op jit(solution)/shard_map/ppermute | solution.py:20
  23.3 5.7 %collective-permute-done.3 = bf16[256,1024]{0,1:T(8,128)(2,1)S(1)} collective-permute-done((bf16[256,1024]{0,1:T(8,128)(2,1)S(1)}, bf16[256,1024]{0,1:T(8,128)(2,1)S(1)}, u32[]{:S(2)}, u32[]{:S(2)}) %collective-permute-start.3) | collective-permute-done | bytes 524320 | tf_op jit(solution)/shard_map/ppermute | solution.py:20
  31.0 3.3 %collective-permute-start.4 = (bf16[136,1024]{0,1:T(8,128)(2,1)}, bf16[136,1024]{0,1:T(8,128)(2,1)}, u32[]{:S(2)}, u32[]{:S(2)}) collective-permute-start(bf16[136,1024]{0,1:T(8,128)(2,1)} %slice.120), channel_id=1, source_target_pairs={{0,2},{2,4},{4,6},{6,8},{8,10},{10,12},{12,14},{14,16},{16,18},{18... | collective-permute-start | bytes 835592 | tf_op jit(solution)/shard_map/ppermute | solution.py:20
  34.3 1.4 %pad_maximum_fusion.1 = bf16[896,1024]{0,1:T(8,128)(2,1)S(1)} fusion(bf16[256,1024]{0,1:T(8,128)(2,1)S(1)} %copy.59, bf16[256,1024]{0,1:T(8,128)(2,1)} %collective-permute-done.2, bf16[256,1024]{0,1:T(8,128)(2,1)} %copy-done.3, bf16[128,1024]{0,1:T(8,128)(2,1)S(1)} %collective-permute-done.1), kind=kLoop, calls=%fused_computation.36 | loop fusion | flops 7340032 | bytes 3670016 | tf_op jit(solution)/shard_map/concatenate | solution.py:81
  35.7 7.3 %fusion.57 = (f32[8,256]{1,0:T(8,128)S(1)}, f32[8,256,896]{1,2,0:T(8,128)}) fusion(pred[256,896]{0,1:T(8,128)(4,1)} %fusion.39, bf16[896,8,128]{0,2,1:T(8,128)(2,1)S(1)} %bitcast.101, bf16[256,8,128]{0,2,1:T(8,128)(2,1)} %bitcast.107), kind=kOutput, calls=%fused_computation.105 | convolution fusion | flops 478937984 | bytes 9936896 | tf_op jit(solution)/shard_map/sub | solution.py:104
  43.0 3.8 %fusion.16 = bf16[8,256,896]{1,2,0:T(8,128)(2,1)S(1)} fusion(f32[8,256,896]{1,2,0:T(8,128)} %get-tuple-element.36, f32[8,256]{1,0:T(8,128)S(1)} %get-tuple-element.35), kind=kLoop, calls=%fused_computation.33 | loop fusion | flops 3670016 | bytes 11018240 | tf_op jit(solution)/shard_map/convert_element_type | solution.py:107
  46.8 2.2 %pad_maximum_fusion = bf16[904,1024]{0,1:T(8,128)(2,1)S(1)} fusion(bf16[256,1024]{0,1:T(8,128)(2,1)S(1)} %copy.65, bf16[256,1024]{0,1:T(8,128)(2,1)} %collective-permute-done.5, bf16[256,1024]{0,1:T(8,128)(2,1)S(1)} %copy-done.2, bf16[136,1024]{0,1:T(8,128)(2,1)} %collective-permute-done.4), kind=kLoop, calls=%fused_computation.34 | loop fusion | flops 7405568 | bytes 3702784 | tf_op jit(solution)/shard_map/concatenate | solution.py:81
  49.1 3.4 %fusion.8 = bf16[896,1024]{0,1:T(8,128)(2,1)S(1)} fusion(f32[1024]{0:T(1024)S(1)} %bitcast.129, f32[1024]{0:T(1024)S(1)} %bitcast.131, f32[1024]{0:T(1024)S(1)} %bitcast.127, f32[1024]{0:T(1024)S(1)} %bitcast.125, bf16[904,1024]{0,1:T(8,128)(2,1)S(1)} %pad_maximum_fusion), kind=kLoop, calls=%fused_computation.23 | loop fusion | flops 11010048 | bytes 9191424 | tf_op jit(solution)/shard_map/convert_element_type | solution.py:91
  54.5 4.4 %collective-permute-done.6 = f32[3,256]{1,0:T(4,128)S(1)} collective-permute-done((f32[3,256]{1,0:T(4,128)S(1)}, f32[3,256]{1,0:T(4,128)S(1)}, u32[]{:S(2)}, u32[]{:S(2)}) %collective-permute-start.6) | collective-permute-done | bytes 3104 | tf_op jit(solution)/shard_map/ppermute | solution.py:42
  60.7 3.9 %fusion.9 = (f32[1024]{0:T(1024)S(1)}, f32[1024]{0:T(1024)S(1)}, f32[1024]{0:T(1024)S(1)}, f32[1024]{0:T(1024)S(1)}) fusion(bf16[904,1024]{0,1:T(8,128)(2,1)S(1)} %pad_maximum_fusion, f32[8,128,896]{2,1,0:T(8,128)S(1)} %fusion.59), kind=kLoop, calls=%fused_computation.24 | loop fusion | flops 11005952 | bytes 11026432 | tf_op jit(solution)/shard_map/reduce_sum | solution.py:152
  64.9 1.5 %multiply_convert_fusion = bf16[8,256,896]{1,2,0:T(8,128)(2,1)S(1)} fusion(f32[8,256]{1,0:T(8,128)S(1)} %bitcast.142, f32[8,256,896]{1,2,0:T(8,128)S(1)} %bitcast.104, f32[8,256]{1,0:T(8,128)S(1)} %get-tuple-element.35, bf16[256,8,128]{0,2,1:T(8,128)(2,1)S(1)} %bitcast.111, bf16[896,8,128]{0,2,1:T(8,128)(2,1)S(1)} %bitcast.106), kind=kOutput, calls=%fused_computation.2 | convolution fusion | flops 477102080 | bytes 13385728 | tf_op jit(solution)/shard_map/thd,uhd->htu/dot_general | solution.py:136
  66.4 1.7 %collective-permute-start.14 = (f32[4,1024]{1,0:T(4,128)S(1)}, f32[4,1024]{1,0:T(4,128)S(1)}, u32[]{:S(2)}, u32[]{:S(2)}) collective-permute-start(f32[4,1024]{1,0:T(4,128)S(1)} %fusion.50), channel_id=1, source_target_pairs={{0,4},{2,6},{4,0},{6,2},{8,12},{10,14},{12,8},{14,10},{16,20},{18,... | collective-permute-start | bytes 49160 | tf_op jit(solution)/shard_map/ppermute | solution.py:34
  70.2 3.3 %collective-permute-start.15 = (f32[4,1024]{1,0:T(4,128)S(1)}, f32[4,1024]{1,0:T(4,128)S(1)}, u32[]{:S(2)}, u32[]{:S(2)}) collective-permute-start(f32[4,1024]{1,0:T(4,128)S(1)} %fusion.74), channel_id=1, source_target_pairs={{0,8},{2,10},{4,12},{6,14},{8,0},{10,2},{12,4},{14,6},{16,24},{18,... | collective-permute-start | bytes 49160 | tf_op jit(solution)/shard_map/ppermute | solution.py:34
  75.6 2.3 %collective-permute-start.16 = (f32[4,1024]{1,0:T(4,128)S(1)}, f32[4,1024]{1,0:T(4,128)S(1)}, u32[]{:S(2)}, u32[]{:S(2)}) collective-permute-start(f32[4,1024]{1,0:T(4,128)S(1)} %add.164), channel_id=1, source_target_pairs={{0,16},{2,18},{4,20},{6,22},{8,24},{10,26},{12,28},{14,30},{16,0},... | collective-permute-start | bytes 49160 | tf_op jit(solution)/shard_map/ppermute | solution.py:34
  77.8 5.2 %fusion.51 = (bf16[904,1024]{0,1:T(8,128)(2,1)S(1)}, f32[904,1024]{0,1:T(8,128)S(1)}) fusion(f32[907,1024]{0,1:T(8,128)S(1)} %maximum_maximum_fusion, f32[1024]{0:T(1024)S(1)} %bitcast.130, f32[1024]{0:T(1024)S(1)} %bitcast.132, f32[1024]{0:T(1024)S(1)} %bitcast.128, f32[896,1024]{0,1:T(8,128)S(1)} %bitcast.99, f32[1024]{0:T(1024)S(1)} %bitcast.126), kind=kLoop, calls=%fused_computation.101 | loop fusion | flops 7405568 | bytes 20348928 | tf_op jit(solution)/shard_map/convert.5
  83.0 2.2 %collective-permute-start.17 = (f32[4,1024]{1,0:T(4,128)S(1)}, f32[4,1024]{1,0:T(4,128)S(1)}, u32[]{:S(2)}, u32[]{:S(2)}) collective-permute-start(f32[4,1024]{1,0:T(4,128)S(1)} %add.165), channel_id=1, source_target_pairs={{0,32},{2,34},{4,36},{6,38},{8,40},{10,42},{12,44},{14,46},{16,48}... | collective-permute-start | bytes 49160 | tf_op jit(solution)/shard_map/ppermute | solution.py:34
  85.8 1.3 collective-permute-start.8
  88.3 1.3 collective-permute-start.11
  89.6 6.4 %collective-permute-start.18 = (f32[4,1024]{1,0:T(4,128)S(1)}, f32[4,1024]{1,0:T(4,128)S(1)}, u32[]{:S(2)}, u32[]{:S(2)}) collective-permute-start(f32[4,1024]{1,0:T(4,128)S(1)} %add.166), channel_id=1, source_target_pairs={{0,64},{2,66},{4,68},{6,70},{8,72},{10,74},{12,76},{14,78},{16,80}... | collective-permute-start | bytes 49160 | tf_op jit(solution)/shard_map/ppermute | solution.py:34
  96.2 10.9 %collective-permute-done.18 = f32[4,1024]{1,0:T(4,128)S(1)} collective-permute-done((f32[4,1024]{1,0:T(4,128)S(1)}, f32[4,1024]{1,0:T(4,128)S(1)}, u32[]{:S(2)}, u32[]{:S(2)}) %collective-permute-start.18) | collective-permute-done | bytes 16416 | tf_op jit(solution)/shard_map/ppermute | solution.py:34
  107.0 3.0 %collective-permute-start.19 = (f32[4,1024]{1,0:T(4,128)S(1)}, f32[4,1024]{1,0:T(4,128)S(1)}, u32[]{:S(2)}, u32[]{:S(2)}) collective-permute-start(f32[4,1024]{1,0:T(4,128)S(1)} %add.167), channel_id=1, source_target_pairs={{0,128},{2,130},{4,132},{6,134},{8,136},{10,138},{12,140},{14,142}... | collective-permute-start | bytes 49160 | tf_op jit(solution)/shard_map/ppermute | solution.py:34
  111.2 1.3 collective-permute-start.9
  112.6 1.3 fusion.33
  113.9 1.3 collective-permute-start.12
  117.6 7.2 %collective-permute-done.9 = bf16[256,1024]{0,1:T(8,128)(2,1)} collective-permute-done((bf16[256,1024]{0,1:T(8,128)(2,1)}, bf16[256,1024]{0,1:T(8,128)(2,1)}, u32[]{:S(2)}, u32[]{:S(2)}) %collective-permute-start.9) | collective-permute-done | bytes 524320 | tf_op jit(solution)/shard_map/ppermute | solution.py:20
  124.8 1.4 %fusion.26 = bf16[256,1024]{0,1:T(8,128)(2,1)S(1)} fusion(bf16[256,1024]{0,1:T(8,128)(2,1)} %copy-done.5, f32[256,8,128]{0,2,1:T(8,128)S(1)} %get-tuple-element.27, bf16[256,1024]{0,1:T(8,128)(2,1)} %collective-permute-done.9, pred[]{:T(512)S(6)} %eq.29), kind=kLoop, calls=%fused_computation.53 | loop fusion | flops 1572864 | bytes 2621441 | tf_op jit(solution)/shard_map/convert_element_type | solution.py:188
  127.2 3.2 %collective-permute-done.12 = bf16[256,1024]{0,1:T(8,128)(2,1)} collective-permute-done((bf16[256,1024]{0,1:T(8,128)(2,1)}, bf16[256,1024]{0,1:T(8,128)(2,1)}, u32[]{:S(2)}, u32[]{:S(2)}) %collective-permute-start.12) | collective-permute-done | bytes 524320 | tf_op jit(solution)/shard_map/ppermute | solution.py:20
  130.4 1.9 %fusion.31 = bf16[256,1024]{0,1:T(8,128)(2,1)S(1)} fusion(bf16[256,1024]{0,1:T(8,128)(2,1)S(1)} %copy-done.7, f32[904,1024]{0,1:T(8,128)} %copy-done, bf16[256,1024]{0,1:T(8,128)(2,1)} %collective-permute-done.12, pred[]{:T(512)S(6)} %eq.29), kind=kLoop, calls=%fused_computation.58 | loop fusion | flops 1572864 | bytes 2621441 | tf_op jit(solution)/shard_map/convert_element_type | solution.py:189
  (102 shorter events, 23.0 us)
Async XLA Ops:
  0.6 18.1 %copy-start.8 = (bf16[256,1024]{1,0:T(8,128)(2,1)S(1)}, bf16[256,1024]{1,0:T(8,128)(2,1)}, u32[]{:S(2)}) copy-start(bf16[256,1024]{1,0:T(8,128)(2,1)} %param.8) | copy-start | bytes 1572868
  0.6 19.1 %copy-start.9 = (bf16[256,1024]{1,0:T(8,128)(2,1)S(1)}, bf16[256,1024]{1,0:T(8,128)(2,1)}, u32[]{:S(2)}) copy-start(bf16[256,1024]{1,0:T(8,128)(2,1)} %param.11) | copy-start | bytes 1572868
  0.7 20.2 %copy-start.11 = (f32[4,1024]{1,0:T(4,128)S(1)}, f32[4,1024]{1,0:T(4,128)}, u32[]{:S(2)}) copy-start(f32[4,1024]{1,0:T(4,128)} %param.13) | copy-start | bytes 49156
  2.0 15.8 %collective-permute-start = (bf16[256,1024]{0,1:T(8,128)(2,1)S(1)}, bf16[256,1024]{0,1:T(8,128)(2,1)S(1)}, u32[]{:S(2)}, u32[]{:S(2)}) collective-permute-start(bf16[256,1024]{0,1:T(8,128)(2,1)S(1)} %copy.59), channel_id=1, source_target_pairs={{0,4},{2,6},{4,8},{6,10},{8,12},{10,14},{12,16},{14,18},{16,20},{1... | collective-permute-start | bytes 1572872 | tf_op jit(solution)/shard_map/ppermute | solution.py:20
  6.8 22.3 %collective-permute-start.3 = (bf16[256,1024]{0,1:T(8,128)(2,1)S(1)}, bf16[256,1024]{0,1:T(8,128)(2,1)S(1)}, u32[]{:S(2)}, u32[]{:S(2)}) collective-permute-start(bf16[256,1024]{0,1:T(8,128)(2,1)S(1)} %copy.65), channel_id=1, source_target_pairs={{0,4},{2,6},{4,8},{6,10},{8,12},{10,14},{12,16},{14,18},{16,20},{1... | collective-permute-start | bytes 1572872 | tf_op jit(solution)/shard_map/ppermute | solution.py:20
  17.8 16.5 %copy-start.3 = (bf16[256,1024]{0,1:T(8,128)(2,1)}, bf16[256,1024]{0,1:T(8,128)(2,1)S(1)}, u32[]{:S(2)}) copy-start(bf16[256,1024]{0,1:T(8,128)(2,1)S(1)} %collective-permute-done) | copy-start | bytes 1572868
  18.7 15.6 %collective-permute-start.2 = (bf16[256,1024]{0,1:T(8,128)(2,1)}, bf16[256,1024]{0,1:T(8,128)(2,1)}, u32[]{:S(2)}, u32[]{:S(2)}) collective-permute-start(bf16[256,1024]{0,1:T(8,128)(2,1)} %broadcast_select_fusion.1), channel_id=1, source_target_pairs={{0,2},{2,0},{4,6},{6,4},{8,10},{10,8},{12,14},{14,12},{16,18},{18,... | collective-permute-start | bytes 1572872 | tf_op jit(solution)/shard_map/ppermute | solution.py:25
  20.9 13.4 %collective-permute-start.1 = (bf16[128,1024]{0,1:T(8,128)(2,1)S(1)}, bf16[128,1024]{0,1:T(8,128)(2,1)S(1)}, u32[]{:S(2)}, u32[]{:S(2)}) collective-permute-start(bf16[128,1024]{0,1:T(8,128)(2,1)S(1)} %slice.119), channel_id=1, source_target_pairs={{0,2},{2,4},{4,6},{6,8},{8,10},{10,12},{12,14},{14,16},{16,18},{18... | collective-permute-start | bytes 786440 | tf_op jit(solution)/shard_map/ppermute | solution.py:20
  29.0 5.2 %copy-start.1 = (bf16[256,1024]{0,1:T(8,128)(2,1)}, bf16[256,1024]{0,1:T(8,128)(2,1)S(1)}, u32[]{:S(2)}) copy-start(bf16[256,1024]{0,1:T(8,128)(2,1)S(1)} %collective-permute-done.3) | copy-start | bytes 1572868
  30.0 16.8 %collective-permute-start.5 = (bf16[256,1024]{0,1:T(8,128)(2,1)}, bf16[256,1024]{0,1:T(8,128)(2,1)}, u32[]{:S(2)}, u32[]{:S(2)}) collective-permute-start(bf16[256,1024]{0,1:T(8,128)(2,1)} %broadcast_select_fusion), channel_id=1, source_target_pairs={{0,2},{2,0},{4,6},{6,4},{8,10},{10,8},{12,14},{14,12},{16,18},{18,... | collective-permute-start | bytes 1572872 | tf_op jit(solution)/shard_map/ppermute | solution.py:25
  31.0 15.8 %collective-permute-start.4 = (bf16[136,1024]{0,1:T(8,128)(2,1)}, bf16[136,1024]{0,1:T(8,128)(2,1)}, u32[]{:S(2)}, u32[]{:S(2)}) collective-permute-start(bf16[136,1024]{0,1:T(8,128)(2,1)} %slice.120), channel_id=1, source_target_pairs={{0,2},{2,4},{4,6},{6,8},{8,10},{10,12},{12,14},{14,16},{16,18},{18... | collective-permute-start | bytes 835592 | tf_op jit(solution)/shard_map/ppermute | solution.py:20
  43.0 3.8 %copy-start.2 = (bf16[256,1024]{0,1:T(8,128)(2,1)S(1)}, bf16[256,1024]{0,1:T(8,128)(2,1)}, u32[]{:S(2)}) copy-start(bf16[256,1024]{0,1:T(8,128)(2,1)} %copy-done.1) | copy-start | bytes 1572868
  53.6 5.4 %collective-permute-start.6 = (f32[3,256]{1,0:T(4,128)S(1)}, f32[3,256]{1,0:T(4,128)S(1)}, u32[]{:S(2)}, u32[]{:S(2)}) collective-permute-start(f32[3,256]{1,0:T(4,128)S(1)} %pad_maximum_fusion.3), channel_id=1, source_target_pairs={{0,1},{1,0},{2,3},{3,2},{4,5},{5,4},{6,7},{7,6},{8,9},{9,8},{10,11... | collective-permute-start | bytes 9224 | tf_op jit(solution)/shard_map/ppermute | solution.py:42
  59.5 5.4 %slice-start = ((s8[7340032]{0:T(1024)(128)(4,1)}), s8[4194304]{0:T(1024)(128)(4,1)S(1)}, s32[]{:S(2)}) async-start(s8[7340032]{0:T(1024)(128)(4,1)} %bitcast.103), calls=%async_computation | async-start | bytes 8388608
  60.7 4.2 %slice-start.1 = ((s8[7340032]{0:T(1024)(128)(4,1)}), s8[3145728]{0:T(1024)(128)(4,1)S(1)}, s32[]{:S(2)}) async-start(s8[7340032]{0:T(1024)(128)(4,1)} %bitcast.103), calls=%async_computation.1 | async-start | bytes 6291456
  64.7 1.7 %collective-permute-start.13 = (f32[4,1024]{1,0:T(4,128)S(1)}, f32[4,1024]{1,0:T(4,128)S(1)}, u32[]{:S(2)}, u32[]{:S(2)}) collective-permute-start(f32[4,1024]{1,0:T(4,128)S(1)} %pad_maximum_fusion.2), channel_id=1, source_target_pairs={{0,2},{2,0},{4,6},{6,4},{8,10},{10,8},{12,14},{14,12},{16,18},{18,... | collective-permute-start | bytes 49160 | tf_op jit(solution)/shard_map/ppermute | solution.py:34
  66.4 3.8 %collective-permute-start.14 = (f32[4,1024]{1,0:T(4,128)S(1)}, f32[4,1024]{1,0:T(4,128)S(1)}, u32[]{:S(2)}, u32[]{:S(2)}) collective-permute-start(f32[4,1024]{1,0:T(4,128)S(1)} %fusion.50), channel_id=1, source_target_pairs={{0,4},{2,6},{4,0},{6,2},{8,12},{10,14},{12,8},{14,10},{16,20},{18,... | collective-permute-start | bytes 49160 | tf_op jit(solution)/shard_map/ppermute | solution.py:34
  69.4 40.7 %collective-permute-start.7 = (bf16[256,1024]{0,1:T(8,128)(2,1)S(1)}, bf16[256,1024]{0,1:T(8,128)(2,1)S(1)}, u32[]{:S(2)}, u32[]{:S(2)}) collective-permute-start(bf16[256,1024]{0,1:T(8,128)(2,1)S(1)} %bitcast.112), channel_id=1, source_target_pairs={{0,2},{2,0},{4,6},{6,4},{8,10},{10,8},{12,14},{14,12},{16,18},{18,... | collective-permute-start | bytes 1572872 | tf_op jit(solution)/shard_map/ppermute | solution.py:25
  70.2 5.3 %collective-permute-start.15 = (f32[4,1024]{1,0:T(4,128)S(1)}, f32[4,1024]{1,0:T(4,128)S(1)}, u32[]{:S(2)}, u32[]{:S(2)}) collective-permute-start(f32[4,1024]{1,0:T(4,128)S(1)} %fusion.74), channel_id=1, source_target_pairs={{0,8},{2,10},{4,12},{6,14},{8,0},{10,2},{12,4},{14,6},{16,24},{18,... | collective-permute-start | bytes 49160 | tf_op jit(solution)/shard_map/ppermute | solution.py:34
  75.6 7.5 %collective-permute-start.16 = (f32[4,1024]{1,0:T(4,128)S(1)}, f32[4,1024]{1,0:T(4,128)S(1)}, u32[]{:S(2)}, u32[]{:S(2)}) collective-permute-start(f32[4,1024]{1,0:T(4,128)S(1)} %add.164), channel_id=1, source_target_pairs={{0,16},{2,18},{4,20},{6,22},{8,24},{10,26},{12,28},{14,30},{16,0},... | collective-permute-start | bytes 49160 | tf_op jit(solution)/shard_map/ppermute | solution.py:34
  83.0 29.5 %copy-start = (f32[904,1024]{0,1:T(8,128)}, f32[904,1024]{0,1:T(8,128)S(1)}, u32[]{:S(2)}) copy-start(f32[904,1024]{0,1:T(8,128)S(1)} %get-tuple-element.23) | copy-start | bytes 11108356
  83.0 6.6 %collective-permute-start.17 = (f32[4,1024]{1,0:T(4,128)S(1)}, f32[4,1024]{1,0:T(4,128)S(1)}, u32[]{:S(2)}, u32[]{:S(2)}) collective-permute-start(f32[4,1024]{1,0:T(4,128)S(1)} %add.165), channel_id=1, source_target_pairs={{0,32},{2,34},{4,36},{6,38},{8,40},{10,42},{12,44},{14,46},{16,48}... | collective-permute-start | bytes 49160 | tf_op jit(solution)/shard_map/ppermute | solution.py:34
  85.8 24.3 %collective-permute-start.8 = (bf16[136,1024]{0,1:T(8,128)(2,1)S(1)}, bf16[136,1024]{0,1:T(8,128)(2,1)S(1)}, u32[]{:S(2)}, u32[]{:S(2)}) collective-permute-start(bf16[136,1024]{0,1:T(8,128)(2,1)S(1)} %pad_slice_fusion), channel_id=1, source_target_pairs={{2,0},{4,2},{6,4},{8,6},{10,8},{12,10},{14,12},{16,14},{18,16},{20... | collective-permute-start | bytes 835592 | tf_op jit(solution)/shard_map/ppermute | solution.py:20
  87.1 25.4 %collective-permute-start.10 = (bf16[256,1024]{0,1:T(8,128)(2,1)S(1)}, bf16[256,1024]{0,1:T(8,128)(2,1)S(1)}, u32[]{:S(2)}, u32[]{:S(2)}) collective-permute-start(bf16[256,1024]{0,1:T(8,128)(2,1)S(1)} %slice.135), channel_id=1, source_target_pairs={{0,2},{2,0},{4,6},{6,4},{8,10},{10,8},{12,14},{14,12},{16,18},{18,... | collective-permute-start | bytes 1572872 | tf_op jit(solution)/shard_map/ppermute | solution.py:25
  88.3 24.2 %collective-permute-start.11 = (bf16[136,1024]{0,1:T(8,128)(2,1)S(1)}, bf16[136,1024]{0,1:T(8,128)(2,1)S(1)}, u32[]{:S(2)}, u32[]{:S(2)}) collective-permute-start(bf16[136,1024]{0,1:T(8,128)(2,1)S(1)} %slice.137), channel_id=1, source_target_pairs={{2,0},{4,2},{6,4},{8,6},{10,8},{12,10},{14,12},{16,14},{18,16},{20... | collective-permute-start | bytes 835592 | tf_op jit(solution)/shard_map/ppermute | solution.py:20
  89.6 17.4 %collective-permute-start.18 = (f32[4,1024]{1,0:T(4,128)S(1)}, f32[4,1024]{1,0:T(4,128)S(1)}, u32[]{:S(2)}, u32[]{:S(2)}) collective-permute-start(f32[4,1024]{1,0:T(4,128)S(1)} %add.166), channel_id=1, source_target_pairs={{0,64},{2,66},{4,68},{6,70},{8,72},{10,74},{12,76},{14,78},{16,80}... | collective-permute-start | bytes 49160 | tf_op jit(solution)/shard_map/ppermute | solution.py:34
  107.0 9.9 %collective-permute-start.19 = (f32[4,1024]{1,0:T(4,128)S(1)}, f32[4,1024]{1,0:T(4,128)S(1)}, u32[]{:S(2)}, u32[]{:S(2)}) collective-permute-start(f32[4,1024]{1,0:T(4,128)S(1)} %add.167), channel_id=1, source_target_pairs={{0,128},{2,130},{4,132},{6,134},{8,136},{10,138},{12,140},{14,142}... | collective-permute-start | bytes 49160 | tf_op jit(solution)/shard_map/ppermute | solution.py:34
  110.1 5.9 %copy-start.5 = (bf16[256,1024]{0,1:T(8,128)(2,1)}, bf16[256,1024]{0,1:T(8,128)(2,1)S(1)}, u32[]{:S(2)}) copy-start(bf16[256,1024]{0,1:T(8,128)(2,1)S(1)} %collective-permute-done.7) | copy-start | bytes 1572868
  111.2 13.5 %collective-permute-start.9 = (bf16[256,1024]{0,1:T(8,128)(2,1)}, bf16[256,1024]{0,1:T(8,128)(2,1)}, u32[]{:S(2)}, u32[]{:S(2)}) collective-permute-start(bf16[256,1024]{0,1:T(8,128)(2,1)} %fusion.28), channel_id=1, source_target_pairs={{4,0},{6,2},{8,4},{10,6},{12,8},{14,10},{16,12},{18,14},{20,16},{2... | collective-permute-start | bytes 1572872 | tf_op jit(solution)/shard_map/ppermute | solution.py:20
  112.5 3.4 %copy-start.6 = (bf16[256,1024]{0,1:T(8,128)(2,1)}, bf16[256,1024]{0,1:T(8,128)(2,1)S(1)}, u32[]{:S(2)}) copy-start(bf16[256,1024]{0,1:T(8,128)(2,1)S(1)} %collective-permute-done.10) | copy-start | bytes 1572868
  113.9 16.5 %collective-permute-start.12 = (bf16[256,1024]{0,1:T(8,128)(2,1)}, bf16[256,1024]{0,1:T(8,128)(2,1)}, u32[]{:S(2)}, u32[]{:S(2)}) collective-permute-start(bf16[256,1024]{0,1:T(8,128)(2,1)} %fusion.33), channel_id=1, source_target_pairs={{4,0},{6,2},{8,4},{10,6},{12,8},{14,10},{16,12},{18,14},{20,16},{2... | collective-permute-start | bytes 1572872 | tf_op jit(solution)/shard_map/ppermute | solution.py:20
  116.0 14.4 %copy-start.7 = (bf16[256,1024]{0,1:T(8,128)(2,1)S(1)}, bf16[256,1024]{0,1:T(8,128)(2,1)}, u32[]{:S(2)}) copy-start(bf16[256,1024]{0,1:T(8,128)(2,1)} %copy-done.6) | copy-start | bytes 1572868
  (3 other events, 8.5 us)

commit v14 on v13

--- a/solution.py
+++ b/solution.py
@@ -165,8 +165,8 @@
     for tap_index in range(tap_count):
         value_sum = value_sum + conv_weight[tap_index] * padded_value[tap_index : tap_index + key_count + far_lead]
 
-    def relay_back(grads):
-        cut_third = row_count - far_rows + far_lead
+    def relay_back(grads, lead_rows):
+        cut_third = row_count - far_rows + lead_rows
         grad_third = grads[:cut_third]
         grad_second = grads[cut_third : cut_third + row_count]
         grad_first = grads[cut_third + row_count : cut_third + 2 * row_count]
@@ -174,14 +174,14 @@
         back_third = from_behind(grad_third.astype(jnp.bfloat16), "tm", -1).astype(jnp.float32)
         back_first = chip_swap(grad_first.astype(jnp.bfloat16), "tm").astype(jnp.float32)
         grad_second = grad_second + jnp.concatenate(
-            [jnp.zeros((far_rows - far_lead, grads.shape[1]), jnp.float32), back_third], 0
+            [jnp.zeros((far_rows - lead_rows, grads.shape[1]), jnp.float32), back_third], 0
         )
         grad_second = grad_second + jnp.where(even, 0.0, back_first)
         back_second = from_behind(grad_second.astype(jnp.bfloat16), "tm", -2).astype(jnp.float32)
         return grad_own + jnp.where(even, back_first, 0.0) + back_second
 
-    value_total = relay_back(value_sum)
-    key_total = relay_back(jnp.concatenate([lead, key_part], 0))
+    value_total = relay_back(value_sum, far_lead)
+    key_total = relay_back(key_part, 0)
 
     return (
         query_grad.reshape(row_count, channels).astype(jnp.bfloat16),

time: 135 us -> 137 us (1.015)
  starting transfers between devices: 39.2 us -> 42.6 us
  waiting for transfers between devices: 39.3 us -> 37.8 us
    ppermute x7, starting transfers between devices: 19.1 us -> 22.7 us  [all_sum(): lax.ppermute(block, axis, [(i, i ^ stride) for i in range(size)])]
    ppermute x7, waiting for transfers between devices: 12.4 us -> 10.1 us  [all_sum(): lax.ppermute(block, axis, [(i, i ^ stride) for i in range(size)])]
  transfers between devices with their start and end apart: 20 -> 20, of which waited for: 8 -> 10; matrix products, arithmetic and copies ran while one was open for 28% -> 27% of each run, Pallas kernels for 0% -> 0%
where the time goes in v14:
time: 137 us; the launch traced here: 135 us
  starting transfers between devices  42.6 us (31%)
  waiting for transfers between devices  37.8 us (28%)
  other arithmetic  31.2 us (23%)
  matrix products  12.7 us (9%)
  local copies, waits for them, and re-layouts  9.38 us (7%)
    ppermute x8, waiting for transfers between devices, from_behind(): return lax.ppermute(block, axis, route)  23.1 us
    ppermute x7, starting transfers between devices, all_sum(): lax.ppermute(block, axis, [(i, i ^ stride) for i in range(size)])  22.7 us
    ppermute x8, starting transfers between devices, from_behind(): return lax.ppermute(block, axis, route)  17.8 us
    ppermute x7, waiting for transfers between devices, all_sum(): lax.ppermute(block, axis, [(i, i ^ stride) for i in range(size)])  10.1 us
    sub x1, matrix products, body(): expo = jnp.where(mask[None], jnp.exp(scores - row_peak[..., None]), 0.0)  7.3 us
    unnamed x37, local copies, waits for them, and re-layouts  6.62 us
    another operation x1, other arithmetic  5.16 us
    ppermute x1, waiting for transfers between devices, pair_sum(): return block + lax.ppermute(block, axis, [(0, 1), (1, 0)])  4.5 us
  transfers between devices with their start and end apart: 20, of which 10 were waited for; matrix products, arithmetic and copies ran while one was open for 27% of the time, Pallas kernels for 0%

profile of v14, /device:TPU:4, one launch (start us, length us, event | category | flops | bytes accessed | tf_op | source)
XLA Modules:
  0.0 134.8 jit_solution(4331692941104904281)
XLA Ops:
  0.7 1.3 copy.59
  2.0 3.5 %collective-permute-start = (bf16[256,1024]{0,1:T(8,128)(2,1)S(1)}, bf16[256,1024]{0,1:T(8,128)(2,1)S(1)}, u32[]{:S(2)}, u32[]{:S(2)}) collective-permute-start(bf16[256,1024]{0,1:T(8,128)(2,1)S(1)} %copy.59), channel_id=1, source_target_pairs={{0,4},{2,6},{4,8},{6,10},{8,12},{10,14},{12,16},{14,18},{16,20},{1... | collective-permute-start | bytes 1572872 | tf_op jit(solution)/shard_map/ppermute | solution.py:20
  6.8 3.5 %collective-permute-start.3 = (bf16[256,1024]{0,1:T(8,128)(2,1)S(1)}, bf16[256,1024]{0,1:T(8,128)(2,1)S(1)}, u32[]{:S(2)}, u32[]{:S(2)}) collective-permute-start(bf16[256,1024]{0,1:T(8,128)(2,1)S(1)} %copy.65), channel_id=1, source_target_pairs={{0,4},{2,6},{4,8},{6,10},{8,12},{10,14},{12,16},{14,18},{16,20},{1... | collective-permute-start | bytes 1572872 | tf_op jit(solution)/shard_map/ppermute | solution.py:20
  11.4 6.4 %collective-permute-done = bf16[256,1024]{0,1:T(8,128)(2,1)S(1)} collective-permute-done((bf16[256,1024]{0,1:T(8,128)(2,1)S(1)}, bf16[256,1024]{0,1:T(8,128)(2,1)S(1)}, u32[]{:S(2)}, u32[]{:S(2)}) %collective-permute-start) | collective-permute-done | bytes 524320 | tf_op jit(solution)/shard_map/ppermute | solution.py:20
  20.9 2.4 %collective-permute-start.1 = (bf16[128,1024]{0,1:T(8,128)(2,1)S(1)}, bf16[128,1024]{0,1:T(8,128)(2,1)S(1)}, u32[]{:S(2)}, u32[]{:S(2)}) collective-permute-start(bf16[128,1024]{0,1:T(8,128)(2,1)S(1)} %slice.120), channel_id=1, source_target_pairs={{0,2},{2,4},{4,6},{6,8},{8,10},{10,12},{12,14},{14,16},{16,18},{18... | collective-permute-start | bytes 786440 | tf_op jit(solution)/shard_map/ppermute | solution.py:20
  23.3 5.7 %collective-permute-done.3 = bf16[256,1024]{0,1:T(8,128)(2,1)S(1)} collective-permute-done((bf16[256,1024]{0,1:T(8,128)(2,1)S(1)}, bf16[256,1024]{0,1:T(8,128)(2,1)S(1)}, u32[]{:S(2)}, u32[]{:S(2)}) %collective-permute-start.3) | collective-permute-done | bytes 524320 | tf_op jit(solution)/shard_map/ppermute | solution.py:20
  31.0 3.3 %collective-permute-start.4 = (bf16[136,1024]{0,1:T(8,128)(2,1)}, bf16[136,1024]{0,1:T(8,128)(2,1)}, u32[]{:S(2)}, u32[]{:S(2)}) collective-permute-start(bf16[136,1024]{0,1:T(8,128)(2,1)} %slice.121), channel_id=1, source_target_pairs={{0,2},{2,4},{4,6},{6,8},{8,10},{10,12},{12,14},{14,16},{16,18},{18... | collective-permute-start | bytes 835592 | tf_op jit(solution)/shard_map/ppermute | solution.py:20
  34.3 1.4 %pad_maximum_fusion.1 = bf16[896,1024]{0,1:T(8,128)(2,1)S(1)} fusion(bf16[256,1024]{0,1:T(8,128)(2,1)S(1)} %copy.59, bf16[256,1024]{0,1:T(8,128)(2,1)} %collective-permute-done.2, bf16[256,1024]{0,1:T(8,128)(2,1)} %copy-done.3, bf16[128,1024]{0,1:T(8,128)(2,1)S(1)} %collective-permute-done.1), kind=kLoop, calls=%fused_computation.35 | loop fusion | flops 7340032 | bytes 3670016 | tf_op jit(solution)/shard_map/concatenate | solution.py:81
  35.7 7.3 %fusion.57 = (f32[8,256]{1,0:T(8,128)S(1)}, f32[8,256,896]{1,2,0:T(8,128)}) fusion(pred[256,896]{0,1:T(8,128)(4,1)} %fusion.39, bf16[896,8,128]{0,2,1:T(8,128)(2,1)S(1)} %bitcast.100, bf16[256,8,128]{0,2,1:T(8,128)(2,1)} %bitcast.106), kind=kOutput, calls=%fused_computation.104 | convolution fusion | flops 478937984 | bytes 9936896 | tf_op jit(solution)/shard_map/sub | solution.py:104
  43.0 3.8 %fusion.16 = bf16[8,256,896]{1,2,0:T(8,128)(2,1)S(1)} fusion(f32[8,256,896]{1,2,0:T(8,128)} %get-tuple-element.36, f32[8,256]{1,0:T(8,128)S(1)} %get-tuple-element.35), kind=kLoop, calls=%fused_computation.33 | loop fusion | flops 3670016 | bytes 11018240 | tf_op jit(solution)/shard_map/convert_element_type | solution.py:107
  46.8 2.2 %pad_maximum_fusion = bf16[904,1024]{0,1:T(8,128)(2,1)S(1)} fusion(bf16[256,1024]{0,1:T(8,128)(2,1)S(1)} %copy.65, bf16[256,1024]{0,1:T(8,128)(2,1)} %collective-permute-done.5, bf16[256,1024]{0,1:T(8,128)(2,1)S(1)} %copy-done.2, bf16[136,1024]{0,1:T(8,128)(2,1)} %collective-permute-done.4), kind=kLoop, calls=%fused_computation.34 | loop fusion | flops 7405568 | bytes 3702784 | tf_op jit(solution)/shard_map/concatenate | solution.py:81
  49.1 3.4 %fusion.8 = bf16[896,1024]{0,1:T(8,128)(2,1)S(1)} fusion(f32[1024]{0:T(1024)S(1)} %bitcast.129, f32[1024]{0:T(1024)S(1)} %bitcast.131, f32[1024]{0:T(1024)S(1)} %bitcast.127, f32[1024]{0:T(1024)S(1)} %bitcast.125, bf16[904,1024]{0,1:T(8,128)(2,1)S(1)} %pad_maximum_fusion), kind=kLoop, calls=%fused_computation.23 | loop fusion | flops 11010048 | bytes 9191424 | tf_op jit(solution)/shard_map/convert_element_type | solution.py:91
  54.5 4.5 %collective-permute-done.6 = f32[3,256]{1,0:T(4,128)S(1)} collective-permute-done((f32[3,256]{1,0:T(4,128)S(1)}, f32[3,256]{1,0:T(4,128)S(1)}, u32[]{:S(2)}, u32[]{:S(2)}) %collective-permute-start.6) | collective-permute-done | bytes 3104 | tf_op jit(solution)/shard_map/ppermute | solution.py:42
  60.7 3.9 %fusion.9 = (f32[1024]{0:T(1024)S(1)}, f32[1024]{0:T(1024)S(1)}, f32[1024]{0:T(1024)S(1)}, f32[1024]{0:T(1024)S(1)}) fusion(bf16[904,1024]{0,1:T(8,128)(2,1)S(1)} %pad_maximum_fusion, f32[8,128,896]{2,1,0:T(8,128)S(1)} %fusion.59), kind=kLoop, calls=%fused_computation.24 | loop fusion | flops 11005952 | bytes 11026432 | tf_op jit(solution)/shard_map/reduce_sum | solution.py:152
  66.0 1.7 %collective-permute-start.14 = (f32[4,1024]{1,0:T(4,128)S(1)}, f32[4,1024]{1,0:T(4,128)S(1)}, u32[]{:S(2)}, u32[]{:S(2)}) collective-permute-start(f32[4,1024]{1,0:T(4,128)S(1)} %fusion.50), channel_id=1, source_target_pairs={{0,4},{2,6},{4,0},{6,2},{8,12},{10,14},{12,8},{14,10},{16,20},{18,... | collective-permute-start | bytes 49160 | tf_op jit(solution)/shard_map/ppermute | solution.py:34
  67.7 1.4 %multiply_convert_fusion = bf16[8,256,896]{1,2,0:T(8,128)(2,1)S(1)} fusion(f32[8,256]{1,0:T(8,128)S(1)} %bitcast.142, f32[8,256,896]{1,2,0:T(8,128)S(1)} %bitcast.103, f32[8,256]{1,0:T(8,128)S(1)} %get-tuple-element.35, bf16[256,8,128]{0,2,1:T(8,128)(2,1)S(1)} %bitcast.110, bf16[896,8,128]{0,2,1:T(8,128)(2,1)S(1)} %bitcast.105), kind=kOutput, calls=%fused_computation.2 | convolution fusion | flops 477102080 | bytes 13385728 | tf_op jit(solution)/shard_map/thd,uhd->htu/dot_general | solution.py:136
  69.8 3.4 %collective-permute-start.15 = (f32[4,1024]{1,0:T(4,128)S(1)}, f32[4,1024]{1,0:T(4,128)S(1)}, u32[]{:S(2)}, u32[]{:S(2)}) collective-permute-start(f32[4,1024]{1,0:T(4,128)S(1)} %fusion.74), channel_id=1, source_target_pairs={{0,8},{2,10},{4,12},{6,14},{8,0},{10,2},{12,4},{14,6},{16,24},{18,... | collective-permute-start | bytes 49160 | tf_op jit(solution)/shard_map/ppermute | solution.py:34
  75.2 2.2 %collective-permute-start.16 = (f32[4,1024]{1,0:T(4,128)S(1)}, f32[4,1024]{1,0:T(4,128)S(1)}, u32[]{:S(2)}, u32[]{:S(2)}) collective-permute-start(f32[4,1024]{1,0:T(4,128)S(1)} %add.162), channel_id=1, source_target_pairs={{0,16},{2,18},{4,20},{6,22},{8,24},{10,26},{12,28},{14,30},{16,0},... | collective-permute-start | bytes 49160 | tf_op jit(solution)/shard_map/ppermute | solution.py:34
  79.1 3.6 %collective-permute-start.17 = (f32[4,1024]{1,0:T(4,128)S(1)}, f32[4,1024]{1,0:T(4,128)S(1)}, u32[]{:S(2)}, u32[]{:S(2)}) collective-permute-start(f32[4,1024]{1,0:T(4,128)S(1)} %add.163), channel_id=1, source_target_pairs={{0,32},{2,34},{4,36},{6,38},{8,40},{10,42},{12,44},{14,46},{16,48}... | collective-permute-start | bytes 49160 | tf_op jit(solution)/shard_map/ppermute | solution.py:34
  82.8 5.2 %fusion.51 = (bf16[904,1024]{0,1:T(8,128)(2,1)S(1)}, f32[904,1024]{0,1:T(8,128)S(1)}) fusion(f32[907,1024]{0,1:T(8,128)S(1)} %maximum_maximum_fusion, f32[1024]{0:T(1024)S(1)} %bitcast.130, f32[1024]{0:T(1024)S(1)} %bitcast.132, f32[1024]{0:T(1024)S(1)} %bitcast.128, f32[896,1024]{0,1:T(8,128)S(1)} %bitcast.99, f32[1024]{0:T(1024)S(1)} %bitcast.126), kind=kLoop, calls=%fused_computation.100 | loop fusion | flops 7405568 | bytes 20348928 | tf_op jit(solution)/shard_map/convert.5
  88.3 1.3 collective-permute-start.8
  90.8 1.3 collective-permute-start.11
  92.1 4.9 %collective-permute-start.18 = (f32[4,1024]{1,0:T(4,128)S(1)}, f32[4,1024]{1,0:T(4,128)S(1)}, u32[]{:S(2)}, u32[]{:S(2)}) collective-permute-start(f32[4,1024]{1,0:T(4,128)S(1)} %add.164), channel_id=1, source_target_pairs={{0,64},{2,66},{4,68},{6,70},{8,72},{10,74},{12,76},{14,78},{16,80}... | collective-permute-start | bytes 49160 | tf_op jit(solution)/shard_map/ppermute | solution.py:34
  97.2 7.3 %collective-permute-done.18 = f32[4,1024]{1,0:T(4,128)S(1)} collective-permute-done((f32[4,1024]{1,0:T(4,128)S(1)}, f32[4,1024]{1,0:T(4,128)S(1)}, u32[]{:S(2)}, u32[]{:S(2)}) %collective-permute-start.18) | collective-permute-done | bytes 16416 | tf_op jit(solution)/shard_map/ppermute | solution.py:34
  104.6 6.5 %collective-permute-start.19 = (f32[4,1024]{1,0:T(4,128)S(1)}, f32[4,1024]{1,0:T(4,128)S(1)}, u32[]{:S(2)}, u32[]{:S(2)}) collective-permute-start(f32[4,1024]{1,0:T(4,128)S(1)} %add.165), channel_id=1, source_target_pairs={{0,128},{2,130},{4,132},{6,134},{8,136},{10,138},{12,140},{14,142}... | collective-permute-start | bytes 49160 | tf_op jit(solution)/shard_map/ppermute | solution.py:34
  112.2 1.3 collective-permute-start.9
  113.5 1.3 fusion.33
  114.8 1.3 collective-permute-start.12
  118.5 7.8 %collective-permute-done.9 = bf16[256,1024]{0,1:T(8,128)(2,1)} collective-permute-done((bf16[256,1024]{0,1:T(8,128)(2,1)}, bf16[256,1024]{0,1:T(8,128)(2,1)}, u32[]{:S(2)}, u32[]{:S(2)}) %collective-permute-start.9) | collective-permute-done | bytes 524320 | tf_op jit(solution)/shard_map/ppermute | solution.py:20
  126.3 1.4 %fusion.26 = bf16[256,1024]{0,1:T(8,128)(2,1)S(1)} fusion(bf16[256,1024]{0,1:T(8,128)(2,1)} %copy-done.5, f32[256,8,128]{0,2,1:T(8,128)S(1)} %get-tuple-element.27, bf16[256,1024]{0,1:T(8,128)(2,1)} %collective-permute-done.9, pred[]{:T(512)S(6)} %eq.29), kind=kLoop, calls=%fused_computation.52 | loop fusion | flops 1572864 | bytes 2621441 | tf_op jit(solution)/shard_map/convert_element_type | solution.py:188
  128.7 3.2 %collective-permute-done.12 = bf16[256,1024]{0,1:T(8,128)(2,1)} collective-permute-done((bf16[256,1024]{0,1:T(8,128)(2,1)}, bf16[256,1024]{0,1:T(8,128)(2,1)}, u32[]{:S(2)}, u32[]{:S(2)}) %collective-permute-start.12) | collective-permute-done | bytes 524320 | tf_op jit(solution)/shard_map/ppermute | solution.py:20
  131.9 1.9 %fusion.31 = bf16[256,1024]{0,1:T(8,128)(2,1)S(1)} fusion(bf16[256,1024]{0,1:T(8,128)(2,1)S(1)} %copy-done.7, f32[904,1024]{0,1:T(8,128)} %copy-done, bf16[256,1024]{0,1:T(8,128)(2,1)} %collective-permute-done.12, pred[]{:T(512)S(6)} %eq.29), kind=kLoop, calls=%fused_computation.57 | loop fusion | flops 1572864 | bytes 2621441 | tf_op jit(solution)/shard_map/convert_element_type | solution.py:189
  (102 shorter events, 23.9 us)
Async XLA Ops:
  0.6 18.1 %copy-start.8 = (bf16[256,1024]{1,0:T(8,128)(2,1)S(1)}, bf16[256,1024]{1,0:T(8,128)(2,1)}, u32[]{:S(2)}) copy-start(bf16[256,1024]{1,0:T(8,128)(2,1)} %param.8) | copy-start | bytes 1572868
  0.6 19.1 %copy-start.9 = (bf16[256,1024]{1,0:T(8,128)(2,1)S(1)}, bf16[256,1024]{1,0:T(8,128)(2,1)}, u32[]{:S(2)}) copy-start(bf16[256,1024]{1,0:T(8,128)(2,1)} %param.11) | copy-start | bytes 1572868
  0.7 20.2 %copy-start.11 = (f32[4,1024]{1,0:T(4,128)S(1)}, f32[4,1024]{1,0:T(4,128)}, u32[]{:S(2)}) copy-start(f32[4,1024]{1,0:T(4,128)} %param.13) | copy-start | bytes 49156
  2.0 15.8 %collective-permute-start = (bf16[256,1024]{0,1:T(8,128)(2,1)S(1)}, bf16[256,1024]{0,1:T(8,128)(2,1)S(1)}, u32[]{:S(2)}, u32[]{:S(2)}) collective-permute-start(bf16[256,1024]{0,1:T(8,128)(2,1)S(1)} %copy.59), channel_id=1, source_target_pairs={{0,4},{2,6},{4,8},{6,10},{8,12},{10,14},{12,16},{14,18},{16,20},{1... | collective-permute-start | bytes 1572872 | tf_op jit(solution)/shard_map/ppermute | solution.py:20
  6.8 22.3 %collective-permute-start.3 = (bf16[256,1024]{0,1:T(8,128)(2,1)S(1)}, bf16[256,1024]{0,1:T(8,128)(2,1)S(1)}, u32[]{:S(2)}, u32[]{:S(2)}) collective-permute-start(bf16[256,1024]{0,1:T(8,128)(2,1)S(1)} %copy.65), channel_id=1, source_target_pairs={{0,4},{2,6},{4,8},{6,10},{8,12},{10,14},{12,16},{14,18},{16,20},{1... | collective-permute-start | bytes 1572872 | tf_op jit(solution)/shard_map/ppermute | solution.py:20
  17.8 16.5 %copy-start.3 = (bf16[256,1024]{0,1:T(8,128)(2,1)}, bf16[256,1024]{0,1:T(8,128)(2,1)S(1)}, u32[]{:S(2)}) copy-start(bf16[256,1024]{0,1:T(8,128)(2,1)S(1)} %collective-permute-done) | copy-start | bytes 1572868
  18.7 15.6 %collective-permute-start.2 = (bf16[256,1024]{0,1:T(8,128)(2,1)}, bf16[256,1024]{0,1:T(8,128)(2,1)}, u32[]{:S(2)}, u32[]{:S(2)}) collective-permute-start(bf16[256,1024]{0,1:T(8,128)(2,1)} %broadcast_select_fusion.1), channel_id=1, source_target_pairs={{0,2},{2,0},{4,6},{6,4},{8,10},{10,8},{12,14},{14,12},{16,18},{18,... | collective-permute-start | bytes 1572872 | tf_op jit(solution)/shard_map/ppermute | solution.py:25
  20.9 13.4 %collective-permute-start.1 = (bf16[128,1024]{0,1:T(8,128)(2,1)S(1)}, bf16[128,1024]{0,1:T(8,128)(2,1)S(1)}, u32[]{:S(2)}, u32[]{:S(2)}) collective-permute-start(bf16[128,1024]{0,1:T(8,128)(2,1)S(1)} %slice.120), channel_id=1, source_target_pairs={{0,2},{2,4},{4,6},{6,8},{8,10},{10,12},{12,14},{14,16},{16,18},{18... | collective-permute-start | bytes 786440 | tf_op jit(solution)/shard_map/ppermute | solution.py:20
  29.0 5.2 %copy-start.1 = (bf16[256,1024]{0,1:T(8,128)(2,1)}, bf16[256,1024]{0,1:T(8,128)(2,1)S(1)}, u32[]{:S(2)}) copy-start(bf16[256,1024]{0,1:T(8,128)(2,1)S(1)} %collective-permute-done.3) | copy-start | bytes 1572868
  30.0 16.8 %collective-permute-start.5 = (bf16[256,1024]{0,1:T(8,128)(2,1)}, bf16[256,1024]{0,1:T(8,128)(2,1)}, u32[]{:S(2)}, u32[]{:S(2)}) collective-permute-start(bf16[256,1024]{0,1:T(8,128)(2,1)} %broadcast_select_fusion), channel_id=1, source_target_pairs={{0,2},{2,0},{4,6},{6,4},{8,10},{10,8},{12,14},{14,12},{16,18},{18,... | collective-permute-start | bytes 1572872 | tf_op jit(solution)/shard_map/ppermute | solution.py:25
  31.0 15.8 %collective-permute-start.4 = (bf16[136,1024]{0,1:T(8,128)(2,1)}, bf16[136,1024]{0,1:T(8,128)(2,1)}, u32[]{:S(2)}, u32[]{:S(2)}) collective-permute-start(bf16[136,1024]{0,1:T(8,128)(2,1)} %slice.121), channel_id=1, source_target_pairs={{0,2},{2,4},{4,6},{6,8},{8,10},{10,12},{12,14},{14,16},{16,18},{18... | collective-permute-start | bytes 835592 | tf_op jit(solution)/shard_map/ppermute | solution.py:20
  43.0 3.8 %copy-start.2 = (bf16[256,1024]{0,1:T(8,128)(2,1)S(1)}, bf16[256,1024]{0,1:T(8,128)(2,1)}, u32[]{:S(2)}) copy-start(bf16[256,1024]{0,1:T(8,128)(2,1)} %copy-done.1) | copy-start | bytes 1572868
  53.6 5.4 %collective-permute-start.6 = (f32[3,256]{1,0:T(4,128)S(1)}, f32[3,256]{1,0:T(4,128)S(1)}, u32[]{:S(2)}, u32[]{:S(2)}) collective-permute-start(f32[3,256]{1,0:T(4,128)S(1)} %pad_maximum_fusion.3), channel_id=1, source_target_pairs={{0,1},{1,0},{2,3},{3,2},{4,5},{5,4},{6,7},{7,6},{8,9},{9,8},{10,11... | collective-permute-start | bytes 9224 | tf_op jit(solution)/shard_map/ppermute | solution.py:42
  59.5 8.2 %slice-start = ((s8[7340032]{0:T(1024)(128)(4,1)}), s8[4194304]{0:T(1024)(128)(4,1)S(1)}, s32[]{:S(2)}) async-start(s8[7340032]{0:T(1024)(128)(4,1)} %bitcast.102), calls=%async_computation | async-start | bytes 8388608
  60.7 7.0 %slice-start.1 = ((s8[7340032]{0:T(1024)(128)(4,1)}), s8[3145728]{0:T(1024)(128)(4,1)S(1)}, s32[]{:S(2)}) async-start(s8[7340032]{0:T(1024)(128)(4,1)} %bitcast.102), calls=%async_computation.1 | async-start | bytes 6291456
  64.7 1.3 collective-permute-start.13
  66.0 3.8 %collective-permute-start.14 = (f32[4,1024]{1,0:T(4,128)S(1)}, f32[4,1024]{1,0:T(4,128)S(1)}, u32[]{:S(2)}, u32[]{:S(2)}) collective-permute-start(f32[4,1024]{1,0:T(4,128)S(1)} %fusion.50), channel_id=1, source_target_pairs={{0,4},{2,6},{4,0},{6,2},{8,12},{10,14},{12,8},{14,10},{16,20},{18,... | collective-permute-start | bytes 49160 | tf_op jit(solution)/shard_map/ppermute | solution.py:34
  67.7 5.5 %copy-start.4 = (bf16[256,1024]{0,1:T(8,128)(2,1)S(1)}, bf16[256,1024]{0,1:T(8,128)(2,1)}, u32[]{:S(2)}) copy-start(bf16[256,1024]{0,1:T(8,128)(2,1)} %copy.88) | copy-start | bytes 1572868
  69.8 5.3 %collective-permute-start.15 = (f32[4,1024]{1,0:T(4,128)S(1)}, f32[4,1024]{1,0:T(4,128)S(1)}, u32[]{:S(2)}, u32[]{:S(2)}) collective-permute-start(f32[4,1024]{1,0:T(4,128)S(1)} %fusion.74), channel_id=1, source_target_pairs={{0,8},{2,10},{4,12},{6,14},{8,0},{10,2},{12,4},{14,6},{16,24},{18,... | collective-permute-start | bytes 49160 | tf_op jit(solution)/shard_map/ppermute | solution.py:34
  74.4 36.7 %collective-permute-start.7 = (bf16[256,1024]{0,1:T(8,128)(2,1)S(1)}, bf16[256,1024]{0,1:T(8,128)(2,1)S(1)}, u32[]{:S(2)}, u32[]{:S(2)}) collective-permute-start(bf16[256,1024]{0,1:T(8,128)(2,1)S(1)} %bitcast.111), channel_id=1, source_target_pairs={{0,2},{2,0},{4,6},{6,4},{8,10},{10,8},{12,14},{14,12},{16,18},{18,... | collective-permute-start | bytes 1572872 | tf_op jit(solution)/shard_map/ppermute | solution.py:25
  75.2 4.0 %collective-permute-start.16 = (f32[4,1024]{1,0:T(4,128)S(1)}, f32[4,1024]{1,0:T(4,128)S(1)}, u32[]{:S(2)}, u32[]{:S(2)}) collective-permute-start(f32[4,1024]{1,0:T(4,128)S(1)} %add.162), channel_id=1, source_target_pairs={{0,16},{2,18},{4,20},{6,22},{8,24},{10,26},{12,28},{14,30},{16,0},... | collective-permute-start | bytes 49160 | tf_op jit(solution)/shard_map/ppermute | solution.py:34
  79.1 13.0 %collective-permute-start.17 = (f32[4,1024]{1,0:T(4,128)S(1)}, f32[4,1024]{1,0:T(4,128)S(1)}, u32[]{:S(2)}, u32[]{:S(2)}) collective-permute-start(f32[4,1024]{1,0:T(4,128)S(1)} %add.163), channel_id=1, source_target_pairs={{0,32},{2,34},{4,36},{6,38},{8,40},{10,42},{12,44},{14,46},{16,48}... | collective-permute-start | bytes 49160 | tf_op jit(solution)/shard_map/ppermute | solution.py:34
  87.9 25.5 %copy-start = (f32[904,1024]{0,1:T(8,128)}, f32[904,1024]{0,1:T(8,128)S(1)}, u32[]{:S(2)}) copy-start(f32[904,1024]{0,1:T(8,128)S(1)} %get-tuple-element.23) | copy-start | bytes 11108356
  88.3 22.8 %collective-permute-start.8 = (bf16[128,1024]{0,1:T(8,128)(2,1)S(1)}, bf16[128,1024]{0,1:T(8,128)(2,1)S(1)}, u32[]{:S(2)}, u32[]{:S(2)}) collective-permute-start(bf16[128,1024]{0,1:T(8,128)(2,1)S(1)} %bitcast.112), channel_id=1, source_target_pairs={{2,0},{4,2},{6,4},{8,6},{10,8},{12,10},{14,12},{16,14},{18,16},{20... | collective-permute-start | bytes 786440 | tf_op jit(solution)/shard_map/ppermute | solution.py:20
  89.6 23.8 %collective-permute-start.10 = (bf16[256,1024]{0,1:T(8,128)(2,1)S(1)}, bf16[256,1024]{0,1:T(8,128)(2,1)S(1)}, u32[]{:S(2)}, u32[]{:S(2)}) collective-permute-start(bf16[256,1024]{0,1:T(8,128)(2,1)S(1)} %slice.137), channel_id=1, source_target_pairs={{0,2},{2,0},{4,6},{6,4},{8,10},{10,8},{12,14},{14,12},{16,18},{18,... | collective-permute-start | bytes 1572872 | tf_op jit(solution)/shard_map/ppermute | solution.py:25
  90.8 22.6 %collective-permute-start.11 = (bf16[136,1024]{0,1:T(8,128)(2,1)S(1)}, bf16[136,1024]{0,1:T(8,128)(2,1)S(1)}, u32[]{:S(2)}, u32[]{:S(2)}) collective-permute-start(bf16[136,1024]{0,1:T(8,128)(2,1)S(1)} %slice.139), channel_id=1, source_target_pairs={{2,0},{4,2},{6,4},{8,6},{10,8},{12,10},{14,12},{16,14},{18,16},{20... | collective-permute-start | bytes 835592 | tf_op jit(solution)/shard_map/ppermute | solution.py:20
  92.1 12.4 %collective-permute-start.18 = (f32[4,1024]{1,0:T(4,128)S(1)}, f32[4,1024]{1,0:T(4,128)S(1)}, u32[]{:S(2)}, u32[]{:S(2)}) collective-permute-start(f32[4,1024]{1,0:T(4,128)S(1)} %add.164), channel_id=1, source_target_pairs={{0,64},{2,66},{4,68},{6,70},{8,72},{10,74},{12,76},{14,78},{16,80}... | collective-permute-start | bytes 49160 | tf_op jit(solution)/shard_map/ppermute | solution.py:34
  104.6 13.3 %collective-permute-start.19 = (f32[4,1024]{1,0:T(4,128)S(1)}, f32[4,1024]{1,0:T(4,128)S(1)}, u32[]{:S(2)}, u32[]{:S(2)}) collective-permute-start(f32[4,1024]{1,0:T(4,128)S(1)} %add.165), channel_id=1, source_target_pairs={{0,128},{2,130},{4,132},{6,134},{8,136},{10,138},{12,140},{14,142}... | collective-permute-start | bytes 49160 | tf_op jit(solution)/shard_map/ppermute | solution.py:34
  111.1 5.7 %copy-start.5 = (bf16[256,1024]{0,1:T(8,128)(2,1)}, bf16[256,1024]{0,1:T(8,128)(2,1)S(1)}, u32[]{:S(2)}) copy-start(bf16[256,1024]{0,1:T(8,128)(2,1)S(1)} %collective-permute-done.7) | copy-start | bytes 1572868
  112.2 14.1 %collective-permute-start.9 = (bf16[256,1024]{0,1:T(8,128)(2,1)}, bf16[256,1024]{0,1:T(8,128)(2,1)}, u32[]{:S(2)}, u32[]{:S(2)}) collective-permute-start(bf16[256,1024]{0,1:T(8,128)(2,1)} %fusion.28), channel_id=1, source_target_pairs={{4,0},{6,2},{8,4},{10,6},{12,8},{14,10},{16,12},{18,14},{20,16},{2... | collective-permute-start | bytes 1572872 | tf_op jit(solution)/shard_map/ppermute | solution.py:20
  114.8 17.1 %collective-permute-start.12 = (bf16[256,1024]{0,1:T(8,128)(2,1)}, bf16[256,1024]{0,1:T(8,128)(2,1)}, u32[]{:S(2)}, u32[]{:S(2)}) collective-permute-start(bf16[256,1024]{0,1:T(8,128)(2,1)} %fusion.33), channel_id=1, source_target_pairs={{4,0},{6,2},{8,4},{10,6},{12,8},{14,10},{16,12},{18,14},{20,16},{2... | collective-permute-start | bytes 1572872 | tf_op jit(solution)/shard_map/ppermute | solution.py:20
  116.9 15.0 %copy-start.7 = (bf16[256,1024]{0,1:T(8,128)(2,1)S(1)}, bf16[256,1024]{0,1:T(8,128)(2,1)}, u32[]{:S(2)}) copy-start(bf16[256,1024]{0,1:T(8,128)(2,1)} %copy-done.6) | copy-start | bytes 1572868
  (3 other events, 8.7 us)
